TPU v7x, 512 devices: a whole 4x8x8 slice. The times are simulated.
512 devices in a mesh: tm: 128 (over y, x, z_hi, core), stream: 4 (over z_lo).
Axes of the slice: x: 4, y: 8, z: 8 (z_hi: 2, z_lo: 4; z = z_hi * 4 + z_lo), core: 2. Of those that a mesh axis runs over, the one named last changes fastest.
Arguments:
- series: bfloat16 [4, 16384, 1024], P('stream', 'tm')
- loss_grad: bfloat16 [4, 16384, 1024], P('stream', 'tm'), may hold values from -6 to 6
- query_weight: bfloat16 [1024, 1024], P('stream')
- keyval_weight: bfloat16 [1024, 512], P('stream')
- output_weight: bfloat16 [1024, 1024], P('stream'), may hold values from -0.1875 to 0.1875
- lengths: int32 [4], P('stream'), may hold values from 1 to 16384, as said below
Outputs:
- series_grad: bfloat16 [4, 16384, 1024], P('stream', 'tm')
- keyval_grad: float32 [1024, 512], P('stream')
Inputs may be any that keep to these rules, and one draw needn't show every extreme that they name: `lengths`: one recording in every draw has all 16384 positions valid.
All inputs are finite; a program needn't handle non-finite values.
Results may differ from a plain program's by a relative error of at most 0.025.
The roundings to bfloat16 on the way count: a program that leaves them out, or rounds other values in their place, can miss the bound.
Values may be sent and summed in bfloat16 or wider, within the bound.
No kernel may reach another device: no remote copies, remote signals or barrier semaphores. Data moves between devices by JAX's collectives and lax.ppermute only.
A program may use at most 64 MiB of HBM per device.

v0:
```python
import jax
import jax.numpy as jnp
from jax import lax
from jax.sharding import PartitionSpec as P

HEADS = 16
KV_HEADS = 4
HEAD_DIM = 64
REACH = 4


def shifted(value, axis, steps):
    count = lax.axis_size(axis)
    leading, last = (max(0, -steps), min(count, count - steps))
    return lax.ppermute(value, axis, [(source, source + steps) for source in range(leading, last)])


def contract_last(left, right):
    return lax.dot_general(
        left, right, (((1,), (1,)), ((), ())), preferred_element_type=jnp.float32
    )


def contract_first(left, right):
    return lax.dot_general(
        left, right, (((0,), (0,)), ((), ())), preferred_element_type=jnp.float32
    )


def per_device(series, loss_grad, query_weight, keyval_weight, output_weight, lengths):
    record_rows = series[0]
    outer_grad = loss_grad[0]
    valid_count = lengths[0]
    shard_tokens = record_rows.shape[0]
    keyval_width = keyval_weight.shape[1]
    key_width = keyval_width // 2
    group_size = HEADS // KV_HEADS
    tile_rows = min(128, shard_tokens)
    key_span = REACH * shard_tokens + tile_rows
    score_scale = HEAD_DIM ** (-0.5)
    anchor = lax.axis_index("tm") * shard_tokens
    query_full, keyval_full = (
        lax.all_gather(query_weight, "stream", axis=0, tiled=True),
        lax.all_gather(keyval_weight, "stream", axis=0, tiled=True),
    )
    queries = jnp.dot(record_rows, query_full, preferred_element_type=jnp.float32).astype(
        jnp.bfloat16
    )
    keyvals = jnp.dot(record_rows, keyval_full, preferred_element_type=jnp.float32).astype(
        jnp.bfloat16
    )
    attn_grad = contract_last(
        outer_grad, lax.all_gather(output_weight, "stream", axis=0, tiled=True)
    ).astype(jnp.bfloat16)
    earlier = [shifted(keyvals, "tm", offset) for offset in range(REACH, 0, -1)]
    window_keyvals = jnp.concatenate(earlier + [keyvals], axis=0)
    key_parts = []
    value_parts = []
    query_grads = []
    for head_group in range(KV_HEADS):
        query_cols = slice(
            head_group * group_size * HEAD_DIM, (head_group + 1) * group_size * HEAD_DIM
        )
        key_cols = slice(head_group * HEAD_DIM, (head_group + 1) * HEAD_DIM)
        value_cols = slice(
            key_width + head_group * HEAD_DIM, key_width + (head_group + 1) * HEAD_DIM
        )
        group_key = None
        group_value = None
        query_tile = queries[0:tile_rows, query_cols].reshape(tile_rows, group_size, HEAD_DIM)
        key_tile = window_keyvals[0:key_span, key_cols]
        value_tile = window_keyvals[0:key_span, value_cols]
        query_pos = anchor + 0 + jnp.arange(tile_rows, dtype=jnp.int32)
        key_pos = anchor - REACH * shard_tokens + 0 + jnp.arange(key_span, dtype=jnp.int32)
        live_rows = query_pos < valid_count
        allowed = (key_pos[None, :] <= query_pos[:, None]) & (
            query_pos[:, None] - key_pos[None, :] < REACH * shard_tokens
        )
        allowed = (
            allowed
            & (key_pos[None, :] >= 0)
            & (key_pos[None, :] < valid_count)
            & live_rows[:, None]
        )
        scores = (
            jnp.einsum("qjd,kd->jqk", query_tile, key_tile, preferred_element_type=jnp.float32)
            * score_scale
        )
        masked = jnp.where(allowed, scores, -1e30)
        row_max = jnp.max(masked, axis=-1, keepdims=True)
        terms = jnp.where(allowed, jnp.exp(masked - row_max), 0.0)
        denom = jnp.sum(terms, axis=-1, keepdims=True)
        denom = jnp.where(live_rows[:, None], denom, 1.0)
        attn_probs = (terms / denom).astype(jnp.bfloat16)
        attn_tile = jnp.einsum(
            "jqk,kd->qjd", attn_probs, value_tile, preferred_element_type=jnp.float32
        ).astype(jnp.bfloat16)
        grad_tile = attn_grad[0:tile_rows, query_cols].reshape(tile_rows, group_size, HEAD_DIM)
        row_delta = jnp.sum(
            grad_tile.astype(jnp.float32) * attn_tile.astype(jnp.float32), axis=-1
        ).T[:, :, None]
        prob_grad = jnp.einsum(
            "qjd,kd->jqk", grad_tile, value_tile, preferred_element_type=jnp.float32
        )
        score_grad = (
            attn_probs.astype(jnp.float32) * (prob_grad - row_delta) * score_scale
        ).astype(jnp.bfloat16)
        query_grad = jnp.einsum(
            "jqk,kd->qjd", score_grad, key_tile, preferred_element_type=jnp.float32
        ).astype(jnp.bfloat16)
        key_grad = jnp.einsum(
            "jqk,qjd->kd", score_grad, query_tile, preferred_element_type=jnp.float32
        )
        value_grad = jnp.einsum(
            "jqk,qjd->kd", attn_probs, grad_tile, preferred_element_type=jnp.float32
        )
        group_key = key_grad
        group_value = value_grad
        tile_list = query_grad.reshape(tile_rows, group_size * HEAD_DIM)
        key_parts.append(group_key)
        value_parts.append(group_value)
        query_grads.append(tile_list)
    query_grad_all = jnp.concatenate(query_grads, axis=1)
    partial_value = jnp.concatenate(key_parts + value_parts, axis=1)

    def shard_slot(offset):
        return partial_value[(REACH - offset) * shard_tokens : (REACH - offset + 1) * shard_tokens]

    summed = shard_slot(0)
    for offset in range(1, REACH + 1):
        summed = summed + shifted(shard_slot(offset).astype(jnp.bfloat16), "tm", -offset).astype(
            jnp.float32
        )
    keyval_grads = summed.astype(jnp.bfloat16)
    input_grad = contract_last(query_grad_all, query_full) + contract_last(
        keyval_grads, keyval_full
    )
    input_grad = input_grad.astype(jnp.bfloat16)
    grad_shard = lax.psum_scatter(
        contract_first(record_rows, keyval_grads).astype(jnp.bfloat16),
        "stream",
        scatter_dimension=0,
        tiled=True,
    ).astype(jnp.float32)
    weight_grad = lax.psum(grad_shard, "tm")
    return (input_grad[None], weight_grad)


def solution(mesh):
    placed = (
        P("stream", "tm", None),
        P("stream", "tm", None),
        P("stream", None),
        P("stream", None),
        P("stream", None),
        P("stream"),
    )
    return jax.shard_map(
        per_device,
        mesh=mesh,
        in_specs=placed,
        out_specs=(P("stream", "tm", None), P("stream", None)),
        check_vma=False,
    )
```

profile of v0, /device:TPU:1, one launch (start us, length us, event | category | flops | bytes accessed | tf_op | source)
XLA Modules:
  0.0 1054.6 jit_solution(8423110423319587656)
XLA Ops:
  7.2 0.7 all-gather.4.cloned.1.call-update
  8.0 0.7 all-gather.8.cloned.1.call-update
  8.7 0.7 all-gather.6.cloned.1.call-update
  10.2 41.8 %all-gather.4.cloned.1.call-done = bf16[1024,512]{1,0:T(8,128)(2,1)} async-done(((bf16[256,512]{1,0:T(8,128)(2,1)}), bf16[1024,512]{1,0:T(8,128)(2,1)}) %all-gather.4.cloned.1.call-update) | async-done | bytes 1048592 | tf_op jit(solution)/shard_map/all_gather | solution.py:44
  52.0 1.5 convolution_convert_fusion.3
  53.5 3.9 collective-permute-start.1
  57.4 3.1 collective-permute-start
  60.5 0.3 fusion.70
  60.9 6.8 collective-permute-start.3
  67.7 5.6 collective-permute-start.2
  73.3 6.6 collective-permute-done.2
  79.9 33.0 %all-gather.8.cloned.1.call-done = bf16[1024,1024]{1,0:T(8,128)(2,1)} async-done(((bf16[256,1024]{1,0:T(8,128)(2,1)}), bf16[1024,1024]{1,0:T(8,128)(2,1)}) %all-gather.8.cloned.1.call-update) | async-done | bytes 2097168 | tf_op jit(solution)/shard_map/all_gather | solution.py:53
  113.0 2.4 convolution_convert_fusion.1
  115.4 0.7 copy.63
  116.2 0.7 copy.87
  116.9 0.7 copy.79
  117.6 0.7 copy.71
  118.4 49.5 %all-gather.6.cloned.1.call-done = bf16[1024,1024]{1,0:T(8,128)(2,1)} async-done(((bf16[256,1024]{1,0:T(8,128)(2,1)}), bf16[1024,1024]{1,0:T(8,128)(2,1)}) %all-gather.6.cloned.1.call-update) | async-done | bytes 2097168 | tf_op jit(solution)/shard_map/all_gather | solution.py:43
  167.9 2.0 convolution_convert_fusion.2
  170.0 0.7 copy.61
  171.0 0.7 copy.69
  171.7 0.7 fusion.108
  172.4 1.7 fusion.107
  174.1 1.7 fusion.106
  175.8 3.2 fusion.105
  179.0 0.7 broadcast_select_fusion.3
  179.8 0.4 fusion.66
  180.2 0.4 fusion.40
  180.6 0.5 copy-done.4
  181.2 0.3 copy-done.8
  181.5 0.3 fusion.65
  181.8 0.4 fusion.39
  182.3 0.7 copy-done.10
  183.0 0.4 fusion.64
  183.4 0.4 fusion.38
  183.9 0.7 copy-done.9
  184.6 0.3 fusion.63
  184.9 0.4 fusion.37
  185.3 0.3 fusion.50
  185.7 0.3 fusion.49
  186.1 0.3 fusion.48
  186.4 0.3 fusion.47
  186.7 0.3 fusion.46
  187.1 0.3 fusion.45
  187.4 0.3 fusion.44
  187.7 0.3 fusion.43
  188.2 2.9 collective-permute-start.4
  191.1 1.3 collective-permute-start.7
  192.4 1.3 collective-permute-start.6
  193.7 1.3 collective-permute-start.5
  195.0 3.5 collective-permute-done.4
  198.5 4.1 collective-permute-done.6
  202.6 3.5 collective-permute-done.5
  206.2 0.6 copy-done.5
  206.8 1.4 fusion.36
  208.3 0.3 convolution_convert_fusion.4
  208.9 0.3 convolution_convert_fusion.8
  209.5 0.7 copy-done.1
  210.2 0.8 fusion.75
  211.1 0.4 copy-done.2
  211.5 1.2 fusion.42
  212.7 37.9 %reduce-scatter.2.cloned.1.call-done = bf16[256,512]{0,1:T(8,128)(2,1)} async-done(((bf16[1024,512]{0,1:T(8,128)(2,1)}), bf16[256,512]{0,1:T(8,128)(2,1)}) %reduce-scatter.2.cloned.1.call-update) | async-done | bytes 262160 | tf_op jit(solution)/shard_map/reduce_scatter | solution.py:139
  250.5 796.5 %all-reduce.1 = f32[256,512]{0,1:T(8,128)S(1)} all-reduce(bf16[256,512]{0,1:T(8,128)(2,1)} %reduce-scatter.2.cloned.1.call-done), channel_id=1, replica_groups=mesh['tm'=128,'stream'=4] {'tm'}, use_global_device_ids=true, to_apply=%region_13.14 | all-reduce | flops 131072 | bytes 786432 | tf_op jit(solution)/shard_map/psum | solution.py:145
  1047.0 1.0 copy.101
  (62 shorter events, 1.9 us)
Async XLA Ops:
  7.2 44.8 %copy-start = (bf16[1,128,1024]{2,1,0:T(8,128)(2,1)S(1)}, bf16[1,128,1024]{2,1,0:T(8,128)(2,1)}, u32[]{:S(2)}) copy-start(bf16[1,128,1024]{2,1,0:T(8,128)(2,1)} %param.6) | copy-start | bytes 786436
  7.2 44.8 %all-gather.4.cloned.1.call-start = ((), (), s32[]{:S(2)}) async-start(), calls=%async_computation.1 | async-start | bytes 1310720 | tf_op jit(solution)/shard_map/all_gather | solution.py:44
  7.9 105.1 %all-gather.8.cloned.1.call-start = ((), (), s32[]{:S(2)}) async-start(), calls=%async_computation.3 | async-start | bytes 2621440 | tf_op jit(solution)/shard_map/all_gather | solution.py:53
  8.7 159.2 %all-gather.6.cloned.1.call-start = ((), (), s32[]{:S(2)}) async-start(), calls=%async_computation.2 | async-start | bytes 2621440 | tf_op jit(solution)/shard_map/all_gather | solution.py:43
  9.4 241.1 %reduce-scatter.2.cloned.1.call-start = ((), (), s32[]{:S(2)}) async-start(), calls=%async_computation.4 | async-start | bytes 1310720 | tf_op jit(solution)/shard_map/reduce_scatter | solution.py:139
  10.2 102.8 %copy-start.11 = (bf16[1,128,1024]{2,1,0:T(8,128)(2,1)S(1)}, bf16[1,128,1024]{2,1,0:T(8,128)(2,1)}, u32[]{:S(2)}) copy-start(bf16[1,128,1024]{2,1,0:T(8,128)(2,1)} %param.7) | copy-start | bytes 786436
  53.5 19.7 %collective-permute-start.1 = (bf16[128,512]{1,0:T(8,128)(2,1)S(1)}, bf16[128,512]{1,0:T(8,128)(2,1)S(1)}, u32[]{:S(2)}, u32[]{:S(2)}) collective-permute-start(bf16[128,512]{1,0:T(8,128)(2,1)S(1)} %convolution_convert_fusion.3), channel_id=1, source_target_pairs={{0,12},{4,16},{8,20},{12,24},{16,28},{20,32},{24,36},{28,40},{32,4... | collective-permute-start | bytes 393224 | tf_op jit(solution)/shard_map/ppermute | solution.py:15
  57.4 15.8 %collective-permute-start = (bf16[128,512]{1,0:T(8,128)(2,1)S(1)}, bf16[128,512]{1,0:T(8,128)(2,1)S(1)}, u32[]{:S(2)}, u32[]{:S(2)}) collective-permute-start(bf16[128,512]{1,0:T(8,128)(2,1)S(1)} %convolution_convert_fusion.3), channel_id=1, source_target_pairs={{0,16},{4,20},{8,24},{12,28},{16,32},{20,36},{24,40},{28,44},{32,4... | collective-permute-start | bytes 393224 | tf_op jit(solution)/shard_map/ppermute | solution.py:15
  60.9 111.5 %copy-start.18 = (pred[128,640]{0,1:T(8,128)(4,1)}, pred[128,640]{0,1:T(8,128)(4,1)S(1)}, u32[]{:S(2)}) copy-start(pred[128,640]{0,1:T(8,128)(4,1)S(1)} %fusion.70) | copy-start | bytes 245764
  60.9 19.0 %collective-permute-start.3 = (bf16[128,512]{1,0:T(8,128)(2,1)S(1)}, bf16[128,512]{1,0:T(8,128)(2,1)S(1)}, u32[]{:S(2)}, u32[]{:S(2)}) collective-permute-start(bf16[128,512]{1,0:T(8,128)(2,1)S(1)} %convolution_convert_fusion.3), channel_id=1, source_target_pairs={{0,4},{4,8},{8,12},{12,16},{16,20},{20,24},{24,28},{28,32},{32,36}... | collective-permute-start | bytes 393224 | tf_op jit(solution)/shard_map/ppermute | solution.py:15
  67.7 12.2 %collective-permute-start.2 = (bf16[128,512]{1,0:T(8,128)(2,1)S(1)}, bf16[128,512]{1,0:T(8,128)(2,1)S(1)}, u32[]{:S(2)}, u32[]{:S(2)}) collective-permute-start(bf16[128,512]{1,0:T(8,128)(2,1)S(1)} %convolution_convert_fusion.3), channel_id=1, source_target_pairs={{0,8},{4,12},{8,16},{12,20},{16,24},{20,28},{24,32},{28,36},{32,40... | collective-permute-start | bytes 393224 | tf_op jit(solution)/shard_map/ppermute | solution.py:15
  170.8 1.6 copy-start.12
  170.9 1.5 copy-start.14
  179.0 0.8 copy-start.7
  179.8 1.3 copy-start.4
  180.6 0.9 copy-start.8
  182.2 0.8 copy-start.10
  182.3 1.5 copy-start.3
  183.8 0.8 copy-start.9
  183.9 1.4 copy-start.16
  184.9 0.8 copy-start.17
  184.9 1.2 copy-start.15
  185.3 1.1 copy-start.13
  188.2 10.3 collective-permute-start.4
  191.1 7.4 collective-permute-start.7
  192.4 10.2 collective-permute-start.6
  193.7 12.4 %collective-permute-start.5 = (bf16[128,512]{0,1:T(8,128)(2,1)S(1)}, bf16[128,512]{0,1:T(8,128)(2,1)S(1)}, u32[]{:S(2)}, u32[]{:S(2)}) collective-permute-start(bf16[128,512]{0,1:T(8,128)(2,1)S(1)} %get-tuple-element.9), channel_id=1, source_target_pairs={{8,0},{12,4},{16,8},{20,12},{24,16},{28,20},{32,24},{36,28},{40,32... | collective-permute-start | bytes 393224 | tf_op jit(solution)/shard_map/ppermute | solution.py:15
  206.2 0.7 copy-start.5
  208.6 1.6 copy-start.1
  210.2 1.2 copy-start.2
  210.2 1.2 copy-start.6
Sparse Core Ops, SparseCore 0:
  10.1 41.8 all-gather.3
  54.1 58.8 all-gather.7
  115.1 52.7 all-gather.5
  208.4 42.0 reduce-scatter.1
where the time goes:
time: 1060 us; the launch traced here: 1050 us
  blocking collectives  797 us (75%)
  waiting for transfers between devices  182 us (17%)
  starting transfers between devices  26.2 us (2%)
  matrix products  23.2 us (2%)
  between operations  15 us (1%)
    psum x1, blocking collectives, per_device(): weight_grad = lax.psum(grad_shard, 'tm')  797 us
    all_gather x1, waiting for transfers between devices, per_device(): lax.all_gather(query_weight, 'stream', axis=0, tiled=True)  49.5 us
    all_gather x1, waiting for transfers between devices, per_device(): lax.all_gather(keyval_weight, 'stream', axis=0, tiled=True)  41.8 us
    reduce_scatter x1, waiting for transfers between devices, per_device(): lax.psum_scatter(contract_first(record_rows, keyval_grads).astype(jnp.bfl...  37.9 us
    all_gather x1, waiting for transfers between devices, per_device(): lax.all_gather(output_weight, 'stream', axis=0, tiled=True)  33 us
    ppermute x8, starting transfers between devices, shifted(): lax.ppermute(value, axis, [(source, source + steps) for source in range(l...  26.1 us
  transfers between devices with their start and end apart: 12, of which 8 were waited for; matrix products, arithmetic and copies ran while one was open for 1% of the time, Pallas kernels for 0%

commit v1 on v0

--- a/solution.py
+++ b/solution.py
@@ -13,6 +13,35 @@
     count = lax.axis_size(axis)
     leading, last = (max(0, -steps), min(count, count - steps))
     return lax.ppermute(value, axis, [(source, source + steps) for source in range(leading, last)])
+
+
+def xor_swap(value, axis, bit):
+    count = lax.axis_size(axis)
+    return lax.ppermute(value, axis, [(source, source ^ (1 << bit)) for source in range(count)])
+
+
+def tree_psum(value, axis):
+    count = lax.axis_size(axis)
+    bits = count.bit_length() - 1
+    if count != 1 << bits or value.shape[0] % count:
+        return lax.psum(value, axis)
+    order = [b for b in (0, 2, 4, 1, 3, 5, 6) if b < bits] + list(range(7, bits))
+    index = lax.axis_index(axis)
+    current = value
+    for bit in order:
+        half = current.shape[0] // 2
+        upper = ((index >> bit) & 1) == 1
+        low, high = current[:half], current[half:]
+        keep = jnp.where(upper, high, low)
+        send = jnp.where(upper, low, high)
+        current = keep + xor_swap(send, axis, bit)
+    for bit in reversed(order):
+        upper = ((index >> bit) & 1) == 1
+        other = xor_swap(current, axis, bit)
+        current = jnp.where(
+            upper, jnp.concatenate([other, current]), jnp.concatenate([current, other])
+        )
+    return current
 
 
 def contract_last(left, right):
@@ -142,7 +171,7 @@
         scatter_dimension=0,
         tiled=True,
     ).astype(jnp.float32)
-    weight_grad = lax.psum(grad_shard, "tm")
+    weight_grad = tree_psum(grad_shard, "tm")
     return (input_grad[None], weight_grad)
 
 

time: 1060 us -> 399 us (0.38)
  blocking collectives: 797 us -> 0 us
  waiting for transfers between devices: 182 us -> 265 us
  starting transfers between devices: 26.2 us -> 83.9 us
    psum x1 -> x0, blocking collectives: 797 us -> none  [per_device(): weight_grad = lax.psum(grad_shard, 'tm')]
    ppermute x0 -> x14, waiting for transfers between devices: none -> 76.4 us  [xor_swap(): lax.ppermute(value, axis, [(source, source ^ 1 << bit) for source in rang...]
    ppermute x0 -> x14, starting transfers between devices: none -> 57.7 us  [xor_swap(): lax.ppermute(value, axis, [(source, source ^ 1 << bit) for source in rang...]
  transfers between devices with their start and end apart: 12 -> 26, of which waited for: 8 -> 21; matrix products, arithmetic and copies ran while one was open for 1% -> 2% of each run, Pallas kernels for 0% -> 0%
where the time goes in v1:
time: 399 us; the launch traced here: 398 us
  waiting for transfers between devices  265 us (66%)
  starting transfers between devices  83.9 us (21%)
  matrix products  21.7 us (5%)
  between operations  15.3 us (4%)
  other arithmetic  6.53 us (2%)
  local copies, waits for them, and re-layouts  5.47 us (1%)
    ppermute x14, waiting for transfers between devices, xor_swap(): lax.ppermute(value, axis, [(source, source ^ 1 << bit) for source in rang...  76.4 us
    ppermute x14, starting transfers between devices, xor_swap(): lax.ppermute(value, axis, [(source, source ^ 1 << bit) for source in rang...  57.7 us
    all_gather x1, waiting for transfers between devices, per_device(): lax.all_gather(query_weight, 'stream', axis=0, tiled=True)  52 us
    reduce_scatter x1, waiting for transfers between devices, per_device(): lax.psum_scatter(contract_first(record_rows, keyval_grads).astype(jnp.bfl...  42.2 us
    all_gather x1, waiting for transfers between devices, per_device(): lax.all_gather(keyval_weight, 'stream', axis=0, tiled=True)  41.8 us
    all_gather x1, waiting for transfers between devices, per_device(): lax.all_gather(output_weight, 'stream', axis=0, tiled=True)  33.1 us
    ppermute x8, starting transfers between devices, shifted(): lax.ppermute(value, axis, [(source, source + steps) for source in range(l...  26.1 us
    ppermute x8, waiting for transfers between devices, shifted(): lax.ppermute(value, axis, [(source, source + steps) for source in range(l...  17.7 us
  transfers between devices with their start and end apart: 26, of which 21 were waited for; matrix products, arithmetic and copies ran while one was open for 2% of the time, Pallas kernels for 0%

profile of v1, /device:TPU:1, one launch (start us, length us, event | category | flops | bytes accessed | tf_op | source)
XLA Modules:
  0.0 398.1 jit_solution(10040253825793885623)
XLA Ops:
  7.2 0.7 all-gather.4.cloned.1.call-update
  8.0 0.7 all-gather.8.cloned.1.call-update
  8.7 0.7 all-gather.6.cloned.1.call-update
  10.2 41.8 %all-gather.4.cloned.1.call-done = bf16[1024,512]{1,0:T(8,128)(2,1)} async-done(((bf16[256,512]{1,0:T(8,128)(2,1)}), bf16[1024,512]{1,0:T(8,128)(2,1)}) %all-gather.4.cloned.1.call-update) | async-done | bytes 1048592 | tf_op jit(solution)/shard_map/all_gather | solution.py:73
  52.0 1.5 convolution_convert_fusion.3
  53.5 3.9 collective-permute-start.1
  57.4 3.1 collective-permute-start
  60.9 6.8 %collective-permute-start.3 = (bf16[128,512]{1,0:T(8,128)(2,1)S(1)}, bf16[128,512]{1,0:T(8,128)(2,1)S(1)}, u32[]{:S(2)}, u32[]{:S(2)}) collective-permute-start(bf16[128,512]{1,0:T(8,128)(2,1)S(1)} %convolution_convert_fusion.3), channel_id=1, source_target_pairs={{0,4},{4,8},{8,12},{12,16},{16,20},{20,24},{24,28},{28,32},{32,36}... | collective-permute-start | bytes 393224 | tf_op jit(solution)/shard_map/ppermute | solution.py:15
  67.7 5.6 %collective-permute-start.2 = (bf16[128,512]{1,0:T(8,128)(2,1)S(1)}, bf16[128,512]{1,0:T(8,128)(2,1)S(1)}, u32[]{:S(2)}, u32[]{:S(2)}) collective-permute-start(bf16[128,512]{1,0:T(8,128)(2,1)S(1)} %convolution_convert_fusion.3), channel_id=1, source_target_pairs={{0,8},{4,12},{8,16},{12,20},{16,24},{20,28},{24,32},{28,36},{32,40... | collective-permute-start | bytes 393224 | tf_op jit(solution)/shard_map/ppermute | solution.py:15
  73.3 6.6 %collective-permute-done.2 = bf16[128,512]{1,0:T(8,128)(2,1)S(1)} collective-permute-done((bf16[128,512]{1,0:T(8,128)(2,1)S(1)}, bf16[128,512]{1,0:T(8,128)(2,1)S(1)}, u32[]{:S(2)}, u32[]{:S(2)}) %collective-permute-start.2) | collective-permute-done | bytes 131104 | tf_op jit(solution)/shard_map/ppermute | solution.py:15
  79.9 33.1 %all-gather.8.cloned.1.call-done = bf16[1024,1024]{1,0:T(8,128)(2,1)} async-done(((bf16[256,1024]{1,0:T(8,128)(2,1)}), bf16[1024,1024]{1,0:T(8,128)(2,1)}) %all-gather.8.cloned.1.call-update) | async-done | bytes 2097168 | tf_op jit(solution)/shard_map/all_gather | solution.py:82
  113.0 2.4 convolution_convert_fusion.1
  115.9 52.0 %all-gather.6.cloned.1.call-done = bf16[1024,1024]{1,0:T(8,128)(2,1)} async-done(((bf16[256,1024]{1,0:T(8,128)(2,1)}), bf16[1024,1024]{1,0:T(8,128)(2,1)}) %all-gather.6.cloned.1.call-update) | async-done | bytes 2097168 | tf_op jit(solution)/shard_map/all_gather | solution.py:72
  167.9 2.0 convolution_convert_fusion.2
  170.4 1.8 fusion.108
  172.2 1.7 fusion.107
  173.9 1.7 fusion.106
  175.6 0.7 fusion.105
  176.3 1.4 divide_convert_fusion
  179.8 0.7 copy-done.7
  184.9 2.9 collective-permute-start.4
  187.7 1.3 collective-permute-start.7
  189.0 1.3 collective-permute-start.6
  190.3 1.3 collective-permute-start.5
  191.6 3.5 collective-permute-done.4
  195.2 4.1 %collective-permute-done.6 = bf16[128,512]{0,1:T(8,128)(2,1)S(1)} collective-permute-done((bf16[128,512]{0,1:T(8,128)(2,1)S(1)}, bf16[128,512]{0,1:T(8,128)(2,1)S(1)}, u32[]{:S(2)}, u32[]{:S(2)}) %collective-permute-start.6) | collective-permute-done | bytes 131104 | tf_op jit(solution)/shard_map/ppermute | solution.py:15
  199.3 3.4 collective-permute-done.5
  202.9 0.6 copy-done.9
  203.5 1.4 fusion.36
  204.9 42.2 %reduce-scatter.2.cloned.1.call-done = bf16[256,512]{0,1:T(8,128)(2,1)} async-done(((bf16[1024,512]{0,1:T(8,128)(2,1)}), bf16[256,512]{0,1:T(8,128)(2,1)}) %reduce-scatter.2.cloned.1.call-update) | async-done | bytes 262160 | tf_op jit(solution)/shard_map/reduce_scatter | solution.py:168
  247.1 1.0 convert_element_type.199
  248.2 2.8 collective-permute-start.8
  250.9 1.1 collective-permute-done.8
  252.2 3.1 collective-permute-start.9
  255.4 6.3 %collective-permute-done.9 = f32[64,512]{0,1:T(8,128)S(1)} collective-permute-done((f32[64,512]{0,1:T(8,128)S(1)}, f32[64,512]{0,1:T(8,128)S(1)}, u32[]{:S(2)}, u32[]{:S(2)}) %collective-permute-start.9) | collective-permute-done | bytes 131104 | tf_op jit(solution)/shard_map/ppermute | solution.py:20
  261.9 3.1 collective-permute-start.10
  265.0 5.4 %collective-permute-done.10 = f32[32,512]{0,1:T(8,128)S(1)} collective-permute-done((f32[32,512]{0,1:T(8,128)S(1)}, f32[32,512]{0,1:T(8,128)S(1)}, u32[]{:S(2)}, u32[]{:S(2)}) %collective-permute-start.10) | collective-permute-done | bytes 65568 | tf_op jit(solution)/shard_map/ppermute | solution.py:20
  270.7 5.3 %collective-permute-start.11 = (f32[16,512]{0,1:T(8,128)S(1)}, f32[16,512]{0,1:T(8,128)S(1)}, u32[]{:S(2)}, u32[]{:S(2)}) collective-permute-start(f32[16,512]{0,1:T(8,128)S(1)} %slice_select_fusion.3), channel_id=1, source_target_pairs={{0,8},{4,12},{8,0},{12,4},{16,24},{20,28},{24,16},{28,20},{32,40},... | collective-permute-start | bytes 98312 | tf_op jit(solution)/shard_map/ppermute | solution.py:20
  276.0 12.8 %collective-permute-done.11 = f32[16,512]{0,1:T(8,128)S(1)} collective-permute-done((f32[16,512]{0,1:T(8,128)S(1)}, f32[16,512]{0,1:T(8,128)S(1)}, u32[]{:S(2)}, u32[]{:S(2)}) %collective-permute-start.11) | collective-permute-done | bytes 32800 | tf_op jit(solution)/shard_map/ppermute | solution.py:20
  289.1 3.8 collective-permute-start.12
  292.8 5.3 %collective-permute-done.12 = f32[8,512]{0,1:T(8,128)S(1)} collective-permute-done((f32[8,512]{0,1:T(8,128)S(1)}, f32[8,512]{0,1:T(8,128)S(1)}, u32[]{:S(2)}, u32[]{:S(2)}) %collective-permute-start.12) | collective-permute-done | bytes 16416 | tf_op jit(solution)/shard_map/ppermute | solution.py:20
  298.4 3.3 collective-permute-start.13
  301.7 11.5 %collective-permute-done.13 = f32[4,512]{0,1:T(8,128)S(1)} collective-permute-done((f32[4,512]{0,1:T(8,128)S(1)}, f32[4,512]{0,1:T(8,128)S(1)}, u32[]{:S(2)}, u32[]{:S(2)}) %collective-permute-start.13) | collective-permute-done | bytes 8224 | tf_op jit(solution)/shard_map/ppermute | solution.py:20
  313.6 5.6 %collective-permute-start.14 = (f32[2,512]{0,1:T(8,128)S(1)}, f32[2,512]{0,1:T(8,128)S(1)}, u32[]{:S(2)}, u32[]{:S(2)}) collective-permute-start(f32[2,512]{0,1:T(8,128)S(1)} %slice_select_fusion), channel_id=1, source_target_pairs={{0,256},{4,260},{8,264},{12,268},{16,272},{20,276},{24,280},{28,28... | collective-permute-start | bytes 12296 | tf_op jit(solution)/shard_map/ppermute | solution.py:20
  319.2 13.6 %collective-permute-done.14 = f32[2,512]{0,1:T(8,128)S(1)} collective-permute-done((f32[2,512]{0,1:T(8,128)S(1)}, f32[2,512]{0,1:T(8,128)S(1)}, u32[]{:S(2)}, u32[]{:S(2)}) %collective-permute-start.14) | collective-permute-done | bytes 4128 | tf_op jit(solution)/shard_map/ppermute | solution.py:20
  332.8 0.8 select_add_fusion
  333.6 4.1 %collective-permute-start.15 = (f32[2,512]{0,1:T(8,128)}, f32[2,512]{0,1:T(8,128)}, u32[]{:S(2)}, u32[]{:S(2)}) collective-permute-start(f32[2,512]{0,1:T(8,128)} %select_add_fusion), channel_id=1, source_target_pairs={{0,256},{4,260},{8,264},{12,268},{16,272},{20,276},{24,280},{28,28... | collective-permute-start | bytes 12296 | tf_op jit(solution)/shard_map/ppermute | solution.py:20
  337.7 1.1 copy.143
  338.8 7.8 %collective-permute-done.15 = f32[2,512]{0,1:T(8,128)} collective-permute-done((f32[2,512]{0,1:T(8,128)}, f32[2,512]{0,1:T(8,128)}, u32[]{:S(2)}, u32[]{:S(2)}) %collective-permute-start.15) | collective-permute-done | bytes 4128 | tf_op jit(solution)/shard_map/ppermute | solution.py:20
  346.6 1.1 copy.142
  347.6 1.9 collective-permute-start.16
  349.6 3.4 collective-permute-done.16
  353.0 5.8 %collective-permute-start.17 = (f32[8,512]{1,0:T(8,128)S(1)}, f32[8,512]{1,0:T(8,128)S(1)}, u32[]{:S(2)}, u32[]{:S(2)}) collective-permute-start(f32[8,512]{1,0:T(8,128)S(1)} %maximum_select_fusion.5), channel_id=1, source_target_pairs={{0,32},{4,36},{8,40},{12,44},{16,48},{20,52},{24,56},{28,60},{32,0... | collective-permute-start | bytes 49160 | tf_op jit(solution)/shard_map/ppermute | solution.py:20
  359.1 0.8 collective-permute-done.17
  359.9 6.4 %collective-permute-start.18 = (f32[16,512]{1,0:T(8,128)S(1)}, f32[16,512]{1,0:T(8,128)S(1)}, u32[]{:S(2)}, u32[]{:S(2)}) collective-permute-start(f32[16,512]{1,0:T(8,128)S(1)} %maximum_select_fusion.4), channel_id=1, source_target_pairs={{0,8},{4,12},{8,0},{12,4},{16,24},{20,28},{24,16},{28,20},{32,40},... | collective-permute-start | bytes 98312 | tf_op jit(solution)/shard_map/ppermute | solution.py:20
  366.6 2.2 collective-permute-done.18
  368.8 2.1 collective-permute-start.19
  371.2 2.7 collective-permute-done.19
  374.0 1.9 collective-permute-start.20
  376.2 3.5 collective-permute-done.20
  379.7 8.6 %collective-permute-start.21 = (f32[128,512]{1,0:T(8,128)S(1)}, f32[128,512]{1,0:T(8,128)S(1)}, u32[]{:S(2)}, u32[]{:S(2)}) collective-permute-start(f32[128,512]{1,0:T(8,128)S(1)} %maximum_select_fusion.1), channel_id=1, source_target_pairs={{0,4},{4,0},{8,12},{12,8},{16,20},{20,16},{24,28},{28,24},{32,36},... | collective-permute-start | bytes 786440 | tf_op jit(solution)/shard_map/ppermute | solution.py:20
  388.3 0.8 fusion.75
  389.5 1.2 fusion.42
  390.7 0.8 maximum_select_fusion
  (98 shorter events, 11.2 us)
Async XLA Ops:
  7.2 44.8 %copy-start = (bf16[1,128,1024]{2,1,0:T(8,128)(2,1)S(1)}, bf16[1,128,1024]{2,1,0:T(8,128)(2,1)}, u32[]{:S(2)}) copy-start(bf16[1,128,1024]{2,1,0:T(8,128)(2,1)} %param.6) | copy-start | bytes 786436
  7.2 44.8 %all-gather.4.cloned.1.call-start = ((), (), s32[]{:S(2)}) async-start(), calls=%async_computation.1 | async-start | bytes 1310720 | tf_op jit(solution)/shard_map/all_gather | solution.py:73
  7.9 105.0 %all-gather.8.cloned.1.call-start = ((), (), s32[]{:S(2)}) async-start(), calls=%async_computation.3 | async-start | bytes 2621440 | tf_op jit(solution)/shard_map/all_gather | solution.py:82
  8.7 159.2 %all-gather.6.cloned.1.call-start = ((), (), s32[]{:S(2)}) async-start(), calls=%async_computation.2 | async-start | bytes 2621440 | tf_op jit(solution)/shard_map/all_gather | solution.py:72
  9.4 237.7 %reduce-scatter.2.cloned.1.call-start = ((), (), s32[]{:S(2)}) async-start(), calls=%async_computation.4 | async-start | bytes 1310720 | tf_op jit(solution)/shard_map/reduce_scatter | solution.py:168
  10.2 102.8 %copy-start.11 = (bf16[1,128,1024]{2,1,0:T(8,128)(2,1)S(1)}, bf16[1,128,1024]{2,1,0:T(8,128)(2,1)}, u32[]{:S(2)}) copy-start(bf16[1,128,1024]{2,1,0:T(8,128)(2,1)} %param.7) | copy-start | bytes 786436
  53.5 19.7 %collective-permute-start.1 = (bf16[128,512]{1,0:T(8,128)(2,1)S(1)}, bf16[128,512]{1,0:T(8,128)(2,1)S(1)}, u32[]{:S(2)}, u32[]{:S(2)}) collective-permute-start(bf16[128,512]{1,0:T(8,128)(2,1)S(1)} %convolution_convert_fusion.3), channel_id=1, source_target_pairs={{0,12},{4,16},{8,20},{12,24},{16,28},{20,32},{24,36},{28,40},{32,4... | collective-permute-start | bytes 393224 | tf_op jit(solution)/shard_map/ppermute | solution.py:15
  57.4 15.8 %collective-permute-start = (bf16[128,512]{1,0:T(8,128)(2,1)S(1)}, bf16[128,512]{1,0:T(8,128)(2,1)S(1)}, u32[]{:S(2)}, u32[]{:S(2)}) collective-permute-start(bf16[128,512]{1,0:T(8,128)(2,1)S(1)} %convolution_convert_fusion.3), channel_id=1, source_target_pairs={{0,16},{4,20},{8,24},{12,28},{16,32},{20,36},{24,40},{28,44},{32,4... | collective-permute-start | bytes 393224 | tf_op jit(solution)/shard_map/ppermute | solution.py:15
  60.9 19.0 %collective-permute-start.3 = (bf16[128,512]{1,0:T(8,128)(2,1)S(1)}, bf16[128,512]{1,0:T(8,128)(2,1)S(1)}, u32[]{:S(2)}, u32[]{:S(2)}) collective-permute-start(bf16[128,512]{1,0:T(8,128)(2,1)S(1)} %convolution_convert_fusion.3), channel_id=1, source_target_pairs={{0,4},{4,8},{8,12},{12,16},{16,20},{20,24},{24,28},{28,32},{32,36}... | collective-permute-start | bytes 393224 | tf_op jit(solution)/shard_map/ppermute | solution.py:15
  67.7 12.2 %collective-permute-start.2 = (bf16[128,512]{1,0:T(8,128)(2,1)S(1)}, bf16[128,512]{1,0:T(8,128)(2,1)S(1)}, u32[]{:S(2)}, u32[]{:S(2)}) collective-permute-start(bf16[128,512]{1,0:T(8,128)(2,1)S(1)} %convolution_convert_fusion.3), channel_id=1, source_target_pairs={{0,8},{4,12},{8,16},{12,20},{16,24},{20,28},{24,32},{28,36},{32,40... | collective-permute-start | bytes 393224 | tf_op jit(solution)/shard_map/ppermute | solution.py:15
  177.7 1.3 copy-start.8
  178.5 4.6 %copy-start.5 = (bf16[4,128,640]{1,2,0:T(8,128)(2,1)}, bf16[4,128,640]{1,2,0:T(8,128)(2,1)S(1)}, u32[]{:S(2)}) copy-start(bf16[4,128,640]{1,2,0:T(8,128)(2,1)S(1)} %fusion.40) | copy-start | bytes 1966084
  179.1 1.3 copy-start.7
  179.8 3.0 copy-start.3
  184.9 10.3 %collective-permute-start.4 = (bf16[128,512]{0,1:T(8,128)(2,1)S(1)}, bf16[128,512]{0,1:T(8,128)(2,1)S(1)}, u32[]{:S(2)}, u32[]{:S(2)}) collective-permute-start(bf16[128,512]{0,1:T(8,128)(2,1)S(1)} %get-tuple-element.6), channel_id=1, source_target_pairs={{4,0},{8,4},{12,8},{16,12},{20,16},{24,20},{28,24},{32,28},{36,32}... | collective-permute-start | bytes 393224 | tf_op jit(solution)/shard_map/ppermute | solution.py:15
  187.7 7.4 %collective-permute-start.7 = (bf16[128,512]{0,1:T(8,128)(2,1)S(1)}, bf16[128,512]{0,1:T(8,128)(2,1)S(1)}, u32[]{:S(2)}, u32[]{:S(2)}) collective-permute-start(bf16[128,512]{0,1:T(8,128)(2,1)S(1)} %get-tuple-element.7), channel_id=1, source_target_pairs={{16,0},{20,4},{24,8},{28,12},{32,16},{36,20},{40,24},{44,28},{48,3... | collective-permute-start | bytes 393224 | tf_op jit(solution)/shard_map/ppermute | solution.py:15
  189.0 10.3 %collective-permute-start.6 = (bf16[128,512]{0,1:T(8,128)(2,1)S(1)}, bf16[128,512]{0,1:T(8,128)(2,1)S(1)}, u32[]{:S(2)}, u32[]{:S(2)}) collective-permute-start(bf16[128,512]{0,1:T(8,128)(2,1)S(1)} %get-tuple-element.8), channel_id=1, source_target_pairs={{12,0},{16,4},{20,8},{24,12},{28,16},{32,20},{36,24},{40,28},{44,3... | collective-permute-start | bytes 393224 | tf_op jit(solution)/shard_map/ppermute | solution.py:15
  190.3 12.4 %collective-permute-start.5 = (bf16[128,512]{0,1:T(8,128)(2,1)S(1)}, bf16[128,512]{0,1:T(8,128)(2,1)S(1)}, u32[]{:S(2)}, u32[]{:S(2)}) collective-permute-start(bf16[128,512]{0,1:T(8,128)(2,1)S(1)} %get-tuple-element.9), channel_id=1, source_target_pairs={{8,0},{12,4},{16,8},{20,12},{24,16},{28,20},{32,24},{36,28},{40,32... | collective-permute-start | bytes 393224 | tf_op jit(solution)/shard_map/ppermute | solution.py:15
  202.8 0.7 copy-start.9
  248.2 3.9 collective-permute-start.8
  252.2 9.4 %collective-permute-start.9 = (f32[64,512]{0,1:T(8,128)S(1)}, f32[64,512]{0,1:T(8,128)S(1)}, u32[]{:S(2)}, u32[]{:S(2)}) collective-permute-start(f32[64,512]{0,1:T(8,128)S(1)} %slice_select_fusion.5), channel_id=1, source_target_pairs={{0,16},{4,20},{8,24},{12,28},{16,0},{20,4},{24,8},{28,12},{32,48},... | collective-permute-start | bytes 393224 | tf_op jit(solution)/shard_map/ppermute | solution.py:20
  261.9 8.5 %collective-permute-start.10 = (f32[32,512]{0,1:T(8,128)S(1)}, f32[32,512]{0,1:T(8,128)S(1)}, u32[]{:S(2)}, u32[]{:S(2)}) collective-permute-start(f32[32,512]{0,1:T(8,128)S(1)} %slice_select_fusion.4), channel_id=1, source_target_pairs={{0,64},{4,68},{8,72},{12,76},{16,80},{20,84},{24,88},{28,92},{32,9... | collective-permute-start | bytes 196616 | tf_op jit(solution)/shard_map/ppermute | solution.py:20
  270.7 18.1 %collective-permute-start.11 = (f32[16,512]{0,1:T(8,128)S(1)}, f32[16,512]{0,1:T(8,128)S(1)}, u32[]{:S(2)}, u32[]{:S(2)}) collective-permute-start(f32[16,512]{0,1:T(8,128)S(1)} %slice_select_fusion.3), channel_id=1, source_target_pairs={{0,8},{4,12},{8,0},{12,4},{16,24},{20,28},{24,16},{28,20},{32,40},... | collective-permute-start | bytes 98312 | tf_op jit(solution)/shard_map/ppermute | solution.py:20
  289.1 9.1 %collective-permute-start.12 = (f32[8,512]{0,1:T(8,128)S(1)}, f32[8,512]{0,1:T(8,128)S(1)}, u32[]{:S(2)}, u32[]{:S(2)}) collective-permute-start(f32[8,512]{0,1:T(8,128)S(1)} %slice_select_fusion.2), channel_id=1, source_target_pairs={{0,32},{4,36},{8,40},{12,44},{16,48},{20,52},{24,56},{28,60},{32,0... | collective-permute-start | bytes 49160 | tf_op jit(solution)/shard_map/ppermute | solution.py:20
  298.4 14.8 %collective-permute-start.13 = (f32[4,512]{0,1:T(8,128)S(1)}, f32[4,512]{0,1:T(8,128)S(1)}, u32[]{:S(2)}, u32[]{:S(2)}) collective-permute-start(f32[4,512]{0,1:T(8,128)S(1)} %slice_select_fusion.1), channel_id=1, source_target_pairs={{0,128},{4,132},{8,136},{12,140},{16,144},{20,148},{24,152},{28,15... | collective-permute-start | bytes 24584 | tf_op jit(solution)/shard_map/ppermute | solution.py:20
  313.4 45.4 %copy-start.6 = (bf16[4,128,640]{1,2,0:T(8,128)(2,1)S(1)}, bf16[4,128,640]{1,2,0:T(8,128)(2,1)}, u32[]{:S(2)}) copy-start(bf16[4,128,640]{1,2,0:T(8,128)(2,1)} %copy-done.5) | copy-start | bytes 1966084
  313.6 52.8 %copy-start.4 = (bf16[4,128,640]{1,2,0:T(8,128)(2,1)S(1)}, bf16[4,128,640]{1,2,0:T(8,128)(2,1)}, u32[]{:S(2)}) copy-start(bf16[4,128,640]{1,2,0:T(8,128)(2,1)} %copy-done.3) | copy-start | bytes 1966084
  313.6 19.2 %collective-permute-start.14 = (f32[2,512]{0,1:T(8,128)S(1)}, f32[2,512]{0,1:T(8,128)S(1)}, u32[]{:S(2)}, u32[]{:S(2)}) collective-permute-start(f32[2,512]{0,1:T(8,128)S(1)} %slice_select_fusion), channel_id=1, source_target_pairs={{0,256},{4,260},{8,264},{12,268},{16,272},{20,276},{24,280},{28,28... | collective-permute-start | bytes 12296 | tf_op jit(solution)/shard_map/ppermute | solution.py:20
  333.6 12.9 %collective-permute-start.15 = (f32[2,512]{0,1:T(8,128)}, f32[2,512]{0,1:T(8,128)}, u32[]{:S(2)}, u32[]{:S(2)}) collective-permute-start(f32[2,512]{0,1:T(8,128)} %select_add_fusion), channel_id=1, source_target_pairs={{0,256},{4,260},{8,264},{12,268},{16,272},{20,276},{24,280},{28,28... | collective-permute-start | bytes 12296 | tf_op jit(solution)/shard_map/ppermute | solution.py:20
  347.6 5.3 %collective-permute-start.16 = (f32[4,512]{1,0:T(4,128)S(1)}, f32[4,512]{1,0:T(4,128)S(1)}, u32[]{:S(2)}, u32[]{:S(2)}) collective-permute-start(f32[4,512]{1,0:T(4,128)S(1)} %maximum_select_fusion.6), channel_id=1, source_target_pairs={{0,128},{4,132},{8,136},{12,140},{16,144},{20,148},{24,152},{28,15... | collective-permute-start | bytes 24584 | tf_op jit(solution)/shard_map/ppermute | solution.py:20
  353.0 6.9 %collective-permute-start.17 = (f32[8,512]{1,0:T(8,128)S(1)}, f32[8,512]{1,0:T(8,128)S(1)}, u32[]{:S(2)}, u32[]{:S(2)}) collective-permute-start(f32[8,512]{1,0:T(8,128)S(1)} %maximum_select_fusion.5), channel_id=1, source_target_pairs={{0,32},{4,36},{8,40},{12,44},{16,48},{20,52},{24,56},{28,60},{32,0... | collective-permute-start | bytes 49160 | tf_op jit(solution)/shard_map/ppermute | solution.py:20
  359.9 8.9 %collective-permute-start.18 = (f32[16,512]{1,0:T(8,128)S(1)}, f32[16,512]{1,0:T(8,128)S(1)}, u32[]{:S(2)}, u32[]{:S(2)}) collective-permute-start(f32[16,512]{1,0:T(8,128)S(1)} %maximum_select_fusion.4), channel_id=1, source_target_pairs={{0,8},{4,12},{8,0},{12,4},{16,24},{20,28},{24,16},{28,20},{32,40},... | collective-permute-start | bytes 98312 | tf_op jit(solution)/shard_map/ppermute | solution.py:20
  368.8 19.5 %copy-start.1 = (bf16[1024,1024]{1,0:T(8,128)(2,1)S(1)}, bf16[1024,1024]{1,0:T(8,128)(2,1)}, u32[]{:S(2)}) copy-start(bf16[1024,1024]{1,0:T(8,128)(2,1)} %all-gather.6.cloned.1.call-done) | copy-start | bytes 6291460
  368.8 5.1 %collective-permute-start.19 = (f32[32,512]{1,0:T(8,128)S(1)}, f32[32,512]{1,0:T(8,128)S(1)}, u32[]{:S(2)}, u32[]{:S(2)}) collective-permute-start(f32[32,512]{1,0:T(8,128)S(1)} %maximum_select_fusion.3), channel_id=1, source_target_pairs={{0,64},{4,68},{8,72},{12,76},{16,80},{20,84},{24,88},{28,92},{32,9... | collective-permute-start | bytes 196616 | tf_op jit(solution)/shard_map/ppermute | solution.py:20
  374.0 5.7 %collective-permute-start.20 = (f32[64,512]{1,0:T(8,128)S(1)}, f32[64,512]{1,0:T(8,128)S(1)}, u32[]{:S(2)}, u32[]{:S(2)}) collective-permute-start(f32[64,512]{1,0:T(8,128)S(1)} %maximum_select_fusion.2), channel_id=1, source_target_pairs={{0,16},{4,20},{8,24},{12,28},{16,0},{20,4},{24,8},{28,12},{32,48},... | collective-permute-start | bytes 393224 | tf_op jit(solution)/shard_map/ppermute | solution.py:20
  379.7 11.0 %collective-permute-start.21 = (f32[128,512]{1,0:T(8,128)S(1)}, f32[128,512]{1,0:T(8,128)S(1)}, u32[]{:S(2)}, u32[]{:S(2)}) collective-permute-start(f32[128,512]{1,0:T(8,128)S(1)} %maximum_select_fusion.1), channel_id=1, source_target_pairs={{0,4},{4,0},{8,12},{12,8},{16,20},{20,16},{24,28},{28,24},{32,36},... | collective-permute-start | bytes 786440 | tf_op jit(solution)/shard_map/ppermute | solution.py:20
  388.3 1.2 copy-start.2
  388.3 1.2 copy-start.10
Sparse Core Ops, SparseCore 0:
  10.1 41.8 all-gather.3
  54.1 58.8 all-gather.7
  115.1 52.7 all-gather.5
  205.0 42.0 reduce-scatter.1

commit v2 on v1

--- a/solution.py
+++ b/solution.py
@@ -68,19 +68,23 @@
     key_span = REACH * shard_tokens + tile_rows
     score_scale = HEAD_DIM ** (-0.5)
     anchor = lax.axis_index("tm") * shard_tokens
-    query_full, keyval_full = (
-        lax.all_gather(query_weight, "stream", axis=0, tiled=True),
-        lax.all_gather(keyval_weight, "stream", axis=0, tiled=True),
+    query_width = query_weight.shape[1]
+    weights_full = lax.all_gather(
+        jnp.concatenate([query_weight, keyval_weight, output_weight], axis=1),
+        "stream",
+        axis=0,
+        tiled=True,
     )
+    query_full = weights_full[:, :query_width]
+    keyval_full = weights_full[:, query_width : query_width + keyval_width]
+    output_full = weights_full[:, query_width + keyval_width :]
     queries = jnp.dot(record_rows, query_full, preferred_element_type=jnp.float32).astype(
         jnp.bfloat16
     )
     keyvals = jnp.dot(record_rows, keyval_full, preferred_element_type=jnp.float32).astype(
         jnp.bfloat16
     )
-    attn_grad = contract_last(
-        outer_grad, lax.all_gather(output_weight, "stream", axis=0, tiled=True)
-    ).astype(jnp.bfloat16)
+    attn_grad = contract_last(outer_grad, output_full).astype(jnp.bfloat16)
     earlier = [shifted(keyvals, "tm", offset) for offset in range(REACH, 0, -1)]
     window_keyvals = jnp.concatenate(earlier + [keyvals], axis=0)
     key_parts = []

time: 399 us -> 381 us (0.955)
  waiting for transfers between devices: 265 us -> 226 us
  starting transfers between devices: 83.9 us -> 99.2 us
    all_gather x3 -> x1, waiting for transfers between devices: 127 us -> 109 us  [per_device(): lax.all_gather(jnp.concatenate([query_weight, keyval_weight, output_weigh...]
    ppermute x14, starting transfers between devices: 57.7 us -> 72.9 us  [xor_swap(): lax.ppermute(value, axis, [(source, source ^ 1 << bit) for source in rang...]
    ppermute x14, waiting for transfers between devices: 76.4 us -> 63 us  [xor_swap(): lax.ppermute(value, axis, [(source, source ^ 1 << bit) for source in rang...]
    ppermute x8, waiting for transfers between devices: 17.7 us -> 8.64 us  [shifted(): lax.ppermute(value, axis, [(source, source + steps) for source in range(l...]
  transfers between devices with their start and end apart: 26 -> 24, of which waited for: 21 -> 19; matrix products, arithmetic and copies ran while one was open for 2% -> 3% of each run, Pallas kernels for 0% -> 0%
where the time goes in v2:
time: 381 us; the launch traced here: 379 us
  waiting for transfers between devices  226 us (59%)
  starting transfers between devices  99.2 us (26%)
  matrix products  24.9 us (7%)
  between operations  15.5 us (4%)
  other arithmetic  9.03 us (2%)
  local copies, waits for them, and re-layouts  4.18 us (1%)
    all_gather x1, waiting for transfers between devices, per_device(): lax.all_gather(jnp.concatenate([query_weight, keyval_weight, output_weigh...  109 us
    ppermute x14, starting transfers between devices, xor_swap(): lax.ppermute(value, axis, [(source, source ^ 1 << bit) for source in rang...  72.9 us
    ppermute x14, waiting for transfers between devices, xor_swap(): lax.ppermute(value, axis, [(source, source ^ 1 << bit) for source in rang...  63 us
    reduce_scatter x1, waiting for transfers between devices, per_device(): lax.psum_scatter(contract_first(record_rows, keyval_grads).astype(jnp.bfl...  45.9 us
    ppermute x8, starting transfers between devices, shifted(): lax.ppermute(value, axis, [(source, source + steps) for source in range(l...  26.2 us
    ppermute x8, waiting for transfers between devices, shifted(): lax.ppermute(value, axis, [(source, source + steps) for source in range(l...  8.64 us
  transfers between devices with their start and end apart: 24, of which 19 were waited for; matrix products, arithmetic and copies ran while one was open for 3% of the time, Pallas kernels for 0%

profile of v2, /device:TPU:1, one launch (start us, length us, event | category | flops | bytes accessed | tf_op | source)
XLA Modules:
  0.0 379.2 jit_solution(1801174199442456565)
XLA Ops:
  7.2 2.5 pad_maximum_fusion
  10.9 108.9 %all-gather.2.cloned.1.call-done = bf16[1024,2560]{1,0:T(8,128)(2,1)} async-done(((bf16[256,2560]{1,0:T(8,128)(2,1)}), bf16[1024,2560]{1,0:T(8,128)(2,1)}) %all-gather.2.cloned.1.call-update) | async-done | bytes 5242896 | tf_op jit(solution)/shard_map/all_gather | solution.py:72
  119.8 1.5 fusion.69
  121.3 3.1 collective-permute-start
  124.4 3.9 %collective-permute-start.1 = (bf16[128,512]{1,0:T(8,128)(2,1)S(1)}, bf16[128,512]{1,0:T(8,128)(2,1)S(1)}, u32[]{:S(2)}, u32[]{:S(2)}) collective-permute-start(bf16[128,512]{1,0:T(8,128)(2,1)S(1)} %fusion.69), channel_id=1, source_target_pairs={{0,12},{4,16},{8,20},{12,24},{16,28},{20,32},{24,36},{28,40},{32,4... | collective-permute-start | bytes 393224 | tf_op jit(solution)/shard_map/ppermute | solution.py:15
  128.3 6.5 %collective-permute-start.2 = (bf16[128,512]{1,0:T(8,128)(2,1)S(1)}, bf16[128,512]{1,0:T(8,128)(2,1)S(1)}, u32[]{:S(2)}, u32[]{:S(2)}) collective-permute-start(bf16[128,512]{1,0:T(8,128)(2,1)S(1)} %fusion.69), channel_id=1, source_target_pairs={{0,8},{4,12},{8,16},{12,20},{16,24},{20,28},{24,32},{28,36},{32,40... | collective-permute-start | bytes 393224 | tf_op jit(solution)/shard_map/ppermute | solution.py:15
  134.8 6.9 %collective-permute-start.3 = (bf16[128,512]{1,0:T(8,128)(2,1)S(1)}, bf16[128,512]{1,0:T(8,128)(2,1)S(1)}, u32[]{:S(2)}, u32[]{:S(2)}) collective-permute-start(bf16[128,512]{1,0:T(8,128)(2,1)S(1)} %fusion.69), channel_id=1, source_target_pairs={{0,4},{4,8},{8,12},{12,16},{16,20},{20,24},{24,28},{28,32},{32,36}... | collective-permute-start | bytes 393224 | tf_op jit(solution)/shard_map/ppermute | solution.py:15
  141.8 2.3 fusion.54
  144.1 2.4 fusion.57
  146.6 1.7 fusion.128
  148.3 0.6 fusion.125
  149.0 1.8 fusion.126
  150.7 1.7 fusion.127
  152.5 1.4 divide_convert_fusion
  153.9 0.4 fusion.85
  154.3 0.4 fusion.46
  154.7 0.5 copy-done.6
  156.0 0.7 copy-done.5
  157.1 0.4 fusion.44
  161.1 1.3 collective-permute-start.7
  162.4 1.3 collective-permute-start.6
  163.7 1.3 collective-permute-start.5
  165.0 1.9 collective-permute-start.4
  166.9 1.4 collective-permute-done.7
  168.3 1.3 collective-permute-done.6
  169.6 4.7 %collective-permute-done.5 = bf16[128,512]{0,1:T(8,128)(2,1)S(1)} collective-permute-done((bf16[128,512]{0,1:T(8,128)(2,1)S(1)}, bf16[128,512]{0,1:T(8,128)(2,1)S(1)}, u32[]{:S(2)}, u32[]{:S(2)}) %collective-permute-start.5) | collective-permute-done | bytes 131104 | tf_op jit(solution)/shard_map/ppermute | solution.py:15
  174.4 1.2 collective-permute-done.4
  175.7 0.6 copy-done.7
  176.3 1.4 fusion.42
  177.8 45.9 %reduce-scatter.2.cloned.1.call-done = bf16[256,512]{0,1:T(8,128)(2,1)} async-done(((bf16[1024,512]{0,1:T(8,128)(2,1)}), bf16[256,512]{0,1:T(8,128)(2,1)}) %reduce-scatter.2.cloned.1.call-update) | async-done | bytes 262160 | tf_op jit(solution)/shard_map/reduce_scatter | solution.py:172
  223.6 1.0 convert_element_type.211
  224.7 2.8 collective-permute-start.8
  227.4 1.1 collective-permute-done.8
  228.8 3.1 collective-permute-start.9
  231.9 6.3 %collective-permute-done.9 = f32[64,512]{0,1:T(8,128)S(1)} collective-permute-done((f32[64,512]{0,1:T(8,128)S(1)}, f32[64,512]{0,1:T(8,128)S(1)}, u32[]{:S(2)}, u32[]{:S(2)}) %collective-permute-start.9) | collective-permute-done | bytes 131104 | tf_op jit(solution)/shard_map/ppermute | solution.py:20
  238.4 3.1 collective-permute-start.10
  241.6 5.4 %collective-permute-done.10 = f32[32,512]{0,1:T(8,128)S(1)} collective-permute-done((f32[32,512]{0,1:T(8,128)S(1)}, f32[32,512]{0,1:T(8,128)S(1)}, u32[]{:S(2)}, u32[]{:S(2)}) %collective-permute-start.10) | collective-permute-done | bytes 65568 | tf_op jit(solution)/shard_map/ppermute | solution.py:20
  247.2 5.2 %collective-permute-start.11 = (f32[16,512]{0,1:T(8,128)S(1)}, f32[16,512]{0,1:T(8,128)S(1)}, u32[]{:S(2)}, u32[]{:S(2)}) collective-permute-start(f32[16,512]{0,1:T(8,128)S(1)} %slice_select_fusion.3), channel_id=1, source_target_pairs={{0,8},{4,12},{8,0},{12,4},{16,24},{20,28},{24,16},{28,20},{32,40},... | collective-permute-start | bytes 98312 | tf_op jit(solution)/shard_map/ppermute | solution.py:20
  252.4 11.9 %collective-permute-done.11 = f32[16,512]{0,1:T(8,128)S(1)} collective-permute-done((f32[16,512]{0,1:T(8,128)S(1)}, f32[16,512]{0,1:T(8,128)S(1)}, u32[]{:S(2)}, u32[]{:S(2)}) %collective-permute-start.11) | collective-permute-done | bytes 32800 | tf_op jit(solution)/shard_map/ppermute | solution.py:20
  264.6 4.6 %collective-permute-start.12 = (f32[8,512]{0,1:T(8,128)S(1)}, f32[8,512]{0,1:T(8,128)S(1)}, u32[]{:S(2)}, u32[]{:S(2)}) collective-permute-start(f32[8,512]{0,1:T(8,128)S(1)} %slice_select_fusion.2), channel_id=1, source_target_pairs={{0,32},{4,36},{8,40},{12,44},{16,48},{20,52},{24,56},{28,60},{32,0... | collective-permute-start | bytes 49160 | tf_op jit(solution)/shard_map/ppermute | solution.py:20
  269.2 4.0 %collective-permute-done.12 = f32[8,512]{0,1:T(8,128)S(1)} collective-permute-done((f32[8,512]{0,1:T(8,128)S(1)}, f32[8,512]{0,1:T(8,128)S(1)}, u32[]{:S(2)}, u32[]{:S(2)}) %collective-permute-start.12) | collective-permute-done | bytes 16416 | tf_op jit(solution)/shard_map/ppermute | solution.py:20
  273.5 4.1 %collective-permute-start.13 = (f32[4,512]{0,1:T(8,128)S(1)}, f32[4,512]{0,1:T(8,128)S(1)}, u32[]{:S(2)}, u32[]{:S(2)}) collective-permute-start(f32[4,512]{0,1:T(8,128)S(1)} %slice_select_fusion.1), channel_id=1, source_target_pairs={{0,128},{4,132},{8,136},{12,140},{16,144},{20,148},{24,152},{28,15... | collective-permute-start | bytes 24584 | tf_op jit(solution)/shard_map/ppermute | solution.py:20
  277.6 10.6 %collective-permute-done.13 = f32[4,512]{0,1:T(8,128)S(1)} collective-permute-done((f32[4,512]{0,1:T(8,128)S(1)}, f32[4,512]{0,1:T(8,128)S(1)}, u32[]{:S(2)}, u32[]{:S(2)}) %collective-permute-start.13) | collective-permute-done | bytes 8224 | tf_op jit(solution)/shard_map/ppermute | solution.py:20
  288.5 7.4 %collective-permute-start.14 = (f32[2,512]{0,1:T(8,128)S(1)}, f32[2,512]{0,1:T(8,128)S(1)}, u32[]{:S(2)}, u32[]{:S(2)}) collective-permute-start(f32[2,512]{0,1:T(8,128)S(1)} %slice_select_fusion), channel_id=1, source_target_pairs={{0,256},{4,260},{8,264},{12,268},{16,272},{20,276},{24,280},{28,28... | collective-permute-start | bytes 12296 | tf_op jit(solution)/shard_map/ppermute | solution.py:20
  295.9 7.4 %collective-permute-done.14 = f32[2,512]{0,1:T(8,128)S(1)} collective-permute-done((f32[2,512]{0,1:T(8,128)S(1)}, f32[2,512]{0,1:T(8,128)S(1)}, u32[]{:S(2)}, u32[]{:S(2)}) %collective-permute-start.14) | collective-permute-done | bytes 4128 | tf_op jit(solution)/shard_map/ppermute | solution.py:20
  303.2 0.8 select_add_fusion
  304.1 7.3 %collective-permute-start.15 = (f32[2,512]{0,1:T(8,128)}, f32[2,512]{0,1:T(8,128)}, u32[]{:S(2)}, u32[]{:S(2)}) collective-permute-start(f32[2,512]{0,1:T(8,128)} %select_add_fusion), channel_id=1, source_target_pairs={{0,256},{4,260},{8,264},{12,268},{16,272},{20,276},{24,280},{28,28... | collective-permute-start | bytes 12296 | tf_op jit(solution)/shard_map/ppermute | solution.py:20
  311.4 1.1 copy.74
  312.4 6.0 %collective-permute-done.15 = f32[2,512]{0,1:T(8,128)} collective-permute-done((f32[2,512]{0,1:T(8,128)}, f32[2,512]{0,1:T(8,128)}, u32[]{:S(2)}, u32[]{:S(2)}) %collective-permute-start.15) | collective-permute-done | bytes 4128 | tf_op jit(solution)/shard_map/ppermute | solution.py:20
  318.5 1.1 copy.73
  319.6 1.9 collective-permute-start.16
  321.5 3.4 collective-permute-done.16
  324.9 5.0 %collective-permute-start.17 = (f32[8,512]{1,0:T(8,128)S(1)}, f32[8,512]{1,0:T(8,128)S(1)}, u32[]{:S(2)}, u32[]{:S(2)}) collective-permute-start(f32[8,512]{1,0:T(8,128)S(1)} %maximum_select_fusion.5), channel_id=1, source_target_pairs={{0,32},{4,36},{8,40},{12,44},{16,48},{20,52},{24,56},{28,60},{32,0... | collective-permute-start | bytes 49160 | tf_op jit(solution)/shard_map/ppermute | solution.py:20
  330.2 0.8 collective-permute-done.17
  331.0 11.4 %collective-permute-start.18 = (f32[16,512]{1,0:T(8,128)S(1)}, f32[16,512]{1,0:T(8,128)S(1)}, u32[]{:S(2)}, u32[]{:S(2)}) collective-permute-start(f32[16,512]{1,0:T(8,128)S(1)} %maximum_select_fusion.4), channel_id=1, source_target_pairs={{0,8},{4,12},{8,0},{12,4},{16,24},{20,28},{24,16},{28,20},{32,40},... | collective-permute-start | bytes 98312 | tf_op jit(solution)/shard_map/ppermute | solution.py:20
  342.7 1.0 collective-permute-done.18
  343.7 1.9 collective-permute-start.19
  346.0 3.0 collective-permute-done.19
  349.0 7.8 %collective-permute-start.20 = (f32[64,512]{1,0:T(8,128)S(1)}, f32[64,512]{1,0:T(8,128)S(1)}, u32[]{:S(2)}, u32[]{:S(2)}) collective-permute-start(f32[64,512]{1,0:T(8,128)S(1)} %maximum_select_fusion.2), channel_id=1, source_target_pairs={{0,16},{4,20},{8,24},{12,28},{16,0},{20,4},{24,8},{28,12},{32,48},... | collective-permute-start | bytes 393224 | tf_op jit(solution)/shard_map/ppermute | solution.py:20
  357.1 2.1 collective-permute-done.20
  359.2 7.4 %collective-permute-start.21 = (f32[128,512]{1,0:T(8,128)S(1)}, f32[128,512]{1,0:T(8,128)S(1)}, u32[]{:S(2)}, u32[]{:S(2)}) collective-permute-start(f32[128,512]{1,0:T(8,128)S(1)} %maximum_select_fusion.1), channel_id=1, source_target_pairs={{0,4},{4,0},{8,12},{12,8},{16,20},{20,16},{24,28},{28,24},{32,36},... | collective-permute-start | bytes 786440 | tf_op jit(solution)/shard_map/ppermute | solution.py:20
  366.6 2.5 fusion.6
  369.1 2.4 fusion.60
  371.5 0.8 maximum_select_fusion
  (81 shorter events, 8.1 us)
Async XLA Ops:
  7.2 112.6 %copy-start = (bf16[1,128,1024]{2,1,0:T(8,128)(2,1)S(1)}, bf16[1,128,1024]{2,1,0:T(8,128)(2,1)}, u32[]{:S(2)}) copy-start(bf16[1,128,1024]{2,1,0:T(8,128)(2,1)} %param.6) | copy-start | bytes 786436
  7.2 112.6 %all-gather.2.cloned.1.call-start = ((), (), s32[]{:S(2)}) async-start(), calls=%async_computation.1 | async-start | bytes 6553600 | tf_op jit(solution)/shard_map/all_gather | solution.py:72
  9.7 132.0 %copy-start.9 = (bf16[1,128,1024]{2,1,0:T(8,128)(2,1)S(1)}, bf16[1,128,1024]{2,1,0:T(8,128)(2,1)}, u32[]{:S(2)}) copy-start(bf16[1,128,1024]{2,1,0:T(8,128)(2,1)} %param.7) | copy-start | bytes 786436
  9.8 213.9 %reduce-scatter.2.cloned.1.call-start = ((), (), s32[]{:S(2)}) async-start(), calls=%async_computation.2 | async-start | bytes 1310720 | tf_op jit(solution)/shard_map/reduce_scatter | solution.py:172
  121.3 25.2 %collective-permute-start = (bf16[128,512]{1,0:T(8,128)(2,1)S(1)}, bf16[128,512]{1,0:T(8,128)(2,1)S(1)}, u32[]{:S(2)}, u32[]{:S(2)}) collective-permute-start(bf16[128,512]{1,0:T(8,128)(2,1)S(1)} %fusion.69), channel_id=1, source_target_pairs={{0,16},{4,20},{8,24},{12,28},{16,32},{20,36},{24,40},{28,44},{32,4... | collective-permute-start | bytes 393224 | tf_op jit(solution)/shard_map/ppermute | solution.py:15
  124.4 22.1 %collective-permute-start.1 = (bf16[128,512]{1,0:T(8,128)(2,1)S(1)}, bf16[128,512]{1,0:T(8,128)(2,1)S(1)}, u32[]{:S(2)}, u32[]{:S(2)}) collective-permute-start(bf16[128,512]{1,0:T(8,128)(2,1)S(1)} %fusion.69), channel_id=1, source_target_pairs={{0,12},{4,16},{8,20},{12,24},{16,28},{20,32},{24,36},{28,40},{32,4... | collective-permute-start | bytes 393224 | tf_op jit(solution)/shard_map/ppermute | solution.py:15
  128.3 18.2 %collective-permute-start.2 = (bf16[128,512]{1,0:T(8,128)(2,1)S(1)}, bf16[128,512]{1,0:T(8,128)(2,1)S(1)}, u32[]{:S(2)}, u32[]{:S(2)}) collective-permute-start(bf16[128,512]{1,0:T(8,128)(2,1)S(1)} %fusion.69), channel_id=1, source_target_pairs={{0,8},{4,12},{8,16},{12,20},{16,24},{20,28},{24,32},{28,36},{32,40... | collective-permute-start | bytes 393224 | tf_op jit(solution)/shard_map/ppermute | solution.py:15
  134.8 11.7 %collective-permute-start.3 = (bf16[128,512]{1,0:T(8,128)(2,1)S(1)}, bf16[128,512]{1,0:T(8,128)(2,1)S(1)}, u32[]{:S(2)}, u32[]{:S(2)}) collective-permute-start(bf16[128,512]{1,0:T(8,128)(2,1)S(1)} %fusion.69), channel_id=1, source_target_pairs={{0,4},{4,8},{8,12},{12,16},{16,20},{20,24},{24,28},{28,32},{32,36}... | collective-permute-start | bytes 393224 | tf_op jit(solution)/shard_map/ppermute | solution.py:15
  153.9 1.3 copy-start.6
  154.7 4.6 %copy-start.3 = (bf16[4,128,640]{1,2,0:T(8,128)(2,1)}, bf16[4,128,640]{1,2,0:T(8,128)(2,1)S(1)}, u32[]{:S(2)}) copy-start(bf16[4,128,640]{1,2,0:T(8,128)(2,1)S(1)} %fusion.46) | copy-start | bytes 1966084
  155.3 1.3 copy-start.5
  156.0 3.0 copy-start.1
  161.1 7.2 %collective-permute-start.7 = (bf16[128,512]{0,1:T(8,128)(2,1)S(1)}, bf16[128,512]{0,1:T(8,128)(2,1)S(1)}, u32[]{:S(2)}, u32[]{:S(2)}) collective-permute-start(bf16[128,512]{0,1:T(8,128)(2,1)S(1)} %get-tuple-element.5), channel_id=1, source_target_pairs={{16,0},{20,4},{24,8},{28,12},{32,16},{36,20},{40,24},{44,28},{48,3... | collective-permute-start | bytes 393224 | tf_op jit(solution)/shard_map/ppermute | solution.py:15
  162.4 7.2 %collective-permute-start.6 = (bf16[128,512]{0,1:T(8,128)(2,1)S(1)}, bf16[128,512]{0,1:T(8,128)(2,1)S(1)}, u32[]{:S(2)}, u32[]{:S(2)}) collective-permute-start(bf16[128,512]{0,1:T(8,128)(2,1)S(1)} %get-tuple-element.6), channel_id=1, source_target_pairs={{12,0},{16,4},{20,8},{24,12},{28,16},{32,20},{36,24},{40,28},{44,3... | collective-permute-start | bytes 393224 | tf_op jit(solution)/shard_map/ppermute | solution.py:15
  163.7 10.7 %collective-permute-start.5 = (bf16[128,512]{0,1:T(8,128)(2,1)S(1)}, bf16[128,512]{0,1:T(8,128)(2,1)S(1)}, u32[]{:S(2)}, u32[]{:S(2)}) collective-permute-start(bf16[128,512]{0,1:T(8,128)(2,1)S(1)} %get-tuple-element.7), channel_id=1, source_target_pairs={{8,0},{12,4},{16,8},{20,12},{24,16},{28,20},{32,24},{36,28},{40,32... | collective-permute-start | bytes 393224 | tf_op jit(solution)/shard_map/ppermute | solution.py:15
  165.0 10.6 %collective-permute-start.4 = (bf16[128,512]{0,1:T(8,128)(2,1)S(1)}, bf16[128,512]{0,1:T(8,128)(2,1)S(1)}, u32[]{:S(2)}, u32[]{:S(2)}) collective-permute-start(bf16[128,512]{0,1:T(8,128)(2,1)S(1)} %get-tuple-element.4), channel_id=1, source_target_pairs={{4,0},{8,4},{12,8},{16,12},{20,16},{24,20},{28,24},{32,28},{36,32}... | collective-permute-start | bytes 393224 | tf_op jit(solution)/shard_map/ppermute | solution.py:15
  175.7 0.7 copy-start.7
  224.7 3.9 %collective-permute-start.8 = (f32[128,512]{0,1:T(8,128)S(1)}, f32[128,512]{0,1:T(8,128)S(1)}, u32[]{:S(2)}, u32[]{:S(2)}) collective-permute-start(f32[128,512]{0,1:T(8,128)S(1)} %slice_select_fusion.6), channel_id=1, source_target_pairs={{0,4},{4,0},{8,12},{12,8},{16,20},{20,16},{24,28},{28,24},{32,36},... | collective-permute-start | bytes 786440 | tf_op jit(solution)/shard_map/ppermute | solution.py:20
  228.8 9.4 %collective-permute-start.9 = (f32[64,512]{0,1:T(8,128)S(1)}, f32[64,512]{0,1:T(8,128)S(1)}, u32[]{:S(2)}, u32[]{:S(2)}) collective-permute-start(f32[64,512]{0,1:T(8,128)S(1)} %slice_select_fusion.5), channel_id=1, source_target_pairs={{0,16},{4,20},{8,24},{12,28},{16,0},{20,4},{24,8},{28,12},{32,48},... | collective-permute-start | bytes 393224 | tf_op jit(solution)/shard_map/ppermute | solution.py:20
  238.4 8.5 %collective-permute-start.10 = (f32[32,512]{0,1:T(8,128)S(1)}, f32[32,512]{0,1:T(8,128)S(1)}, u32[]{:S(2)}, u32[]{:S(2)}) collective-permute-start(f32[32,512]{0,1:T(8,128)S(1)} %slice_select_fusion.4), channel_id=1, source_target_pairs={{0,64},{4,68},{8,72},{12,76},{16,80},{20,84},{24,88},{28,92},{32,9... | collective-permute-start | bytes 196616 | tf_op jit(solution)/shard_map/ppermute | solution.py:20
  247.2 17.1 %collective-permute-start.11 = (f32[16,512]{0,1:T(8,128)S(1)}, f32[16,512]{0,1:T(8,128)S(1)}, u32[]{:S(2)}, u32[]{:S(2)}) collective-permute-start(f32[16,512]{0,1:T(8,128)S(1)} %slice_select_fusion.3), channel_id=1, source_target_pairs={{0,8},{4,12},{8,0},{12,4},{16,24},{20,28},{24,16},{28,20},{32,40},... | collective-permute-start | bytes 98312 | tf_op jit(solution)/shard_map/ppermute | solution.py:20
  264.6 8.6 %collective-permute-start.12 = (f32[8,512]{0,1:T(8,128)S(1)}, f32[8,512]{0,1:T(8,128)S(1)}, u32[]{:S(2)}, u32[]{:S(2)}) collective-permute-start(f32[8,512]{0,1:T(8,128)S(1)} %slice_select_fusion.2), channel_id=1, source_target_pairs={{0,32},{4,36},{8,40},{12,44},{16,48},{20,52},{24,56},{28,60},{32,0... | collective-permute-start | bytes 49160 | tf_op jit(solution)/shard_map/ppermute | solution.py:20
  273.5 14.7 %collective-permute-start.13 = (f32[4,512]{0,1:T(8,128)S(1)}, f32[4,512]{0,1:T(8,128)S(1)}, u32[]{:S(2)}, u32[]{:S(2)}) collective-permute-start(f32[4,512]{0,1:T(8,128)S(1)} %slice_select_fusion.1), channel_id=1, source_target_pairs={{0,128},{4,132},{8,136},{12,140},{16,144},{20,148},{24,152},{28,15... | collective-permute-start | bytes 24584 | tf_op jit(solution)/shard_map/ppermute | solution.py:20
  288.3 41.5 %copy-start.4 = (bf16[4,128,640]{1,2,0:T(8,128)(2,1)S(1)}, bf16[4,128,640]{1,2,0:T(8,128)(2,1)}, u32[]{:S(2)}) copy-start(bf16[4,128,640]{1,2,0:T(8,128)(2,1)} %copy-done.3) | copy-start | bytes 1966084
  288.5 53.9 %copy-start.2 = (bf16[4,128,640]{1,2,0:T(8,128)(2,1)S(1)}, bf16[4,128,640]{1,2,0:T(8,128)(2,1)}, u32[]{:S(2)}) copy-start(bf16[4,128,640]{1,2,0:T(8,128)(2,1)} %copy-done.1) | copy-start | bytes 1966084
  288.5 14.8 %collective-permute-start.14 = (f32[2,512]{0,1:T(8,128)S(1)}, f32[2,512]{0,1:T(8,128)S(1)}, u32[]{:S(2)}, u32[]{:S(2)}) collective-permute-start(f32[2,512]{0,1:T(8,128)S(1)} %slice_select_fusion), channel_id=1, source_target_pairs={{0,256},{4,260},{8,264},{12,268},{16,272},{20,276},{24,280},{28,28... | collective-permute-start | bytes 12296 | tf_op jit(solution)/shard_map/ppermute | solution.py:20
  304.1 14.4 %collective-permute-start.15 = (f32[2,512]{0,1:T(8,128)}, f32[2,512]{0,1:T(8,128)}, u32[]{:S(2)}, u32[]{:S(2)}) collective-permute-start(f32[2,512]{0,1:T(8,128)} %select_add_fusion), channel_id=1, source_target_pairs={{0,256},{4,260},{8,264},{12,268},{16,272},{20,276},{24,280},{28,28... | collective-permute-start | bytes 12296 | tf_op jit(solution)/shard_map/ppermute | solution.py:20
  319.6 5.3 %collective-permute-start.16 = (f32[4,512]{1,0:T(4,128)S(1)}, f32[4,512]{1,0:T(4,128)S(1)}, u32[]{:S(2)}, u32[]{:S(2)}) collective-permute-start(f32[4,512]{1,0:T(4,128)S(1)} %maximum_select_fusion.6), channel_id=1, source_target_pairs={{0,128},{4,132},{8,136},{12,140},{16,144},{20,148},{24,152},{28,15... | collective-permute-start | bytes 24584 | tf_op jit(solution)/shard_map/ppermute | solution.py:20
  324.9 6.1 %collective-permute-start.17 = (f32[8,512]{1,0:T(8,128)S(1)}, f32[8,512]{1,0:T(8,128)S(1)}, u32[]{:S(2)}, u32[]{:S(2)}) collective-permute-start(f32[8,512]{1,0:T(8,128)S(1)} %maximum_select_fusion.5), channel_id=1, source_target_pairs={{0,32},{4,36},{8,40},{12,44},{16,48},{20,52},{24,56},{28,60},{32,0... | collective-permute-start | bytes 49160 | tf_op jit(solution)/shard_map/ppermute | solution.py:20
  331.0 12.7 %collective-permute-start.18 = (f32[16,512]{1,0:T(8,128)S(1)}, f32[16,512]{1,0:T(8,128)S(1)}, u32[]{:S(2)}, u32[]{:S(2)}) collective-permute-start(f32[16,512]{1,0:T(8,128)S(1)} %maximum_select_fusion.4), channel_id=1, source_target_pairs={{0,8},{4,12},{8,0},{12,4},{16,24},{20,28},{24,16},{28,20},{32,40},... | collective-permute-start | bytes 98312 | tf_op jit(solution)/shard_map/ppermute | solution.py:20
  343.7 5.3 %collective-permute-start.19 = (f32[32,512]{1,0:T(8,128)S(1)}, f32[32,512]{1,0:T(8,128)S(1)}, u32[]{:S(2)}, u32[]{:S(2)}) collective-permute-start(f32[32,512]{1,0:T(8,128)S(1)} %maximum_select_fusion.3), channel_id=1, source_target_pairs={{0,64},{4,68},{8,72},{12,76},{16,80},{20,84},{24,88},{28,92},{32,9... | collective-permute-start | bytes 196616 | tf_op jit(solution)/shard_map/ppermute | solution.py:20
  349.0 10.2 %collective-permute-start.20 = (f32[64,512]{1,0:T(8,128)S(1)}, f32[64,512]{1,0:T(8,128)S(1)}, u32[]{:S(2)}, u32[]{:S(2)}) collective-permute-start(f32[64,512]{1,0:T(8,128)S(1)} %maximum_select_fusion.2), channel_id=1, source_target_pairs={{0,16},{4,20},{8,24},{12,28},{16,0},{20,4},{24,8},{28,12},{32,48},... | collective-permute-start | bytes 393224 | tf_op jit(solution)/shard_map/ppermute | solution.py:20
  359.2 12.3 %collective-permute-start.21 = (f32[128,512]{1,0:T(8,128)S(1)}, f32[128,512]{1,0:T(8,128)S(1)}, u32[]{:S(2)}, u32[]{:S(2)}) collective-permute-start(f32[128,512]{1,0:T(8,128)S(1)} %maximum_select_fusion.1), channel_id=1, source_target_pairs={{0,4},{4,0},{8,12},{12,8},{16,20},{20,16},{24,28},{28,24},{32,36},... | collective-permute-start | bytes 786440 | tf_op jit(solution)/shard_map/ppermute | solution.py:20
  366.6 2.5 copy-start.8
Sparse Core Ops, SparseCore 0:
  10.1 109.5 all-gather.1
  177.9 45.6 reduce-scatter.1

commit v3 on v2

--- a/solution.py
+++ b/solution.py
@@ -44,6 +44,58 @@
     return current
 
 
+def digit_target(source, stride, size, offset):
+    digit = (source // stride) % size
+    return source + (((digit + offset) % size) - digit) * stride
+
+
+def scatter_stage(value, axis, stride, size, wire):
+    block = value.shape[0] // size
+    digit = (lax.axis_index(axis) // stride) % size
+    count = lax.axis_size(axis)
+    total = lax.dynamic_slice_in_dim(value, digit * block, block, 0).astype(jnp.float32)
+    for offset in range(1, size):
+        part = lax.dynamic_slice_in_dim(value, ((digit + offset) % size) * block, block, 0)
+        pairs = [(source, digit_target(source, stride, size, offset)) for source in range(count)]
+        total = total + lax.ppermute(part.astype(wire), axis, pairs).astype(jnp.float32)
+    return total
+
+
+def gather_stage(value, axis, stride, size):
+    block = value.shape[0]
+    digit = (lax.axis_index(axis) // stride) % size
+    count = lax.axis_size(axis)
+    full = jnp.zeros((block * size,) + value.shape[1:], value.dtype)
+    full = lax.dynamic_update_slice_in_dim(full, value, digit * block, 0)
+    for offset in range(1, size):
+        pairs = [(source, digit_target(source, stride, size, offset)) for source in range(count)]
+        moved = lax.ppermute(value, axis, pairs)
+        full = lax.dynamic_update_slice_in_dim(full, moved, ((digit - offset) % size) * block, 0)
+    return full
+
+
+TM_STAGES = ((4, 4), (16, 8), (1, 4))
+
+
+def staged_grad_sum(partial):
+    stream_count = lax.axis_size("stream")
+    tm_count = lax.axis_size("tm")
+    product = 1
+    for _, size in TM_STAGES:
+        product *= size
+    if product != tm_count or partial.shape[0] % (stream_count * tm_count):
+        shard = lax.psum_scatter(
+            partial.astype(jnp.bfloat16), "stream", scatter_dimension=0, tiled=True
+        ).astype(jnp.float32)
+        return tree_psum(shard, "tm")
+    current = scatter_stage(partial, "stream", 1, stream_count, jnp.bfloat16)
+    for stride, size in TM_STAGES:
+        current = scatter_stage(current, "tm", stride, size, jnp.float32)
+    for stride, size in reversed(TM_STAGES):
+        current = gather_stage(current, "tm", stride, size)
+    return current
+
+
 def contract_last(left, right):
     return lax.dot_general(
         left, right, (((1,), (1,)), ((), ())), preferred_element_type=jnp.float32
@@ -169,13 +221,7 @@
         keyval_grads, keyval_full
     )
     input_grad = input_grad.astype(jnp.bfloat16)
-    grad_shard = lax.psum_scatter(
-        contract_first(record_rows, keyval_grads).astype(jnp.bfloat16),
-        "stream",
-        scatter_dimension=0,
-        tiled=True,
-    ).astype(jnp.float32)
-    weight_grad = tree_psum(grad_shard, "tm")
+    weight_grad = staged_grad_sum(contract_first(record_rows, keyval_grads))
     return (input_grad[None], weight_grad)
 
 

time: 381 us -> 419 us (1.100)
  starting transfers between devices: 99.2 us -> 155 us
  waiting for transfers between devices: 226 us -> 201 us
    ppermute x14 -> x29, starting transfers between devices: 72.9 us -> 129 us  [the longest x16 68.7 us: scatter_stage(): lax.ppermute(part.astype(wire), axis, pairs).astype(jnp.float32)]
    reduce_scatter x1 -> x0, waiting for transfers between devices: 45.9 us -> none  [per_device(): lax.psum_scatter(contract_first(record_rows, keyval_grads).astype(jnp.bfl...]
    ppermute x14 -> x29, waiting for transfers between devices: 63 us -> 83.8 us  [the longest x16 66.5 us: scatter_stage(): lax.ppermute(part.astype(wire), axis, pairs).astype(jnp.float32)]
  transfers between devices with their start and end apart: 24 -> 38, of which waited for: 19 -> 20; matrix products, arithmetic and copies ran while one was open for 3% -> 3% of each run, Pallas kernels for 0% -> 0%
where the time goes in v3:
time: 419 us; the launch traced here: 414 us
  waiting for transfers between devices  201 us (48%)
  starting transfers between devices  155 us (37%)
  matrix products  26.3 us (6%)
  between operations  16.5 us (4%)
  local copies, waits for them, and re-layouts  7.51 us (2%)
  other arithmetic  7.08 us (2%)
    all_gather x1, waiting for transfers between devices, per_device(): lax.all_gather(jnp.concatenate([query_weight, keyval_weight, output_weigh...  109 us
    ppermute x16, starting transfers between devices, scatter_stage(): lax.ppermute(part.astype(wire), axis, pairs).astype(jnp.float32)  68.7 us
    ppermute x16, waiting for transfers between devices, scatter_stage(): lax.ppermute(part.astype(wire), axis, pairs).astype(jnp.float32)  66.5 us
    ppermute x13, starting transfers between devices, gather_stage(): moved = lax.ppermute(value, axis, pairs)  60.3 us
    ppermute x8, starting transfers between devices, shifted(): lax.ppermute(value, axis, [(source, source + steps) for source in range(l...  26.2 us
    ppermute x13, waiting for transfers between devices, gather_stage(): moved = lax.ppermute(value, axis, pairs)  17.3 us
  transfers between devices with their start and end apart: 38, of which 20 were waited for; matrix products, arithmetic and copies ran while one was open for 3% of the time, Pallas kernels for 0%

profile of v3, /device:TPU:1, one launch (start us, length us, event | category | flops | bytes accessed | tf_op | source)
XLA Modules:
  0.0 413.6 jit_solution(13408181809525043693)
XLA Ops:
  7.2 2.5 pad_maximum_fusion
  10.8 108.9 %all-gather.2.cloned.1.call-done = bf16[1024,2560]{1,0:T(8,128)(2,1)} async-done(((bf16[256,2560]{1,0:T(8,128)(2,1)}), bf16[1024,2560]{1,0:T(8,128)(2,1)}) %all-gather.2.cloned.1.call-update) | async-done | bytes 5242896 | tf_op jit(solution)/shard_map/all_gather | solution.py:124
  119.8 1.5 fusion.68
  121.3 3.1 collective-permute-start
  124.4 3.9 collective-permute-start.1
  128.3 6.5 %collective-permute-start.2 = (bf16[128,512]{1,0:T(8,128)(2,1)S(1)}, bf16[128,512]{1,0:T(8,128)(2,1)S(1)}, u32[]{:S(2)}, u32[]{:S(2)}) collective-permute-start(bf16[128,512]{1,0:T(8,128)(2,1)S(1)} %fusion.68), channel_id=1, source_target_pairs={{0,8},{4,12},{8,16},{12,20},{16,24},{20,28},{24,32},{28,36},{32,40... | collective-permute-start | bytes 393224 | tf_op jit(solution)/shard_map/ppermute | solution.py:15
  134.8 6.9 %collective-permute-start.3 = (bf16[128,512]{1,0:T(8,128)(2,1)S(1)}, bf16[128,512]{1,0:T(8,128)(2,1)S(1)}, u32[]{:S(2)}, u32[]{:S(2)}) collective-permute-start(bf16[128,512]{1,0:T(8,128)(2,1)S(1)} %fusion.68), channel_id=1, source_target_pairs={{0,4},{4,8},{8,12},{12,16},{16,20},{20,24},{24,28},{28,32},{32,36}... | collective-permute-start | bytes 393224 | tf_op jit(solution)/shard_map/ppermute | solution.py:15
  141.8 2.3 fusion.53
  144.8 2.3 fusion.56
  147.9 1.7 fusion.133
  150.3 1.7 fusion.131
  152.0 3.2 fusion.132
  155.9 1.4 divide_convert_fusion
  166.0 1.3 collective-permute-start.7
  167.3 1.3 collective-permute-start.6
  168.6 1.3 collective-permute-start.5
  169.9 1.9 collective-permute-start.4
  172.3 1.2 collective-permute-done.6
  173.6 4.6 %collective-permute-done.5 = bf16[128,512]{0,1:T(8,128)(2,1)S(1)} collective-permute-done((bf16[128,512]{0,1:T(8,128)(2,1)S(1)}, bf16[128,512]{0,1:T(8,128)(2,1)S(1)}, u32[]{:S(2)}, u32[]{:S(2)}) %collective-permute-start.5) | collective-permute-done | bytes 131104 | tf_op jit(solution)/shard_map/ppermute | solution.py:15
  178.2 2.0 collective-permute-done.4
  181.6 5.9 %collective-permute-start.10 = (bf16[256,512]{0,1:T(8,128)(2,1)}, bf16[256,512]{0,1:T(8,128)(2,1)}, u32[]{:S(2)}, u32[]{:S(2)}) collective-permute-start(bf16[256,512]{0,1:T(8,128)(2,1)} %get-tuple-element.3), channel_id=1, source_target_pairs={{0,3},{1,0},{2,1},{3,2},{4,7},{5,4},{6,5},{7,6},{8,11},{9,8},{10,9... | collective-permute-start | bytes 786440 | tf_op jit(solution)/shard_map/ppermute | solution.py:60
  187.5 4.3 %collective-permute-start.9 = (bf16[256,512]{0,1:T(8,128)(2,1)}, bf16[256,512]{0,1:T(8,128)(2,1)}, u32[]{:S(2)}, u32[]{:S(2)}) collective-permute-start(bf16[256,512]{0,1:T(8,128)(2,1)} %get-tuple-element.4), channel_id=1, source_target_pairs={{0,2},{1,3},{2,0},{3,1},{4,6},{5,7},{6,4},{7,5},{8,10},{9,11},{10,... | collective-permute-start | bytes 786440 | tf_op jit(solution)/shard_map/ppermute | solution.py:60
  191.8 3.4 collective-permute-start.8
  195.7 1.4 convolution_convert_fusion.1
  197.2 15.3 %collective-permute-done.9 = bf16[256,512]{0,1:T(8,128)(2,1)} collective-permute-done((bf16[256,512]{0,1:T(8,128)(2,1)}, bf16[256,512]{0,1:T(8,128)(2,1)}, u32[]{:S(2)}, u32[]{:S(2)}) %collective-permute-start.9) | collective-permute-done | bytes 262176 | tf_op jit(solution)/shard_map/ppermute | solution.py:60
  212.5 1.2 fusion.88
  214.0 7.9 %collective-permute-start.13 = (f32[64,512]{0,1:T(8,128)S(1)}, f32[64,512]{0,1:T(8,128)S(1)}, u32[]{:S(2)}, u32[]{:S(2)}) collective-permute-start(f32[64,512]{0,1:T(8,128)S(1)} %get-tuple-element.10), channel_id=1, source_target_pairs={{0,48},{4,52},{8,56},{12,60},{16,0},{20,4},{24,8},{28,12},{32,16},... | collective-permute-start | bytes 393224 | tf_op jit(solution)/shard_map/ppermute | solution.py:60
  221.9 2.2 collective-permute-start.12
  224.1 2.9 collective-permute-start.11
  227.3 6.1 %collective-permute-done.13 = f32[64,512]{0,1:T(8,128)S(1)} collective-permute-done((f32[64,512]{0,1:T(8,128)S(1)}, f32[64,512]{0,1:T(8,128)S(1)}, u32[]{:S(2)}, u32[]{:S(2)}) %collective-permute-start.13) | collective-permute-done | bytes 131104 | tf_op jit(solution)/shard_map/ppermute | solution.py:60
  233.4 5.8 %collective-permute-done.11 = f32[64,512]{0,1:T(8,128)S(1)} collective-permute-done((f32[64,512]{0,1:T(8,128)S(1)}, f32[64,512]{0,1:T(8,128)S(1)}, u32[]{:S(2)}, u32[]{:S(2)}) %collective-permute-start.11) | collective-permute-done | bytes 131104 | tf_op jit(solution)/shard_map/ppermute | solution.py:60
  239.9 5.7 %collective-permute-start.20 = (f32[8,512]{0,1:T(8,128)S(1)}, f32[8,512]{0,1:T(8,128)S(1)}, u32[]{:S(2)}, u32[]{:S(2)}) collective-permute-start(f32[8,512]{0,1:T(8,128)S(1)} %get-tuple-element.16), channel_id=1, source_target_pairs={{0,448},{4,452},{8,456},{12,460},{16,464},{20,468},{24,472},{28,47... | collective-permute-start | bytes 49160 | tf_op jit(solution)/shard_map/ppermute | solution.py:60
  245.6 3.5 collective-permute-start.19
  249.5 2.3 collective-permute-start.18
  251.8 6.5 %collective-permute-start.17 = (f32[8,512]{0,1:T(8,128)S(1)}, f32[8,512]{0,1:T(8,128)S(1)}, u32[]{:S(2)}, u32[]{:S(2)}) collective-permute-start(f32[8,512]{0,1:T(8,128)S(1)} %get-tuple-element.19), channel_id=1, source_target_pairs={{0,256},{4,260},{8,264},{12,268},{16,272},{20,276},{24,280},{28,28... | collective-permute-start | bytes 49160 | tf_op jit(solution)/shard_map/ppermute | solution.py:60
  258.3 1.9 collective-permute-start.16
  260.2 4.2 %collective-permute-start.15 = (f32[8,512]{0,1:T(8,128)S(1)}, f32[8,512]{0,1:T(8,128)S(1)}, u32[]{:S(2)}, u32[]{:S(2)}) collective-permute-start(f32[8,512]{0,1:T(8,128)S(1)} %get-tuple-element.21), channel_id=1, source_target_pairs={{0,128},{4,132},{8,136},{12,140},{16,144},{20,148},{24,152},{28,15... | collective-permute-start | bytes 49160 | tf_op jit(solution)/shard_map/ppermute | solution.py:60
  264.4 3.1 collective-permute-start.14
  267.8 22.2 %collective-permute-done.18 = f32[8,512]{0,1:T(8,128)S(1)} collective-permute-done((f32[8,512]{0,1:T(8,128)S(1)}, f32[8,512]{0,1:T(8,128)S(1)}, u32[]{:S(2)}, u32[]{:S(2)}) %collective-permute-start.18) | collective-permute-done | bytes 16416 | tf_op jit(solution)/shard_map/ppermute | solution.py:60
  290.0 3.6 collective-permute-done.15
  293.7 11.8 %collective-permute-done.14 = f32[8,512]{0,1:T(8,128)S(1)} collective-permute-done((f32[8,512]{0,1:T(8,128)S(1)}, f32[8,512]{0,1:T(8,128)S(1)}, u32[]{:S(2)}, u32[]{:S(2)}) %collective-permute-start.14) | collective-permute-done | bytes 16416 | tf_op jit(solution)/shard_map/ppermute | solution.py:60
  305.9 2.4 collective-permute-start.23
  308.3 5.2 %collective-permute-start.22 = (f32[2,512]{0,1:T(8,128)S(1)}, f32[2,512]{0,1:T(8,128)S(1)}, u32[]{:S(2)}, u32[]{:S(2)}) collective-permute-start(f32[2,512]{0,1:T(8,128)S(1)} %get-tuple-element.14), channel_id=1, source_target_pairs={{0,8},{4,12},{8,0},{12,4},{16,24},{20,28},{24,16},{28,20},{32,40},... | collective-permute-start | bytes 12296 | tf_op jit(solution)/shard_map/ppermute | solution.py:60
  313.5 7.3 %collective-permute-start.21 = (f32[2,512]{0,1:T(8,128)S(1)}, f32[2,512]{0,1:T(8,128)S(1)}, u32[]{:S(2)}, u32[]{:S(2)}) collective-permute-start(f32[2,512]{0,1:T(8,128)S(1)} %get-tuple-element.12), channel_id=1, source_target_pairs={{0,4},{4,8},{8,12},{12,0},{16,20},{20,24},{24,28},{28,16},{32,36},... | collective-permute-start | bytes 12296 | tf_op jit(solution)/shard_map/ppermute | solution.py:60
  320.8 2.4 fusion.6
  323.3 1.6 collective-permute-done.21
  325.1 8.4 %collective-permute-start.24 = (f32[2,512]{0,1:T(8,128)S(1)}, f32[2,512]{0,1:T(8,128)S(1)}, u32[]{:S(2)}, u32[]{:S(2)}) collective-permute-start(f32[2,512]{0,1:T(8,128)S(1)} %add_add_fusion), channel_id=1, source_target_pairs={{0,4},{4,8},{8,12},{12,0},{16,20},{20,24},{24,28},{28,16},{32,36},... | collective-permute-start | bytes 12296 | tf_op jit(solution)/shard_map/ppermute | solution.py:72
  333.6 4.0 collective-permute-start.25
  337.6 1.9 collective-permute-start.26
  339.5 2.3 collective-permute-done.24
  342.0 8.9 %collective-permute-done.25 = f32[2,512]{0,1:T(8,128)S(1)} collective-permute-done((f32[2,512]{0,1:T(8,128)S(1)}, f32[2,512]{0,1:T(8,128)S(1)}, u32[]{:S(2)}, u32[]{:S(2)}) %collective-permute-start.25) | collective-permute-done | bytes 4128 | tf_op jit(solution)/shard_map/ppermute | solution.py:72
  351.6 1.9 collective-permute-start.27
  353.6 2.0 collective-permute-start.28
  355.6 20.4 %collective-permute-start.29 = (f32[8,512]{1,0:T(8,128)S(1)}, f32[8,512]{1,0:T(8,128)S(1)}, u32[]{:S(2)}, u32[]{:S(2)}) collective-permute-start(f32[8,512]{1,0:T(8,128)S(1)} %constant_dynamic-update-slice_fusion.17), channel_id=1, source_target_pairs={{0,192},{4,196},{8,200},{12,204},{16,208},{20,212},{24,216},{28,22... | collective-permute-start | bytes 49160 | tf_op jit(solution)/shard_map/ppermute | solution.py:72
  376.0 1.9 collective-permute-start.30
  377.9 6.1 %collective-permute-start.31 = (f32[8,512]{1,0:T(8,128)S(1)}, f32[8,512]{1,0:T(8,128)S(1)}, u32[]{:S(2)}, u32[]{:S(2)}) collective-permute-start(f32[8,512]{1,0:T(8,128)S(1)} %constant_dynamic-update-slice_fusion.17), channel_id=1, source_target_pairs={{0,320},{4,324},{8,328},{12,332},{16,336},{20,340},{24,344},{28,34... | collective-permute-start | bytes 49160 | tf_op jit(solution)/shard_map/ppermute | solution.py:72
  384.0 1.9 collective-permute-start.32
  386.0 3.4 collective-permute-start.33
  389.6 2.3 collective-permute-done.33
  391.9 1.9 collective-permute-start.34
  393.9 2.4 fusion.59
  396.3 3.6 collective-permute-start.35
  399.9 2.9 collective-permute-start.36
  403.6 2.4 collective-permute-done.36
  (139 shorter events, 18.6 us)
Async XLA Ops:
  7.2 112.6 %copy-start = (bf16[1,128,1024]{2,1,0:T(8,128)(2,1)S(1)}, bf16[1,128,1024]{2,1,0:T(8,128)(2,1)}, u32[]{:S(2)}) copy-start(bf16[1,128,1024]{2,1,0:T(8,128)(2,1)} %param.6) | copy-start | bytes 786436
  7.2 112.6 %all-gather.2.cloned.1.call-start = ((), (), s32[]{:S(2)}) async-start(), calls=%async_computation | async-start | bytes 6553600 | tf_op jit(solution)/shard_map/all_gather | solution.py:124
  9.7 132.0 %copy-start.21 = (bf16[1,128,1024]{2,1,0:T(8,128)(2,1)S(1)}, bf16[1,128,1024]{2,1,0:T(8,128)(2,1)}, u32[]{:S(2)}) copy-start(bf16[1,128,1024]{2,1,0:T(8,128)(2,1)} %param.7) | copy-start | bytes 786436
  10.8 138.8 %copy-start.20 = (pred[128,640]{0,1:T(8,128)(4,1)}, pred[128,640]{0,1:T(8,128)(4,1)S(1)}, u32[]{:S(2)}) copy-start(pred[128,640]{0,1:T(8,128)(4,1)S(1)} %fusion.92) | copy-start | bytes 245764
  121.3 26.5 %collective-permute-start = (bf16[128,512]{1,0:T(8,128)(2,1)S(1)}, bf16[128,512]{1,0:T(8,128)(2,1)S(1)}, u32[]{:S(2)}, u32[]{:S(2)}) collective-permute-start(bf16[128,512]{1,0:T(8,128)(2,1)S(1)} %fusion.68), channel_id=1, source_target_pairs={{0,16},{4,20},{8,24},{12,28},{16,32},{20,36},{24,40},{28,44},{32,4... | collective-permute-start | bytes 393224 | tf_op jit(solution)/shard_map/ppermute | solution.py:15
  124.4 23.4 %collective-permute-start.1 = (bf16[128,512]{1,0:T(8,128)(2,1)S(1)}, bf16[128,512]{1,0:T(8,128)(2,1)S(1)}, u32[]{:S(2)}, u32[]{:S(2)}) collective-permute-start(bf16[128,512]{1,0:T(8,128)(2,1)S(1)} %fusion.68), channel_id=1, source_target_pairs={{0,12},{4,16},{8,20},{12,24},{16,28},{20,32},{24,36},{28,40},{32,4... | collective-permute-start | bytes 393224 | tf_op jit(solution)/shard_map/ppermute | solution.py:15
  128.3 19.5 %collective-permute-start.2 = (bf16[128,512]{1,0:T(8,128)(2,1)S(1)}, bf16[128,512]{1,0:T(8,128)(2,1)S(1)}, u32[]{:S(2)}, u32[]{:S(2)}) collective-permute-start(bf16[128,512]{1,0:T(8,128)(2,1)S(1)} %fusion.68), channel_id=1, source_target_pairs={{0,8},{4,12},{8,16},{12,20},{16,24},{20,28},{24,32},{28,36},{32,40... | collective-permute-start | bytes 393224 | tf_op jit(solution)/shard_map/ppermute | solution.py:15
  134.8 13.0 %collective-permute-start.3 = (bf16[128,512]{1,0:T(8,128)(2,1)S(1)}, bf16[128,512]{1,0:T(8,128)(2,1)S(1)}, u32[]{:S(2)}, u32[]{:S(2)}) collective-permute-start(bf16[128,512]{1,0:T(8,128)(2,1)S(1)} %fusion.68), channel_id=1, source_target_pairs={{0,4},{4,8},{8,12},{12,16},{16,20},{20,24},{24,28},{28,32},{32,36}... | collective-permute-start | bytes 393224 | tf_op jit(solution)/shard_map/ppermute | solution.py:15
  147.8 1.9 copy-start.14
  147.8 1.9 copy-start.18
  155.2 2.1 copy-start.9
  157.3 1.3 copy-start.8
  158.1 6.0 %copy-start.7 = (bf16[4,128,640]{1,2,0:T(8,128)(2,1)}, bf16[4,128,640]{1,2,0:T(8,128)(2,1)S(1)}, u32[]{:S(2)}) copy-start(bf16[4,128,640]{1,2,0:T(8,128)(2,1)S(1)} %fusion.45) | copy-start | bytes 1966084
  158.2 1.0 copy-start.10
  159.7 4.1 copy-start.5
  159.8 0.9 copy-start.11
  161.5 1.9 copy-start.3
  161.5 0.9 copy-start.12
  161.6 1.4 copy-start.19
  162.6 0.8 copy-start.17
  162.7 1.2 copy-start.16
  163.0 1.1 copy-start.1
  163.0 1.1 copy-start.15
  166.0 6.4 %collective-permute-start.7 = (bf16[128,512]{0,1:T(8,128)(2,1)S(1)}, bf16[128,512]{0,1:T(8,128)(2,1)S(1)}, u32[]{:S(2)}, u32[]{:S(2)}) collective-permute-start(bf16[128,512]{0,1:T(8,128)(2,1)S(1)} %get-tuple-element.6), channel_id=1, source_target_pairs={{16,0},{20,4},{24,8},{28,12},{32,16},{36,20},{40,24},{44,28},{48,3... | collective-permute-start | bytes 393224 | tf_op jit(solution)/shard_map/ppermute | solution.py:15
  167.3 6.3 %collective-permute-start.6 = (bf16[128,512]{0,1:T(8,128)(2,1)S(1)}, bf16[128,512]{0,1:T(8,128)(2,1)S(1)}, u32[]{:S(2)}, u32[]{:S(2)}) collective-permute-start(bf16[128,512]{0,1:T(8,128)(2,1)S(1)} %get-tuple-element.7), channel_id=1, source_target_pairs={{12,0},{16,4},{20,8},{24,12},{28,16},{32,20},{36,24},{40,28},{44,3... | collective-permute-start | bytes 393224 | tf_op jit(solution)/shard_map/ppermute | solution.py:15
  168.6 9.6 %collective-permute-start.5 = (bf16[128,512]{0,1:T(8,128)(2,1)S(1)}, bf16[128,512]{0,1:T(8,128)(2,1)S(1)}, u32[]{:S(2)}, u32[]{:S(2)}) collective-permute-start(bf16[128,512]{0,1:T(8,128)(2,1)S(1)} %get-tuple-element.8), channel_id=1, source_target_pairs={{8,0},{12,4},{16,8},{20,12},{24,16},{28,20},{32,24},{36,28},{40,32... | collective-permute-start | bytes 393224 | tf_op jit(solution)/shard_map/ppermute | solution.py:15
  169.9 10.3 %collective-permute-start.4 = (bf16[128,512]{0,1:T(8,128)(2,1)S(1)}, bf16[128,512]{0,1:T(8,128)(2,1)S(1)}, u32[]{:S(2)}, u32[]{:S(2)}) collective-permute-start(bf16[128,512]{0,1:T(8,128)(2,1)S(1)} %get-tuple-element.5), channel_id=1, source_target_pairs={{4,0},{8,4},{12,8},{16,12},{20,16},{24,20},{28,24},{32,28},{36,32}... | collective-permute-start | bytes 393224 | tf_op jit(solution)/shard_map/ppermute | solution.py:15
  181.6 15.6 %collective-permute-start.10 = (bf16[256,512]{0,1:T(8,128)(2,1)}, bf16[256,512]{0,1:T(8,128)(2,1)}, u32[]{:S(2)}, u32[]{:S(2)}) collective-permute-start(bf16[256,512]{0,1:T(8,128)(2,1)} %get-tuple-element.3), channel_id=1, source_target_pairs={{0,3},{1,0},{2,1},{3,2},{4,7},{5,4},{6,5},{7,6},{8,11},{9,8},{10,9... | collective-permute-start | bytes 786440 | tf_op jit(solution)/shard_map/ppermute | solution.py:60
  187.5 25.0 %collective-permute-start.9 = (bf16[256,512]{0,1:T(8,128)(2,1)}, bf16[256,512]{0,1:T(8,128)(2,1)}, u32[]{:S(2)}, u32[]{:S(2)}) collective-permute-start(bf16[256,512]{0,1:T(8,128)(2,1)} %get-tuple-element.4), channel_id=1, source_target_pairs={{0,2},{1,3},{2,0},{3,1},{4,6},{5,7},{6,4},{7,5},{8,10},{9,11},{10,... | collective-permute-start | bytes 786440 | tf_op jit(solution)/shard_map/ppermute | solution.py:60
  191.8 20.7 %collective-permute-start.8 = (bf16[256,512]{0,1:T(8,128)(2,1)S(1)}, bf16[256,512]{0,1:T(8,128)(2,1)}, u32[]{:S(2)}, u32[]{:S(2)}) collective-permute-start(bf16[256,512]{0,1:T(8,128)(2,1)S(1)} %get-tuple-element.2), channel_id=1, source_target_pairs={{0,1},{1,2},{2,3},{3,0},{4,5},{5,6},{6,7},{7,4},{8,9},{9,10},{10,1... | collective-permute-start | bytes 786440 | tf_op jit(solution)/shard_map/ppermute | solution.py:60
  197.1 30.0 %copy-start.6 = (bf16[4,128,640]{1,2,0:T(8,128)(2,1)S(1)}, bf16[4,128,640]{1,2,0:T(8,128)(2,1)}, u32[]{:S(2)}) copy-start(bf16[4,128,640]{1,2,0:T(8,128)(2,1)} %copy-done.5) | copy-start | bytes 1966084
  214.0 19.4 %collective-permute-start.13 = (f32[64,512]{0,1:T(8,128)S(1)}, f32[64,512]{0,1:T(8,128)S(1)}, u32[]{:S(2)}, u32[]{:S(2)}) collective-permute-start(f32[64,512]{0,1:T(8,128)S(1)} %get-tuple-element.10), channel_id=1, source_target_pairs={{0,48},{4,52},{8,56},{12,60},{16,0},{20,4},{24,8},{28,12},{32,16},... | collective-permute-start | bytes 393224 | tf_op jit(solution)/shard_map/ppermute | solution.py:60
  221.9 11.5 %collective-permute-start.12 = (f32[64,512]{0,1:T(8,128)S(1)}, f32[64,512]{0,1:T(8,128)S(1)}, u32[]{:S(2)}, u32[]{:S(2)}) collective-permute-start(f32[64,512]{0,1:T(8,128)S(1)} %get-tuple-element.11), channel_id=1, source_target_pairs={{0,32},{4,36},{8,40},{12,44},{16,48},{20,52},{24,56},{28,60},{32,0... | collective-permute-start | bytes 393224 | tf_op jit(solution)/shard_map/ppermute | solution.py:60
  224.1 15.1 %collective-permute-start.11 = (f32[64,512]{0,1:T(8,128)S(1)}, f32[64,512]{0,1:T(8,128)S(1)}, u32[]{:S(2)}, u32[]{:S(2)}) collective-permute-start(f32[64,512]{0,1:T(8,128)S(1)} %get-tuple-element.9), channel_id=1, source_target_pairs={{0,16},{4,20},{8,24},{12,28},{16,32},{20,36},{24,40},{28,44},{32,4... | collective-permute-start | bytes 393224 | tf_op jit(solution)/shard_map/ppermute | solution.py:60
  239.4 9.8 %copy-start.4 = (bf16[4,128,640]{1,2,0:T(8,128)(2,1)S(1)}, bf16[4,128,640]{1,2,0:T(8,128)(2,1)}, u32[]{:S(2)}) copy-start(bf16[4,128,640]{1,2,0:T(8,128)(2,1)} %copy-done.3) | copy-start | bytes 1966084
  239.4 28.1 %copy-start.2 = (bf16[4,128,640]{1,2,0:T(8,128)(2,1)S(1)}, bf16[4,128,640]{1,2,0:T(8,128)(2,1)}, u32[]{:S(2)}) copy-start(bf16[4,128,640]{1,2,0:T(8,128)(2,1)} %copy-done.1) | copy-start | bytes 1966084
  239.9 20.3 %collective-permute-start.20 = (f32[8,512]{0,1:T(8,128)S(1)}, f32[8,512]{0,1:T(8,128)S(1)}, u32[]{:S(2)}, u32[]{:S(2)}) collective-permute-start(f32[8,512]{0,1:T(8,128)S(1)} %get-tuple-element.16), channel_id=1, source_target_pairs={{0,448},{4,452},{8,456},{12,460},{16,464},{20,468},{24,472},{28,47... | collective-permute-start | bytes 49160 | tf_op jit(solution)/shard_map/ppermute | solution.py:60
  245.6 18.8 %collective-permute-start.19 = (f32[8,512]{0,1:T(8,128)S(1)}, f32[8,512]{0,1:T(8,128)S(1)}, u32[]{:S(2)}, u32[]{:S(2)}) collective-permute-start(f32[8,512]{0,1:T(8,128)S(1)} %get-tuple-element.17), channel_id=1, source_target_pairs={{0,384},{4,388},{8,392},{12,396},{16,400},{20,404},{24,408},{28,41... | collective-permute-start | bytes 49160 | tf_op jit(solution)/shard_map/ppermute | solution.py:60
  249.5 40.5 %collective-permute-start.18 = (f32[8,512]{0,1:T(8,128)S(1)}, f32[8,512]{0,1:T(8,128)S(1)}, u32[]{:S(2)}, u32[]{:S(2)}) collective-permute-start(f32[8,512]{0,1:T(8,128)S(1)} %get-tuple-element.18), channel_id=1, source_target_pairs={{0,320},{4,324},{8,328},{12,332},{16,336},{20,340},{24,344},{28,34... | collective-permute-start | bytes 49160 | tf_op jit(solution)/shard_map/ppermute | solution.py:60
  251.8 38.2 %collective-permute-start.17 = (f32[8,512]{0,1:T(8,128)S(1)}, f32[8,512]{0,1:T(8,128)S(1)}, u32[]{:S(2)}, u32[]{:S(2)}) collective-permute-start(f32[8,512]{0,1:T(8,128)S(1)} %get-tuple-element.19), channel_id=1, source_target_pairs={{0,256},{4,260},{8,264},{12,268},{16,272},{20,276},{24,280},{28,28... | collective-permute-start | bytes 49160 | tf_op jit(solution)/shard_map/ppermute | solution.py:60
  258.3 31.7 %collective-permute-start.16 = (f32[8,512]{0,1:T(8,128)S(1)}, f32[8,512]{0,1:T(8,128)S(1)}, u32[]{:S(2)}, u32[]{:S(2)}) collective-permute-start(f32[8,512]{0,1:T(8,128)S(1)} %get-tuple-element.20), channel_id=1, source_target_pairs={{0,192},{4,196},{8,200},{12,204},{16,208},{20,212},{24,216},{28,22... | collective-permute-start | bytes 49160 | tf_op jit(solution)/shard_map/ppermute | solution.py:60
  260.2 33.4 %collective-permute-start.15 = (f32[8,512]{0,1:T(8,128)S(1)}, f32[8,512]{0,1:T(8,128)S(1)}, u32[]{:S(2)}, u32[]{:S(2)}) collective-permute-start(f32[8,512]{0,1:T(8,128)S(1)} %get-tuple-element.21), channel_id=1, source_target_pairs={{0,128},{4,132},{8,136},{12,140},{16,144},{20,148},{24,152},{28,15... | collective-permute-start | bytes 49160 | tf_op jit(solution)/shard_map/ppermute | solution.py:60
  264.4 41.0 %collective-permute-start.14 = (f32[8,512]{0,1:T(8,128)S(1)}, f32[8,512]{0,1:T(8,128)S(1)}, u32[]{:S(2)}, u32[]{:S(2)}) collective-permute-start(f32[8,512]{0,1:T(8,128)S(1)} %get-tuple-element.15), channel_id=1, source_target_pairs={{0,64},{4,68},{8,72},{12,76},{16,80},{20,84},{24,88},{28,92},{32,9... | collective-permute-start | bytes 49160 | tf_op jit(solution)/shard_map/ppermute | solution.py:60
  305.9 17.4 %collective-permute-start.23 = (f32[2,512]{0,1:T(8,128)S(1)}, f32[2,512]{0,1:T(8,128)S(1)}, u32[]{:S(2)}, u32[]{:S(2)}) collective-permute-start(f32[2,512]{0,1:T(8,128)S(1)} %get-tuple-element.13), channel_id=1, source_target_pairs={{0,12},{4,0},{8,4},{12,8},{16,28},{20,16},{24,20},{28,24},{32,44},... | collective-permute-start | bytes 12296 | tf_op jit(solution)/shard_map/ppermute | solution.py:60
  308.3 15.0 %collective-permute-start.22 = (f32[2,512]{0,1:T(8,128)S(1)}, f32[2,512]{0,1:T(8,128)S(1)}, u32[]{:S(2)}, u32[]{:S(2)}) collective-permute-start(f32[2,512]{0,1:T(8,128)S(1)} %get-tuple-element.14), channel_id=1, source_target_pairs={{0,8},{4,12},{8,0},{12,4},{16,24},{20,28},{24,16},{28,20},{32,40},... | collective-permute-start | bytes 12296 | tf_op jit(solution)/shard_map/ppermute | solution.py:60
  313.5 11.4 %collective-permute-start.21 = (f32[2,512]{0,1:T(8,128)S(1)}, f32[2,512]{0,1:T(8,128)S(1)}, u32[]{:S(2)}, u32[]{:S(2)}) collective-permute-start(f32[2,512]{0,1:T(8,128)S(1)} %get-tuple-element.12), channel_id=1, source_target_pairs={{0,4},{4,8},{8,12},{12,0},{16,20},{20,24},{24,28},{28,16},{32,36},... | collective-permute-start | bytes 12296 | tf_op jit(solution)/shard_map/ppermute | solution.py:60
  325.1 16.7 %collective-permute-start.24 = (f32[2,512]{0,1:T(8,128)S(1)}, f32[2,512]{0,1:T(8,128)S(1)}, u32[]{:S(2)}, u32[]{:S(2)}) collective-permute-start(f32[2,512]{0,1:T(8,128)S(1)} %add_add_fusion), channel_id=1, source_target_pairs={{0,4},{4,8},{8,12},{12,0},{16,20},{20,24},{24,28},{28,16},{32,36},... | collective-permute-start | bytes 12296 | tf_op jit(solution)/shard_map/ppermute | solution.py:72
  333.6 17.3 %collective-permute-start.25 = (f32[2,512]{0,1:T(8,128)S(1)}, f32[2,512]{0,1:T(8,128)S(1)}, u32[]{:S(2)}, u32[]{:S(2)}) collective-permute-start(f32[2,512]{0,1:T(8,128)S(1)} %add_add_fusion), channel_id=1, source_target_pairs={{0,8},{4,12},{8,0},{12,4},{16,24},{20,28},{24,16},{28,20},{32,40},... | collective-permute-start | bytes 12296 | tf_op jit(solution)/shard_map/ppermute | solution.py:72
  337.6 13.9 %collective-permute-start.26 = (f32[2,512]{0,1:T(8,128)S(1)}, f32[2,512]{0,1:T(8,128)S(1)}, u32[]{:S(2)}, u32[]{:S(2)}) collective-permute-start(f32[2,512]{0,1:T(8,128)S(1)} %add_add_fusion), channel_id=1, source_target_pairs={{0,12},{4,0},{8,4},{12,8},{16,28},{20,16},{24,20},{28,24},{32,44},... | collective-permute-start | bytes 12296 | tf_op jit(solution)/shard_map/ppermute | solution.py:72
  351.6 32.4 %collective-permute-start.27 = (f32[8,512]{1,0:T(8,128)S(1)}, f32[8,512]{1,0:T(8,128)S(1)}, u32[]{:S(2)}, u32[]{:S(2)}) collective-permute-start(f32[8,512]{1,0:T(8,128)S(1)} %constant_dynamic-update-slice_fusion.17), channel_id=1, source_target_pairs={{0,64},{4,68},{8,72},{12,76},{16,80},{20,84},{24,88},{28,92},{32,9... | collective-permute-start | bytes 49160 | tf_op jit(solution)/shard_map/ppermute | solution.py:72
  353.6 32.4 %collective-permute-start.28 = (f32[8,512]{1,0:T(8,128)S(1)}, f32[8,512]{1,0:T(8,128)S(1)}, u32[]{:S(2)}, u32[]{:S(2)}) collective-permute-start(f32[8,512]{1,0:T(8,128)S(1)} %constant_dynamic-update-slice_fusion.17), channel_id=1, source_target_pairs={{0,128},{4,132},{8,136},{12,140},{16,144},{20,148},{24,152},{28,15... | collective-permute-start | bytes 49160 | tf_op jit(solution)/shard_map/ppermute | solution.py:72
  355.6 33.8 %collective-permute-start.29 = (f32[8,512]{1,0:T(8,128)S(1)}, f32[8,512]{1,0:T(8,128)S(1)}, u32[]{:S(2)}, u32[]{:S(2)}) collective-permute-start(f32[8,512]{1,0:T(8,128)S(1)} %constant_dynamic-update-slice_fusion.17), channel_id=1, source_target_pairs={{0,192},{4,196},{8,200},{12,204},{16,208},{20,212},{24,216},{28,22... | collective-permute-start | bytes 49160 | tf_op jit(solution)/shard_map/ppermute | solution.py:72
  376.0 13.5 %collective-permute-start.30 = (f32[8,512]{1,0:T(8,128)S(1)}, f32[8,512]{1,0:T(8,128)S(1)}, u32[]{:S(2)}, u32[]{:S(2)}) collective-permute-start(f32[8,512]{1,0:T(8,128)S(1)} %constant_dynamic-update-slice_fusion.17), channel_id=1, source_target_pairs={{0,256},{4,260},{8,264},{12,268},{16,272},{20,276},{24,280},{28,28... | collective-permute-start | bytes 49160 | tf_op jit(solution)/shard_map/ppermute | solution.py:72
  377.9 11.6 %collective-permute-start.31 = (f32[8,512]{1,0:T(8,128)S(1)}, f32[8,512]{1,0:T(8,128)S(1)}, u32[]{:S(2)}, u32[]{:S(2)}) collective-permute-start(f32[8,512]{1,0:T(8,128)S(1)} %constant_dynamic-update-slice_fusion.17), channel_id=1, source_target_pairs={{0,320},{4,324},{8,328},{12,332},{16,336},{20,340},{24,344},{28,34... | collective-permute-start | bytes 49160 | tf_op jit(solution)/shard_map/ppermute | solution.py:72
  384.0 5.6 %collective-permute-start.32 = (f32[8,512]{1,0:T(8,128)S(1)}, f32[8,512]{1,0:T(8,128)S(1)}, u32[]{:S(2)}, u32[]{:S(2)}) collective-permute-start(f32[8,512]{1,0:T(8,128)S(1)} %constant_dynamic-update-slice_fusion.17), channel_id=1, source_target_pairs={{0,384},{4,388},{8,392},{12,396},{16,400},{20,404},{24,408},{28,41... | collective-permute-start | bytes 49160 | tf_op jit(solution)/shard_map/ppermute | solution.py:72
  386.0 5.9 %collective-permute-start.33 = (f32[8,512]{1,0:T(8,128)S(1)}, f32[8,512]{1,0:T(8,128)S(1)}, u32[]{:S(2)}, u32[]{:S(2)}) collective-permute-start(f32[8,512]{1,0:T(8,128)S(1)} %constant_dynamic-update-slice_fusion.17), channel_id=1, source_target_pairs={{0,448},{4,452},{8,456},{12,460},{16,464},{20,468},{24,472},{28,47... | collective-permute-start | bytes 49160 | tf_op jit(solution)/shard_map/ppermute | solution.py:72
  391.9 10.9 %collective-permute-start.34 = (f32[64,512]{1,0:T(8,128)S(1)}, f32[64,512]{1,0:T(8,128)S(1)}, u32[]{:S(2)}, u32[]{:S(2)}) collective-permute-start(f32[64,512]{1,0:T(8,128)S(1)} %constant_dynamic-update-slice_fusion.9), channel_id=1, source_target_pairs={{0,16},{4,20},{8,24},{12,28},{16,32},{20,36},{24,40},{28,44},{32,4... | collective-permute-start | bytes 393224 | tf_op jit(solution)/shard_map/ppermute | solution.py:72
  396.3 7.3 %collective-permute-start.35 = (f32[64,512]{1,0:T(8,128)S(1)}, f32[64,512]{1,0:T(8,128)S(1)}, u32[]{:S(2)}, u32[]{:S(2)}) collective-permute-start(f32[64,512]{1,0:T(8,128)S(1)} %constant_dynamic-update-slice_fusion.9), channel_id=1, source_target_pairs={{0,32},{4,36},{8,40},{12,44},{16,48},{20,52},{24,56},{28,60},{32,0... | collective-permute-start | bytes 393224 | tf_op jit(solution)/shard_map/ppermute | solution.py:72
  399.9 6.1 %collective-permute-start.36 = (f32[64,512]{1,0:T(8,128)S(1)}, f32[64,512]{1,0:T(8,128)S(1)}, u32[]{:S(2)}, u32[]{:S(2)}) collective-permute-start(f32[64,512]{1,0:T(8,128)S(1)} %constant_dynamic-update-slice_fusion.9), channel_id=1, source_target_pairs={{0,48},{4,52},{8,56},{12,60},{16,0},{20,4},{24,8},{28,12},{32,16},... | collective-permute-start | bytes 393224 | tf_op jit(solution)/shard_map/ppermute | solution.py:72
  406.0 0.8 copy-start.13
Sparse Core Ops, SparseCore 0:
  10.1 109.5 all-gather.1

commit v4 on v2

--- a/solution.py
+++ b/solution.py
@@ -44,6 +44,47 @@
     return current
 
 
+def halve_stage(value, axis, bit, wire):
+    half = value.shape[0] // 2
+    upper = ((lax.axis_index(axis) >> bit) & 1) == 1
+    low, high = value[:half], value[half:]
+    keep = jnp.where(upper, high, low).astype(jnp.float32)
+    send = jnp.where(upper, low, high)
+    return keep + xor_swap(send.astype(wire), axis, bit).astype(jnp.float32)
+
+
+def double_stage(value, axis, bit):
+    upper = ((lax.axis_index(axis) >> bit) & 1) == 1
+    other = xor_swap(value, axis, bit)
+    return jnp.where(upper, jnp.concatenate([other, value]), jnp.concatenate([value, other]))
+
+
+def grad_sum(partial):
+    stream_count = lax.axis_size("stream")
+    tm_count = lax.axis_size("tm")
+    stream_bits = stream_count.bit_length() - 1
+    tm_bits = tm_count.bit_length() - 1
+    if (
+        stream_count != 1 << stream_bits
+        or tm_count != 1 << tm_bits
+        or partial.shape[0] % (2 * stream_count)
+    ):
+        shard = lax.psum_scatter(
+            partial.astype(jnp.bfloat16), "stream", scatter_dimension=0, tiled=True
+        ).astype(jnp.float32)
+        return lax.psum(shard, "tm")
+    current = partial
+    for bit in reversed(range(stream_bits)):
+        current = halve_stage(current, "stream", bit, jnp.bfloat16)
+    if tm_bits == 0:
+        return current
+    current = halve_stage(current, "tm", 0, jnp.float32)
+    for bit in (2, 4, 1, 3, 5, 6) + tuple(range(7, tm_bits)):
+        if bit < tm_bits:
+            current = current + xor_swap(current, "tm", bit)
+    return double_stage(current, "tm", 0)
+
+
 def contract_last(left, right):
     return lax.dot_general(
         left, right, (((1,), (1,)), ((), ())), preferred_element_type=jnp.float32
@@ -169,13 +210,7 @@
         keyval_grads, keyval_full
     )
     input_grad = input_grad.astype(jnp.bfloat16)
-    grad_shard = lax.psum_scatter(
-        contract_first(record_rows, keyval_grads).astype(jnp.bfloat16),
-        "stream",
-        scatter_dimension=0,
-        tiled=True,
-    ).astype(jnp.float32)
-    weight_grad = tree_psum(grad_shard, "tm")
+    weight_grad = grad_sum(contract_first(record_rows, keyval_grads))
     return (input_grad[None], weight_grad)
 
 

time: 381 us -> 332 us (0.87)
  waiting for transfers between devices: 226 us -> 182 us
  starting transfers between devices: 99.2 us -> 94.7 us
    reduce_scatter x1 -> x0, waiting for transfers between devices: 45.9 us -> none  [per_device(): lax.psum_scatter(contract_first(record_rows, keyval_grads).astype(jnp.bfl...]
    ppermute x14 -> x10, starting transfers between devices: 72.9 us -> 68.5 us  [xor_swap(): lax.ppermute(value, axis, [(source, source ^ 1 << bit) for source in rang...]
    ppermute x14 -> x10, waiting for transfers between devices: 63 us -> 64.8 us  [xor_swap(): lax.ppermute(value, axis, [(source, source ^ 1 << bit) for source in rang...]
  transfers between devices with their start and end apart: 24 -> 19, of which waited for: 19 -> 14; matrix products, arithmetic and copies ran while one was open for 3% -> 4% of each run, Pallas kernels for 0% -> 0%
where the time goes in v4:
time: 332 us; the launch traced here: 330 us
  waiting for transfers between devices  182 us (55%)
  starting transfers between devices  94.7 us (29%)
  matrix products  25.3 us (8%)
  between operations  15.5 us (5%)
  other arithmetic  7.3 us (2%)
  local copies, waits for them, and re-layouts  5.1 us (2%)
    all_gather x1, waiting for transfers between devices, per_device(): lax.all_gather(jnp.concatenate([query_weight, keyval_weight, output_weigh...  109 us
    ppermute x10, starting transfers between devices, xor_swap(): lax.ppermute(value, axis, [(source, source ^ 1 << bit) for source in rang...  68.5 us
    ppermute x10, waiting for transfers between devices, xor_swap(): lax.ppermute(value, axis, [(source, source ^ 1 << bit) for source in rang...  64.8 us
    ppermute x8, starting transfers between devices, shifted(): lax.ppermute(value, axis, [(source, source + steps) for source in range(l...  26.2 us
    ppermute x8, waiting for transfers between devices, shifted(): lax.ppermute(value, axis, [(source, source + steps) for source in range(l...  8.28 us
    sub x4, matrix products, per_device(): terms = jnp.where(allowed, jnp.exp(masked - row_max), 0.0)  7.32 us
    dot_general x3, matrix products, contract_last(): lax.dot_general(left, right, (((1,), (1,)), ((), ())), preferred_element_...  7.14 us
  transfers between devices with their start and end apart: 19, of which 14 were waited for; matrix products, arithmetic and copies ran while one was open for 4% of the time, Pallas kernels for 0%

profile of v4, /device:TPU:1, one launch (start us, length us, event | category | flops | bytes accessed | tf_op | source)
XLA Modules:
  0.0 329.9 jit_solution(3549933381106386381)
XLA Ops:
  7.2 2.5 pad_maximum_fusion
  10.5 0.3 fusion.90
  10.8 108.9 %all-gather.2.cloned.1.call-done = bf16[1024,2560]{1,0:T(8,128)(2,1)} async-done(((bf16[256,2560]{1,0:T(8,128)(2,1)}), bf16[1024,2560]{1,0:T(8,128)(2,1)}) %all-gather.2.cloned.1.call-update) | async-done | bytes 5242896 | tf_op jit(solution)/shard_map/all_gather | solution.py:113
  119.8 1.5 fusion.68
  121.3 3.1 collective-permute-start
  124.4 3.9 %collective-permute-start.1 = (bf16[128,512]{1,0:T(8,128)(2,1)S(1)}, bf16[128,512]{1,0:T(8,128)(2,1)S(1)}, u32[]{:S(2)}, u32[]{:S(2)}) collective-permute-start(bf16[128,512]{1,0:T(8,128)(2,1)S(1)} %fusion.68), channel_id=1, source_target_pairs={{0,12},{4,16},{8,20},{12,24},{16,28},{20,32},{24,36},{28,40},{32,4... | collective-permute-start | bytes 393224 | tf_op jit(solution)/shard_map/ppermute | solution.py:15
  128.3 6.5 %collective-permute-start.2 = (bf16[128,512]{1,0:T(8,128)(2,1)S(1)}, bf16[128,512]{1,0:T(8,128)(2,1)S(1)}, u32[]{:S(2)}, u32[]{:S(2)}) collective-permute-start(bf16[128,512]{1,0:T(8,128)(2,1)S(1)} %fusion.68), channel_id=1, source_target_pairs={{0,8},{4,12},{8,16},{12,20},{16,24},{20,28},{24,32},{28,36},{32,40... | collective-permute-start | bytes 393224 | tf_op jit(solution)/shard_map/ppermute | solution.py:15
  134.8 6.9 %collective-permute-start.3 = (bf16[128,512]{1,0:T(8,128)(2,1)S(1)}, bf16[128,512]{1,0:T(8,128)(2,1)S(1)}, u32[]{:S(2)}, u32[]{:S(2)}) collective-permute-start(bf16[128,512]{1,0:T(8,128)(2,1)S(1)} %fusion.68), channel_id=1, source_target_pairs={{0,4},{4,8},{8,12},{12,16},{16,20},{20,24},{24,28},{28,32},{32,36}... | collective-permute-start | bytes 393224 | tf_op jit(solution)/shard_map/ppermute | solution.py:15
  141.8 2.3 fusion.53
  144.1 0.7 fusion.123
  144.8 2.3 fusion.56
  147.1 0.7 fusion.122
  147.9 1.7 fusion.127
  149.7 0.6 fusion.124
  150.3 1.7 fusion.125
  152.0 3.3 fusion.126
  155.3 0.7 broadcast_select_fusion.3
  156.0 1.4 divide_convert_fusion
  157.4 0.4 fusion.84
  157.8 0.4 fusion.45
  158.2 0.5 copy-done.11
  158.8 0.3 copy-done.13
  159.4 0.4 fusion.44
  159.9 0.8 copy-done.14
  160.7 0.4 fusion.82
  161.1 0.4 fusion.43
  161.7 0.8 copy-done.15
  162.7 0.4 fusion.42
  164.9 0.3 fusion.62
  165.5 0.3 fusion.60
  166.0 1.3 collective-permute-start.7
  167.3 1.3 collective-permute-start.6
  168.6 1.3 collective-permute-start.5
  169.9 1.9 collective-permute-start.4
  171.9 0.5 collective-permute-done.7
  172.4 1.3 collective-permute-done.6
  173.6 4.7 %collective-permute-done.5 = bf16[128,512]{0,1:T(8,128)(2,1)S(1)} collective-permute-done((bf16[128,512]{0,1:T(8,128)(2,1)S(1)}, bf16[128,512]{0,1:T(8,128)(2,1)S(1)}, u32[]{:S(2)}, u32[]{:S(2)}) %collective-permute-start.5) | collective-permute-done | bytes 131104 | tf_op jit(solution)/shard_map/ppermute | solution.py:15
  178.4 1.8 collective-permute-done.4
  180.2 0.4 convolution_bitcast_fusion
  180.8 8.5 %collective-permute-start.8 = (bf16[512,512]{0,1:T(8,128)(2,1)S(1)}, bf16[512,512]{0,1:T(8,128)(2,1)}, u32[]{:S(2)}, u32[]{:S(2)}) collective-permute-start(bf16[512,512]{0,1:T(8,128)(2,1)S(1)} %select_convert_fusion), channel_id=1, source_target_pairs={{0,2},{1,3},{2,0},{3,1},{4,6},{5,7},{6,4},{7,5},{8,10},{9,11},{10,... | collective-permute-start | bytes 1572872 | tf_op jit(solution)/shard_map/ppermute | solution.py:20
  189.3 22.0 %collective-permute-done.8 = bf16[512,512]{0,1:T(8,128)(2,1)} collective-permute-done((bf16[512,512]{0,1:T(8,128)(2,1)S(1)}, bf16[512,512]{0,1:T(8,128)(2,1)}, u32[]{:S(2)}, u32[]{:S(2)}) %collective-permute-start.8) | collective-permute-done | bytes 524320 | tf_op jit(solution)/shard_map/ppermute | solution.py:20
  211.2 1.3 convert_add_fusion
  212.6 1.9 collective-permute-start.9
  214.5 7.5 %collective-permute-done.9 = bf16[256,512]{0,1:T(8,128)(2,1)S(1)} collective-permute-done((bf16[256,512]{0,1:T(8,128)(2,1)S(1)}, bf16[256,512]{0,1:T(8,128)(2,1)S(1)}, u32[]{:S(2)}, u32[]{:S(2)}) %collective-permute-start.9) | collective-permute-done | bytes 262176 | tf_op jit(solution)/shard_map/ppermute | solution.py:20
  222.1 3.1 collective-permute-start.10
  225.3 1.1 collective-permute-done.10
  226.5 4.5 %collective-permute-start.11 = (f32[128,512]{0,1:T(8,128)S(1)}, f32[128,512]{0,1:T(8,128)S(1)}, u32[]{:S(2)}, u32[]{:S(2)}) collective-permute-start(f32[128,512]{0,1:T(8,128)S(1)} %select_add_fusion), channel_id=1, source_target_pairs={{0,16},{4,20},{8,24},{12,28},{16,0},{20,4},{24,8},{28,12},{32,48},... | collective-permute-start | bytes 786440 | tf_op jit(solution)/shard_map/ppermute | solution.py:20
  231.0 6.4 %collective-permute-done.11 = f32[128,512]{0,1:T(8,128)S(1)} collective-permute-done((f32[128,512]{0,1:T(8,128)S(1)}, f32[128,512]{0,1:T(8,128)S(1)}, u32[]{:S(2)}, u32[]{:S(2)}) %collective-permute-start.11) | collective-permute-done | bytes 262176 | tf_op jit(solution)/shard_map/ppermute | solution.py:20
  237.4 7.4 %collective-permute-start.12 = (f32[128,512]{0,1:T(8,128)S(1)}, f32[128,512]{0,1:T(8,128)S(1)}, u32[]{:S(2)}, u32[]{:S(2)}) collective-permute-start(f32[128,512]{0,1:T(8,128)S(1)} %add.96), channel_id=1, source_target_pairs={{0,64},{4,68},{8,72},{12,76},{16,80},{20,84},{24,88},{28,92},{32,9... | collective-permute-start | bytes 786440 | tf_op jit(solution)/shard_map/ppermute | solution.py:20
  244.8 5.4 %collective-permute-done.12 = f32[128,512]{0,1:T(8,128)S(1)} collective-permute-done((f32[128,512]{0,1:T(8,128)S(1)}, f32[128,512]{0,1:T(8,128)S(1)}, u32[]{:S(2)}, u32[]{:S(2)}) %collective-permute-start.12) | collective-permute-done | bytes 262176 | tf_op jit(solution)/shard_map/ppermute | solution.py:20
  250.3 4.6 %collective-permute-start.13 = (f32[128,512]{0,1:T(8,128)S(1)}, f32[128,512]{0,1:T(8,128)S(1)}, u32[]{:S(2)}, u32[]{:S(2)}) collective-permute-start(f32[128,512]{0,1:T(8,128)S(1)} %add.97), channel_id=1, source_target_pairs={{0,8},{4,12},{8,0},{12,4},{16,24},{20,28},{24,16},{28,20},{32,40},... | collective-permute-start | bytes 786440 | tf_op jit(solution)/shard_map/ppermute | solution.py:20
  254.9 7.4 %collective-permute-done.13 = f32[128,512]{0,1:T(8,128)S(1)} collective-permute-done((f32[128,512]{0,1:T(8,128)S(1)}, f32[128,512]{0,1:T(8,128)S(1)}, u32[]{:S(2)}, u32[]{:S(2)}) %collective-permute-start.13) | collective-permute-done | bytes 262176 | tf_op jit(solution)/shard_map/ppermute | solution.py:20
  262.3 5.8 %collective-permute-start.14 = (f32[128,512]{0,1:T(8,128)S(1)}, f32[128,512]{0,1:T(8,128)S(1)}, u32[]{:S(2)}, u32[]{:S(2)}) collective-permute-start(f32[128,512]{0,1:T(8,128)S(1)} %add.98), channel_id=1, source_target_pairs={{0,32},{4,36},{8,40},{12,44},{16,48},{20,52},{24,56},{28,60},{32,0... | collective-permute-start | bytes 786440 | tf_op jit(solution)/shard_map/ppermute | solution.py:20
  268.1 3.7 %collective-permute-done.14 = f32[128,512]{0,1:T(8,128)S(1)} collective-permute-done((f32[128,512]{0,1:T(8,128)S(1)}, f32[128,512]{0,1:T(8,128)S(1)}, u32[]{:S(2)}, u32[]{:S(2)}) %collective-permute-start.14) | collective-permute-done | bytes 262176 | tf_op jit(solution)/shard_map/ppermute | solution.py:20
  271.9 8.2 %collective-permute-start.15 = (f32[128,512]{0,1:T(8,128)S(1)}, f32[128,512]{0,1:T(8,128)S(1)}, u32[]{:S(2)}, u32[]{:S(2)}) collective-permute-start(f32[128,512]{0,1:T(8,128)S(1)} %add.99), channel_id=1, source_target_pairs={{0,128},{4,132},{8,136},{12,140},{16,144},{20,148},{24,152},{28,15... | collective-permute-start | bytes 786440 | tf_op jit(solution)/shard_map/ppermute | solution.py:20
  280.1 0.3 convolution_convert_fusion.1
  280.8 3.7 %collective-permute-done.15 = f32[128,512]{0,1:T(8,128)S(1)} collective-permute-done((f32[128,512]{0,1:T(8,128)S(1)}, f32[128,512]{0,1:T(8,128)S(1)}, u32[]{:S(2)}, u32[]{:S(2)}) %collective-permute-start.15) | collective-permute-done | bytes 262176 | tf_op jit(solution)/shard_map/ppermute | solution.py:20
  284.6 17.8 %collective-permute-start.16 = (f32[128,512]{0,1:T(8,128)S(1)}, f32[128,512]{0,1:T(8,128)S(1)}, u32[]{:S(2)}, u32[]{:S(2)}) collective-permute-start(f32[128,512]{0,1:T(8,128)S(1)} %add.100), channel_id=1, source_target_pairs={{0,256},{4,260},{8,264},{12,268},{16,272},{20,276},{24,280},{28,28... | collective-permute-start | bytes 786440 | tf_op jit(solution)/shard_map/ppermute | solution.py:20
  302.4 0.3 convolution_convert_fusion.5
  303.0 7.6 %collective-permute-done.16 = f32[128,512]{0,1:T(8,128)S(1)} collective-permute-done((f32[128,512]{0,1:T(8,128)S(1)}, f32[128,512]{0,1:T(8,128)S(1)}, u32[]{:S(2)}, u32[]{:S(2)}) %collective-permute-start.16) | collective-permute-done | bytes 262176 | tf_op jit(solution)/shard_map/ppermute | solution.py:20
  310.6 6.6 %collective-permute-start.17 = (f32[128,512]{0,1:T(8,128)S(1)}, f32[128,512]{0,1:T(8,128)S(1)}, u32[]{:S(2)}, u32[]{:S(2)}) collective-permute-start(f32[128,512]{0,1:T(8,128)S(1)} %add.101), channel_id=1, source_target_pairs={{0,4},{4,0},{8,12},{12,8},{16,20},{20,16},{24,28},{28,24},{32,36},... | collective-permute-start | bytes 786440 | tf_op jit(solution)/shard_map/ppermute | solution.py:20
  317.2 2.4 fusion.6
  319.7 2.4 fusion.59
  322.1 1.0 copy.40
  (88 shorter events, 4.4 us)
Async XLA Ops:
  7.2 112.6 %copy-start = (bf16[1,128,1024]{2,1,0:T(8,128)(2,1)S(1)}, bf16[1,128,1024]{2,1,0:T(8,128)(2,1)}, u32[]{:S(2)}) copy-start(bf16[1,128,1024]{2,1,0:T(8,128)(2,1)} %param.6) | copy-start | bytes 786436
  7.2 112.6 %all-gather.2.cloned.1.call-start = ((), (), s32[]{:S(2)}) async-start(), calls=%async_computation | async-start | bytes 6553600 | tf_op jit(solution)/shard_map/all_gather | solution.py:113
  9.7 132.0 %copy-start.23 = (bf16[1,128,1024]{2,1,0:T(8,128)(2,1)S(1)}, bf16[1,128,1024]{2,1,0:T(8,128)(2,1)}, u32[]{:S(2)}) copy-start(bf16[1,128,1024]{2,1,0:T(8,128)(2,1)} %param.7) | copy-start | bytes 786436
  10.8 138.8 %copy-start.22 = (pred[128,640]{0,1:T(8,128)(4,1)}, pred[128,640]{0,1:T(8,128)(4,1)S(1)}, u32[]{:S(2)}) copy-start(pred[128,640]{0,1:T(8,128)(4,1)S(1)} %fusion.90) | copy-start | bytes 245764
  121.3 26.5 %collective-permute-start = (bf16[128,512]{1,0:T(8,128)(2,1)S(1)}, bf16[128,512]{1,0:T(8,128)(2,1)S(1)}, u32[]{:S(2)}, u32[]{:S(2)}) collective-permute-start(bf16[128,512]{1,0:T(8,128)(2,1)S(1)} %fusion.68), channel_id=1, source_target_pairs={{0,16},{4,20},{8,24},{12,28},{16,32},{20,36},{24,40},{28,44},{32,4... | collective-permute-start | bytes 393224 | tf_op jit(solution)/shard_map/ppermute | solution.py:15
  124.4 23.4 %collective-permute-start.1 = (bf16[128,512]{1,0:T(8,128)(2,1)S(1)}, bf16[128,512]{1,0:T(8,128)(2,1)S(1)}, u32[]{:S(2)}, u32[]{:S(2)}) collective-permute-start(bf16[128,512]{1,0:T(8,128)(2,1)S(1)} %fusion.68), channel_id=1, source_target_pairs={{0,12},{4,16},{8,20},{12,24},{16,28},{20,32},{24,36},{28,40},{32,4... | collective-permute-start | bytes 393224 | tf_op jit(solution)/shard_map/ppermute | solution.py:15
  128.3 19.5 %collective-permute-start.2 = (bf16[128,512]{1,0:T(8,128)(2,1)S(1)}, bf16[128,512]{1,0:T(8,128)(2,1)S(1)}, u32[]{:S(2)}, u32[]{:S(2)}) collective-permute-start(bf16[128,512]{1,0:T(8,128)(2,1)S(1)} %fusion.68), channel_id=1, source_target_pairs={{0,8},{4,12},{8,16},{12,20},{16,24},{20,28},{24,32},{28,36},{32,40... | collective-permute-start | bytes 393224 | tf_op jit(solution)/shard_map/ppermute | solution.py:15
  134.8 13.0 %collective-permute-start.3 = (bf16[128,512]{1,0:T(8,128)(2,1)S(1)}, bf16[128,512]{1,0:T(8,128)(2,1)S(1)}, u32[]{:S(2)}, u32[]{:S(2)}) collective-permute-start(bf16[128,512]{1,0:T(8,128)(2,1)S(1)} %fusion.68), channel_id=1, source_target_pairs={{0,4},{4,8},{8,12},{12,16},{16,20},{20,24},{24,28},{28,32},{32,36}... | collective-permute-start | bytes 393224 | tf_op jit(solution)/shard_map/ppermute | solution.py:15
  147.8 1.9 copy-start.16
  147.8 1.9 copy-start.20
  147.9 14.8 %copy-start.1 = (bf16[640,512]{1,0:T(8,128)(2,1)}, bf16[640,512]{1,0:T(8,128)(2,1)S(1)}, u32[]{:S(2)}) copy-start(bf16[640,512]{1,0:T(8,128)(2,1)S(1)} %constant_dynamic-update-slice_fusion) | copy-start | bytes 1966084
  155.3 2.2 copy-start.12
  157.4 1.3 copy-start.11
  158.2 6.0 %copy-start.3 = (bf16[4,128,640]{1,2,0:T(8,128)(2,1)}, bf16[4,128,640]{1,2,0:T(8,128)(2,1)S(1)}, u32[]{:S(2)}) copy-start(bf16[4,128,640]{1,2,0:T(8,128)(2,1)S(1)} %fusion.45) | copy-start | bytes 1966084
  158.2 1.0 copy-start.13
  159.8 4.1 %copy-start.7 = (bf16[4,128,640]{1,2,0:T(8,128)(2,1)}, bf16[4,128,640]{1,2,0:T(8,128)(2,1)S(1)}, u32[]{:S(2)}) copy-start(bf16[4,128,640]{1,2,0:T(8,128)(2,1)S(1)} %fusion.44) | copy-start | bytes 1966084
  159.8 0.9 copy-start.14
  161.5 1.9 copy-start.5
  161.5 0.9 copy-start.15
  161.7 1.4 copy-start.21
  162.7 0.8 copy-start.19
  162.7 1.2 copy-start.18
  163.1 1.1 copy-start.9
  163.1 1.1 copy-start.17
  166.0 6.3 %collective-permute-start.7 = (bf16[128,512]{0,1:T(8,128)(2,1)S(1)}, bf16[128,512]{0,1:T(8,128)(2,1)S(1)}, u32[]{:S(2)}, u32[]{:S(2)}) collective-permute-start(bf16[128,512]{0,1:T(8,128)(2,1)S(1)} %get-tuple-element.5), channel_id=1, source_target_pairs={{16,0},{20,4},{24,8},{28,12},{32,16},{36,20},{40,24},{44,28},{48,3... | collective-permute-start | bytes 393224 | tf_op jit(solution)/shard_map/ppermute | solution.py:15
  167.3 6.3 %collective-permute-start.6 = (bf16[128,512]{0,1:T(8,128)(2,1)S(1)}, bf16[128,512]{0,1:T(8,128)(2,1)S(1)}, u32[]{:S(2)}, u32[]{:S(2)}) collective-permute-start(bf16[128,512]{0,1:T(8,128)(2,1)S(1)} %get-tuple-element.6), channel_id=1, source_target_pairs={{12,0},{16,4},{20,8},{24,12},{28,16},{32,20},{36,24},{40,28},{44,3... | collective-permute-start | bytes 393224 | tf_op jit(solution)/shard_map/ppermute | solution.py:15
  168.6 9.7 %collective-permute-start.5 = (bf16[128,512]{0,1:T(8,128)(2,1)S(1)}, bf16[128,512]{0,1:T(8,128)(2,1)S(1)}, u32[]{:S(2)}, u32[]{:S(2)}) collective-permute-start(bf16[128,512]{0,1:T(8,128)(2,1)S(1)} %get-tuple-element.7), channel_id=1, source_target_pairs={{8,0},{12,4},{16,8},{20,12},{24,16},{28,20},{32,24},{36,28},{40,32... | collective-permute-start | bytes 393224 | tf_op jit(solution)/shard_map/ppermute | solution.py:15
  169.9 10.2 %collective-permute-start.4 = (bf16[128,512]{0,1:T(8,128)(2,1)S(1)}, bf16[128,512]{0,1:T(8,128)(2,1)S(1)}, u32[]{:S(2)}, u32[]{:S(2)}) collective-permute-start(bf16[128,512]{0,1:T(8,128)(2,1)S(1)} %get-tuple-element.4), channel_id=1, source_target_pairs={{4,0},{8,4},{12,8},{16,12},{20,16},{24,20},{28,24},{32,28},{36,32}... | collective-permute-start | bytes 393224 | tf_op jit(solution)/shard_map/ppermute | solution.py:15
  180.8 30.5 %collective-permute-start.8 = (bf16[512,512]{0,1:T(8,128)(2,1)S(1)}, bf16[512,512]{0,1:T(8,128)(2,1)}, u32[]{:S(2)}, u32[]{:S(2)}) collective-permute-start(bf16[512,512]{0,1:T(8,128)(2,1)S(1)} %select_convert_fusion), channel_id=1, source_target_pairs={{0,2},{1,3},{2,0},{3,1},{4,6},{5,7},{6,4},{7,5},{8,10},{9,11},{10,... | collective-permute-start | bytes 1572872 | tf_op jit(solution)/shard_map/ppermute | solution.py:20
  212.6 9.4 %collective-permute-start.9 = (bf16[256,512]{0,1:T(8,128)(2,1)S(1)}, bf16[256,512]{0,1:T(8,128)(2,1)S(1)}, u32[]{:S(2)}, u32[]{:S(2)}) collective-permute-start(bf16[256,512]{0,1:T(8,128)(2,1)S(1)} %select_convert_fusion.1), channel_id=1, source_target_pairs={{0,1},{1,0},{2,3},{3,2},{4,5},{5,4},{6,7},{7,6},{8,9},{9,8},{10,11... | collective-permute-start | bytes 786440 | tf_op jit(solution)/shard_map/ppermute | solution.py:20
  222.1 4.3 %collective-permute-start.10 = (f32[128,512]{0,1:T(8,128)S(1)}, f32[128,512]{0,1:T(8,128)S(1)}, u32[]{:S(2)}, u32[]{:S(2)}) collective-permute-start(f32[128,512]{0,1:T(8,128)S(1)} %slice_select_fusion), channel_id=1, source_target_pairs={{0,4},{4,0},{8,12},{12,8},{16,20},{20,16},{24,28},{28,24},{32,36},... | collective-permute-start | bytes 786440 | tf_op jit(solution)/shard_map/ppermute | solution.py:20
  226.5 10.9 %collective-permute-start.11 = (f32[128,512]{0,1:T(8,128)S(1)}, f32[128,512]{0,1:T(8,128)S(1)}, u32[]{:S(2)}, u32[]{:S(2)}) collective-permute-start(f32[128,512]{0,1:T(8,128)S(1)} %select_add_fusion), channel_id=1, source_target_pairs={{0,16},{4,20},{8,24},{12,28},{16,0},{20,4},{24,8},{28,12},{32,48},... | collective-permute-start | bytes 786440 | tf_op jit(solution)/shard_map/ppermute | solution.py:20
  237.4 42.8 %copy-start.2 = (bf16[640,512]{1,0:T(8,128)(2,1)S(1)}, bf16[640,512]{1,0:T(8,128)(2,1)}, u32[]{:S(2)}) copy-start(bf16[640,512]{1,0:T(8,128)(2,1)} %copy-done.1) | copy-start | bytes 1966084
  237.4 42.8 %copy-start.4 = (bf16[4,128,640]{1,2,0:T(8,128)(2,1)S(1)}, bf16[4,128,640]{1,2,0:T(8,128)(2,1)}, u32[]{:S(2)}) copy-start(bf16[4,128,640]{1,2,0:T(8,128)(2,1)} %copy-done.3) | copy-start | bytes 1966084
  237.4 12.9 %collective-permute-start.12 = (f32[128,512]{0,1:T(8,128)S(1)}, f32[128,512]{0,1:T(8,128)S(1)}, u32[]{:S(2)}, u32[]{:S(2)}) collective-permute-start(f32[128,512]{0,1:T(8,128)S(1)} %add.96), channel_id=1, source_target_pairs={{0,64},{4,68},{8,72},{12,76},{16,80},{20,84},{24,88},{28,92},{32,9... | collective-permute-start | bytes 786440 | tf_op jit(solution)/shard_map/ppermute | solution.py:20
  250.3 30.2 %copy-start.8 = (bf16[4,128,640]{1,2,0:T(8,128)(2,1)S(1)}, bf16[4,128,640]{1,2,0:T(8,128)(2,1)}, u32[]{:S(2)}) copy-start(bf16[4,128,640]{1,2,0:T(8,128)(2,1)} %copy-done.7) | copy-start | bytes 1966084
  250.3 12.0 %collective-permute-start.13 = (f32[128,512]{0,1:T(8,128)S(1)}, f32[128,512]{0,1:T(8,128)S(1)}, u32[]{:S(2)}, u32[]{:S(2)}) collective-permute-start(f32[128,512]{0,1:T(8,128)S(1)} %add.97), channel_id=1, source_target_pairs={{0,8},{4,12},{8,0},{12,4},{16,24},{20,28},{24,16},{28,20},{32,40},... | collective-permute-start | bytes 786440 | tf_op jit(solution)/shard_map/ppermute | solution.py:20
  262.3 9.5 %collective-permute-start.14 = (f32[128,512]{0,1:T(8,128)S(1)}, f32[128,512]{0,1:T(8,128)S(1)}, u32[]{:S(2)}, u32[]{:S(2)}) collective-permute-start(f32[128,512]{0,1:T(8,128)S(1)} %add.98), channel_id=1, source_target_pairs={{0,32},{4,36},{8,40},{12,44},{16,48},{20,52},{24,56},{28,60},{32,0... | collective-permute-start | bytes 786440 | tf_op jit(solution)/shard_map/ppermute | solution.py:20
  271.9 30.5 %copy-start.6 = (bf16[4,128,640]{1,2,0:T(8,128)(2,1)S(1)}, bf16[4,128,640]{1,2,0:T(8,128)(2,1)}, u32[]{:S(2)}) copy-start(bf16[4,128,640]{1,2,0:T(8,128)(2,1)} %copy-done.5) | copy-start | bytes 1966084
  271.9 12.6 %collective-permute-start.15 = (f32[128,512]{0,1:T(8,128)S(1)}, f32[128,512]{0,1:T(8,128)S(1)}, u32[]{:S(2)}, u32[]{:S(2)}) collective-permute-start(f32[128,512]{0,1:T(8,128)S(1)} %add.99), channel_id=1, source_target_pairs={{0,128},{4,132},{8,136},{12,140},{16,144},{20,148},{24,152},{28,15... | collective-permute-start | bytes 786440 | tf_op jit(solution)/shard_map/ppermute | solution.py:20
  280.5 22.2 %copy-start.10 = (bf16[4,128,640]{1,2,0:T(8,128)(2,1)S(1)}, bf16[4,128,640]{1,2,0:T(8,128)(2,1)}, u32[]{:S(2)}) copy-start(bf16[4,128,640]{1,2,0:T(8,128)(2,1)} %copy-done.9) | copy-start | bytes 1966084
  284.6 26.0 %collective-permute-start.16 = (f32[128,512]{0,1:T(8,128)S(1)}, f32[128,512]{0,1:T(8,128)S(1)}, u32[]{:S(2)}, u32[]{:S(2)}) collective-permute-start(f32[128,512]{0,1:T(8,128)S(1)} %add.100), channel_id=1, source_target_pairs={{0,256},{4,260},{8,264},{12,268},{16,272},{20,276},{24,280},{28,28... | collective-permute-start | bytes 786440 | tf_op jit(solution)/shard_map/ppermute | solution.py:20
  310.6 11.5 %collective-permute-start.17 = (f32[128,512]{0,1:T(8,128)S(1)}, f32[128,512]{0,1:T(8,128)S(1)}, u32[]{:S(2)}, u32[]{:S(2)}) collective-permute-start(f32[128,512]{0,1:T(8,128)S(1)} %add.101), channel_id=1, source_target_pairs={{0,4},{4,0},{8,12},{12,8},{16,20},{20,16},{24,28},{28,24},{32,36},... | collective-permute-start | bytes 786440 | tf_op jit(solution)/shard_map/ppermute | solution.py:20
Sparse Core Ops, SparseCore 0:
  10.1 109.5 all-gather.1

commit v5 on v4

--- a/solution.py
+++ b/solution.py
@@ -73,9 +73,16 @@
             partial.astype(jnp.bfloat16), "stream", scatter_dimension=0, tiled=True
         ).astype(jnp.float32)
         return lax.psum(shard, "tm")
-    current = partial
-    for bit in reversed(range(stream_bits)):
-        current = halve_stage(current, "stream", bit, jnp.bfloat16)
+    stream_index = lax.axis_index("stream")
+    current = partial.reshape((2,) * stream_bits + (-1,) + partial.shape[1:])
+    for bit in range(stream_bits):
+        axis_pos = stream_bits - 1 - bit
+        upper = ((stream_index >> bit) & 1) == 1
+        low = lax.index_in_dim(current, 0, axis_pos, keepdims=False)
+        high = lax.index_in_dim(current, 1, axis_pos, keepdims=False)
+        keep = jnp.where(upper, high, low).astype(jnp.float32)
+        send = jnp.where(upper, low, high).astype(jnp.bfloat16)
+        current = keep + xor_swap(send, "stream", bit).astype(jnp.float32)
     if tm_bits == 0:
         return current
     current = halve_stage(current, "tm", 0, jnp.float32)
@@ -110,12 +117,22 @@
     score_scale = HEAD_DIM ** (-0.5)
     anchor = lax.axis_index("tm") * shard_tokens
     query_width = query_weight.shape[1]
-    weights_full = lax.all_gather(
-        jnp.concatenate([query_weight, keyval_weight, output_weight], axis=1),
-        "stream",
-        axis=0,
-        tiled=True,
-    )
+    weights_local = jnp.concatenate([query_weight, keyval_weight, output_weight], axis=1)
+    if lax.axis_size("tm") % 2 == 0 and weights_local.shape[1] % 256 == 0:
+        half_width = weights_local.shape[1] // 2
+        core = lax.axis_index("tm") % 2
+        mine = lax.all_gather(
+            lax.dynamic_slice_in_dim(weights_local, core * half_width, half_width, 1),
+            "stream",
+            axis=0,
+            tiled=True,
+        )
+        other = xor_swap(mine, "tm", 0)
+        weights_full = jnp.concatenate(
+            [jnp.where(core == 0, mine, other), jnp.where(core == 0, other, mine)], axis=1
+        )
+    else:
+        weights_full = lax.all_gather(weights_local, "stream", axis=0, tiled=True)
     query_full = weights_full[:, :query_width]
     keyval_full = weights_full[:, query_width : query_width + keyval_width]
     output_full = weights_full[:, query_width + keyval_width :]

time: 332 us -> 323 us (0.973)
  waiting for transfers between devices: 182 us -> 163 us
  local copies, waits for them, and re-layouts: 5.1 us -> 23.3 us
  starting transfers between devices: 94.7 us -> 78.8 us
  other arithmetic: 7.3 us -> 17.2 us
    all_gather x1, waiting for transfers between devices: 109 us -> 67.5 us  [per_device(): lax.all_gather(lax.dynamic_slice_in_dim(weights_local, core * half_width,...]
    ppermute x10 -> x11, waiting for transfers between devices: 64.8 us -> 85.2 us  [xor_swap(): lax.ppermute(value, axis, [(source, source ^ 1 << bit) for source in rang...]
    ppermute x10 -> x11, starting transfers between devices: 68.5 us -> 52.5 us  [xor_swap(): lax.ppermute(value, axis, [(source, source ^ 1 << bit) for source in rang...]
    unnamed x53 -> x60, local copies, waits for them, and re-layouts: 3.62 us -> 11.6 us
    slice x0 -> x1, local copies, waits for them, and re-layouts: none -> 5.33 us  [grad_sum(): high = lax.index_in_dim(current, 1, axis_pos, keepdims=False)]
    dot_general x3, matrix products: 7.14 us -> 2.72 us  [contract_last(): lax.dot_general(left, right, (((1,), (1,)), ((), ())), preferred_element_...]
    reshape x0 -> x1, local copies, waits for them, and re-layouts: none -> 3.99 us  [grad_sum(): current = partial.reshape((2,) * stream_bits + (-1,) + partial.shape[1:])]
    sub x4, matrix products: 7.32 us -> 11.2 us  [per_device(): terms = jnp.where(allowed, jnp.exp(masked - row_max), 0.0)]
  transfers between devices with their start and end apart: 19 -> 20, of which waited for: 14 -> 15; matrix products, arithmetic and copies ran while one was open for 4% -> 2% of each run, Pallas kernels for 0% -> 0%
where the time goes in v5:
time: 323 us; the launch traced here: 322 us
  waiting for transfers between devices  163 us (50%)
  starting transfers between devices  78.8 us (24%)
  local copies, waits for them, and re-layouts  23.3 us (7%)
  matrix products  23.3 us (7%)
  other arithmetic  17.2 us (5%)
  between operations  15.5 us (5%)
    ppermute x11, waiting for transfers between devices, xor_swap(): lax.ppermute(value, axis, [(source, source ^ 1 << bit) for source in rang...  85.2 us
    all_gather x1, waiting for transfers between devices, per_device(): lax.all_gather(lax.dynamic_slice_in_dim(weights_local, core * half_width,...  67.5 us
    ppermute x11, starting transfers between devices, xor_swap(): lax.ppermute(value, axis, [(source, source ^ 1 << bit) for source in rang...  52.5 us
    ppermute x8, starting transfers between devices, shifted(): lax.ppermute(value, axis, [(source, source + steps) for source in range(l...  26.2 us
    unnamed x60, local copies, waits for them, and re-layouts  11.6 us
    sub x4, matrix products, per_device(): terms = jnp.where(allowed, jnp.exp(masked - row_max), 0.0)  11.2 us
    ppermute x8, waiting for transfers between devices, shifted(): lax.ppermute(value, axis, [(source, source + steps) for source in range(l...  10.8 us
  transfers between devices with their start and end apart: 20, of which 15 were waited for; matrix products, arithmetic and copies ran while one was open for 2% of the time, Pallas kernels for 0%

profile of v5, /device:TPU:1, one launch (start us, length us, event | category | flops | bytes accessed | tf_op | source)
XLA Modules:
  0.0 321.6 jit_solution(12958836466588536639)
XLA Ops:
  7.2 2.3 fusion.85
  9.6 67.5 %all-gather.2.cloned.1.call-done = bf16[1024,1280]{1,0:T(8,128)(2,1)} async-done(((bf16[256,1280]{1,0:T(8,128)(2,1)}), bf16[1024,1280]{1,0:T(8,128)(2,1)}) %all-gather.2.cloned.1.call-update) | async-done | bytes 2621456 | tf_op jit(solution)/shard_map/all_gather | solution.py:124
  77.1 2.8 collective-permute-start
  80.6 1.0 fusion.90
  81.6 3.2 collective-permute-done
  84.8 2.9 broadcast_select_fusion.1
  88.1 6.4 %collective-permute-start.4 = (bf16[128,512]{1,0:T(8,128)(2,1)S(1)}, bf16[128,512]{1,0:T(8,128)(2,1)S(1)}, u32[]{:S(2)}, u32[]{:S(2)}) collective-permute-start(bf16[128,512]{1,0:T(8,128)(2,1)S(1)} %fusion.75), channel_id=1, source_target_pairs={{0,4},{4,8},{8,12},{12,16},{16,20},{20,24},{24,28},{28,32},{32,36}... | collective-permute-start | bytes 393224 | tf_op jit(solution)/shard_map/ppermute | solution.py:15
  94.5 4.0 %collective-permute-start.3 = (bf16[128,512]{1,0:T(8,128)(2,1)S(1)}, bf16[128,512]{1,0:T(8,128)(2,1)S(1)}, u32[]{:S(2)}, u32[]{:S(2)}) collective-permute-start(bf16[128,512]{1,0:T(8,128)(2,1)S(1)} %fusion.75), channel_id=1, source_target_pairs={{0,8},{4,12},{8,16},{12,20},{16,24},{20,28},{24,32},{28,36},{32,40... | collective-permute-start | bytes 393224 | tf_op jit(solution)/shard_map/ppermute | solution.py:15
  98.5 1.4 collective-permute-start.2
  99.9 3.6 %collective-permute-start.1 = (bf16[128,512]{1,0:T(8,128)(2,1)S(1)}, bf16[128,512]{1,0:T(8,128)(2,1)S(1)}, u32[]{:S(2)}, u32[]{:S(2)}) collective-permute-start(bf16[128,512]{1,0:T(8,128)(2,1)S(1)} %fusion.75), channel_id=1, source_target_pairs={{0,16},{4,20},{8,24},{12,28},{16,32},{20,36},{24,40},{28,44},{32,4... | collective-permute-start | bytes 393224 | tf_op jit(solution)/shard_map/ppermute | solution.py:15
  103.6 0.8 fusion.64
  104.4 0.7 fusion.61
  105.1 0.7 fusion.125
  105.8 0.7 fusion.124
  106.6 2.7 fusion.126
  109.3 2.6 fusion.128
  111.9 2.7 fusion.127
  114.6 3.2 %fusion.129 = (f32[4,128]{1,0:T(4,128)}, f32[4,128,640]{1,2,0:T(8,128)}) fusion(bf16[128,4,64]{0,2,1:T(8,128)(2,1)} %bitcast.311, pred[128,640]{0,1:T(8,128)(4,1)} %fusion.90, bf16[640,512]{1,0:T(8,128)(2,1)S(1)} %constant_dynamic-update-slice_fusion), kind=kOutput, calls=%fused_computation.184 | convolution fusion | flops 43582080 | bytes 1705984 | tf_op jit(solution)/shard_map/sub | solution.py:182
  117.9 0.7 broadcast_select_fusion.2
  118.6 1.4 divide_convert_fusion.3
  121.2 0.5 copy-done.4
  122.5 0.6 copy-done.14
  128.4 1.0 fusion.123
  129.6 6.7 %collective-permute-start.5 = (bf16[128,512]{0,1:T(8,128)(2,1)}, bf16[128,512]{0,1:T(8,128)(2,1)}, u32[]{:S(2)}, u32[]{:S(2)}) collective-permute-start(bf16[128,512]{0,1:T(8,128)(2,1)} %get-tuple-element.6), channel_id=1, source_target_pairs={{4,0},{8,4},{12,8},{16,12},{20,16},{24,20},{28,24},{32,28},{36,32}... | collective-permute-start | bytes 393224 | tf_op jit(solution)/shard_map/ppermute | solution.py:15
  136.3 1.3 collective-permute-start.8
  137.6 1.3 collective-permute-start.7
  138.9 1.5 collective-permute-start.6
  140.4 0.7 collective-permute-done.5
  141.1 1.5 collective-permute-done.8
  142.7 3.9 %collective-permute-done.7 = bf16[128,512]{0,1:T(8,128)(2,1)} collective-permute-done((bf16[128,512]{0,1:T(8,128)(2,1)}, bf16[128,512]{0,1:T(8,128)(2,1)}, u32[]{:S(2)}, u32[]{:S(2)}) %collective-permute-start.7) | collective-permute-done | bytes 131104 | tf_op jit(solution)/shard_map/ppermute | solution.py:15
  146.5 4.7 %collective-permute-done.6 = bf16[128,512]{0,1:T(8,128)(2,1)} collective-permute-done((bf16[128,512]{0,1:T(8,128)(2,1)}, bf16[128,512]{0,1:T(8,128)(2,1)}, u32[]{:S(2)}, u32[]{:S(2)}) %collective-permute-start.6) | collective-permute-done | bytes 131104 | tf_op jit(solution)/shard_map/ppermute | solution.py:15
  151.2 1.2 fusion.95
  152.5 0.7 copy-done.16
  153.1 1.7 convolution_bitcast_fusion
  154.9 4.0 %reshape.144 = f32[2,2,256,512]{2,1,0,3:T(2,128)} reshape(f32[1024,512]{0,1:T(8,128)} %convolution_bitcast_fusion) | data formatting | bytes 4194304 | tf_op jit(solution)/shard_map/reshape | solution.py:77
  158.8 5.3 %fusion.122 = (f32[2,1,256,512]{2,1,0,3:T(1,128)}, f32[2,1,256,512]{2,1,0,3:T(1,128)}) fusion(f32[2,2,256,512]{2,1,0,3:T(2,128)} %reshape.144), kind=kLoop, calls=%fused_computation.177 | loop fusion | bytes 4194304 | tf_op jit(solution)/shard_map/slice | solution.py:82
  164.2 3.6 %copy.90 = f32[2,1,256,512]{3,2,0,1:T(8,128)} copy(f32[2,1,256,512]{2,1,0,3:T(1,128)} %get-tuple-element.4) | data formatting | bytes 2097152
  167.8 3.6 %copy.91 = f32[2,1,256,512]{3,2,0,1:T(8,128)} copy(f32[2,1,256,512]{2,1,0,3:T(1,128)} %get-tuple-element.5) | data formatting | bytes 2097152
  171.4 2.2 fusion.86
  173.6 6.7 %collective-permute-start.9 = (bf16[2,256,512]{2,1,0:T(8,128)(2,1)}, bf16[2,256,512]{2,1,0:T(8,128)(2,1)}, u32[]{:S(2)}, u32[]{:S(2)}) collective-permute-start(bf16[2,256,512]{2,1,0:T(8,128)(2,1)} %fusion.86), channel_id=1, source_target_pairs={{0,1},{1,0},{2,3},{3,2},{4,5},{5,4},{6,7},{7,6},{8,9},{9,8},{10,11... | collective-permute-start | bytes 1572872 | tf_op jit(solution)/shard_map/ppermute | solution.py:20
  180.3 12.3 %collective-permute-done.9 = bf16[2,256,512]{2,1,0:T(8,128)(2,1)} collective-permute-done((bf16[2,256,512]{2,1,0:T(8,128)(2,1)}, bf16[2,256,512]{2,1,0:T(8,128)(2,1)}, u32[]{:S(2)}, u32[]{:S(2)}) %collective-permute-start.9) | collective-permute-done | bytes 524320 | tf_op jit(solution)/shard_map/ppermute | solution.py:20
  192.6 1.7 bitcast_add_fusion
  194.2 1.0 copy-done.3
  195.2 0.8 fusion.91
  196.0 2.0 collective-permute-start.10
  198.0 14.0 %collective-permute-done.10 = bf16[256,512]{1,0:T(8,128)(2,1)} collective-permute-done((bf16[256,512]{1,0:T(8,128)(2,1)}, bf16[256,512]{1,0:T(8,128)(2,1)}, u32[]{:S(2)}, u32[]{:S(2)}) %collective-permute-start.10) | collective-permute-done | bytes 262176 | tf_op jit(solution)/shard_map/ppermute | solution.py:20
  212.0 1.4 bitcast_add_fusion.1
  213.5 3.3 %collective-permute-start.11 = (f32[128,512]{1,0:T(8,128)S(1)}, f32[128,512]{1,0:T(8,128)S(1)}, u32[]{:S(2)}, u32[]{:S(2)}) collective-permute-start(f32[128,512]{1,0:T(8,128)S(1)} %slice_select_fusion), channel_id=1, source_target_pairs={{0,4},{4,0},{8,12},{12,8},{16,20},{20,16},{24,28},{28,24},{32,36},... | collective-permute-start | bytes 786440 | tf_op jit(solution)/shard_map/ppermute | solution.py:20
  216.8 1.1 collective-permute-done.11
  218.0 4.9 %collective-permute-start.12 = (f32[128,512]{1,0:T(8,128)S(1)}, f32[128,512]{1,0:T(8,128)S(1)}, u32[]{:S(2)}, u32[]{:S(2)}) collective-permute-start(f32[128,512]{1,0:T(8,128)S(1)} %select_add_fusion), channel_id=1, source_target_pairs={{0,16},{4,20},{8,24},{12,28},{16,0},{20,4},{24,8},{28,12},{32,48},... | collective-permute-start | bytes 786440 | tf_op jit(solution)/shard_map/ppermute | solution.py:20
  222.9 6.4 %collective-permute-done.12 = f32[128,512]{1,0:T(8,128)S(1)} collective-permute-done((f32[128,512]{1,0:T(8,128)S(1)}, f32[128,512]{1,0:T(8,128)S(1)}, u32[]{:S(2)}, u32[]{:S(2)}) %collective-permute-start.12) | collective-permute-done | bytes 262176 | tf_op jit(solution)/shard_map/ppermute | solution.py:20
  229.3 7.0 %collective-permute-start.13 = (f32[128,512]{1,0:T(8,128)S(1)}, f32[128,512]{1,0:T(8,128)S(1)}, u32[]{:S(2)}, u32[]{:S(2)}) collective-permute-start(f32[128,512]{1,0:T(8,128)S(1)} %add.105), channel_id=1, source_target_pairs={{0,64},{4,68},{8,72},{12,76},{16,80},{20,84},{24,88},{28,92},{32,9... | collective-permute-start | bytes 786440 | tf_op jit(solution)/shard_map/ppermute | solution.py:20
  236.4 5.4 %collective-permute-done.13 = f32[128,512]{1,0:T(8,128)S(1)} collective-permute-done((f32[128,512]{1,0:T(8,128)S(1)}, f32[128,512]{1,0:T(8,128)S(1)}, u32[]{:S(2)}, u32[]{:S(2)}) %collective-permute-start.13) | collective-permute-done | bytes 262176 | tf_op jit(solution)/shard_map/ppermute | solution.py:20
  241.8 5.7 %collective-permute-start.14 = (f32[128,512]{1,0:T(8,128)S(1)}, f32[128,512]{1,0:T(8,128)S(1)}, u32[]{:S(2)}, u32[]{:S(2)}) collective-permute-start(f32[128,512]{1,0:T(8,128)S(1)} %add.106), channel_id=1, source_target_pairs={{0,8},{4,12},{8,0},{12,4},{16,24},{20,28},{24,16},{28,20},{32,40},... | collective-permute-start | bytes 786440 | tf_op jit(solution)/shard_map/ppermute | solution.py:20
  247.5 13.2 %collective-permute-done.14 = f32[128,512]{1,0:T(8,128)S(1)} collective-permute-done((f32[128,512]{1,0:T(8,128)S(1)}, f32[128,512]{1,0:T(8,128)S(1)}, u32[]{:S(2)}, u32[]{:S(2)}) %collective-permute-start.14) | collective-permute-done | bytes 262176 | tf_op jit(solution)/shard_map/ppermute | solution.py:20
  260.8 2.1 collective-permute-start.15
  263.4 7.5 %collective-permute-done.15 = f32[128,512]{1,0:T(8,128)S(1)} collective-permute-done((f32[128,512]{1,0:T(8,128)S(1)}, f32[128,512]{1,0:T(8,128)S(1)}, u32[]{:S(2)}, u32[]{:S(2)}) %collective-permute-start.15) | collective-permute-done | bytes 262176 | tf_op jit(solution)/shard_map/ppermute | solution.py:20
  271.0 6.0 %collective-permute-start.16 = (f32[128,512]{1,0:T(8,128)S(1)}, f32[128,512]{1,0:T(8,128)S(1)}, u32[]{:S(2)}, u32[]{:S(2)}) collective-permute-start(f32[128,512]{1,0:T(8,128)S(1)} %add.108), channel_id=1, source_target_pairs={{0,128},{4,132},{8,136},{12,140},{16,144},{20,148},{24,152},{28,15... | collective-permute-start | bytes 786440 | tf_op jit(solution)/shard_map/ppermute | solution.py:20
  277.7 10.8 %collective-permute-done.16 = f32[128,512]{1,0:T(8,128)S(1)} collective-permute-done((f32[128,512]{1,0:T(8,128)S(1)}, f32[128,512]{1,0:T(8,128)S(1)}, u32[]{:S(2)}, u32[]{:S(2)}) %collective-permute-start.16) | collective-permute-done | bytes 262176 | tf_op jit(solution)/shard_map/ppermute | solution.py:20
  288.5 8.9 %collective-permute-start.17 = (f32[128,512]{1,0:T(8,128)S(1)}, f32[128,512]{1,0:T(8,128)S(1)}, u32[]{:S(2)}, u32[]{:S(2)}) collective-permute-start(f32[128,512]{1,0:T(8,128)S(1)} %add.109), channel_id=1, source_target_pairs={{0,256},{4,260},{8,264},{12,268},{16,272},{20,276},{24,280},{28,28... | collective-permute-start | bytes 786440 | tf_op jit(solution)/shard_map/ppermute | solution.py:20
  298.0 11.3 %collective-permute-done.17 = f32[128,512]{1,0:T(8,128)S(1)} collective-permute-done((f32[128,512]{1,0:T(8,128)S(1)}, f32[128,512]{1,0:T(8,128)S(1)}, u32[]{:S(2)}, u32[]{:S(2)}) %collective-permute-start.17) | collective-permute-done | bytes 262176 | tf_op jit(solution)/shard_map/ppermute | solution.py:20
  309.3 3.0 collective-permute-start.18
  312.4 1.5 fusion.58
  313.9 0.8 maximum_select_fusion
  (101 shorter events, 9.7 us)
Async XLA Ops:
  7.2 80.6 %copy-start = (bf16[1,128,1024]{2,1,0:T(8,128)(2,1)S(1)}, bf16[1,128,1024]{2,1,0:T(8,128)(2,1)}, u32[]{:S(2)}) copy-start(bf16[1,128,1024]{2,1,0:T(8,128)(2,1)} %param.6) | copy-start | bytes 786436
  7.2 69.9 %all-gather.2.cloned.1.call-start = ((), (), s32[]{:S(2)}) async-start(), calls=%async_computation | async-start | bytes 3276800 | tf_op jit(solution)/shard_map/all_gather | solution.py:124
  77.1 7.7 %collective-permute-start = (bf16[1024,1280]{1,0:T(8,128)(2,1)}, bf16[1024,1280]{1,0:T(8,128)(2,1)}, u32[]{:S(2)}, u32[]{:S(2)}) collective-permute-start(bf16[1024,1280]{1,0:T(8,128)(2,1)} %all-gather.2.cloned.1.call-done), channel_id=1, source_target_pairs={{0,4},{4,0},{8,12},{12,8},{16,20},{20,16},{24,28},{28,24},{32,36},... | collective-permute-start | bytes 7864328 | tf_op jit(solution)/shard_map/ppermute | solution.py:20
  87.7 16.6 %copy-start.1 = (bf16[1024,512]{1,0:T(8,128)(2,1)}, bf16[1024,512]{1,0:T(8,128)(2,1)S(1)}, u32[]{:S(2)}) copy-start(bf16[1024,512]{1,0:T(8,128)(2,1)S(1)} %pad_maximum_fusion) | copy-start | bytes 3145732
  88.1 16.3 %copy-start.26 = (bf16[1,128,1024]{2,1,0:T(8,128)(2,1)S(1)}, bf16[1,128,1024]{2,1,0:T(8,128)(2,1)}, u32[]{:S(2)}) copy-start(bf16[1,128,1024]{2,1,0:T(8,128)(2,1)} %param.7) | copy-start | bytes 786436
  88.1 18.5 %collective-permute-start.4 = (bf16[128,512]{1,0:T(8,128)(2,1)S(1)}, bf16[128,512]{1,0:T(8,128)(2,1)S(1)}, u32[]{:S(2)}, u32[]{:S(2)}) collective-permute-start(bf16[128,512]{1,0:T(8,128)(2,1)S(1)} %fusion.75), channel_id=1, source_target_pairs={{0,4},{4,8},{8,12},{12,16},{16,20},{20,24},{24,28},{28,32},{32,36}... | collective-permute-start | bytes 393224 | tf_op jit(solution)/shard_map/ppermute | solution.py:15
  94.5 12.0 %collective-permute-start.3 = (bf16[128,512]{1,0:T(8,128)(2,1)S(1)}, bf16[128,512]{1,0:T(8,128)(2,1)S(1)}, u32[]{:S(2)}, u32[]{:S(2)}) collective-permute-start(bf16[128,512]{1,0:T(8,128)(2,1)S(1)} %fusion.75), channel_id=1, source_target_pairs={{0,8},{4,12},{8,16},{12,20},{16,24},{20,28},{24,32},{28,36},{32,40... | collective-permute-start | bytes 393224 | tf_op jit(solution)/shard_map/ppermute | solution.py:15
  98.5 8.0 %collective-permute-start.2 = (bf16[128,512]{1,0:T(8,128)(2,1)S(1)}, bf16[128,512]{1,0:T(8,128)(2,1)S(1)}, u32[]{:S(2)}, u32[]{:S(2)}) collective-permute-start(bf16[128,512]{1,0:T(8,128)(2,1)S(1)} %fusion.75), channel_id=1, source_target_pairs={{0,12},{4,16},{8,20},{12,24},{16,28},{20,32},{24,36},{28,40},{32,4... | collective-permute-start | bytes 393224 | tf_op jit(solution)/shard_map/ppermute | solution.py:15
  99.9 6.6 %collective-permute-start.1 = (bf16[128,512]{1,0:T(8,128)(2,1)S(1)}, bf16[128,512]{1,0:T(8,128)(2,1)S(1)}, u32[]{:S(2)}, u32[]{:S(2)}) collective-permute-start(bf16[128,512]{1,0:T(8,128)(2,1)S(1)} %fusion.75), channel_id=1, source_target_pairs={{0,16},{4,20},{8,24},{12,28},{16,32},{20,36},{24,40},{28,44},{32,4... | collective-permute-start | bytes 393224 | tf_op jit(solution)/shard_map/ppermute | solution.py:15
  117.9 2.1 copy-start.21
  120.0 0.8 copy-start.25
  120.3 1.4 copy-start.15
  120.8 0.9 copy-start.4
  120.8 1.0 copy-start.19
  121.8 1.3 copy-start.14
  122.5 3.9 %copy-start.8 = (bf16[4,128,640]{1,2,0:T(8,128)(2,1)}, bf16[4,128,640]{1,2,0:T(8,128)(2,1)S(1)}, u32[]{:S(2)}) copy-start(bf16[4,128,640]{1,2,0:T(8,128)(2,1)S(1)} %fusion.44) | copy-start | bytes 1966084
  122.5 1.0 copy-start.20
  123.2 1.3 copy-start.13
  124.2 1.8 copy-start.6
  124.2 1.0 copy-start.18
  124.7 1.3 copy-start.24
  125.6 0.8 copy-start.23
  125.6 1.2 copy-start.22
  126.0 1.0 copy-start.10
  128.4 1.3 copy-start.12
  129.6 11.5 %collective-permute-start.5 = (bf16[128,512]{0,1:T(8,128)(2,1)}, bf16[128,512]{0,1:T(8,128)(2,1)}, u32[]{:S(2)}, u32[]{:S(2)}) collective-permute-start(bf16[128,512]{0,1:T(8,128)(2,1)} %get-tuple-element.6), channel_id=1, source_target_pairs={{4,0},{8,4},{12,8},{16,12},{20,16},{24,20},{28,24},{32,28},{36,32}... | collective-permute-start | bytes 393224 | tf_op jit(solution)/shard_map/ppermute | solution.py:15
  136.3 6.3 %collective-permute-start.8 = (bf16[128,512]{0,1:T(8,128)(2,1)}, bf16[128,512]{0,1:T(8,128)(2,1)}, u32[]{:S(2)}, u32[]{:S(2)}) collective-permute-start(bf16[128,512]{0,1:T(8,128)(2,1)} %get-tuple-element.7), channel_id=1, source_target_pairs={{16,0},{20,4},{24,8},{28,12},{32,16},{36,20},{40,24},{44,28},{48,3... | collective-permute-start | bytes 393224 | tf_op jit(solution)/shard_map/ppermute | solution.py:15
  137.6 8.9 %collective-permute-start.7 = (bf16[128,512]{0,1:T(8,128)(2,1)}, bf16[128,512]{0,1:T(8,128)(2,1)}, u32[]{:S(2)}, u32[]{:S(2)}) collective-permute-start(bf16[128,512]{0,1:T(8,128)(2,1)} %get-tuple-element.8), channel_id=1, source_target_pairs={{12,0},{16,4},{20,8},{24,12},{28,16},{32,20},{36,24},{40,28},{44,3... | collective-permute-start | bytes 393224 | tf_op jit(solution)/shard_map/ppermute | solution.py:15
  138.9 12.3 %collective-permute-start.6 = (bf16[128,512]{0,1:T(8,128)(2,1)}, bf16[128,512]{0,1:T(8,128)(2,1)}, u32[]{:S(2)}, u32[]{:S(2)}) collective-permute-start(bf16[128,512]{0,1:T(8,128)(2,1)} %get-tuple-element.9), channel_id=1, source_target_pairs={{8,0},{12,4},{16,8},{20,12},{24,16},{28,20},{32,24},{36,28},{40,32... | collective-permute-start | bytes 393224 | tf_op jit(solution)/shard_map/ppermute | solution.py:15
  152.4 0.7 copy-start.16
  173.6 19.0 %collective-permute-start.9 = (bf16[2,256,512]{2,1,0:T(8,128)(2,1)}, bf16[2,256,512]{2,1,0:T(8,128)(2,1)}, u32[]{:S(2)}, u32[]{:S(2)}) collective-permute-start(bf16[2,256,512]{2,1,0:T(8,128)(2,1)} %fusion.86), channel_id=1, source_target_pairs={{0,1},{1,0},{2,3},{3,2},{4,5},{5,4},{6,7},{7,6},{8,9},{9,8},{10,11... | collective-permute-start | bytes 1572872 | tf_op jit(solution)/shard_map/ppermute | solution.py:20
  194.2 1.0 copy-start.3
  196.0 16.0 %collective-permute-start.10 = (bf16[256,512]{1,0:T(8,128)(2,1)}, bf16[256,512]{1,0:T(8,128)(2,1)}, u32[]{:S(2)}, u32[]{:S(2)}) collective-permute-start(bf16[256,512]{1,0:T(8,128)(2,1)} %fusion.91), channel_id=1, source_target_pairs={{0,2},{1,3},{2,0},{3,1},{4,6},{5,7},{6,4},{7,5},{8,10},{9,11},{10,... | collective-permute-start | bytes 786440 | tf_op jit(solution)/shard_map/ppermute | solution.py:20
  213.5 4.4 %collective-permute-start.11 = (f32[128,512]{1,0:T(8,128)S(1)}, f32[128,512]{1,0:T(8,128)S(1)}, u32[]{:S(2)}, u32[]{:S(2)}) collective-permute-start(f32[128,512]{1,0:T(8,128)S(1)} %slice_select_fusion), channel_id=1, source_target_pairs={{0,4},{4,0},{8,12},{12,8},{16,20},{20,16},{24,28},{28,24},{32,36},... | collective-permute-start | bytes 786440 | tf_op jit(solution)/shard_map/ppermute | solution.py:20
  218.0 44.9 %copy-start.5 = (bf16[4,128,640]{1,2,0:T(8,128)(2,1)S(1)}, bf16[4,128,640]{1,2,0:T(8,128)(2,1)}, u32[]{:S(2)}) copy-start(bf16[4,128,640]{1,2,0:T(8,128)(2,1)} %copy-done.4) | copy-start | bytes 1966084
  218.0 11.3 %collective-permute-start.12 = (f32[128,512]{1,0:T(8,128)S(1)}, f32[128,512]{1,0:T(8,128)S(1)}, u32[]{:S(2)}, u32[]{:S(2)}) collective-permute-start(f32[128,512]{1,0:T(8,128)S(1)} %select_add_fusion), channel_id=1, source_target_pairs={{0,16},{4,20},{8,24},{12,28},{16,0},{20,4},{24,8},{28,12},{32,48},... | collective-permute-start | bytes 786440 | tf_op jit(solution)/shard_map/ppermute | solution.py:20
  229.3 33.8 %copy-start.9 = (bf16[4,128,640]{1,2,0:T(8,128)(2,1)S(1)}, bf16[4,128,640]{1,2,0:T(8,128)(2,1)}, u32[]{:S(2)}) copy-start(bf16[4,128,640]{1,2,0:T(8,128)(2,1)} %copy-done.8) | copy-start | bytes 1966084
  229.3 12.5 %collective-permute-start.13 = (f32[128,512]{1,0:T(8,128)S(1)}, f32[128,512]{1,0:T(8,128)S(1)}, u32[]{:S(2)}, u32[]{:S(2)}) collective-permute-start(f32[128,512]{1,0:T(8,128)S(1)} %add.105), channel_id=1, source_target_pairs={{0,64},{4,68},{8,72},{12,76},{16,80},{20,84},{24,88},{28,92},{32,9... | collective-permute-start | bytes 786440 | tf_op jit(solution)/shard_map/ppermute | solution.py:20
  241.8 18.9 %collective-permute-start.14 = (f32[128,512]{1,0:T(8,128)S(1)}, f32[128,512]{1,0:T(8,128)S(1)}, u32[]{:S(2)}, u32[]{:S(2)}) collective-permute-start(f32[128,512]{1,0:T(8,128)S(1)} %add.106), channel_id=1, source_target_pairs={{0,8},{4,12},{8,0},{12,4},{16,24},{20,28},{24,16},{28,20},{32,40},... | collective-permute-start | bytes 786440 | tf_op jit(solution)/shard_map/ppermute | solution.py:20
  260.8 16.2 %copy-start.7 = (bf16[4,128,640]{1,2,0:T(8,128)(2,1)S(1)}, bf16[4,128,640]{1,2,0:T(8,128)(2,1)}, u32[]{:S(2)}) copy-start(bf16[4,128,640]{1,2,0:T(8,128)(2,1)} %copy-done.6) | copy-start | bytes 1966084
  260.8 10.1 %collective-permute-start.15 = (f32[128,512]{1,0:T(8,128)S(1)}, f32[128,512]{1,0:T(8,128)S(1)}, u32[]{:S(2)}, u32[]{:S(2)}) collective-permute-start(f32[128,512]{1,0:T(8,128)S(1)} %add.107), channel_id=1, source_target_pairs={{0,32},{4,36},{8,40},{12,44},{16,48},{20,52},{24,56},{28,60},{32,0... | collective-permute-start | bytes 786440 | tf_op jit(solution)/shard_map/ppermute | solution.py:20
  263.2 14.2 %copy-start.11 = (bf16[4,128,640]{1,2,0:T(8,128)(2,1)S(1)}, bf16[4,128,640]{1,2,0:T(8,128)(2,1)}, u32[]{:S(2)}) copy-start(bf16[4,128,640]{1,2,0:T(8,128)(2,1)} %copy-done.10) | copy-start | bytes 1966084
  270.9 26.5 %copy-start.2 = (bf16[1024,512]{1,0:T(8,128)(2,1)S(1)}, bf16[1024,512]{1,0:T(8,128)(2,1)}, u32[]{:S(2)}) copy-start(bf16[1024,512]{1,0:T(8,128)(2,1)} %copy-done.1) | copy-start | bytes 3145732
  271.0 26.5 %copy-start.17 = (bf16[128,512]{0,1:T(8,128)(2,1)S(1)}, bf16[128,512]{0,1:T(8,128)(2,1)}, u32[]{:S(2)}) copy-start(bf16[128,512]{0,1:T(8,128)(2,1)} %copy-done.16) | copy-start | bytes 393220
  271.0 17.5 %collective-permute-start.16 = (f32[128,512]{1,0:T(8,128)S(1)}, f32[128,512]{1,0:T(8,128)S(1)}, u32[]{:S(2)}, u32[]{:S(2)}) collective-permute-start(f32[128,512]{1,0:T(8,128)S(1)} %add.108), channel_id=1, source_target_pairs={{0,128},{4,132},{8,136},{12,140},{16,144},{20,148},{24,152},{28,15... | collective-permute-start | bytes 786440 | tf_op jit(solution)/shard_map/ppermute | solution.py:20
  288.5 20.8 %collective-permute-start.17 = (f32[128,512]{1,0:T(8,128)S(1)}, f32[128,512]{1,0:T(8,128)S(1)}, u32[]{:S(2)}, u32[]{:S(2)}) collective-permute-start(f32[128,512]{1,0:T(8,128)S(1)} %add.109), channel_id=1, source_target_pairs={{0,256},{4,260},{8,264},{12,268},{16,272},{20,276},{24,280},{28,28... | collective-permute-start | bytes 786440 | tf_op jit(solution)/shard_map/ppermute | solution.py:20
  309.3 4.6 %collective-permute-start.18 = (f32[128,512]{1,0:T(8,128)S(1)}, f32[128,512]{1,0:T(8,128)S(1)}, u32[]{:S(2)}, u32[]{:S(2)}) collective-permute-start(f32[128,512]{1,0:T(8,128)S(1)} %add.110), channel_id=1, source_target_pairs={{0,4},{4,0},{8,12},{12,8},{16,20},{20,16},{24,28},{28,24},{32,36},... | collective-permute-start | bytes 786440 | tf_op jit(solution)/shard_map/ppermute | solution.py:20
Sparse Core Ops, SparseCore 0:
  10.1 66.9 all-gather.1

commit v6 on v5

--- a/solution.py
+++ b/solution.py
@@ -67,22 +67,27 @@
     if (
         stream_count != 1 << stream_bits
         or tm_count != 1 << tm_bits
-        or partial.shape[0] % (2 * stream_count)
+        or partial[0].shape[1] % (2 * stream_count)
     ):
         shard = lax.psum_scatter(
-            partial.astype(jnp.bfloat16), "stream", scatter_dimension=0, tiled=True
+            contract_first(*partial).astype(jnp.bfloat16), "stream", scatter_dimension=0, tiled=True
         ).astype(jnp.float32)
         return lax.psum(shard, "tm")
     stream_index = lax.axis_index("stream")
-    current = partial.reshape((2,) * stream_bits + (-1,) + partial.shape[1:])
-    for bit in range(stream_bits):
-        axis_pos = stream_bits - 1 - bit
-        upper = ((stream_index >> bit) & 1) == 1
-        low = lax.index_in_dim(current, 0, axis_pos, keepdims=False)
-        high = lax.index_in_dim(current, 1, axis_pos, keepdims=False)
-        keep = jnp.where(upper, high, low).astype(jnp.float32)
-        send = jnp.where(upper, low, high).astype(jnp.bfloat16)
-        current = keep + xor_swap(send, "stream", bit).astype(jnp.float32)
+    rows, grads = partial
+    tokens, features = rows.shape
+    if stream_bits == 0:
+        current = contract_first(rows, grads)
+    else:
+        paired = rows.reshape(tokens, stream_count // 2, 2, features // stream_count)
+        even = paired[:, :, 0].reshape(tokens, features // 2)
+        odd = paired[:, :, 1].reshape(tokens, features // 2)
+        upper = (stream_index & 1) == 1
+        keep = contract_first(jnp.where(upper, odd, even), grads)
+        send = contract_first(jnp.where(upper, even, odd), grads).astype(jnp.bfloat16)
+        current = keep + xor_swap(send, "stream", 0).astype(jnp.float32)
+    for bit in reversed(range(1, stream_bits)):
+        current = halve_stage(current, "stream", bit, jnp.bfloat16)
     if tm_bits == 0:
         return current
     current = halve_stage(current, "tm", 0, jnp.float32)
@@ -227,7 +232,7 @@
         keyval_grads, keyval_full
     )
     input_grad = input_grad.astype(jnp.bfloat16)
-    weight_grad = grad_sum(contract_first(record_rows, keyval_grads))
+    weight_grad = grad_sum((record_rows, keyval_grads))
     return (input_grad[None], weight_grad)
 
 

time: 323 us -> 300 us (0.929)
  local copies, waits for them, and re-layouts: 23.3 us -> 6.54 us
  other arithmetic: 17.2 us -> 12.9 us
    unnamed x60 -> x59, local copies, waits for them, and re-layouts: 11.6 us -> 5 us
    slice x1 -> x0, local copies, waits for them, and re-layouts: 5.33 us -> none  [grad_sum(): high = lax.index_in_dim(current, 1, axis_pos, keepdims=False)]
    reshape x1 -> x0, local copies, waits for them, and re-layouts: 3.99 us -> none  [grad_sum(): current = partial.reshape((2,) * stream_bits + (-1,) + partial.shape[1:])]
  transfers between devices with their start and end apart: 20 -> 20, of which waited for: 15 -> 14; matrix products, arithmetic and copies ran while one was open for 2% -> 3% of each run, Pallas kernels for 0% -> 0%
where the time goes in v6:
time: 300 us; the launch traced here: 299 us
  waiting for transfers between devices  162 us (54%)
  starting transfers between devices  78.5 us (26%)
  matrix products  24.2 us (8%)
  between operations  15.5 us (5%)
  other arithmetic  12.9 us (4%)
  local copies, waits for them, and re-layouts  6.54 us (2%)
    ppermute x11, waiting for transfers between devices, xor_swap(): lax.ppermute(value, axis, [(source, source ^ 1 << bit) for source in rang...  84.3 us
    all_gather x1, waiting for transfers between devices, per_device(): lax.all_gather(lax.dynamic_slice_in_dim(weights_local, core * half_width,...  67.4 us
    ppermute x11, starting transfers between devices, xor_swap(): lax.ppermute(value, axis, [(source, source ^ 1 << bit) for source in rang...  52.5 us
    ppermute x8, starting transfers between devices, shifted(): lax.ppermute(value, axis, [(source, source + steps) for source in range(l...  25.9 us
    sub x4, matrix products, per_device(): terms = jnp.where(allowed, jnp.exp(masked - row_max), 0.0)  11.3 us
    ppermute x8, waiting for transfers between devices, shifted(): lax.ppermute(value, axis, [(source, source + steps) for source in range(l...  9.96 us
  transfers between devices with their start and end apart: 20, of which 14 were waited for; matrix products, arithmetic and copies ran while one was open for 3% of the time, Pallas kernels for 0%

profile of v6, /device:TPU:1, one launch (start us, length us, event | category | flops | bytes accessed | tf_op | source)
XLA Modules:
  0.0 299.3 jit_solution(7855845362204616660)
XLA Ops:
  7.3 2.4 fusion.85
  9.6 67.4 %all-gather.2.cloned.1.call-done = bf16[1024,1280]{1,0:T(8,128)(2,1)} async-done(((bf16[256,1280]{1,0:T(8,128)(2,1)}), bf16[1024,1280]{1,0:T(8,128)(2,1)}) %all-gather.2.cloned.1.call-update) | async-done | bytes 2621456 | tf_op jit(solution)/shard_map/all_gather | solution.py:129
  77.1 2.8 collective-permute-start
  80.6 0.8 copy.104
  81.5 1.0 fusion.89
  82.4 2.3 collective-permute-done
  84.8 2.9 broadcast_select_fusion.1
  88.1 6.3 %collective-permute-start.4 = (bf16[128,512]{1,0:T(8,128)(2,1)S(1)}, bf16[128,512]{1,0:T(8,128)(2,1)S(1)}, u32[]{:S(2)}, u32[]{:S(2)}) collective-permute-start(bf16[128,512]{1,0:T(8,128)(2,1)S(1)} %fusion.75), channel_id=1, source_target_pairs={{0,4},{4,8},{8,12},{12,16},{16,20},{20,24},{24,28},{28,32},{32,36}... | collective-permute-start | bytes 393224 | tf_op jit(solution)/shard_map/ppermute | solution.py:15
  94.3 4.0 %collective-permute-start.3 = (bf16[128,512]{1,0:T(8,128)(2,1)S(1)}, bf16[128,512]{1,0:T(8,128)(2,1)S(1)}, u32[]{:S(2)}, u32[]{:S(2)}) collective-permute-start(bf16[128,512]{1,0:T(8,128)(2,1)S(1)} %fusion.75), channel_id=1, source_target_pairs={{0,8},{4,12},{8,16},{12,20},{16,24},{20,28},{24,32},{28,36},{32,40... | collective-permute-start | bytes 393224 | tf_op jit(solution)/shard_map/ppermute | solution.py:15
  98.4 1.4 collective-permute-start.2
  99.8 3.6 %collective-permute-start.1 = (bf16[128,512]{1,0:T(8,128)(2,1)S(1)}, bf16[128,512]{1,0:T(8,128)(2,1)S(1)}, u32[]{:S(2)}, u32[]{:S(2)}) collective-permute-start(bf16[128,512]{1,0:T(8,128)(2,1)S(1)} %fusion.75), channel_id=1, source_target_pairs={{0,16},{4,20},{8,24},{12,28},{16,32},{20,36},{24,40},{28,44},{32,4... | collective-permute-start | bytes 393224 | tf_op jit(solution)/shard_map/ppermute | solution.py:15
  103.4 0.8 fusion.64
  104.2 0.7 fusion.61
  104.9 0.7 fusion.121
  105.6 0.7 fusion.120
  106.5 2.7 fusion.122
  109.2 2.6 fusion.124
  111.8 2.7 fusion.123
  114.5 3.2 %fusion.125 = (f32[4,128]{1,0:T(4,128)}, f32[4,128,640]{1,2,0:T(8,128)}) fusion(bf16[128,4,64]{0,2,1:T(8,128)(2,1)} %bitcast.306, pred[128,640]{0,1:T(8,128)(4,1)} %fusion.89, bf16[640,512]{1,0:T(8,128)(2,1)S(1)} %constant_dynamic-update-slice_fusion), kind=kOutput, calls=%fused_computation.181 | convolution fusion | flops 43582080 | bytes 1705984 | tf_op jit(solution)/shard_map/sub | solution.py:187
  117.7 0.7 broadcast_select_fusion.4
  118.5 1.4 divide_convert_fusion.3
  120.2 0.4 fusion.42
  121.0 0.5 copy-done.4
  122.4 0.6 copy-done.15
  123.7 0.4 fusion.43
  124.6 0.5 copy-done.19
  125.1 0.4 multiply_reduce_fusion
  125.4 0.4 fusion.45
  128.4 6.7 %collective-permute-start.5 = (bf16[128,512]{0,1:T(8,128)(2,1)S(1)}, bf16[128,512]{0,1:T(8,128)(2,1)S(1)}, u32[]{:S(2)}, u32[]{:S(2)}) collective-permute-start(bf16[128,512]{0,1:T(8,128)(2,1)S(1)} %get-tuple-element.4), channel_id=1, source_target_pairs={{4,0},{8,4},{12,8},{16,12},{20,16},{24,20},{28,24},{32,28},{36,32}... | collective-permute-start | bytes 393224 | tf_op jit(solution)/shard_map/ppermute | solution.py:15
  135.1 1.3 collective-permute-start.8
  136.4 1.3 collective-permute-start.7
  137.7 1.3 collective-permute-start.6
  139.1 0.7 broadcast_select_fusion.2
  139.7 1.4 collective-permute-done.8
  141.1 3.9 %collective-permute-done.7 = bf16[128,512]{0,1:T(8,128)(2,1)S(1)} collective-permute-done((bf16[128,512]{0,1:T(8,128)(2,1)S(1)}, bf16[128,512]{0,1:T(8,128)(2,1)S(1)}, u32[]{:S(2)}, u32[]{:S(2)}) %collective-permute-start.7) | collective-permute-done | bytes 131104 | tf_op jit(solution)/shard_map/ppermute | solution.py:15
  145.0 4.7 %collective-permute-done.6 = bf16[128,512]{0,1:T(8,128)(2,1)S(1)} collective-permute-done((bf16[128,512]{0,1:T(8,128)(2,1)S(1)}, bf16[128,512]{0,1:T(8,128)(2,1)S(1)}, u32[]{:S(2)}, u32[]{:S(2)}) %collective-permute-start.6) | collective-permute-done | bytes 131104 | tf_op jit(solution)/shard_map/ppermute | solution.py:15
  149.8 0.7 copy-done.12
  150.4 1.1 convolution_convert_fusion
  151.5 6.7 %collective-permute-start.9 = (bf16[512,512]{1,0:T(8,128)(2,1)}, bf16[512,512]{1,0:T(8,128)(2,1)}, u32[]{:S(2)}, u32[]{:S(2)}) collective-permute-start(bf16[512,512]{1,0:T(8,128)(2,1)} %convolution_convert_fusion), channel_id=1, source_target_pairs={{0,1},{1,0},{2,3},{3,2},{4,5},{5,4},{6,7},{7,6},{8,9},{9,8},{10,11... | collective-permute-start | bytes 1572872 | tf_op jit(solution)/shard_map/ppermute | solution.py:20
  158.2 12.3 %collective-permute-done.9 = bf16[512,512]{1,0:T(8,128)(2,1)} collective-permute-done((bf16[512,512]{1,0:T(8,128)(2,1)}, bf16[512,512]{1,0:T(8,128)(2,1)}, u32[]{:S(2)}, u32[]{:S(2)}) %collective-permute-start.9) | collective-permute-done | bytes 524320 | tf_op jit(solution)/shard_map/ppermute | solution.py:20
  170.5 1.5 convolution_add_fusion
  172.0 1.0 copy-done.3
  173.0 0.8 select_convert_fusion
  173.7 2.1 collective-permute-start.10
  175.8 13.9 %collective-permute-done.10 = bf16[256,512]{1,0:T(8,128)(2,1)} collective-permute-done((bf16[256,512]{1,0:T(8,128)(2,1)}, bf16[256,512]{1,0:T(8,128)(2,1)}, u32[]{:S(2)}, u32[]{:S(2)}) %collective-permute-start.10) | collective-permute-done | bytes 262176 | tf_op jit(solution)/shard_map/ppermute | solution.py:20
  189.8 1.4 convert_add_fusion
  191.2 3.3 %collective-permute-start.11 = (f32[128,512]{1,0:T(8,128)S(1)}, f32[128,512]{1,0:T(8,128)S(1)}, u32[]{:S(2)}, u32[]{:S(2)}) collective-permute-start(f32[128,512]{1,0:T(8,128)S(1)} %slice_select_fusion), channel_id=1, source_target_pairs={{0,4},{4,0},{8,12},{12,8},{16,20},{20,16},{24,28},{28,24},{32,36},... | collective-permute-start | bytes 786440 | tf_op jit(solution)/shard_map/ppermute | solution.py:20
  194.5 1.1 collective-permute-done.11
  195.7 4.9 %collective-permute-start.12 = (f32[128,512]{1,0:T(8,128)S(1)}, f32[128,512]{1,0:T(8,128)S(1)}, u32[]{:S(2)}, u32[]{:S(2)}) collective-permute-start(f32[128,512]{1,0:T(8,128)S(1)} %select_add_fusion), channel_id=1, source_target_pairs={{0,16},{4,20},{8,24},{12,28},{16,0},{20,4},{24,8},{28,12},{32,48},... | collective-permute-start | bytes 786440 | tf_op jit(solution)/shard_map/ppermute | solution.py:20
  200.7 6.4 %collective-permute-done.12 = f32[128,512]{1,0:T(8,128)S(1)} collective-permute-done((f32[128,512]{1,0:T(8,128)S(1)}, f32[128,512]{1,0:T(8,128)S(1)}, u32[]{:S(2)}, u32[]{:S(2)}) %collective-permute-start.12) | collective-permute-done | bytes 262176 | tf_op jit(solution)/shard_map/ppermute | solution.py:20
  207.1 7.1 %collective-permute-start.13 = (f32[128,512]{1,0:T(8,128)S(1)}, f32[128,512]{1,0:T(8,128)S(1)}, u32[]{:S(2)}, u32[]{:S(2)}) collective-permute-start(f32[128,512]{1,0:T(8,128)S(1)} %add.105), channel_id=1, source_target_pairs={{0,64},{4,68},{8,72},{12,76},{16,80},{20,84},{24,88},{28,92},{32,9... | collective-permute-start | bytes 786440 | tf_op jit(solution)/shard_map/ppermute | solution.py:20
  214.2 5.4 %collective-permute-done.13 = f32[128,512]{1,0:T(8,128)S(1)} collective-permute-done((f32[128,512]{1,0:T(8,128)S(1)}, f32[128,512]{1,0:T(8,128)S(1)}, u32[]{:S(2)}, u32[]{:S(2)}) %collective-permute-start.13) | collective-permute-done | bytes 262176 | tf_op jit(solution)/shard_map/ppermute | solution.py:20
  219.6 5.7 %collective-permute-start.14 = (f32[128,512]{1,0:T(8,128)S(1)}, f32[128,512]{1,0:T(8,128)S(1)}, u32[]{:S(2)}, u32[]{:S(2)}) collective-permute-start(f32[128,512]{1,0:T(8,128)S(1)} %add.106), channel_id=1, source_target_pairs={{0,8},{4,12},{8,0},{12,4},{16,24},{20,28},{24,16},{28,20},{32,40},... | collective-permute-start | bytes 786440 | tf_op jit(solution)/shard_map/ppermute | solution.py:20
  225.3 13.3 %collective-permute-done.14 = f32[128,512]{1,0:T(8,128)S(1)} collective-permute-done((f32[128,512]{1,0:T(8,128)S(1)}, f32[128,512]{1,0:T(8,128)S(1)}, u32[]{:S(2)}, u32[]{:S(2)}) %collective-permute-start.14) | collective-permute-done | bytes 262176 | tf_op jit(solution)/shard_map/ppermute | solution.py:20
  238.6 2.1 collective-permute-start.15
  241.2 7.5 %collective-permute-done.15 = f32[128,512]{1,0:T(8,128)S(1)} collective-permute-done((f32[128,512]{1,0:T(8,128)S(1)}, f32[128,512]{1,0:T(8,128)S(1)}, u32[]{:S(2)}, u32[]{:S(2)}) %collective-permute-start.15) | collective-permute-done | bytes 262176 | tf_op jit(solution)/shard_map/ppermute | solution.py:20
  248.8 5.9 %collective-permute-start.16 = (f32[128,512]{1,0:T(8,128)S(1)}, f32[128,512]{1,0:T(8,128)S(1)}, u32[]{:S(2)}, u32[]{:S(2)}) collective-permute-start(f32[128,512]{1,0:T(8,128)S(1)} %add.108), channel_id=1, source_target_pairs={{0,128},{4,132},{8,136},{12,140},{16,144},{20,148},{24,152},{28,15... | collective-permute-start | bytes 786440 | tf_op jit(solution)/shard_map/ppermute | solution.py:20
  255.5 10.7 %collective-permute-done.16 = f32[128,512]{1,0:T(8,128)S(1)} collective-permute-done((f32[128,512]{1,0:T(8,128)S(1)}, f32[128,512]{1,0:T(8,128)S(1)}, u32[]{:S(2)}, u32[]{:S(2)}) %collective-permute-start.16) | collective-permute-done | bytes 262176 | tf_op jit(solution)/shard_map/ppermute | solution.py:20
  266.2 9.0 %collective-permute-start.17 = (f32[128,512]{1,0:T(8,128)S(1)}, f32[128,512]{1,0:T(8,128)S(1)}, u32[]{:S(2)}, u32[]{:S(2)}) collective-permute-start(f32[128,512]{1,0:T(8,128)S(1)} %add.109), channel_id=1, source_target_pairs={{0,256},{4,260},{8,264},{12,268},{16,272},{20,276},{24,280},{28,28... | collective-permute-start | bytes 786440 | tf_op jit(solution)/shard_map/ppermute | solution.py:20
  275.2 0.5 fusion.126
  275.7 11.3 %collective-permute-done.17 = f32[128,512]{1,0:T(8,128)S(1)} collective-permute-done((f32[128,512]{1,0:T(8,128)S(1)}, f32[128,512]{1,0:T(8,128)S(1)}, u32[]{:S(2)}, u32[]{:S(2)}) %collective-permute-start.17) | collective-permute-done | bytes 262176 | tf_op jit(solution)/shard_map/ppermute | solution.py:20
  287.1 3.0 %collective-permute-start.18 = (f32[128,512]{1,0:T(8,128)S(1)}, f32[128,512]{1,0:T(8,128)S(1)}, u32[]{:S(2)}, u32[]{:S(2)}) collective-permute-start(f32[128,512]{1,0:T(8,128)S(1)} %add.110), channel_id=1, source_target_pairs={{0,4},{4,0},{8,12},{12,8},{16,20},{20,16},{24,28},{28,24},{32,36},... | collective-permute-start | bytes 786440 | tf_op jit(solution)/shard_map/ppermute | solution.py:20
  290.1 1.5 fusion.58
  291.6 0.8 maximum_select_fusion
  (98 shorter events, 7.2 us)
Async XLA Ops:
  7.2 97.0 %copy-start = (bf16[1,128,1024]{2,1,0:T(8,128)(2,1)S(1)}, bf16[1,128,1024]{2,1,0:T(8,128)(2,1)}, u32[]{:S(2)}) copy-start(bf16[1,128,1024]{2,1,0:T(8,128)(2,1)} %param.7) | copy-start | bytes 786436
  7.2 69.9 %all-gather.2.cloned.1.call-start = ((), (), s32[]{:S(2)}) async-start(), calls=%async_computation | async-start | bytes 3276800 | tf_op jit(solution)/shard_map/all_gather | solution.py:129
  7.2 73.3 %copy-start.18 = (bf16[1,128,1024]{2,1,0:T(8,128)(2,1)S(1)}, bf16[1,128,1024]{2,1,0:T(8,128)(2,1)}, u32[]{:S(2)}) copy-start(bf16[1,128,1024]{2,1,0:T(8,128)(2,1)} %param.6) | copy-start | bytes 786436
  77.1 7.7 %collective-permute-start = (bf16[1024,1280]{1,0:T(8,128)(2,1)}, bf16[1024,1280]{1,0:T(8,128)(2,1)}, u32[]{:S(2)}, u32[]{:S(2)}) collective-permute-start(bf16[1024,1280]{1,0:T(8,128)(2,1)} %all-gather.2.cloned.1.call-done), channel_id=1, source_target_pairs={{0,4},{4,0},{8,12},{12,8},{16,20},{20,16},{24,28},{28,24},{32,36},... | collective-permute-start | bytes 7864328 | tf_op jit(solution)/shard_map/ppermute | solution.py:20
  87.7 16.5 %copy-start.1 = (bf16[1024,512]{1,0:T(8,128)(2,1)}, bf16[1024,512]{1,0:T(8,128)(2,1)S(1)}, u32[]{:S(2)}) copy-start(bf16[1024,512]{1,0:T(8,128)(2,1)S(1)} %pad_maximum_fusion) | copy-start | bytes 3145732
  88.1 18.4 %collective-permute-start.4 = (bf16[128,512]{1,0:T(8,128)(2,1)S(1)}, bf16[128,512]{1,0:T(8,128)(2,1)S(1)}, u32[]{:S(2)}, u32[]{:S(2)}) collective-permute-start(bf16[128,512]{1,0:T(8,128)(2,1)S(1)} %fusion.75), channel_id=1, source_target_pairs={{0,4},{4,8},{8,12},{12,16},{16,20},{20,24},{24,28},{28,32},{32,36}... | collective-permute-start | bytes 393224 | tf_op jit(solution)/shard_map/ppermute | solution.py:15
  94.3 12.1 %collective-permute-start.3 = (bf16[128,512]{1,0:T(8,128)(2,1)S(1)}, bf16[128,512]{1,0:T(8,128)(2,1)S(1)}, u32[]{:S(2)}, u32[]{:S(2)}) collective-permute-start(bf16[128,512]{1,0:T(8,128)(2,1)S(1)} %fusion.75), channel_id=1, source_target_pairs={{0,8},{4,12},{8,16},{12,20},{16,24},{20,28},{24,32},{28,36},{32,40... | collective-permute-start | bytes 393224 | tf_op jit(solution)/shard_map/ppermute | solution.py:15
  98.4 8.0 %collective-permute-start.2 = (bf16[128,512]{1,0:T(8,128)(2,1)S(1)}, bf16[128,512]{1,0:T(8,128)(2,1)S(1)}, u32[]{:S(2)}, u32[]{:S(2)}) collective-permute-start(bf16[128,512]{1,0:T(8,128)(2,1)S(1)} %fusion.75), channel_id=1, source_target_pairs={{0,12},{4,16},{8,20},{12,24},{16,28},{20,32},{24,36},{28,40},{32,4... | collective-permute-start | bytes 393224 | tf_op jit(solution)/shard_map/ppermute | solution.py:15
  99.8 6.6 %collective-permute-start.1 = (bf16[128,512]{1,0:T(8,128)(2,1)S(1)}, bf16[128,512]{1,0:T(8,128)(2,1)S(1)}, u32[]{:S(2)}, u32[]{:S(2)}) collective-permute-start(bf16[128,512]{1,0:T(8,128)(2,1)S(1)} %fusion.75), channel_id=1, source_target_pairs={{0,16},{4,20},{8,24},{12,28},{16,32},{20,36},{24,40},{28,44},{32,4... | collective-permute-start | bytes 393224 | tf_op jit(solution)/shard_map/ppermute | solution.py:15
  117.7 2.2 copy-start.22
  119.9 0.8 copy-start.26
  120.2 1.4 copy-start.16
  120.7 0.8 copy-start.4
  120.7 1.0 copy-start.20
  121.7 1.3 copy-start.15
  122.3 3.9 %copy-start.8 = (bf16[4,128,640]{1,2,0:T(8,128)(2,1)}, bf16[4,128,640]{1,2,0:T(8,128)(2,1)S(1)}, u32[]{:S(2)}) copy-start(bf16[4,128,640]{1,2,0:T(8,128)(2,1)S(1)} %fusion.44) | copy-start | bytes 1966084
  122.4 1.0 copy-start.21
  123.1 1.3 copy-start.14
  124.1 1.8 copy-start.6
  124.1 0.9 copy-start.19
  124.6 1.3 copy-start.25
  125.4 0.8 copy-start.24
  125.4 1.2 copy-start.23
  125.9 1.0 copy-start.10
  128.2 10.8 %copy-start.17 = (bf16[1,128,1024]{1,2,0:T(8,128)(2,1)S(1)}, bf16[1,128,1024]{1,2,0:T(8,128)(2,1)}, u32[]{:S(2)}) copy-start(bf16[1,128,1024]{1,2,0:T(8,128)(2,1)} %copy.104) | copy-start | bytes 786436
  128.4 11.3 %collective-permute-start.5 = (bf16[128,512]{0,1:T(8,128)(2,1)S(1)}, bf16[128,512]{0,1:T(8,128)(2,1)S(1)}, u32[]{:S(2)}, u32[]{:S(2)}) collective-permute-start(bf16[128,512]{0,1:T(8,128)(2,1)S(1)} %get-tuple-element.4), channel_id=1, source_target_pairs={{4,0},{8,4},{12,8},{16,12},{20,16},{24,20},{28,24},{32,28},{36,32}... | collective-permute-start | bytes 393224 | tf_op jit(solution)/shard_map/ppermute | solution.py:15
  135.1 6.0 %collective-permute-start.8 = (bf16[128,512]{0,1:T(8,128)(2,1)S(1)}, bf16[128,512]{0,1:T(8,128)(2,1)S(1)}, u32[]{:S(2)}, u32[]{:S(2)}) collective-permute-start(bf16[128,512]{0,1:T(8,128)(2,1)S(1)} %get-tuple-element.5), channel_id=1, source_target_pairs={{16,0},{20,4},{24,8},{28,12},{32,16},{36,20},{40,24},{44,28},{48,3... | collective-permute-start | bytes 393224 | tf_op jit(solution)/shard_map/ppermute | solution.py:15
  136.4 8.6 %collective-permute-start.7 = (bf16[128,512]{0,1:T(8,128)(2,1)S(1)}, bf16[128,512]{0,1:T(8,128)(2,1)S(1)}, u32[]{:S(2)}, u32[]{:S(2)}) collective-permute-start(bf16[128,512]{0,1:T(8,128)(2,1)S(1)} %get-tuple-element.6), channel_id=1, source_target_pairs={{12,0},{16,4},{20,8},{24,12},{28,16},{32,20},{36,24},{40,28},{44,3... | collective-permute-start | bytes 393224 | tf_op jit(solution)/shard_map/ppermute | solution.py:15
  137.7 11.9 %collective-permute-start.6 = (bf16[128,512]{0,1:T(8,128)(2,1)S(1)}, bf16[128,512]{0,1:T(8,128)(2,1)S(1)}, u32[]{:S(2)}, u32[]{:S(2)}) collective-permute-start(bf16[128,512]{0,1:T(8,128)(2,1)S(1)} %get-tuple-element.7), channel_id=1, source_target_pairs={{8,0},{12,4},{16,8},{20,12},{24,16},{28,20},{32,24},{36,28},{40,32... | collective-permute-start | bytes 393224 | tf_op jit(solution)/shard_map/ppermute | solution.py:15
  149.8 0.7 copy-start.12
  151.5 19.0 %collective-permute-start.9 = (bf16[512,512]{1,0:T(8,128)(2,1)}, bf16[512,512]{1,0:T(8,128)(2,1)}, u32[]{:S(2)}, u32[]{:S(2)}) collective-permute-start(bf16[512,512]{1,0:T(8,128)(2,1)} %convolution_convert_fusion), channel_id=1, source_target_pairs={{0,1},{1,0},{2,3},{3,2},{4,5},{5,4},{6,7},{7,6},{8,9},{9,8},{10,11... | collective-permute-start | bytes 1572872 | tf_op jit(solution)/shard_map/ppermute | solution.py:20
  172.0 1.0 copy-start.3
  173.7 16.0 %collective-permute-start.10 = (bf16[256,512]{1,0:T(8,128)(2,1)}, bf16[256,512]{1,0:T(8,128)(2,1)}, u32[]{:S(2)}, u32[]{:S(2)}) collective-permute-start(bf16[256,512]{1,0:T(8,128)(2,1)} %select_convert_fusion), channel_id=1, source_target_pairs={{0,2},{1,3},{2,0},{3,1},{4,6},{5,7},{6,4},{7,5},{8,10},{9,11},{10,... | collective-permute-start | bytes 786440 | tf_op jit(solution)/shard_map/ppermute | solution.py:20
  191.2 4.4 %collective-permute-start.11 = (f32[128,512]{1,0:T(8,128)S(1)}, f32[128,512]{1,0:T(8,128)S(1)}, u32[]{:S(2)}, u32[]{:S(2)}) collective-permute-start(f32[128,512]{1,0:T(8,128)S(1)} %slice_select_fusion), channel_id=1, source_target_pairs={{0,4},{4,0},{8,12},{12,8},{16,20},{20,16},{24,28},{28,24},{32,36},... | collective-permute-start | bytes 786440 | tf_op jit(solution)/shard_map/ppermute | solution.py:20
  195.7 44.9 %copy-start.5 = (bf16[4,128,640]{1,2,0:T(8,128)(2,1)S(1)}, bf16[4,128,640]{1,2,0:T(8,128)(2,1)}, u32[]{:S(2)}) copy-start(bf16[4,128,640]{1,2,0:T(8,128)(2,1)} %copy-done.4) | copy-start | bytes 1966084
  195.7 11.3 %collective-permute-start.12 = (f32[128,512]{1,0:T(8,128)S(1)}, f32[128,512]{1,0:T(8,128)S(1)}, u32[]{:S(2)}, u32[]{:S(2)}) collective-permute-start(f32[128,512]{1,0:T(8,128)S(1)} %select_add_fusion), channel_id=1, source_target_pairs={{0,16},{4,20},{8,24},{12,28},{16,0},{20,4},{24,8},{28,12},{32,48},... | collective-permute-start | bytes 786440 | tf_op jit(solution)/shard_map/ppermute | solution.py:20
  207.1 33.9 %copy-start.9 = (bf16[4,128,640]{1,2,0:T(8,128)(2,1)S(1)}, bf16[4,128,640]{1,2,0:T(8,128)(2,1)}, u32[]{:S(2)}) copy-start(bf16[4,128,640]{1,2,0:T(8,128)(2,1)} %copy-done.8) | copy-start | bytes 1966084
  207.1 12.5 %collective-permute-start.13 = (f32[128,512]{1,0:T(8,128)S(1)}, f32[128,512]{1,0:T(8,128)S(1)}, u32[]{:S(2)}, u32[]{:S(2)}) collective-permute-start(f32[128,512]{1,0:T(8,128)S(1)} %add.105), channel_id=1, source_target_pairs={{0,64},{4,68},{8,72},{12,76},{16,80},{20,84},{24,88},{28,92},{32,9... | collective-permute-start | bytes 786440 | tf_op jit(solution)/shard_map/ppermute | solution.py:20
  219.6 18.9 %collective-permute-start.14 = (f32[128,512]{1,0:T(8,128)S(1)}, f32[128,512]{1,0:T(8,128)S(1)}, u32[]{:S(2)}, u32[]{:S(2)}) collective-permute-start(f32[128,512]{1,0:T(8,128)S(1)} %add.106), channel_id=1, source_target_pairs={{0,8},{4,12},{8,0},{12,4},{16,24},{20,28},{24,16},{28,20},{32,40},... | collective-permute-start | bytes 786440 | tf_op jit(solution)/shard_map/ppermute | solution.py:20
  238.6 16.1 %copy-start.7 = (bf16[4,128,640]{1,2,0:T(8,128)(2,1)S(1)}, bf16[4,128,640]{1,2,0:T(8,128)(2,1)}, u32[]{:S(2)}) copy-start(bf16[4,128,640]{1,2,0:T(8,128)(2,1)} %copy-done.6) | copy-start | bytes 1966084
  238.6 10.1 %collective-permute-start.15 = (f32[128,512]{1,0:T(8,128)S(1)}, f32[128,512]{1,0:T(8,128)S(1)}, u32[]{:S(2)}, u32[]{:S(2)}) collective-permute-start(f32[128,512]{1,0:T(8,128)S(1)} %add.107), channel_id=1, source_target_pairs={{0,32},{4,36},{8,40},{12,44},{16,48},{20,52},{24,56},{28,60},{32,0... | collective-permute-start | bytes 786440 | tf_op jit(solution)/shard_map/ppermute | solution.py:20
  241.0 14.1 %copy-start.11 = (bf16[4,128,640]{1,2,0:T(8,128)(2,1)S(1)}, bf16[4,128,640]{1,2,0:T(8,128)(2,1)}, u32[]{:S(2)}) copy-start(bf16[4,128,640]{1,2,0:T(8,128)(2,1)} %copy-done.10) | copy-start | bytes 1966084
  248.8 26.4 %copy-start.2 = (bf16[1024,512]{1,0:T(8,128)(2,1)S(1)}, bf16[1024,512]{1,0:T(8,128)(2,1)}, u32[]{:S(2)}) copy-start(bf16[1024,512]{1,0:T(8,128)(2,1)} %copy-done.1) | copy-start | bytes 3145732
  248.8 26.4 %copy-start.13 = (bf16[128,512]{0,1:T(8,128)(2,1)S(1)}, bf16[128,512]{0,1:T(8,128)(2,1)}, u32[]{:S(2)}) copy-start(bf16[128,512]{0,1:T(8,128)(2,1)} %copy-done.12) | copy-start | bytes 393220
  248.8 17.4 %collective-permute-start.16 = (f32[128,512]{1,0:T(8,128)S(1)}, f32[128,512]{1,0:T(8,128)S(1)}, u32[]{:S(2)}, u32[]{:S(2)}) collective-permute-start(f32[128,512]{1,0:T(8,128)S(1)} %add.108), channel_id=1, source_target_pairs={{0,128},{4,132},{8,136},{12,140},{16,144},{20,148},{24,152},{28,15... | collective-permute-start | bytes 786440 | tf_op jit(solution)/shard_map/ppermute | solution.py:20
  266.2 20.8 %collective-permute-start.17 = (f32[128,512]{1,0:T(8,128)S(1)}, f32[128,512]{1,0:T(8,128)S(1)}, u32[]{:S(2)}, u32[]{:S(2)}) collective-permute-start(f32[128,512]{1,0:T(8,128)S(1)} %add.109), channel_id=1, source_target_pairs={{0,256},{4,260},{8,264},{12,268},{16,272},{20,276},{24,280},{28,28... | collective-permute-start | bytes 786440 | tf_op jit(solution)/shard_map/ppermute | solution.py:20
  287.1 4.6 %collective-permute-start.18 = (f32[128,512]{1,0:T(8,128)S(1)}, f32[128,512]{1,0:T(8,128)S(1)}, u32[]{:S(2)}, u32[]{:S(2)}) collective-permute-start(f32[128,512]{1,0:T(8,128)S(1)} %add.110), channel_id=1, source_target_pairs={{0,4},{4,0},{8,12},{12,8},{16,20},{20,16},{24,28},{28,24},{32,36},... | collective-permute-start | bytes 786440 | tf_op jit(solution)/shard_map/ppermute | solution.py:20
Sparse Core Ops, SparseCore 0:
  10.1 66.9 all-gather.1

commit v7 on v6

--- a/solution.py
+++ b/solution.py
@@ -57,6 +57,9 @@
     upper = ((lax.axis_index(axis) >> bit) & 1) == 1
     other = xor_swap(value, axis, bit)
     return jnp.where(upper, jnp.concatenate([other, value]), jnp.concatenate([value, other]))
+
+
+NEAR_BITS = (0, 2, 4)
 
 
 def grad_sum(partial):
@@ -90,11 +93,16 @@
         current = halve_stage(current, "stream", bit, jnp.bfloat16)
     if tm_bits == 0:
         return current
-    current = halve_stage(current, "tm", 0, jnp.float32)
-    for bit in (2, 4, 1, 3, 5, 6) + tuple(range(7, tm_bits)):
-        if bit < tm_bits:
+    near = [bit for bit in NEAR_BITS if bit < tm_bits and current.shape[0] % 2 == 0]
+    near = near[: max(0, (current.shape[0]).bit_length() - 1)]
+    for bit in near:
+        current = halve_stage(current, "tm", bit, jnp.float32)
+    for bit in range(tm_bits):
+        if bit not in near:
             current = current + xor_swap(current, "tm", bit)
-    return double_stage(current, "tm", 0)
+    for bit in reversed(near):
+        current = double_stage(current, "tm", bit)
+    return current
 
 
 def contract_last(left, right):

time: 300 us -> 281 us (0.937)
  waiting for transfers between devices: 162 us -> 130 us
  starting transfers between devices: 78.5 us -> 87 us
    ppermute x11 -> x13, waiting for transfers between devices: 84.3 us -> 52.3 us  [xor_swap(): lax.ppermute(value, axis, [(source, source ^ 1 << bit) for source in rang...]
    ppermute x11 -> x13, starting transfers between devices: 52.5 us -> 61 us  [xor_swap(): lax.ppermute(value, axis, [(source, source ^ 1 << bit) for source in rang...]
  transfers between devices with their start and end apart: 20 -> 22, of which waited for: 14 -> 17; matrix products, arithmetic and copies ran while one was open for 3% -> 3% of each run, Pallas kernels for 0% -> 0%
where the time goes in v7:
time: 281 us; the launch traced here: 280 us
  waiting for transfers between devices  130 us (46%)
  starting transfers between devices  87 us (31%)
  matrix products  25.3 us (9%)
  between operations  15.6 us (6%)
  other arithmetic  14.8 us (5%)
  local copies, waits for them, and re-layouts  6.58 us (2%)
    all_gather x1, waiting for transfers between devices, per_device(): lax.all_gather(lax.dynamic_slice_in_dim(weights_local, core * half_width,...  67.4 us
    ppermute x13, starting transfers between devices, xor_swap(): lax.ppermute(value, axis, [(source, source ^ 1 << bit) for source in rang...  61 us
    ppermute x13, waiting for transfers between devices, xor_swap(): lax.ppermute(value, axis, [(source, source ^ 1 << bit) for source in rang...  52.3 us
    ppermute x8, starting transfers between devices, shifted(): lax.ppermute(value, axis, [(source, source + steps) for source in range(l...  25.9 us
    sub x4, matrix products, per_device(): terms = jnp.where(allowed, jnp.exp(masked - row_max), 0.0)  11.5 us
    ppermute x8, waiting for transfers between devices, shifted(): lax.ppermute(value, axis, [(source, source + steps) for source in range(l...  10.6 us
  transfers between devices with their start and end apart: 22, of which 17 were waited for; matrix products, arithmetic and copies ran while one was open for 3% of the time, Pallas kernels for 0%

profile of v7, /device:TPU:1, one launch (start us, length us, event | category | flops | bytes accessed | tf_op | source)
XLA Modules:
  0.0 279.6 jit_solution(9099747535011255382)
XLA Ops:
  7.3 2.4 fusion.85
  9.6 67.4 %all-gather.2.cloned.1.call-done = bf16[1024,1280]{1,0:T(8,128)(2,1)} async-done(((bf16[256,1280]{1,0:T(8,128)(2,1)}), bf16[1024,1280]{1,0:T(8,128)(2,1)}) %all-gather.2.cloned.1.call-update) | async-done | bytes 2621456 | tf_op jit(solution)/shard_map/all_gather | solution.py:137
  77.1 2.8 %collective-permute-start = (bf16[1024,1280]{1,0:T(8,128)(2,1)}, bf16[1024,1280]{1,0:T(8,128)(2,1)}, u32[]{:S(2)}, u32[]{:S(2)}) collective-permute-start(bf16[1024,1280]{1,0:T(8,128)(2,1)} %all-gather.2.cloned.1.call-done), channel_id=1, source_target_pairs={{0,4},{4,0},{8,12},{12,8},{16,20},{20,16},{24,28},{28,24},{32,36},... | collective-permute-start | bytes 7864328 | tf_op jit(solution)/shard_map/ppermute | solution.py:20
  80.6 0.8 copy.104
  81.5 1.0 fusion.89
  82.4 2.3 collective-permute-done
  84.8 2.9 %broadcast_select_fusion.1 = (bf16[1024,1280]{1,0:T(8,128)(2,1)S(1)}, bf16[1024,1280]{1,0:T(8,128)(2,1)S(1)}) fusion(bf16[1024,1280]{1,0:T(8,128)(2,1)} %all-gather.2.cloned.1.call-done, bf16[1024,1280]{1,0:T(8,128)(2,1)} %collective-permute-done, pred[]{:T(512)S(6)} %eq.24), kind=kLoop, calls=%fused_computation.5 | loop fusion | flops 2621440 | bytes 10485761 | tf_op jit(solution)/shard_map/jit(_where)/select_n | solution.py:145
  88.1 6.3 %collective-permute-start.4 = (bf16[128,512]{1,0:T(8,128)(2,1)S(1)}, bf16[128,512]{1,0:T(8,128)(2,1)S(1)}, u32[]{:S(2)}, u32[]{:S(2)}) collective-permute-start(bf16[128,512]{1,0:T(8,128)(2,1)S(1)} %fusion.75), channel_id=1, source_target_pairs={{0,4},{4,8},{8,12},{12,16},{16,20},{20,24},{24,28},{28,32},{32,36}... | collective-permute-start | bytes 393224 | tf_op jit(solution)/shard_map/ppermute | solution.py:15
  94.3 4.0 %collective-permute-start.3 = (bf16[128,512]{1,0:T(8,128)(2,1)S(1)}, bf16[128,512]{1,0:T(8,128)(2,1)S(1)}, u32[]{:S(2)}, u32[]{:S(2)}) collective-permute-start(bf16[128,512]{1,0:T(8,128)(2,1)S(1)} %fusion.75), channel_id=1, source_target_pairs={{0,8},{4,12},{8,16},{12,20},{16,24},{20,28},{24,32},{28,36},{32,40... | collective-permute-start | bytes 393224 | tf_op jit(solution)/shard_map/ppermute | solution.py:15
  98.4 1.4 collective-permute-start.2
  99.8 3.6 %collective-permute-start.1 = (bf16[128,512]{1,0:T(8,128)(2,1)S(1)}, bf16[128,512]{1,0:T(8,128)(2,1)S(1)}, u32[]{:S(2)}, u32[]{:S(2)}) collective-permute-start(bf16[128,512]{1,0:T(8,128)(2,1)S(1)} %fusion.75), channel_id=1, source_target_pairs={{0,16},{4,20},{8,24},{12,28},{16,32},{20,36},{24,40},{28,44},{32,4... | collective-permute-start | bytes 393224 | tf_op jit(solution)/shard_map/ppermute | solution.py:15
  103.4 0.8 fusion.64
  104.2 0.7 fusion.61
  104.9 0.7 fusion.121
  105.6 0.7 fusion.120
  106.5 2.9 %fusion.122 = (f32[4,128]{1,0:T(4,128)S(1)}, f32[4,128,640]{1,2,0:T(8,128)}) fusion(bf16[128,4,64]{0,2,1:T(8,128)(2,1)} %bitcast.300, pred[128,640]{0,1:T(8,128)(4,1)} %fusion.89, bf16[640,512]{1,0:T(8,128)(2,1)S(1)} %constant_dynamic-update-slice_fusion), kind=kOutput, calls=%fused_computation.184 | convolution fusion | flops 43582080 | bytes 1705984 | tf_op jit(solution)/shard_map/sub | solution.py:195
  109.4 2.6 fusion.124
  112.1 2.7 fusion.123
  114.8 3.2 %fusion.125 = (f32[4,128]{1,0:T(4,128)}, f32[4,128,640]{1,2,0:T(8,128)}) fusion(bf16[128,4,64]{0,2,1:T(8,128)(2,1)} %bitcast.306, pred[128,640]{0,1:T(8,128)(4,1)} %fusion.89, bf16[640,512]{1,0:T(8,128)(2,1)S(1)} %constant_dynamic-update-slice_fusion), kind=kOutput, calls=%fused_computation.187 | convolution fusion | flops 43582080 | bytes 1705984 | tf_op jit(solution)/shard_map/sub | solution.py:195
  118.0 0.7 broadcast_select_fusion.4
  118.7 1.4 divide_convert_fusion.3
  122.6 0.6 copy-done.17
  128.6 6.7 %collective-permute-start.5 = (bf16[128,512]{0,1:T(8,128)(2,1)S(1)}, bf16[128,512]{0,1:T(8,128)(2,1)S(1)}, u32[]{:S(2)}, u32[]{:S(2)}) collective-permute-start(bf16[128,512]{0,1:T(8,128)(2,1)S(1)} %get-tuple-element.4), channel_id=1, source_target_pairs={{4,0},{8,4},{12,8},{16,12},{20,16},{24,20},{28,24},{32,28},{36,32}... | collective-permute-start | bytes 393224 | tf_op jit(solution)/shard_map/ppermute | solution.py:15
  135.4 1.3 collective-permute-start.8
  136.7 1.3 collective-permute-start.7
  138.0 1.3 collective-permute-start.6
  139.8 1.5 collective-permute-done.8
  141.4 3.9 %collective-permute-done.7 = bf16[128,512]{0,1:T(8,128)(2,1)S(1)} collective-permute-done((bf16[128,512]{0,1:T(8,128)(2,1)S(1)}, bf16[128,512]{0,1:T(8,128)(2,1)S(1)}, u32[]{:S(2)}, u32[]{:S(2)}) %collective-permute-start.7) | collective-permute-done | bytes 131104 | tf_op jit(solution)/shard_map/ppermute | solution.py:15
  145.2 4.7 %collective-permute-done.6 = bf16[128,512]{0,1:T(8,128)(2,1)S(1)} collective-permute-done((bf16[128,512]{0,1:T(8,128)(2,1)S(1)}, bf16[128,512]{0,1:T(8,128)(2,1)S(1)}, u32[]{:S(2)}, u32[]{:S(2)}) %collective-permute-start.6) | collective-permute-done | bytes 131104 | tf_op jit(solution)/shard_map/ppermute | solution.py:15
  150.0 1.1 convolution_convert_fusion
  151.1 6.7 %collective-permute-start.9 = (bf16[512,512]{1,0:T(8,128)(2,1)}, bf16[512,512]{1,0:T(8,128)(2,1)}, u32[]{:S(2)}, u32[]{:S(2)}) collective-permute-start(bf16[512,512]{1,0:T(8,128)(2,1)} %convolution_convert_fusion), channel_id=1, source_target_pairs={{0,1},{1,0},{2,3},{3,2},{4,5},{5,4},{6,7},{7,6},{8,9},{9,8},{10,11... | collective-permute-start | bytes 1572872 | tf_op jit(solution)/shard_map/ppermute | solution.py:20
  157.8 12.3 %collective-permute-done.9 = bf16[512,512]{1,0:T(8,128)(2,1)} collective-permute-done((bf16[512,512]{1,0:T(8,128)(2,1)}, bf16[512,512]{1,0:T(8,128)(2,1)}, u32[]{:S(2)}, u32[]{:S(2)}) %collective-permute-start.9) | collective-permute-done | bytes 524320 | tf_op jit(solution)/shard_map/ppermute | solution.py:20
  170.1 1.3 convolution_add_fusion
  171.5 1.0 copy-done.3
  172.5 2.1 collective-permute-start.10
  174.6 13.8 %collective-permute-done.10 = bf16[256,512]{1,0:T(8,128)(2,1)} collective-permute-done((bf16[256,512]{1,0:T(8,128)(2,1)S(1)}, bf16[256,512]{1,0:T(8,128)(2,1)}, u32[]{:S(2)}, u32[]{:S(2)}) %collective-permute-start.10) | collective-permute-done | bytes 262176 | tf_op jit(solution)/shard_map/ppermute | solution.py:20
  188.4 1.4 convert_add_fusion
  189.8 0.7 slice_select_fusion
  190.5 3.3 %collective-permute-start.11 = (f32[128,512]{1,0:T(8,128)}, f32[128,512]{1,0:T(8,128)}, u32[]{:S(2)}, u32[]{:S(2)}) collective-permute-start(f32[128,512]{1,0:T(8,128)} %slice_select_fusion), channel_id=1, source_target_pairs={{0,4},{4,0},{8,12},{12,8},{16,20},{20,16},{24,28},{28,24},{32,36},... | collective-permute-start | bytes 786440 | tf_op jit(solution)/shard_map/ppermute | solution.py:20
  193.8 1.5 collective-permute-done.11
  195.3 1.0 select_add_fusion
  196.3 0.7 copy-done.13
  197.0 0.7 slice_select_fusion.1
  197.7 4.8 %collective-permute-start.12 = (f32[64,512]{1,0:T(8,128)}, f32[64,512]{1,0:T(8,128)}, u32[]{:S(2)}, u32[]{:S(2)}) collective-permute-start(f32[64,512]{1,0:T(8,128)} %slice_select_fusion.1), channel_id=1, source_target_pairs={{0,16},{4,20},{8,24},{12,28},{16,0},{20,4},{24,8},{28,12},{32,48},... | collective-permute-start | bytes 393224 | tf_op jit(solution)/shard_map/ppermute | solution.py:20
  202.5 3.9 %collective-permute-done.12 = f32[64,512]{1,0:T(8,128)} collective-permute-done((f32[64,512]{1,0:T(8,128)}, f32[64,512]{1,0:T(8,128)}, u32[]{:S(2)}, u32[]{:S(2)}) %collective-permute-start.12) | collective-permute-done | bytes 131104 | tf_op jit(solution)/shard_map/ppermute | solution.py:20
  206.3 1.1 select_add_fusion.1
  207.4 7.0 %collective-permute-start.13 = (f32[32,512]{1,0:T(8,128)S(1)}, f32[32,512]{1,0:T(8,128)S(1)}, u32[]{:S(2)}, u32[]{:S(2)}) collective-permute-start(f32[32,512]{1,0:T(8,128)S(1)} %slice_select_fusion.2), channel_id=1, source_target_pairs={{0,64},{4,68},{8,72},{12,76},{16,80},{20,84},{24,88},{28,92},{32,9... | collective-permute-start | bytes 196616 | tf_op jit(solution)/shard_map/ppermute | solution.py:20
  214.5 1.6 collective-permute-done.13
  216.1 5.7 %collective-permute-start.14 = (f32[32,512]{1,0:T(8,128)S(1)}, f32[32,512]{1,0:T(8,128)S(1)}, u32[]{:S(2)}, u32[]{:S(2)}) collective-permute-start(f32[32,512]{1,0:T(8,128)S(1)} %select_add_fusion.2), channel_id=1, source_target_pairs={{0,8},{4,12},{8,0},{12,4},{16,24},{20,28},{24,16},{28,20},{32,40},... | collective-permute-start | bytes 196616 | tf_op jit(solution)/shard_map/ppermute | solution.py:20
  221.8 3.9 %collective-permute-done.14 = f32[32,512]{1,0:T(8,128)S(1)} collective-permute-done((f32[32,512]{1,0:T(8,128)S(1)}, f32[32,512]{1,0:T(8,128)S(1)}, u32[]{:S(2)}, u32[]{:S(2)}) %collective-permute-start.14) | collective-permute-done | bytes 65568 | tf_op jit(solution)/shard_map/ppermute | solution.py:20
  225.8 2.0 collective-permute-start.15
  227.8 1.3 convolution_convert_fusion.8
  229.1 3.2 %collective-permute-done.15 = f32[32,512]{1,0:T(8,128)S(1)} collective-permute-done((f32[32,512]{1,0:T(8,128)S(1)}, f32[32,512]{1,0:T(8,128)S(1)}, u32[]{:S(2)}, u32[]{:S(2)}) %collective-permute-start.15) | collective-permute-done | bytes 65568 | tf_op jit(solution)/shard_map/ppermute | solution.py:20
  232.3 4.8 %collective-permute-start.16 = (f32[32,512]{1,0:T(8,128)S(1)}, f32[32,512]{1,0:T(8,128)S(1)}, u32[]{:S(2)}, u32[]{:S(2)}) collective-permute-start(f32[32,512]{1,0:T(8,128)S(1)} %add.108), channel_id=1, source_target_pairs={{0,128},{4,132},{8,136},{12,140},{16,144},{20,148},{24,152},{28,15... | collective-permute-start | bytes 196616 | tf_op jit(solution)/shard_map/ppermute | solution.py:20
  237.3 1.3 collective-permute-done.16
  238.7 8.9 %collective-permute-start.17 = (f32[32,512]{1,0:T(8,128)S(1)}, f32[32,512]{1,0:T(8,128)S(1)}, u32[]{:S(2)}, u32[]{:S(2)}) collective-permute-start(f32[32,512]{1,0:T(8,128)S(1)} %add.109), channel_id=1, source_target_pairs={{0,256},{4,260},{8,264},{12,268},{16,272},{20,276},{24,280},{28,28... | collective-permute-start | bytes 196616 | tf_op jit(solution)/shard_map/ppermute | solution.py:20
  247.9 1.3 collective-permute-done.17
  249.2 1.9 collective-permute-start.18
  251.5 3.9 %collective-permute-done.18 = f32[32,512]{1,0:T(8,128)S(1)} collective-permute-done((f32[32,512]{1,0:T(8,128)S(1)}, f32[32,512]{1,0:T(8,128)S(1)}, u32[]{:S(2)}, u32[]{:S(2)}) %collective-permute-start.18) | collective-permute-done | bytes 65568 | tf_op jit(solution)/shard_map/ppermute | solution.py:20
  255.4 1.9 collective-permute-start.19
  257.8 3.4 %collective-permute-done.19 = f32[64,512]{1,0:T(8,128)S(1)} collective-permute-done((f32[64,512]{1,0:T(8,128)S(1)}, f32[64,512]{1,0:T(8,128)S(1)}, u32[]{:S(2)}, u32[]{:S(2)}) %collective-permute-start.19) | collective-permute-done | bytes 131104 | tf_op jit(solution)/shard_map/ppermute | solution.py:20
  261.2 9.2 %collective-permute-start.20 = (f32[128,512]{1,0:T(8,128)S(1)}, f32[128,512]{1,0:T(8,128)S(1)}, u32[]{:S(2)}, u32[]{:S(2)}) collective-permute-start(f32[128,512]{1,0:T(8,128)S(1)} %maximum_select_fusion.1), channel_id=1, source_target_pairs={{0,4},{4,0},{8,12},{12,8},{16,20},{20,16},{24,28},{28,24},{32,36},... | collective-permute-start | bytes 786440 | tf_op jit(solution)/shard_map/ppermute | solution.py:20
  270.4 1.5 fusion.58
  271.9 0.8 maximum_select_fusion
  (110 shorter events, 10.4 us)
Async XLA Ops:
  7.2 97.0 %copy-start = (bf16[1,128,1024]{2,1,0:T(8,128)(2,1)S(1)}, bf16[1,128,1024]{2,1,0:T(8,128)(2,1)}, u32[]{:S(2)}) copy-start(bf16[1,128,1024]{2,1,0:T(8,128)(2,1)} %param.7) | copy-start | bytes 786436
  7.2 69.9 %all-gather.2.cloned.1.call-start = ((), (), s32[]{:S(2)}) async-start(), calls=%async_computation | async-start | bytes 3276800 | tf_op jit(solution)/shard_map/all_gather | solution.py:137
  7.2 73.3 %copy-start.20 = (bf16[1,128,1024]{2,1,0:T(8,128)(2,1)S(1)}, bf16[1,128,1024]{2,1,0:T(8,128)(2,1)}, u32[]{:S(2)}) copy-start(bf16[1,128,1024]{2,1,0:T(8,128)(2,1)} %param.6) | copy-start | bytes 786436
  77.1 7.7 %collective-permute-start = (bf16[1024,1280]{1,0:T(8,128)(2,1)}, bf16[1024,1280]{1,0:T(8,128)(2,1)}, u32[]{:S(2)}, u32[]{:S(2)}) collective-permute-start(bf16[1024,1280]{1,0:T(8,128)(2,1)} %all-gather.2.cloned.1.call-done), channel_id=1, source_target_pairs={{0,4},{4,0},{8,12},{12,8},{16,20},{20,16},{24,28},{28,24},{32,36},... | collective-permute-start | bytes 7864328 | tf_op jit(solution)/shard_map/ppermute | solution.py:20
  87.7 16.5 %copy-start.1 = (bf16[1024,512]{1,0:T(8,128)(2,1)}, bf16[1024,512]{1,0:T(8,128)(2,1)S(1)}, u32[]{:S(2)}) copy-start(bf16[1024,512]{1,0:T(8,128)(2,1)S(1)} %pad_maximum_fusion) | copy-start | bytes 3145732
  88.1 18.4 %collective-permute-start.4 = (bf16[128,512]{1,0:T(8,128)(2,1)S(1)}, bf16[128,512]{1,0:T(8,128)(2,1)S(1)}, u32[]{:S(2)}, u32[]{:S(2)}) collective-permute-start(bf16[128,512]{1,0:T(8,128)(2,1)S(1)} %fusion.75), channel_id=1, source_target_pairs={{0,4},{4,8},{8,12},{12,16},{16,20},{20,24},{24,28},{28,32},{32,36}... | collective-permute-start | bytes 393224 | tf_op jit(solution)/shard_map/ppermute | solution.py:15
  94.3 12.0 %collective-permute-start.3 = (bf16[128,512]{1,0:T(8,128)(2,1)S(1)}, bf16[128,512]{1,0:T(8,128)(2,1)S(1)}, u32[]{:S(2)}, u32[]{:S(2)}) collective-permute-start(bf16[128,512]{1,0:T(8,128)(2,1)S(1)} %fusion.75), channel_id=1, source_target_pairs={{0,8},{4,12},{8,16},{12,20},{16,24},{20,28},{24,32},{28,36},{32,40... | collective-permute-start | bytes 393224 | tf_op jit(solution)/shard_map/ppermute | solution.py:15
  98.4 8.0 %collective-permute-start.2 = (bf16[128,512]{1,0:T(8,128)(2,1)S(1)}, bf16[128,512]{1,0:T(8,128)(2,1)S(1)}, u32[]{:S(2)}, u32[]{:S(2)}) collective-permute-start(bf16[128,512]{1,0:T(8,128)(2,1)S(1)} %fusion.75), channel_id=1, source_target_pairs={{0,12},{4,16},{8,20},{12,24},{16,28},{20,32},{24,36},{28,40},{32,4... | collective-permute-start | bytes 393224 | tf_op jit(solution)/shard_map/ppermute | solution.py:15
  99.8 6.6 %collective-permute-start.1 = (bf16[128,512]{1,0:T(8,128)(2,1)S(1)}, bf16[128,512]{1,0:T(8,128)(2,1)S(1)}, u32[]{:S(2)}, u32[]{:S(2)}) collective-permute-start(bf16[128,512]{1,0:T(8,128)(2,1)S(1)} %fusion.75), channel_id=1, source_target_pairs={{0,16},{4,20},{8,24},{12,28},{16,32},{20,36},{24,40},{28,44},{32,4... | collective-permute-start | bytes 393224 | tf_op jit(solution)/shard_map/ppermute | solution.py:15
  106.5 19.2 %copy-start.4 = (bf16[640,512]{1,0:T(8,128)(2,1)}, bf16[640,512]{1,0:T(8,128)(2,1)S(1)}, u32[]{:S(2)}) copy-start(bf16[640,512]{1,0:T(8,128)(2,1)S(1)} %constant_dynamic-update-slice_fusion) | copy-start | bytes 1966084
  118.0 2.1 copy-start.24
  120.1 0.8 copy-start.28
  120.4 1.4 copy-start.18
  121.0 0.8 copy-start.12
  121.0 1.0 copy-start.22
  121.9 1.3 copy-start.17
  122.6 3.9 %copy-start.10 = (bf16[4,128,640]{1,2,0:T(8,128)(2,1)}, bf16[4,128,640]{1,2,0:T(8,128)(2,1)S(1)}, u32[]{:S(2)}) copy-start(bf16[4,128,640]{1,2,0:T(8,128)(2,1)S(1)} %fusion.44) | copy-start | bytes 1966084
  122.6 1.0 copy-start.23
  123.3 1.3 copy-start.16
  124.3 1.8 copy-start.8
  124.3 0.9 copy-start.21
  124.8 1.3 copy-start.27
  125.6 0.8 copy-start.26
  125.7 1.1 copy-start.25
  126.1 1.0 copy-start.6
  128.4 10.8 %copy-start.19 = (bf16[1,128,1024]{1,2,0:T(8,128)(2,1)S(1)}, bf16[1,128,1024]{1,2,0:T(8,128)(2,1)}, u32[]{:S(2)}) copy-start(bf16[1,128,1024]{1,2,0:T(8,128)(2,1)} %copy.104) | copy-start | bytes 786436
  128.6 11.2 %collective-permute-start.5 = (bf16[128,512]{0,1:T(8,128)(2,1)S(1)}, bf16[128,512]{0,1:T(8,128)(2,1)S(1)}, u32[]{:S(2)}, u32[]{:S(2)}) collective-permute-start(bf16[128,512]{0,1:T(8,128)(2,1)S(1)} %get-tuple-element.4), channel_id=1, source_target_pairs={{4,0},{8,4},{12,8},{16,12},{20,16},{24,20},{28,24},{32,28},{36,32}... | collective-permute-start | bytes 393224 | tf_op jit(solution)/shard_map/ppermute | solution.py:15
  135.4 6.0 %collective-permute-start.8 = (bf16[128,512]{0,1:T(8,128)(2,1)S(1)}, bf16[128,512]{0,1:T(8,128)(2,1)S(1)}, u32[]{:S(2)}, u32[]{:S(2)}) collective-permute-start(bf16[128,512]{0,1:T(8,128)(2,1)S(1)} %get-tuple-element.5), channel_id=1, source_target_pairs={{16,0},{20,4},{24,8},{28,12},{32,16},{36,20},{40,24},{44,28},{48,3... | collective-permute-start | bytes 393224 | tf_op jit(solution)/shard_map/ppermute | solution.py:15
  136.7 8.6 %collective-permute-start.7 = (bf16[128,512]{0,1:T(8,128)(2,1)S(1)}, bf16[128,512]{0,1:T(8,128)(2,1)S(1)}, u32[]{:S(2)}, u32[]{:S(2)}) collective-permute-start(bf16[128,512]{0,1:T(8,128)(2,1)S(1)} %get-tuple-element.6), channel_id=1, source_target_pairs={{12,0},{16,4},{20,8},{24,12},{28,16},{32,20},{36,24},{40,28},{44,3... | collective-permute-start | bytes 393224 | tf_op jit(solution)/shard_map/ppermute | solution.py:15
  138.0 12.0 %collective-permute-start.6 = (bf16[128,512]{0,1:T(8,128)(2,1)S(1)}, bf16[128,512]{0,1:T(8,128)(2,1)S(1)}, u32[]{:S(2)}, u32[]{:S(2)}) collective-permute-start(bf16[128,512]{0,1:T(8,128)(2,1)S(1)} %get-tuple-element.7), channel_id=1, source_target_pairs={{8,0},{12,4},{16,8},{20,12},{24,16},{28,20},{32,24},{36,28},{40,32... | collective-permute-start | bytes 393224 | tf_op jit(solution)/shard_map/ppermute | solution.py:15
  150.0 21.4 %copy-start.14 = (bf16[128,512]{0,1:T(8,128)(2,1)}, bf16[128,512]{0,1:T(8,128)(2,1)S(1)}, u32[]{:S(2)}) copy-start(bf16[128,512]{0,1:T(8,128)(2,1)S(1)} %fusion.93) | copy-start | bytes 393220
  151.1 19.0 %collective-permute-start.9 = (bf16[512,512]{1,0:T(8,128)(2,1)}, bf16[512,512]{1,0:T(8,128)(2,1)}, u32[]{:S(2)}, u32[]{:S(2)}) collective-permute-start(bf16[512,512]{1,0:T(8,128)(2,1)} %convolution_convert_fusion), channel_id=1, source_target_pairs={{0,1},{1,0},{2,3},{3,2},{4,5},{5,4},{6,7},{7,6},{8,9},{9,8},{10,11... | collective-permute-start | bytes 1572872 | tf_op jit(solution)/shard_map/ppermute | solution.py:20
  171.5 1.0 copy-start.3
  172.5 15.8 %collective-permute-start.10 = (bf16[256,512]{1,0:T(8,128)(2,1)S(1)}, bf16[256,512]{1,0:T(8,128)(2,1)}, u32[]{:S(2)}, u32[]{:S(2)}) collective-permute-start(bf16[256,512]{1,0:T(8,128)(2,1)S(1)} %select_convert_fusion), channel_id=1, source_target_pairs={{0,2},{1,3},{2,0},{3,1},{4,6},{5,7},{6,4},{7,5},{8,10},{9,11},{10,... | collective-permute-start | bytes 786440 | tf_op jit(solution)/shard_map/ppermute | solution.py:20
  190.5 4.8 %collective-permute-start.11 = (f32[128,512]{1,0:T(8,128)}, f32[128,512]{1,0:T(8,128)}, u32[]{:S(2)}, u32[]{:S(2)}) collective-permute-start(f32[128,512]{1,0:T(8,128)} %slice_select_fusion), channel_id=1, source_target_pairs={{0,4},{4,0},{8,12},{12,8},{16,20},{20,16},{24,28},{28,24},{32,36},... | collective-permute-start | bytes 786440 | tf_op jit(solution)/shard_map/ppermute | solution.py:20
  196.3 0.7 copy-start.13
  197.0 30.7 %copy-start.5 = (bf16[640,512]{1,0:T(8,128)(2,1)S(1)}, bf16[640,512]{1,0:T(8,128)(2,1)}, u32[]{:S(2)}) copy-start(bf16[640,512]{1,0:T(8,128)(2,1)} %copy-done.4) | copy-start | bytes 1966084
  197.7 8.6 %collective-permute-start.12 = (f32[64,512]{1,0:T(8,128)}, f32[64,512]{1,0:T(8,128)}, u32[]{:S(2)}, u32[]{:S(2)}) collective-permute-start(f32[64,512]{1,0:T(8,128)} %slice_select_fusion.1), channel_id=1, source_target_pairs={{0,16},{4,20},{8,24},{12,28},{16,0},{20,4},{24,8},{28,12},{32,48},... | collective-permute-start | bytes 393224 | tf_op jit(solution)/shard_map/ppermute | solution.py:20
  202.5 34.6 %copy-start.11 = (bf16[4,128,640]{1,2,0:T(8,128)(2,1)S(1)}, bf16[4,128,640]{1,2,0:T(8,128)(2,1)}, u32[]{:S(2)}) copy-start(bf16[4,128,640]{1,2,0:T(8,128)(2,1)} %copy-done.10) | copy-start | bytes 1966084
  207.4 40.2 %copy-start.9 = (bf16[4,128,640]{1,2,0:T(8,128)(2,1)S(1)}, bf16[4,128,640]{1,2,0:T(8,128)(2,1)}, u32[]{:S(2)}) copy-start(bf16[4,128,640]{1,2,0:T(8,128)(2,1)} %copy-done.8) | copy-start | bytes 1966084
  207.4 8.7 %collective-permute-start.13 = (f32[32,512]{1,0:T(8,128)S(1)}, f32[32,512]{1,0:T(8,128)S(1)}, u32[]{:S(2)}, u32[]{:S(2)}) collective-permute-start(f32[32,512]{1,0:T(8,128)S(1)} %slice_select_fusion.2), channel_id=1, source_target_pairs={{0,64},{4,68},{8,72},{12,76},{16,80},{20,84},{24,88},{28,92},{32,9... | collective-permute-start | bytes 196616 | tf_op jit(solution)/shard_map/ppermute | solution.py:20
  216.1 9.6 %collective-permute-start.14 = (f32[32,512]{1,0:T(8,128)S(1)}, f32[32,512]{1,0:T(8,128)S(1)}, u32[]{:S(2)}, u32[]{:S(2)}) collective-permute-start(f32[32,512]{1,0:T(8,128)S(1)} %select_add_fusion.2), channel_id=1, source_target_pairs={{0,8},{4,12},{8,0},{12,4},{16,24},{20,28},{24,16},{28,20},{32,40},... | collective-permute-start | bytes 196616 | tf_op jit(solution)/shard_map/ppermute | solution.py:20
  225.8 6.5 %collective-permute-start.15 = (f32[32,512]{1,0:T(8,128)S(1)}, f32[32,512]{1,0:T(8,128)S(1)}, u32[]{:S(2)}, u32[]{:S(2)}) collective-permute-start(f32[32,512]{1,0:T(8,128)S(1)} %add.107), channel_id=1, source_target_pairs={{0,32},{4,36},{8,40},{12,44},{16,48},{20,52},{24,56},{28,60},{32,0... | collective-permute-start | bytes 196616 | tf_op jit(solution)/shard_map/ppermute | solution.py:20
  229.1 22.1 %copy-start.7 = (bf16[4,128,640]{1,2,0:T(8,128)(2,1)S(1)}, bf16[4,128,640]{1,2,0:T(8,128)(2,1)}, u32[]{:S(2)}) copy-start(bf16[4,128,640]{1,2,0:T(8,128)(2,1)} %copy-done.6) | copy-start | bytes 1966084
  232.3 6.4 %collective-permute-start.16 = (f32[32,512]{1,0:T(8,128)S(1)}, f32[32,512]{1,0:T(8,128)S(1)}, u32[]{:S(2)}, u32[]{:S(2)}) collective-permute-start(f32[32,512]{1,0:T(8,128)S(1)} %add.108), channel_id=1, source_target_pairs={{0,128},{4,132},{8,136},{12,140},{16,144},{20,148},{24,152},{28,15... | collective-permute-start | bytes 196616 | tf_op jit(solution)/shard_map/ppermute | solution.py:20
  237.3 20.0 %copy-start.2 = (bf16[1024,512]{1,0:T(8,128)(2,1)S(1)}, bf16[1024,512]{1,0:T(8,128)(2,1)}, u32[]{:S(2)}) copy-start(bf16[1024,512]{1,0:T(8,128)(2,1)} %copy-done.1) | copy-start | bytes 3145732
  237.3 20.0 %copy-start.15 = (bf16[128,512]{0,1:T(8,128)(2,1)S(1)}, bf16[128,512]{0,1:T(8,128)(2,1)}, u32[]{:S(2)}) copy-start(bf16[128,512]{0,1:T(8,128)(2,1)} %copy-done.14) | copy-start | bytes 393220
  238.7 10.5 %collective-permute-start.17 = (f32[32,512]{1,0:T(8,128)S(1)}, f32[32,512]{1,0:T(8,128)S(1)}, u32[]{:S(2)}, u32[]{:S(2)}) collective-permute-start(f32[32,512]{1,0:T(8,128)S(1)} %add.109), channel_id=1, source_target_pairs={{0,256},{4,260},{8,264},{12,268},{16,272},{20,276},{24,280},{28,28... | collective-permute-start | bytes 196616 | tf_op jit(solution)/shard_map/ppermute | solution.py:20
  249.2 6.1 %collective-permute-start.18 = (f32[32,512]{1,0:T(8,128)S(1)}, f32[32,512]{1,0:T(8,128)S(1)}, u32[]{:S(2)}, u32[]{:S(2)}) collective-permute-start(f32[32,512]{1,0:T(8,128)S(1)} %add.110), channel_id=1, source_target_pairs={{0,64},{4,68},{8,72},{12,76},{16,80},{20,84},{24,88},{28,92},{32,9... | collective-permute-start | bytes 196616 | tf_op jit(solution)/shard_map/ppermute | solution.py:20
  255.4 5.8 %collective-permute-start.19 = (f32[64,512]{1,0:T(8,128)S(1)}, f32[64,512]{1,0:T(8,128)S(1)}, u32[]{:S(2)}, u32[]{:S(2)}) collective-permute-start(f32[64,512]{1,0:T(8,128)S(1)} %maximum_select_fusion.2), channel_id=1, source_target_pairs={{0,16},{4,20},{8,24},{12,28},{16,0},{20,4},{24,8},{28,12},{32,48},... | collective-permute-start | bytes 393224 | tf_op jit(solution)/shard_map/ppermute | solution.py:20
  261.2 10.7 %collective-permute-start.20 = (f32[128,512]{1,0:T(8,128)S(1)}, f32[128,512]{1,0:T(8,128)S(1)}, u32[]{:S(2)}, u32[]{:S(2)}) collective-permute-start(f32[128,512]{1,0:T(8,128)S(1)} %maximum_select_fusion.1), channel_id=1, source_target_pairs={{0,4},{4,0},{8,12},{12,8},{16,20},{20,16},{24,28},{28,24},{32,36},... | collective-permute-start | bytes 786440 | tf_op jit(solution)/shard_map/ppermute | solution.py:20
Sparse Core Ops, SparseCore 0:
  10.1 66.9 all-gather.1

commit v8 on v7

--- a/solution.py
+++ b/solution.py
@@ -59,7 +59,7 @@
     return jnp.where(upper, jnp.concatenate([other, value]), jnp.concatenate([value, other]))
 
 
-NEAR_BITS = (0, 2, 4)
+NEAR_BITS = (2, 4)
 
 
 def grad_sum(partial):
@@ -67,42 +67,54 @@
     tm_count = lax.axis_size("tm")
     stream_bits = stream_count.bit_length() - 1
     tm_bits = tm_count.bit_length() - 1
+    rows, grads = partial
+    tokens, features = rows.shape
     if (
         stream_count != 1 << stream_bits
         or tm_count != 1 << tm_bits
-        or partial[0].shape[1] % (2 * stream_count)
+        or stream_bits == 0
+        or tm_bits == 0
+        or features % (2 * stream_count)
+        or grads.shape[1] % 256
     ):
         shard = lax.psum_scatter(
-            contract_first(*partial).astype(jnp.bfloat16), "stream", scatter_dimension=0, tiled=True
+            contract_first(rows, grads).astype(jnp.bfloat16), "stream", scatter_dimension=0, tiled=True
         ).astype(jnp.float32)
         return lax.psum(shard, "tm")
     stream_index = lax.axis_index("stream")
-    rows, grads = partial
-    tokens, features = rows.shape
-    if stream_bits == 0:
-        current = contract_first(rows, grads)
-    else:
-        paired = rows.reshape(tokens, stream_count // 2, 2, features // stream_count)
-        even = paired[:, :, 0].reshape(tokens, features // 2)
-        odd = paired[:, :, 1].reshape(tokens, features // 2)
-        upper = (stream_index & 1) == 1
-        keep = contract_first(jnp.where(upper, odd, even), grads)
-        send = contract_first(jnp.where(upper, even, odd), grads).astype(jnp.bfloat16)
-        current = keep + xor_swap(send, "stream", 0).astype(jnp.float32)
+    core = lax.axis_index("tm") % 2
+    half_cols = grads.shape[1] // 2
+    paired = rows.reshape(tokens, stream_count // 2, 2, features // stream_count)
+    even = paired[:, :, 0].reshape(tokens, features // 2)
+    odd = paired[:, :, 1].reshape(tokens, features // 2)
+    upper = (stream_index & 1) == 1
+    ordered = jnp.concatenate([jnp.where(upper, odd, even), jnp.where(upper, even, odd)], axis=1)
+    mine_cols = lax.dynamic_slice_in_dim(grads, core * half_cols, half_cols, 1)
+    other_cols = lax.dynamic_slice_in_dim(grads, (1 - core) * half_cols, half_cols, 1)
+    current = contract_first(ordered, mine_cols) + xor_swap(
+        contract_first(ordered, other_cols), "tm", 0
+    )
+    half_rows = features // 2
+    current = current[:half_rows] + xor_swap(
+        current[half_rows:].astype(jnp.bfloat16), "stream", 0
+    ).astype(jnp.float32)
     for bit in reversed(range(1, stream_bits)):
         current = halve_stage(current, "stream", bit, jnp.bfloat16)
-    if tm_bits == 0:
-        return current
-    near = [bit for bit in NEAR_BITS if bit < tm_bits and current.shape[0] % 2 == 0]
-    near = near[: max(0, (current.shape[0]).bit_length() - 1)]
+    near = [bit for bit in NEAR_BITS if bit < tm_bits]
+    near = near[: max(0, current.shape[0].bit_length() - 1)]
     for bit in near:
         current = halve_stage(current, "tm", bit, jnp.float32)
-    for bit in range(tm_bits):
+    for bit in range(1, tm_bits):
         if bit not in near:
             current = current + xor_swap(current, "tm", bit)
     for bit in reversed(near):
         current = double_stage(current, "tm", bit)
-    return current
+    other = xor_swap(current, "tm", 0)
+    return jnp.where(
+        core == 1,
+        jnp.concatenate([other, current], axis=1),
+        jnp.concatenate([current, other], axis=1),
+    )
 
 
 def contract_last(left, right):

time: 281 us -> 272 us (0.968)
  waiting for transfers between devices: 130 us -> 111 us
  starting transfers between devices: 87 us -> 95.3 us
    ppermute x13, waiting for transfers between devices: 52.3 us -> 33.2 us  [xor_swap(): lax.ppermute(value, axis, [(source, source ^ 1 << bit) for source in rang...]
    ppermute x13, starting transfers between devices: 61 us -> 69.3 us  [xor_swap(): lax.ppermute(value, axis, [(source, source ^ 1 << bit) for source in rang...]
  transfers between devices with their start and end apart: 22 -> 22, of which waited for: 17 -> 17; matrix products, arithmetic and copies ran while one was open for 3% -> 4% of each run, Pallas kernels for 0% -> 0%
where the time goes in v8:
time: 272 us; the launch traced here: 271 us
  waiting for transfers between devices  111 us (41%)
  starting transfers between devices  95.3 us (35%)
  matrix products  26.8 us (10%)
  between operations  15.6 us (6%)
  other arithmetic  15 us (6%)
  local copies, waits for them, and re-layouts  6.57 us (2%)
    ppermute x13, starting transfers between devices, xor_swap(): lax.ppermute(value, axis, [(source, source ^ 1 << bit) for source in rang...  69.3 us
    all_gather x1, waiting for transfers between devices, per_device(): lax.all_gather(lax.dynamic_slice_in_dim(weights_local, core * half_width,...  67.4 us
    ppermute x13, waiting for transfers between devices, xor_swap(): lax.ppermute(value, axis, [(source, source ^ 1 << bit) for source in rang...  33.2 us
    ppermute x8, starting transfers between devices, shifted(): lax.ppermute(value, axis, [(source, source + steps) for source in range(l...  25.9 us
    sub x4, matrix products, per_device(): terms = jnp.where(allowed, jnp.exp(masked - row_max), 0.0)  11.5 us
    ppermute x8, waiting for transfers between devices, shifted(): lax.ppermute(value, axis, [(source, source + steps) for source in range(l...  10.6 us
  transfers between devices with their start and end apart: 22, of which 17 were waited for; matrix products, arithmetic and copies ran while one was open for 4% of the time, Pallas kernels for 0%

profile of v8, /device:TPU:1, one launch (start us, length us, event | category | flops | bytes accessed | tf_op | source)
XLA Modules:
  0.0 270.6 jit_solution(17298758502524146166)
XLA Ops:
  7.3 2.4 fusion.85
  9.6 67.4 %all-gather.2.cloned.1.call-done = bf16[1024,1280]{1,0:T(8,128)(2,1)} async-done(((bf16[256,1280]{1,0:T(8,128)(2,1)}), bf16[1024,1280]{1,0:T(8,128)(2,1)}) %all-gather.2.cloned.1.call-update) | async-done | bytes 2621456 | tf_op jit(solution)/shard_map/all_gather | solution.py:149
  77.1 2.8 %collective-permute-start = (bf16[1024,1280]{1,0:T(8,128)(2,1)}, bf16[1024,1280]{1,0:T(8,128)(2,1)}, u32[]{:S(2)}, u32[]{:S(2)}) collective-permute-start(bf16[1024,1280]{1,0:T(8,128)(2,1)} %all-gather.2.cloned.1.call-done), channel_id=1, source_target_pairs={{0,4},{4,0},{8,12},{12,8},{16,20},{20,16},{24,28},{28,24},{32,36},... | collective-permute-start | bytes 7864328 | tf_op jit(solution)/shard_map/ppermute | solution.py:20
  80.6 0.8 copy.104
  81.5 1.0 fusion.89
  82.4 2.3 collective-permute-done
  84.8 2.9 %broadcast_select_fusion.1 = (bf16[1024,1280]{1,0:T(8,128)(2,1)S(1)}, bf16[1024,1280]{1,0:T(8,128)(2,1)S(1)}) fusion(bf16[1024,1280]{1,0:T(8,128)(2,1)} %all-gather.2.cloned.1.call-done, bf16[1024,1280]{1,0:T(8,128)(2,1)} %collective-permute-done, pred[]{:T(512)S(6)} %eq.24), kind=kLoop, calls=%fused_computation.5 | loop fusion | flops 2621440 | bytes 10485761 | tf_op jit(solution)/shard_map/jit(_where)/select_n | solution.py:157
  88.1 6.3 %collective-permute-start.4 = (bf16[128,512]{1,0:T(8,128)(2,1)S(1)}, bf16[128,512]{1,0:T(8,128)(2,1)S(1)}, u32[]{:S(2)}, u32[]{:S(2)}) collective-permute-start(bf16[128,512]{1,0:T(8,128)(2,1)S(1)} %fusion.75), channel_id=1, source_target_pairs={{0,4},{4,8},{8,12},{12,16},{16,20},{20,24},{24,28},{28,32},{32,36}... | collective-permute-start | bytes 393224 | tf_op jit(solution)/shard_map/ppermute | solution.py:15
  94.3 4.0 %collective-permute-start.3 = (bf16[128,512]{1,0:T(8,128)(2,1)S(1)}, bf16[128,512]{1,0:T(8,128)(2,1)S(1)}, u32[]{:S(2)}, u32[]{:S(2)}) collective-permute-start(bf16[128,512]{1,0:T(8,128)(2,1)S(1)} %fusion.75), channel_id=1, source_target_pairs={{0,8},{4,12},{8,16},{12,20},{16,24},{20,28},{24,32},{28,36},{32,40... | collective-permute-start | bytes 393224 | tf_op jit(solution)/shard_map/ppermute | solution.py:15
  98.4 1.4 collective-permute-start.2
  99.8 3.6 %collective-permute-start.1 = (bf16[128,512]{1,0:T(8,128)(2,1)S(1)}, bf16[128,512]{1,0:T(8,128)(2,1)S(1)}, u32[]{:S(2)}, u32[]{:S(2)}) collective-permute-start(bf16[128,512]{1,0:T(8,128)(2,1)S(1)} %fusion.75), channel_id=1, source_target_pairs={{0,16},{4,20},{8,24},{12,28},{16,32},{20,36},{24,40},{28,44},{32,4... | collective-permute-start | bytes 393224 | tf_op jit(solution)/shard_map/ppermute | solution.py:15
  103.4 0.8 fusion.64
  104.2 0.7 fusion.61
  104.9 0.7 fusion.128
  105.6 0.7 fusion.127
  106.4 2.9 %fusion.129 = (f32[4,128]{1,0:T(4,128)S(1)}, f32[4,128,640]{1,2,0:T(8,128)}) fusion(bf16[128,4,64]{0,2,1:T(8,128)(2,1)} %bitcast.298, pred[128,640]{0,1:T(8,128)(4,1)} %fusion.89, bf16[640,512]{1,0:T(8,128)(2,1)S(1)} %constant_dynamic-update-slice_fusion), kind=kOutput, calls=%fused_computation.191 | convolution fusion | flops 43582080 | bytes 1705984 | tf_op jit(solution)/shard_map/sub | solution.py:207
  109.4 2.7 fusion.131
  112.0 2.7 fusion.130
  114.7 3.2 %fusion.132 = (f32[4,128]{1,0:T(4,128)}, f32[4,128,640]{1,2,0:T(8,128)}) fusion(bf16[128,4,64]{0,2,1:T(8,128)(2,1)} %bitcast.304, pred[128,640]{0,1:T(8,128)(4,1)} %fusion.89, bf16[640,512]{1,0:T(8,128)(2,1)S(1)} %constant_dynamic-update-slice_fusion), kind=kOutput, calls=%fused_computation.194 | convolution fusion | flops 43582080 | bytes 1705984 | tf_op jit(solution)/shard_map/sub | solution.py:207
  118.0 0.7 broadcast_select_fusion.4
  118.7 1.4 divide_convert_fusion.3
  122.6 0.6 copy-done.14
  128.6 6.7 %collective-permute-start.5 = (bf16[128,512]{0,1:T(8,128)(2,1)S(1)}, bf16[128,512]{0,1:T(8,128)(2,1)S(1)}, u32[]{:S(2)}, u32[]{:S(2)}) collective-permute-start(bf16[128,512]{0,1:T(8,128)(2,1)S(1)} %get-tuple-element.4), channel_id=1, source_target_pairs={{4,0},{8,4},{12,8},{16,12},{20,16},{24,20},{28,24},{32,28},{36,32}... | collective-permute-start | bytes 393224 | tf_op jit(solution)/shard_map/ppermute | solution.py:15
  135.4 1.3 collective-permute-start.8
  136.7 1.3 collective-permute-start.7
  138.0 1.3 collective-permute-start.6
  139.8 1.6 collective-permute-done.8
  141.4 3.9 %collective-permute-done.7 = bf16[128,512]{0,1:T(8,128)(2,1)S(1)} collective-permute-done((bf16[128,512]{0,1:T(8,128)(2,1)S(1)}, bf16[128,512]{0,1:T(8,128)(2,1)S(1)}, u32[]{:S(2)}, u32[]{:S(2)}) %collective-permute-start.7) | collective-permute-done | bytes 131104 | tf_op jit(solution)/shard_map/ppermute | solution.py:15
  145.3 4.7 %collective-permute-done.6 = bf16[128,512]{0,1:T(8,128)(2,1)S(1)} collective-permute-done((bf16[128,512]{0,1:T(8,128)(2,1)S(1)}, bf16[128,512]{0,1:T(8,128)(2,1)S(1)}, u32[]{:S(2)}, u32[]{:S(2)}) %collective-permute-start.6) | collective-permute-done | bytes 131104 | tf_op jit(solution)/shard_map/ppermute | solution.py:15
  150.0 1.3 fusion.104
  151.4 2.4 collective-permute-start.9
  153.8 2.6 collective-permute-done.9
  156.4 1.5 convolution_add_fusion
  157.9 1.0 copy-done.3
  158.9 6.6 %collective-permute-start.10 = (bf16[512,256]{1,0:T(8,128)(2,1)S(1)}, bf16[512,256]{1,0:T(8,128)(2,1)}, u32[]{:S(2)}, u32[]{:S(2)}) collective-permute-start(bf16[512,256]{1,0:T(8,128)(2,1)S(1)} %slice.269), channel_id=1, source_target_pairs={{0,1},{1,0},{2,3},{3,2},{4,5},{5,4},{6,7},{7,6},{8,9},{9,8},{10,11... | collective-permute-start | bytes 786440 | tf_op jit(solution)/shard_map/ppermute | solution.py:20
  165.6 6.5 %collective-permute-done.10 = bf16[512,256]{1,0:T(8,128)(2,1)} collective-permute-done((bf16[512,256]{1,0:T(8,128)(2,1)S(1)}, bf16[512,256]{1,0:T(8,128)(2,1)}, u32[]{:S(2)}, u32[]{:S(2)}) %collective-permute-start.10) | collective-permute-done | bytes 262176 | tf_op jit(solution)/shard_map/ppermute | solution.py:20
  172.0 1.2 slice_add_fusion
  173.2 0.7 select_convert_fusion
  173.9 2.6 collective-permute-start.11
  176.5 7.7 %collective-permute-done.11 = bf16[256,256]{1,0:T(8,128)(2,1)S(1)} collective-permute-done((bf16[256,256]{1,0:T(8,128)(2,1)}, bf16[256,256]{1,0:T(8,128)(2,1)S(1)}, u32[]{:S(2)}, u32[]{:S(2)}) %collective-permute-start.11) | collective-permute-done | bytes 131104 | tf_op jit(solution)/shard_map/ppermute | solution.py:20
  184.3 0.7 copy-done.12
  184.9 0.7 slice_select_fusion
  185.6 5.8 %collective-permute-start.12 = (f32[128,256]{1,0:T(8,128)}, f32[128,256]{1,0:T(8,128)}, u32[]{:S(2)}, u32[]{:S(2)}) collective-permute-start(f32[128,256]{1,0:T(8,128)} %slice_select_fusion), channel_id=1, source_target_pairs={{0,16},{4,20},{8,24},{12,28},{16,0},{20,4},{24,8},{28,12},{32,48},... | collective-permute-start | bytes 393224 | tf_op jit(solution)/shard_map/ppermute | solution.py:20
  191.5 3.7 %collective-permute-done.12 = f32[128,256]{1,0:T(8,128)} collective-permute-done((f32[128,256]{1,0:T(8,128)}, f32[128,256]{1,0:T(8,128)}, u32[]{:S(2)}, u32[]{:S(2)}) %collective-permute-start.12) | collective-permute-done | bytes 131104 | tf_op jit(solution)/shard_map/ppermute | solution.py:20
  195.1 1.1 select_add_fusion
  196.2 5.4 %collective-permute-start.13 = (f32[64,256]{1,0:T(8,128)S(1)}, f32[64,256]{1,0:T(8,128)S(1)}, u32[]{:S(2)}, u32[]{:S(2)}) collective-permute-start(f32[64,256]{1,0:T(8,128)S(1)} %slice_select_fusion.1), channel_id=1, source_target_pairs={{0,64},{4,68},{8,72},{12,76},{16,80},{20,84},{24,88},{28,92},{32,9... | collective-permute-start | bytes 196616 | tf_op jit(solution)/shard_map/ppermute | solution.py:20
  201.6 1.6 collective-permute-done.13
  203.3 0.6 select_add_fusion.1
  203.9 6.8 %collective-permute-start.14 = (f32[64,256]{1,0:T(8,128)}, f32[64,256]{1,0:T(8,128)}, u32[]{:S(2)}, u32[]{:S(2)}) collective-permute-start(f32[64,256]{1,0:T(8,128)} %select_add_fusion.1), channel_id=1, source_target_pairs={{0,8},{4,12},{8,0},{12,4},{16,24},{20,28},{24,16},{28,20},{32,40},... | collective-permute-start | bytes 196616 | tf_op jit(solution)/shard_map/ppermute | solution.py:20
  210.7 2.4 collective-permute-done.14
  213.1 0.9 add.116
  214.0 5.1 %collective-permute-start.15 = (f32[64,256]{1,0:T(8,128)S(1)}, f32[64,256]{1,0:T(8,128)S(1)}, u32[]{:S(2)}, u32[]{:S(2)}) collective-permute-start(f32[64,256]{1,0:T(8,128)S(1)} %add.116), channel_id=1, source_target_pairs={{0,32},{4,36},{8,40},{12,44},{16,48},{20,52},{24,56},{28,60},{32,0... | collective-permute-start | bytes 196616 | tf_op jit(solution)/shard_map/ppermute | solution.py:20
  219.1 1.3 convolution_convert_fusion.7
  220.8 6.8 %collective-permute-start.16 = (f32[64,256]{1,0:T(8,128)S(1)}, f32[64,256]{1,0:T(8,128)S(1)}, u32[]{:S(2)}, u32[]{:S(2)}) collective-permute-start(f32[64,256]{1,0:T(8,128)S(1)} %add.117), channel_id=1, source_target_pairs={{0,128},{4,132},{8,136},{12,140},{16,144},{20,148},{24,152},{28,15... | collective-permute-start | bytes 196616 | tf_op jit(solution)/shard_map/ppermute | solution.py:20
  227.6 1.3 convolution_convert_fusion.3
  229.2 8.3 %collective-permute-start.17 = (f32[64,256]{1,0:T(8,128)S(1)}, f32[64,256]{1,0:T(8,128)S(1)}, u32[]{:S(2)}, u32[]{:S(2)}) collective-permute-start(f32[64,256]{1,0:T(8,128)S(1)} %add.118), channel_id=1, source_target_pairs={{0,256},{4,260},{8,264},{12,268},{16,272},{20,276},{24,280},{28,28... | collective-permute-start | bytes 196616 | tf_op jit(solution)/shard_map/ppermute | solution.py:20
  237.8 1.3 collective-permute-done.17
  239.2 2.5 collective-permute-start.18
  242.0 2.5 collective-permute-done.18
  244.5 3.2 %collective-permute-start.19 = (f32[128,256]{1,0:T(8,128)S(1)}, f32[128,256]{1,0:T(8,128)S(1)}, u32[]{:S(2)}, u32[]{:S(2)}) collective-permute-start(f32[128,256]{1,0:T(8,128)S(1)} %maximum_select_fusion.2), channel_id=1, source_target_pairs={{0,16},{4,20},{8,24},{12,28},{16,0},{20,4},{24,8},{28,12},{32,48},... | collective-permute-start | bytes 393224 | tf_op jit(solution)/shard_map/ppermute | solution.py:20
  248.2 2.0 collective-permute-done.19
  250.2 11.1 %collective-permute-start.20 = (f32[256,256]{1,0:T(8,128)S(1)}, f32[256,256]{1,0:T(8,128)S(1)}, u32[]{:S(2)}, u32[]{:S(2)}) collective-permute-start(f32[256,256]{1,0:T(8,128)S(1)} %maximum_select_fusion.1), channel_id=1, source_target_pairs={{0,4},{4,0},{8,12},{12,8},{16,20},{20,16},{24,28},{28,24},{32,36},... | collective-permute-start | bytes 786440 | tf_op jit(solution)/shard_map/ppermute | solution.py:20
  261.4 1.5 fusion.58
  262.9 0.8 maximum_select_fusion
  (108 shorter events, 10.6 us)
Async XLA Ops:
  7.2 97.0 %copy-start = (bf16[1,128,1024]{2,1,0:T(8,128)(2,1)S(1)}, bf16[1,128,1024]{2,1,0:T(8,128)(2,1)}, u32[]{:S(2)}) copy-start(bf16[1,128,1024]{2,1,0:T(8,128)(2,1)} %param.7) | copy-start | bytes 786436
  7.2 69.9 %all-gather.2.cloned.1.call-start = ((), (), s32[]{:S(2)}) async-start(), calls=%async_computation | async-start | bytes 3276800 | tf_op jit(solution)/shard_map/all_gather | solution.py:149
  7.2 73.3 %copy-start.19 = (bf16[1,128,1024]{2,1,0:T(8,128)(2,1)S(1)}, bf16[1,128,1024]{2,1,0:T(8,128)(2,1)}, u32[]{:S(2)}) copy-start(bf16[1,128,1024]{2,1,0:T(8,128)(2,1)} %param.6) | copy-start | bytes 786436
  77.1 7.7 %collective-permute-start = (bf16[1024,1280]{1,0:T(8,128)(2,1)}, bf16[1024,1280]{1,0:T(8,128)(2,1)}, u32[]{:S(2)}, u32[]{:S(2)}) collective-permute-start(bf16[1024,1280]{1,0:T(8,128)(2,1)} %all-gather.2.cloned.1.call-done), channel_id=1, source_target_pairs={{0,4},{4,0},{8,12},{12,8},{16,20},{20,16},{24,28},{28,24},{32,36},... | collective-permute-start | bytes 7864328 | tf_op jit(solution)/shard_map/ppermute | solution.py:20
  87.7 16.5 %copy-start.1 = (bf16[1024,512]{1,0:T(8,128)(2,1)}, bf16[1024,512]{1,0:T(8,128)(2,1)S(1)}, u32[]{:S(2)}) copy-start(bf16[1024,512]{1,0:T(8,128)(2,1)S(1)} %pad_maximum_fusion) | copy-start | bytes 3145732
  88.1 18.3 %collective-permute-start.4 = (bf16[128,512]{1,0:T(8,128)(2,1)S(1)}, bf16[128,512]{1,0:T(8,128)(2,1)S(1)}, u32[]{:S(2)}, u32[]{:S(2)}) collective-permute-start(bf16[128,512]{1,0:T(8,128)(2,1)S(1)} %fusion.75), channel_id=1, source_target_pairs={{0,4},{4,8},{8,12},{12,16},{16,20},{20,24},{24,28},{28,32},{32,36}... | collective-permute-start | bytes 393224 | tf_op jit(solution)/shard_map/ppermute | solution.py:15
  94.3 12.0 %collective-permute-start.3 = (bf16[128,512]{1,0:T(8,128)(2,1)S(1)}, bf16[128,512]{1,0:T(8,128)(2,1)S(1)}, u32[]{:S(2)}, u32[]{:S(2)}) collective-permute-start(bf16[128,512]{1,0:T(8,128)(2,1)S(1)} %fusion.75), channel_id=1, source_target_pairs={{0,8},{4,12},{8,16},{12,20},{16,24},{20,28},{24,32},{28,36},{32,40... | collective-permute-start | bytes 393224 | tf_op jit(solution)/shard_map/ppermute | solution.py:15
  98.4 7.9 %collective-permute-start.2 = (bf16[128,512]{1,0:T(8,128)(2,1)S(1)}, bf16[128,512]{1,0:T(8,128)(2,1)S(1)}, u32[]{:S(2)}, u32[]{:S(2)}) collective-permute-start(bf16[128,512]{1,0:T(8,128)(2,1)S(1)} %fusion.75), channel_id=1, source_target_pairs={{0,12},{4,16},{8,20},{12,24},{16,28},{20,32},{24,36},{28,40},{32,4... | collective-permute-start | bytes 393224 | tf_op jit(solution)/shard_map/ppermute | solution.py:15
  99.8 6.5 %collective-permute-start.1 = (bf16[128,512]{1,0:T(8,128)(2,1)S(1)}, bf16[128,512]{1,0:T(8,128)(2,1)S(1)}, u32[]{:S(2)}, u32[]{:S(2)}) collective-permute-start(bf16[128,512]{1,0:T(8,128)(2,1)S(1)} %fusion.75), channel_id=1, source_target_pairs={{0,16},{4,20},{8,24},{12,28},{16,32},{20,36},{24,40},{28,44},{32,4... | collective-permute-start | bytes 393224 | tf_op jit(solution)/shard_map/ppermute | solution.py:15
  106.4 19.2 %copy-start.4 = (bf16[640,512]{1,0:T(8,128)(2,1)}, bf16[640,512]{1,0:T(8,128)(2,1)S(1)}, u32[]{:S(2)}) copy-start(bf16[640,512]{1,0:T(8,128)(2,1)S(1)} %constant_dynamic-update-slice_fusion) | copy-start | bytes 1966084
  118.0 2.2 copy-start.23
  120.1 0.8 copy-start.27
  120.4 1.4 copy-start.15
  121.0 0.8 copy-start.11
  121.0 1.0 copy-start.21
  121.9 1.3 copy-start.14
  122.6 3.9 %copy-start.10 = (bf16[4,128,640]{1,2,0:T(8,128)(2,1)}, bf16[4,128,640]{1,2,0:T(8,128)(2,1)S(1)}, u32[]{:S(2)}) copy-start(bf16[4,128,640]{1,2,0:T(8,128)(2,1)S(1)} %fusion.44) | copy-start | bytes 1966084
  122.6 1.0 copy-start.22
  123.3 1.3 copy-start.13
  124.3 1.8 copy-start.8
  124.3 0.9 copy-start.20
  124.8 1.3 copy-start.26
  125.6 0.8 copy-start.25
  125.7 1.1 copy-start.24
  126.1 1.0 copy-start.6
  128.4 10.8 %copy-start.18 = (bf16[1,128,1024]{1,2,0:T(8,128)(2,1)S(1)}, bf16[1,128,1024]{1,2,0:T(8,128)(2,1)}, u32[]{:S(2)}) copy-start(bf16[1,128,1024]{1,2,0:T(8,128)(2,1)} %copy.104) | copy-start | bytes 786436
  128.6 11.2 %collective-permute-start.5 = (bf16[128,512]{0,1:T(8,128)(2,1)S(1)}, bf16[128,512]{0,1:T(8,128)(2,1)S(1)}, u32[]{:S(2)}, u32[]{:S(2)}) collective-permute-start(bf16[128,512]{0,1:T(8,128)(2,1)S(1)} %get-tuple-element.4), channel_id=1, source_target_pairs={{4,0},{8,4},{12,8},{16,12},{20,16},{24,20},{28,24},{32,28},{36,32}... | collective-permute-start | bytes 393224 | tf_op jit(solution)/shard_map/ppermute | solution.py:15
  135.4 6.0 %collective-permute-start.8 = (bf16[128,512]{0,1:T(8,128)(2,1)S(1)}, bf16[128,512]{0,1:T(8,128)(2,1)S(1)}, u32[]{:S(2)}, u32[]{:S(2)}) collective-permute-start(bf16[128,512]{0,1:T(8,128)(2,1)S(1)} %get-tuple-element.5), channel_id=1, source_target_pairs={{16,0},{20,4},{24,8},{28,12},{32,16},{36,20},{40,24},{44,28},{48,3... | collective-permute-start | bytes 393224 | tf_op jit(solution)/shard_map/ppermute | solution.py:15
  136.7 8.6 %collective-permute-start.7 = (bf16[128,512]{0,1:T(8,128)(2,1)S(1)}, bf16[128,512]{0,1:T(8,128)(2,1)S(1)}, u32[]{:S(2)}, u32[]{:S(2)}) collective-permute-start(bf16[128,512]{0,1:T(8,128)(2,1)S(1)} %get-tuple-element.6), channel_id=1, source_target_pairs={{12,0},{16,4},{20,8},{24,12},{28,16},{32,20},{36,24},{40,28},{44,3... | collective-permute-start | bytes 393224 | tf_op jit(solution)/shard_map/ppermute | solution.py:15
  138.0 12.0 %collective-permute-start.6 = (bf16[128,512]{0,1:T(8,128)(2,1)S(1)}, bf16[128,512]{0,1:T(8,128)(2,1)S(1)}, u32[]{:S(2)}, u32[]{:S(2)}) collective-permute-start(bf16[128,512]{0,1:T(8,128)(2,1)S(1)} %get-tuple-element.7), channel_id=1, source_target_pairs={{8,0},{12,4},{16,8},{20,12},{24,16},{28,20},{32,24},{36,28},{40,32... | collective-permute-start | bytes 393224 | tf_op jit(solution)/shard_map/ppermute | solution.py:15
  150.0 7.9 %copy-start.16 = (bf16[128,512]{0,1:T(8,128)(2,1)}, bf16[128,512]{0,1:T(8,128)(2,1)S(1)}, u32[]{:S(2)}) copy-start(bf16[128,512]{0,1:T(8,128)(2,1)S(1)} %fusion.93) | copy-start | bytes 393220
  151.4 5.0 %collective-permute-start.9 = (f32[1024,256]{1,0:T(8,128)}, f32[1024,256]{1,0:T(8,128)}, u32[]{:S(2)}, u32[]{:S(2)}) collective-permute-start(f32[1024,256]{1,0:T(8,128)} %fusion.104), channel_id=1, source_target_pairs={{0,4},{4,0},{8,12},{12,8},{16,20},{20,16},{24,28},{28,24},{32,36},... | collective-permute-start | bytes 3145736 | tf_op jit(solution)/shard_map/ppermute | solution.py:20
  157.9 1.0 copy-start.3
  158.9 13.1 %collective-permute-start.10 = (bf16[512,256]{1,0:T(8,128)(2,1)S(1)}, bf16[512,256]{1,0:T(8,128)(2,1)}, u32[]{:S(2)}, u32[]{:S(2)}) collective-permute-start(bf16[512,256]{1,0:T(8,128)(2,1)S(1)} %slice.269), channel_id=1, source_target_pairs={{0,1},{1,0},{2,3},{3,2},{4,5},{5,4},{6,7},{7,6},{8,9},{9,8},{10,11... | collective-permute-start | bytes 786440 | tf_op jit(solution)/shard_map/ppermute | solution.py:20
  173.9 10.3 %collective-permute-start.11 = (bf16[256,256]{1,0:T(8,128)(2,1)}, bf16[256,256]{1,0:T(8,128)(2,1)S(1)}, u32[]{:S(2)}, u32[]{:S(2)}) collective-permute-start(bf16[256,256]{1,0:T(8,128)(2,1)} %select_convert_fusion), channel_id=1, source_target_pairs={{0,2},{1,3},{2,0},{3,1},{4,6},{5,7},{6,4},{7,5},{8,10},{9,11},{10,... | collective-permute-start | bytes 393224 | tf_op jit(solution)/shard_map/ppermute | solution.py:20
  184.2 0.7 copy-start.12
  184.9 34.2 %copy-start.5 = (bf16[640,512]{1,0:T(8,128)(2,1)S(1)}, bf16[640,512]{1,0:T(8,128)(2,1)}, u32[]{:S(2)}) copy-start(bf16[640,512]{1,0:T(8,128)(2,1)} %copy-done.4) | copy-start | bytes 1966084
  185.6 9.5 %collective-permute-start.12 = (f32[128,256]{1,0:T(8,128)}, f32[128,256]{1,0:T(8,128)}, u32[]{:S(2)}, u32[]{:S(2)}) collective-permute-start(f32[128,256]{1,0:T(8,128)} %slice_select_fusion), channel_id=1, source_target_pairs={{0,16},{4,20},{8,24},{12,28},{16,0},{20,4},{24,8},{28,12},{32,48},... | collective-permute-start | bytes 393224 | tf_op jit(solution)/shard_map/ppermute | solution.py:20
  196.2 7.1 %collective-permute-start.13 = (f32[64,256]{1,0:T(8,128)S(1)}, f32[64,256]{1,0:T(8,128)S(1)}, u32[]{:S(2)}, u32[]{:S(2)}) collective-permute-start(f32[64,256]{1,0:T(8,128)S(1)} %slice_select_fusion.1), channel_id=1, source_target_pairs={{0,64},{4,68},{8,72},{12,76},{16,80},{20,84},{24,88},{28,92},{32,9... | collective-permute-start | bytes 196616 | tf_op jit(solution)/shard_map/ppermute | solution.py:20
  203.9 9.2 %collective-permute-start.14 = (f32[64,256]{1,0:T(8,128)}, f32[64,256]{1,0:T(8,128)}, u32[]{:S(2)}, u32[]{:S(2)}) collective-permute-start(f32[64,256]{1,0:T(8,128)} %select_add_fusion.1), channel_id=1, source_target_pairs={{0,8},{4,12},{8,0},{12,4},{16,24},{20,28},{24,16},{28,20},{32,40},... | collective-permute-start | bytes 196616 | tf_op jit(solution)/shard_map/ppermute | solution.py:20
  210.7 26.8 %copy-start.9 = (bf16[4,128,640]{1,2,0:T(8,128)(2,1)S(1)}, bf16[4,128,640]{1,2,0:T(8,128)(2,1)}, u32[]{:S(2)}) copy-start(bf16[4,128,640]{1,2,0:T(8,128)(2,1)} %copy-done.8) | copy-start | bytes 1966084
  214.0 6.8 %collective-permute-start.15 = (f32[64,256]{1,0:T(8,128)S(1)}, f32[64,256]{1,0:T(8,128)S(1)}, u32[]{:S(2)}, u32[]{:S(2)}) collective-permute-start(f32[64,256]{1,0:T(8,128)S(1)} %add.116), channel_id=1, source_target_pairs={{0,32},{4,36},{8,40},{12,44},{16,48},{20,52},{24,56},{28,60},{32,0... | collective-permute-start | bytes 196616 | tf_op jit(solution)/shard_map/ppermute | solution.py:20
  220.5 21.1 %copy-start.7 = (bf16[4,128,640]{1,2,0:T(8,128)(2,1)S(1)}, bf16[4,128,640]{1,2,0:T(8,128)(2,1)}, u32[]{:S(2)}) copy-start(bf16[4,128,640]{1,2,0:T(8,128)(2,1)} %copy-done.6) | copy-start | bytes 1966084
  220.8 8.4 %collective-permute-start.16 = (f32[64,256]{1,0:T(8,128)S(1)}, f32[64,256]{1,0:T(8,128)S(1)}, u32[]{:S(2)}, u32[]{:S(2)}) collective-permute-start(f32[64,256]{1,0:T(8,128)S(1)} %add.117), channel_id=1, source_target_pairs={{0,128},{4,132},{8,136},{12,140},{16,144},{20,148},{24,152},{28,15... | collective-permute-start | bytes 196616 | tf_op jit(solution)/shard_map/ppermute | solution.py:20
  228.9 18.8 %copy-start.2 = (bf16[1024,512]{1,0:T(8,128)(2,1)S(1)}, bf16[1024,512]{1,0:T(8,128)(2,1)}, u32[]{:S(2)}) copy-start(bf16[1024,512]{1,0:T(8,128)(2,1)} %copy-done.1) | copy-start | bytes 3145732
  228.9 18.8 %copy-start.17 = (bf16[128,512]{0,1:T(8,128)(2,1)S(1)}, bf16[128,512]{0,1:T(8,128)(2,1)}, u32[]{:S(2)}) copy-start(bf16[128,512]{0,1:T(8,128)(2,1)} %copy-done.16) | copy-start | bytes 393220
  229.2 9.9 %collective-permute-start.17 = (f32[64,256]{1,0:T(8,128)S(1)}, f32[64,256]{1,0:T(8,128)S(1)}, u32[]{:S(2)}, u32[]{:S(2)}) collective-permute-start(f32[64,256]{1,0:T(8,128)S(1)} %add.118), channel_id=1, source_target_pairs={{0,256},{4,260},{8,264},{12,268},{16,272},{20,276},{24,280},{28,28... | collective-permute-start | bytes 196616 | tf_op jit(solution)/shard_map/ppermute | solution.py:20
  239.2 5.3 %collective-permute-start.18 = (f32[64,256]{1,0:T(8,128)S(1)}, f32[64,256]{1,0:T(8,128)S(1)}, u32[]{:S(2)}, u32[]{:S(2)}) collective-permute-start(f32[64,256]{1,0:T(8,128)S(1)} %add.119), channel_id=1, source_target_pairs={{0,64},{4,68},{8,72},{12,76},{16,80},{20,84},{24,88},{28,92},{32,9... | collective-permute-start | bytes 196616 | tf_op jit(solution)/shard_map/ppermute | solution.py:20
  244.5 5.7 %collective-permute-start.19 = (f32[128,256]{1,0:T(8,128)S(1)}, f32[128,256]{1,0:T(8,128)S(1)}, u32[]{:S(2)}, u32[]{:S(2)}) collective-permute-start(f32[128,256]{1,0:T(8,128)S(1)} %maximum_select_fusion.2), channel_id=1, source_target_pairs={{0,16},{4,20},{8,24},{12,28},{16,0},{20,4},{24,8},{28,12},{32,48},... | collective-permute-start | bytes 393224 | tf_op jit(solution)/shard_map/ppermute | solution.py:20
  250.2 12.7 %collective-permute-start.20 = (f32[256,256]{1,0:T(8,128)S(1)}, f32[256,256]{1,0:T(8,128)S(1)}, u32[]{:S(2)}, u32[]{:S(2)}) collective-permute-start(f32[256,256]{1,0:T(8,128)S(1)} %maximum_select_fusion.1), channel_id=1, source_target_pairs={{0,4},{4,0},{8,12},{12,8},{16,20},{20,16},{24,28},{28,24},{32,36},... | collective-permute-start | bytes 786440 | tf_op jit(solution)/shard_map/ppermute | solution.py:20
Sparse Core Ops, SparseCore 0:
  10.1 66.9 all-gather.1

commit v9 on v8

--- a/solution.py
+++ b/solution.py
@@ -117,6 +117,38 @@
     )
 
 
+def ring_source(linear, shift, stream_count):
+    tm_index, stream_index = divmod(linear, stream_count)
+    ring = 2 * stream_count
+    position = ((tm_index >> 1) & 1) * stream_count + stream_index
+    moved = (position + shift) % ring
+    tm_moved = (tm_index & ~2) | ((moved // stream_count) << 1)
+    return tm_moved * stream_count + moved % stream_count
+
+
+def ring_pull(value, shift):
+    stream_count = lax.axis_size("stream")
+    total = lax.axis_size("tm") * stream_count
+    pairs = [(ring_source(target, shift, stream_count), target) for target in range(total)]
+    return lax.ppermute(value, ("tm", "stream"), pairs)
+
+
+def ring_gather(block):
+    stream_count = lax.axis_size("stream")
+    if stream_count != 4 or lax.axis_size("tm") % 4 or block.shape[1] % 256:
+        return lax.all_gather(block, "stream", axis=0, tiled=True)
+    rows, width = block.shape
+    stream_index = lax.axis_index("stream")
+    split = width // 2
+    two_away = jnp.concatenate(
+        [ring_pull(block[:, :split], 2), ring_pull(block[:, split:], -2)], axis=1
+    )
+    stacked = jnp.concatenate([block, ring_pull(block, 1), two_away, ring_pull(block, -1)], axis=0)
+    doubled = jnp.concatenate([stacked, stacked], axis=0)
+    start = ((stream_count - stream_index) % stream_count) * rows
+    return lax.dynamic_slice_in_dim(doubled, start, stream_count * rows, 0)
+
+
 def contract_last(left, right):
     return lax.dot_general(
         left, right, (((1,), (1,)), ((), ())), preferred_element_type=jnp.float32
@@ -146,12 +178,7 @@
     if lax.axis_size("tm") % 2 == 0 and weights_local.shape[1] % 256 == 0:
         half_width = weights_local.shape[1] // 2
         core = lax.axis_index("tm") % 2
-        mine = lax.all_gather(
-            lax.dynamic_slice_in_dim(weights_local, core * half_width, half_width, 1),
-            "stream",
-            axis=0,
-            tiled=True,
-        )
+        mine = ring_gather(lax.dynamic_slice_in_dim(weights_local, core * half_width, half_width, 1))
         other = xor_swap(mine, "tm", 0)
         weights_full = jnp.concatenate(
             [jnp.where(core == 0, mine, other), jnp.where(core == 0, other, mine)], axis=1

time: 272 us -> 244 us (0.90)
  waiting for transfers between devices: 111 us -> 66.9 us
  starting transfers between devices: 95.3 us -> 116 us
  between operations: 15.6 us -> 2.25 us
  local copies, waits for them, and re-layouts: 6.57 us -> 13.1 us
    all_gather x1 -> x0, waiting for transfers between devices: 67.4 us -> none  [per_device(): lax.all_gather(lax.dynamic_slice_in_dim(weights_local, core * half_width,...]
    ppermute x0 -> x4, starting transfers between devices: none -> 20.8 us  [ring_pull(): return lax.ppermute(value, ('tm', 'stream'), pairs)]
    ppermute x0 -> x4, waiting for transfers between devices: none -> 18.7 us  [ring_pull(): return lax.ppermute(value, ('tm', 'stream'), pairs)]
    unnamed x0 -> x3, other arithmetic: none -> 4.09 us
    unnamed x61 -> x65, local copies, waits for them, and re-layouts: 5.04 us -> 8.63 us
    ppermute x13, starting transfers between devices: 69.3 us -> 72.9 us  [xor_swap(): lax.ppermute(value, axis, [(source, source ^ 1 << bit) for source in rang...]
    ppermute x8, starting transfers between devices: 25.9 us -> 22.7 us  [shifted(): lax.ppermute(value, axis, [(source, source + steps) for source in range(l...]
    ppermute x13, waiting for transfers between devices: 33.2 us -> 36.2 us  [xor_swap(): lax.ppermute(value, axis, [(source, source ^ 1 << bit) for source in rang...]
  transfers between devices with their start and end apart: 22 -> 25, of which waited for: 17 -> 18; matrix products, arithmetic and copies ran while one was open for 4% -> 5% of each run, Pallas kernels for 0% -> 0%
where the time goes in v9:
time: 244 us; the launch traced here: 243 us
  starting transfers between devices  116 us (48%)
  waiting for transfers between devices  66.9 us (27%)
  matrix products  26.8 us (11%)
  other arithmetic  17.3 us (7%)
  local copies, waits for them, and re-layouts  13.1 us (5%)
    ppermute x13, starting transfers between devices, xor_swap(): lax.ppermute(value, axis, [(source, source ^ 1 << bit) for source in rang...  72.9 us
    ppermute x13, waiting for transfers between devices, xor_swap(): lax.ppermute(value, axis, [(source, source ^ 1 << bit) for source in rang...  36.2 us
    ppermute x8, starting transfers between devices, shifted(): lax.ppermute(value, axis, [(source, source + steps) for source in range(l...  22.7 us
    ppermute x4, starting transfers between devices, ring_pull(): return lax.ppermute(value, ('tm', 'stream'), pairs)  20.8 us
    ppermute x4, waiting for transfers between devices, ring_pull(): return lax.ppermute(value, ('tm', 'stream'), pairs)  18.7 us
    ppermute x8, waiting for transfers between devices, shifted(): lax.ppermute(value, axis, [(source, source + steps) for source in range(l...  12 us
    sub x4, matrix products, per_device(): terms = jnp.where(allowed, jnp.exp(masked - row_max), 0.0)  11.5 us
    unnamed x65, local copies, waits for them, and re-layouts  8.63 us
  transfers between devices with their start and end apart: 25, of which 18 were waited for; matrix products, arithmetic and copies ran while one was open for 5% of the time, Pallas kernels for 0%

profile of v9, /device:TPU:1, one launch (start us, length us, event | category | flops | bytes accessed | tf_op | source)
XLA Modules:
  0.0 242.8 jit_solution(10648865832215953831)
XLA Ops:
  0.7 2.3 constant_dynamic-update-slice_fusion.5
  3.0 11.5 %collective-permute-start = (bf16[256,1280]{1,0:T(8,128)(2,1)S(1)}, bf16[256,1280]{1,0:T(8,128)(2,1)S(1)}, u32[]{:S(2)}, u32[]{:S(2)}) collective-permute-start(bf16[256,1280]{1,0:T(8,128)(2,1)S(1)} %get-tuple-element.3), channel_id=1, source_target_pairs={{1,0},{2,1},{3,2},{8,3},{5,4},{6,5},{7,6},{12,7},{9,8},{10,9},{11,... | collective-permute-start | bytes 1966088 | tf_op jit(solution)/shard_map/ppermute | solution.py:133
  14.5 1.9 collective-permute-start.3
  16.4 1.9 collective-permute-start.2
  18.4 5.5 %collective-permute-start.1 = (bf16[256,640]{1,0:T(8,128)(2,1)S(1)}, bf16[256,640]{1,0:T(8,128)(2,1)S(1)}, u32[]{:S(2)}, u32[]{:S(2)}) collective-permute-start(bf16[256,640]{1,0:T(8,128)(2,1)S(1)} %get-tuple-element.10), channel_id=1, source_target_pairs={{2,0},{3,1},{8,2},{9,3},{6,4},{7,5},{12,6},{13,7},{10,8},{11,9},{0... | collective-permute-start | bytes 983048 | tf_op jit(solution)/shard_map/ppermute | solution.py:133
  23.9 8.1 %collective-permute-done = bf16[256,1280]{1,0:T(8,128)(2,1)S(1)} collective-permute-done((bf16[256,1280]{1,0:T(8,128)(2,1)S(1)}, bf16[256,1280]{1,0:T(8,128)(2,1)S(1)}, u32[]{:S(2)}, u32[]{:S(2)}) %collective-permute-start) | collective-permute-done | bytes 655392 | tf_op jit(solution)/shard_map/ppermute | solution.py:133
  32.0 0.9 constant_dynamic-update-slice_fusion.4
  32.9 10.6 %collective-permute-done.2 = bf16[256,640]{1,0:T(8,128)(2,1)S(1)} collective-permute-done((bf16[256,640]{1,0:T(8,128)(2,1)S(1)}, bf16[256,640]{1,0:T(8,128)(2,1)S(1)}, u32[]{:S(2)}, u32[]{:S(2)}) %collective-permute-start.2) | collective-permute-done | bytes 327712 | tf_op jit(solution)/shard_map/ppermute | solution.py:133
  43.5 0.9 fusion.87
  44.4 0.9 constant_dynamic-update-slice_fusion.3
  45.3 0.9 constant_dynamic-update-slice_fusion.2
  47.1 0.9 fusion.86
  48.0 0.9 constant_dynamic-update-slice_fusion
  48.9 2.0 constant_dynamic-slice_fusion
  50.8 3.8 %collective-permute-start.4 = (bf16[1024,1280]{1,0:T(8,128)(2,1)S(1)}, bf16[1024,1280]{1,0:T(8,128)(2,1)}, u32[]{:S(2)}, u32[]{:S(2)}) collective-permute-start(bf16[1024,1280]{1,0:T(8,128)(2,1)S(1)} %constant_dynamic-slice_fusion), channel_id=1, source_target_pairs={{0,4},{4,0},{8,12},{12,8},{16,20},{20,16},{24,28},{28,24},{32,36},... | collective-permute-start | bytes 7864328 | tf_op jit(solution)/shard_map/ppermute | solution.py:20
  56.2 1.0 fusion.91
  57.2 2.1 collective-permute-done.4
  59.3 3.5 %broadcast_select_fusion.1 = (bf16[1024,1280]{1,0:T(8,128)(2,1)S(1)}, bf16[1024,1280]{1,0:T(8,128)(2,1)S(1)}) fusion(bf16[1024,1280]{1,0:T(8,128)(2,1)} %collective-permute-done.4, pred[]{:T(512)S(6)} %eq.25, bf16[2048,1280]{1,0:T(8,128)(2,1)} %constant_dynamic-update-slice_fusion, s32[]{:T(128)S(6)} %select_n.173), kind=kLoop, calls=%fused_computation.5 | loop fusion | flops 2621440 | bytes 10485765 | tf_op jit(solution)/shard_map/jit(_where)/select_n | solution.py:184
  64.0 3.1 %collective-permute-start.5 = (bf16[128,512]{1,0:T(8,128)(2,1)S(1)}, bf16[128,512]{1,0:T(8,128)(2,1)S(1)}, u32[]{:S(2)}, u32[]{:S(2)}) collective-permute-start(bf16[128,512]{1,0:T(8,128)(2,1)S(1)} %fusion.75), channel_id=1, source_target_pairs={{0,16},{4,20},{8,24},{12,28},{16,32},{20,36},{24,40},{28,44},{32,4... | collective-permute-start | bytes 393224 | tf_op jit(solution)/shard_map/ppermute | solution.py:15
  67.1 3.7 %collective-permute-start.6 = (bf16[128,512]{1,0:T(8,128)(2,1)S(1)}, bf16[128,512]{1,0:T(8,128)(2,1)S(1)}, u32[]{:S(2)}, u32[]{:S(2)}) collective-permute-start(bf16[128,512]{1,0:T(8,128)(2,1)S(1)} %fusion.75), channel_id=1, source_target_pairs={{0,12},{4,16},{8,20},{12,24},{16,28},{20,32},{24,36},{28,40},{32,4... | collective-permute-start | bytes 393224 | tf_op jit(solution)/shard_map/ppermute | solution.py:15
  70.8 3.1 %collective-permute-start.7 = (bf16[128,512]{1,0:T(8,128)(2,1)S(1)}, bf16[128,512]{1,0:T(8,128)(2,1)S(1)}, u32[]{:S(2)}, u32[]{:S(2)}) collective-permute-start(bf16[128,512]{1,0:T(8,128)(2,1)S(1)} %fusion.75), channel_id=1, source_target_pairs={{0,8},{4,12},{8,16},{12,20},{16,24},{20,28},{24,32},{28,36},{32,40... | collective-permute-start | bytes 393224 | tf_op jit(solution)/shard_map/ppermute | solution.py:15
  73.9 7.0 %collective-permute-start.8 = (bf16[128,512]{1,0:T(8,128)(2,1)S(1)}, bf16[128,512]{1,0:T(8,128)(2,1)S(1)}, u32[]{:S(2)}, u32[]{:S(2)}) collective-permute-start(bf16[128,512]{1,0:T(8,128)(2,1)S(1)} %fusion.75), channel_id=1, source_target_pairs={{0,4},{4,8},{8,12},{12,16},{16,20},{20,24},{24,28},{28,32},{32,36}... | collective-permute-start | bytes 393224 | tf_op jit(solution)/shard_map/ppermute | solution.py:15
  83.2 2.4 collective-permute-done.8
  85.6 2.9 %fusion.136 = (f32[4,128]{1,0:T(4,128)S(1)}, f32[4,128,640]{1,2,0:T(8,128)}) fusion(bf16[128,4,64]{0,2,1:T(8,128)(2,1)} %bitcast.304, pred[128,640]{0,1:T(8,128)(4,1)} %fusion.91, bf16[640,512]{1,0:T(8,128)(2,1)S(1)} %constant_dynamic-update-slice_fusion.6), kind=kOutput, calls=%fused_computation.205 | convolution fusion | flops 43582080 | bytes 1705984 | tf_op jit(solution)/shard_map/sub | solution.py:234
  88.5 2.7 %fusion.133 = (f32[4,128]{1,0:T(4,128)S(1)}, f32[4,128,640]{1,2,0:T(8,128)}) fusion(bf16[128,4,64]{0,2,1:T(8,128)(2,1)} %bitcast.298, pred[128,640]{0,1:T(8,128)(4,1)} %fusion.91, bf16[640,512]{1,0:T(8,128)(2,1)S(1)} %constant_dynamic-update-slice_fusion.6), kind=kOutput, calls=%fused_computation.202 | convolution fusion | flops 43582080 | bytes 1705984 | tf_op jit(solution)/shard_map/sub | solution.py:234
  91.2 2.7 %fusion.134 = (f32[4,128]{1,0:T(4,128)S(1)}, f32[4,128,640]{1,2,0:T(8,128)}) fusion(bf16[128,4,64]{0,2,1:T(8,128)(2,1)} %bitcast.302, pred[128,640]{0,1:T(8,128)(4,1)} %fusion.91, bf16[640,512]{1,0:T(8,128)(2,1)S(1)} %constant_dynamic-update-slice_fusion.6), kind=kOutput, calls=%fused_computation.203 | convolution fusion | flops 43582080 | bytes 1705984 | tf_op jit(solution)/shard_map/sub | solution.py:234
  93.9 3.2 %fusion.135 = (f32[4,128]{1,0:T(4,128)}, f32[4,128,640]{1,2,0:T(8,128)}) fusion(bf16[128,4,64]{0,2,1:T(8,128)(2,1)} %bitcast.300, pred[128,640]{0,1:T(8,128)(4,1)} %fusion.91, bf16[640,512]{1,0:T(8,128)(2,1)S(1)} %constant_dynamic-update-slice_fusion.6), kind=kOutput, calls=%fused_computation.204 | convolution fusion | flops 43582080 | bytes 1705984 | tf_op jit(solution)/shard_map/sub | solution.py:234
  97.9 1.4 divide_convert_fusion.3
  107.8 1.3 collective-permute-start.12
  109.1 1.3 collective-permute-start.11
  110.4 1.3 collective-permute-start.10
  111.7 1.9 collective-permute-start.9
  113.7 4.9 %collective-permute-done.11 = bf16[128,512]{0,1:T(8,128)(2,1)S(1)} collective-permute-done((bf16[128,512]{0,1:T(8,128)(2,1)S(1)}, bf16[128,512]{0,1:T(8,128)(2,1)S(1)}, u32[]{:S(2)}, u32[]{:S(2)}) %collective-permute-start.11) | collective-permute-done | bytes 131104 | tf_op jit(solution)/shard_map/ppermute | solution.py:15
  118.6 1.8 collective-permute-done.10
  120.4 2.9 %collective-permute-done.9 = bf16[128,512]{0,1:T(8,128)(2,1)S(1)} collective-permute-done((bf16[128,512]{0,1:T(8,128)(2,1)S(1)}, bf16[128,512]{0,1:T(8,128)(2,1)S(1)}, u32[]{:S(2)}, u32[]{:S(2)}) %collective-permute-start.9) | collective-permute-done | bytes 131104 | tf_op jit(solution)/shard_map/ppermute | solution.py:15
  123.4 1.3 fusion.106
  124.7 2.1 collective-permute-start.13
  126.8 2.8 %collective-permute-done.13 = f32[1024,256]{1,0:T(8,128)} collective-permute-done((f32[1024,256]{1,0:T(8,128)}, f32[1024,256]{1,0:T(8,128)}, u32[]{:S(2)}, u32[]{:S(2)}) %collective-permute-start.13) | collective-permute-done | bytes 1048608 | tf_op jit(solution)/shard_map/ppermute | solution.py:20
  129.6 1.5 convolution_add_fusion
  131.1 1.0 copy-done.3
  132.1 10.1 %collective-permute-start.14 = (bf16[512,256]{1,0:T(8,128)(2,1)S(1)}, bf16[512,256]{1,0:T(8,128)(2,1)}, u32[]{:S(2)}, u32[]{:S(2)}) collective-permute-start(bf16[512,256]{1,0:T(8,128)(2,1)S(1)} %slice.279), channel_id=1, source_target_pairs={{0,1},{1,0},{2,3},{3,2},{4,5},{5,4},{6,7},{7,6},{8,9},{9,8},{10,11... | collective-permute-start | bytes 786440 | tf_op jit(solution)/shard_map/ppermute | solution.py:20
  142.3 6.6 %collective-permute-done.14 = bf16[512,256]{1,0:T(8,128)(2,1)} collective-permute-done((bf16[512,256]{1,0:T(8,128)(2,1)S(1)}, bf16[512,256]{1,0:T(8,128)(2,1)}, u32[]{:S(2)}, u32[]{:S(2)}) %collective-permute-start.14) | collective-permute-done | bytes 262176 | tf_op jit(solution)/shard_map/ppermute | solution.py:20
  148.9 1.2 slice_add_fusion
  150.8 1.9 collective-permute-start.15
  152.7 8.3 %collective-permute-done.15 = bf16[256,256]{1,0:T(8,128)(2,1)S(1)} collective-permute-done((bf16[256,256]{1,0:T(8,128)(2,1)}, bf16[256,256]{1,0:T(8,128)(2,1)S(1)}, u32[]{:S(2)}, u32[]{:S(2)}) %collective-permute-start.15) | collective-permute-done | bytes 131104 | tf_op jit(solution)/shard_map/ppermute | solution.py:20
  162.4 6.4 %collective-permute-start.16 = (f32[128,256]{1,0:T(8,128)}, f32[128,256]{1,0:T(8,128)}, u32[]{:S(2)}, u32[]{:S(2)}) collective-permute-start(f32[128,256]{1,0:T(8,128)} %slice_select_fusion), channel_id=1, source_target_pairs={{0,16},{4,20},{8,24},{12,28},{16,0},{20,4},{24,8},{28,12},{32,48},... | collective-permute-start | bytes 393224 | tf_op jit(solution)/shard_map/ppermute | solution.py:20
  168.8 2.7 %collective-permute-done.16 = f32[128,256]{1,0:T(8,128)} collective-permute-done((f32[128,256]{1,0:T(8,128)}, f32[128,256]{1,0:T(8,128)}, u32[]{:S(2)}, u32[]{:S(2)}) %collective-permute-start.16) | collective-permute-done | bytes 131104 | tf_op jit(solution)/shard_map/ppermute | solution.py:20
  171.5 1.1 select_add_fusion
  172.6 8.3 %collective-permute-start.17 = (f32[64,256]{1,0:T(8,128)S(1)}, f32[64,256]{1,0:T(8,128)S(1)}, u32[]{:S(2)}, u32[]{:S(2)}) collective-permute-start(f32[64,256]{1,0:T(8,128)S(1)} %slice_select_fusion.1), channel_id=1, source_target_pairs={{0,64},{4,68},{8,72},{12,76},{16,80},{20,84},{24,88},{28,92},{32,9... | collective-permute-start | bytes 196616 | tf_op jit(solution)/shard_map/ppermute | solution.py:20
  180.8 1.6 collective-permute-done.17
  183.1 4.2 %collective-permute-start.18 = (f32[64,256]{1,0:T(8,128)}, f32[64,256]{1,0:T(8,128)}, u32[]{:S(2)}, u32[]{:S(2)}) collective-permute-start(f32[64,256]{1,0:T(8,128)} %select_add_fusion.1), channel_id=1, source_target_pairs={{0,8},{4,12},{8,0},{12,4},{16,24},{20,28},{24,16},{28,20},{32,40},... | collective-permute-start | bytes 196616 | tf_op jit(solution)/shard_map/ppermute | solution.py:20
  187.3 5.0 %collective-permute-done.18 = f32[64,256]{1,0:T(8,128)} collective-permute-done((f32[64,256]{1,0:T(8,128)}, f32[64,256]{1,0:T(8,128)}, u32[]{:S(2)}, u32[]{:S(2)}) %collective-permute-start.18) | collective-permute-done | bytes 65568 | tf_op jit(solution)/shard_map/ppermute | solution.py:20
  193.2 4.6 %collective-permute-start.19 = (f32[64,256]{1,0:T(8,128)S(1)}, f32[64,256]{1,0:T(8,128)S(1)}, u32[]{:S(2)}, u32[]{:S(2)}) collective-permute-start(f32[64,256]{1,0:T(8,128)S(1)} %add.124), channel_id=1, source_target_pairs={{0,32},{4,36},{8,40},{12,44},{16,48},{20,52},{24,56},{28,60},{32,0... | collective-permute-start | bytes 196616 | tf_op jit(solution)/shard_map/ppermute | solution.py:20
  197.9 1.4 convolution_convert_fusion.1
  199.7 4.9 %collective-permute-start.20 = (f32[64,256]{1,0:T(8,128)S(1)}, f32[64,256]{1,0:T(8,128)S(1)}, u32[]{:S(2)}, u32[]{:S(2)}) collective-permute-start(f32[64,256]{1,0:T(8,128)S(1)} %add.125), channel_id=1, source_target_pairs={{0,128},{4,132},{8,136},{12,140},{16,144},{20,148},{24,152},{28,15... | collective-permute-start | bytes 196616 | tf_op jit(solution)/shard_map/ppermute | solution.py:20
  204.6 1.3 convolution_convert_fusion.3
  206.3 8.8 %collective-permute-start.21 = (f32[64,256]{1,0:T(8,128)S(1)}, f32[64,256]{1,0:T(8,128)S(1)}, u32[]{:S(2)}, u32[]{:S(2)}) collective-permute-start(f32[64,256]{1,0:T(8,128)S(1)} %add.126), channel_id=1, source_target_pairs={{0,256},{4,260},{8,264},{12,268},{16,272},{20,276},{24,280},{28,28... | collective-permute-start | bytes 196616 | tf_op jit(solution)/shard_map/ppermute | solution.py:20
  215.4 1.7 collective-permute-done.21
  217.2 1.9 collective-permute-start.22
  219.4 2.8 %collective-permute-done.22 = f32[64,256]{1,0:T(8,128)S(1)} collective-permute-done((f32[64,256]{1,0:T(8,128)S(1)}, f32[64,256]{1,0:T(8,128)S(1)}, u32[]{:S(2)}, u32[]{:S(2)}) %collective-permute-start.22) | collective-permute-done | bytes 65568 | tf_op jit(solution)/shard_map/ppermute | solution.py:20
  222.2 3.9 %collective-permute-start.23 = (f32[128,256]{1,0:T(8,128)S(1)}, f32[128,256]{1,0:T(8,128)S(1)}, u32[]{:S(2)}, u32[]{:S(2)}) collective-permute-start(f32[128,256]{1,0:T(8,128)S(1)} %maximum_select_fusion.2), channel_id=1, source_target_pairs={{0,16},{4,20},{8,24},{12,28},{16,0},{20,4},{24,8},{28,12},{32,48},... | collective-permute-start | bytes 393224 | tf_op jit(solution)/shard_map/ppermute | solution.py:20
  226.5 1.8 collective-permute-done.23
  228.4 12.0 %collective-permute-start.24 = (f32[256,256]{1,0:T(8,128)S(1)}, f32[256,256]{1,0:T(8,128)S(1)}, u32[]{:S(2)}, u32[]{:S(2)}) collective-permute-start(f32[256,256]{1,0:T(8,128)S(1)} %maximum_select_fusion.1), channel_id=1, source_target_pairs={{0,4},{4,0},{8,12},{12,8},{16,20},{20,16},{24,28},{28,24},{32,36},... | collective-permute-start | bytes 786440 | tf_op jit(solution)/shard_map/ppermute | solution.py:20
  240.4 1.5 fusion.58
  (122 shorter events, 20.5 us)
Async XLA Ops:
  0.6 80.3 %copy-start = (bf16[1,128,1024]{2,1,0:T(8,128)(2,1)S(1)}, bf16[1,128,1024]{2,1,0:T(8,128)(2,1)}, u32[]{:S(2)}) copy-start(bf16[1,128,1024]{2,1,0:T(8,128)(2,1)} %param.7) | copy-start | bytes 786436
  3.0 29.0 %collective-permute-start = (bf16[256,1280]{1,0:T(8,128)(2,1)S(1)}, bf16[256,1280]{1,0:T(8,128)(2,1)S(1)}, u32[]{:S(2)}, u32[]{:S(2)}) collective-permute-start(bf16[256,1280]{1,0:T(8,128)(2,1)S(1)} %get-tuple-element.3), channel_id=1, source_target_pairs={{1,0},{2,1},{3,2},{8,3},{5,4},{6,5},{7,6},{12,7},{9,8},{10,9},{11,... | collective-permute-start | bytes 1966088 | tf_op jit(solution)/shard_map/ppermute | solution.py:133
  14.5 29.9 %collective-permute-start.3 = (bf16[256,1280]{1,0:T(8,128)(2,1)S(1)}, bf16[256,1280]{1,0:T(8,128)(2,1)S(1)}, u32[]{:S(2)}, u32[]{:S(2)}) collective-permute-start(bf16[256,1280]{1,0:T(8,128)(2,1)S(1)} %get-tuple-element.3), channel_id=1, source_target_pairs={{11,0},{0,1},{1,2},{2,3},{15,4},{4,5},{5,6},{6,7},{3,8},{8,9},{9,1... | collective-permute-start | bytes 1966088 | tf_op jit(solution)/shard_map/ppermute | solution.py:133
  16.4 27.0 %collective-permute-start.2 = (bf16[256,640]{1,0:T(8,128)(2,1)S(1)}, bf16[256,640]{1,0:T(8,128)(2,1)S(1)}, u32[]{:S(2)}, u32[]{:S(2)}) collective-permute-start(bf16[256,640]{1,0:T(8,128)(2,1)S(1)} %get-tuple-element.11), channel_id=1, source_target_pairs={{10,0},{11,1},{0,2},{1,3},{14,4},{15,5},{4,6},{5,7},{2,8},{3,9},{8... | collective-permute-start | bytes 983048 | tf_op jit(solution)/shard_map/ppermute | solution.py:133
  18.4 25.1 %collective-permute-start.1 = (bf16[256,640]{1,0:T(8,128)(2,1)S(1)}, bf16[256,640]{1,0:T(8,128)(2,1)S(1)}, u32[]{:S(2)}, u32[]{:S(2)}) collective-permute-start(bf16[256,640]{1,0:T(8,128)(2,1)S(1)} %get-tuple-element.10), channel_id=1, source_target_pairs={{2,0},{3,1},{8,2},{9,3},{6,4},{7,5},{12,6},{13,7},{10,8},{11,9},{0... | collective-permute-start | bytes 983048 | tf_op jit(solution)/shard_map/ppermute | solution.py:133
  48.9 6.5 %copy-start.19 = (bf16[1,128,1024]{2,1,0:T(8,128)(2,1)S(1)}, bf16[1,128,1024]{2,1,0:T(8,128)(2,1)}, u32[]{:S(2)}) copy-start(bf16[1,128,1024]{2,1,0:T(8,128)(2,1)} %param.6) | copy-start | bytes 786436
  50.8 8.5 %collective-permute-start.4 = (bf16[1024,1280]{1,0:T(8,128)(2,1)S(1)}, bf16[1024,1280]{1,0:T(8,128)(2,1)}, u32[]{:S(2)}, u32[]{:S(2)}) collective-permute-start(bf16[1024,1280]{1,0:T(8,128)(2,1)S(1)} %constant_dynamic-slice_fusion), channel_id=1, source_target_pairs={{0,4},{4,0},{8,12},{12,8},{16,20},{20,16},{24,28},{28,24},{32,36},... | collective-permute-start | bytes 7864328 | tf_op jit(solution)/shard_map/ppermute | solution.py:20
  63.7 18.0 %copy-start.1 = (bf16[1024,512]{1,0:T(8,128)(2,1)}, bf16[1024,512]{1,0:T(8,128)(2,1)S(1)}, u32[]{:S(2)}) copy-start(bf16[1024,512]{1,0:T(8,128)(2,1)S(1)} %pad_maximum_fusion) | copy-start | bytes 3145732
  64.0 19.1 %collective-permute-start.5 = (bf16[128,512]{1,0:T(8,128)(2,1)S(1)}, bf16[128,512]{1,0:T(8,128)(2,1)S(1)}, u32[]{:S(2)}, u32[]{:S(2)}) collective-permute-start(bf16[128,512]{1,0:T(8,128)(2,1)S(1)} %fusion.75), channel_id=1, source_target_pairs={{0,16},{4,20},{8,24},{12,28},{16,32},{20,36},{24,40},{28,44},{32,4... | collective-permute-start | bytes 393224 | tf_op jit(solution)/shard_map/ppermute | solution.py:15
  67.1 16.0 %collective-permute-start.6 = (bf16[128,512]{1,0:T(8,128)(2,1)S(1)}, bf16[128,512]{1,0:T(8,128)(2,1)S(1)}, u32[]{:S(2)}, u32[]{:S(2)}) collective-permute-start(bf16[128,512]{1,0:T(8,128)(2,1)S(1)} %fusion.75), channel_id=1, source_target_pairs={{0,12},{4,16},{8,20},{12,24},{16,28},{20,32},{24,36},{28,40},{32,4... | collective-permute-start | bytes 393224 | tf_op jit(solution)/shard_map/ppermute | solution.py:15
  70.8 12.4 %collective-permute-start.7 = (bf16[128,512]{1,0:T(8,128)(2,1)S(1)}, bf16[128,512]{1,0:T(8,128)(2,1)S(1)}, u32[]{:S(2)}, u32[]{:S(2)}) collective-permute-start(bf16[128,512]{1,0:T(8,128)(2,1)S(1)} %fusion.75), channel_id=1, source_target_pairs={{0,8},{4,12},{8,16},{12,20},{16,24},{20,28},{24,32},{28,36},{32,40... | collective-permute-start | bytes 393224 | tf_op jit(solution)/shard_map/ppermute | solution.py:15
  73.9 11.7 %collective-permute-start.8 = (bf16[128,512]{1,0:T(8,128)(2,1)S(1)}, bf16[128,512]{1,0:T(8,128)(2,1)S(1)}, u32[]{:S(2)}, u32[]{:S(2)}) collective-permute-start(bf16[128,512]{1,0:T(8,128)(2,1)S(1)} %fusion.75), channel_id=1, source_target_pairs={{0,4},{4,8},{8,12},{12,16},{16,20},{20,24},{24,28},{28,32},{32,36}... | collective-permute-start | bytes 393224 | tf_op jit(solution)/shard_map/ppermute | solution.py:15
  85.6 19.2 %copy-start.4 = (bf16[640,512]{1,0:T(8,128)(2,1)}, bf16[640,512]{1,0:T(8,128)(2,1)S(1)}, u32[]{:S(2)}) copy-start(bf16[640,512]{1,0:T(8,128)(2,1)S(1)} %constant_dynamic-update-slice_fusion.6) | copy-start | bytes 1966084
  97.1 2.2 copy-start.23
  99.3 0.8 copy-start.27
  99.6 1.4 copy-start.15
  100.1 0.8 copy-start.6
  100.1 1.0 copy-start.22
  101.1 1.3 copy-start.14
  101.9 3.4 %copy-start.8 = (bf16[4,128,640]{1,2,0:T(8,128)(2,1)}, bf16[4,128,640]{1,2,0:T(8,128)(2,1)S(1)}, u32[]{:S(2)}) copy-start(bf16[4,128,640]{1,2,0:T(8,128)(2,1)S(1)} %fusion.43) | copy-start | bytes 1966084
  101.9 1.0 copy-start.21
  102.5 1.3 copy-start.13
  103.5 2.1 copy-start.10
  103.5 0.9 copy-start.20
  104.0 1.3 copy-start.26
  104.8 0.8 copy-start.25
  104.8 1.1 copy-start.24
  105.3 1.0 copy-start.11
  107.6 6.0 %copy-start.18 = (bf16[1,128,1024]{1,2,0:T(8,128)(2,1)S(1)}, bf16[1,128,1024]{1,2,0:T(8,128)(2,1)}, u32[]{:S(2)}) copy-start(bf16[1,128,1024]{1,2,0:T(8,128)(2,1)} %copy.104) | copy-start | bytes 786436
  107.8 5.9 %collective-permute-start.12 = (bf16[128,512]{0,1:T(8,128)(2,1)S(1)}, bf16[128,512]{0,1:T(8,128)(2,1)S(1)}, u32[]{:S(2)}, u32[]{:S(2)}) collective-permute-start(bf16[128,512]{0,1:T(8,128)(2,1)S(1)} %get-tuple-element.7), channel_id=1, source_target_pairs={{16,0},{20,4},{24,8},{28,12},{32,16},{36,20},{40,24},{44,28},{48,3... | collective-permute-start | bytes 393224 | tf_op jit(solution)/shard_map/ppermute | solution.py:15
  109.1 9.5 %collective-permute-start.11 = (bf16[128,512]{0,1:T(8,128)(2,1)S(1)}, bf16[128,512]{0,1:T(8,128)(2,1)S(1)}, u32[]{:S(2)}, u32[]{:S(2)}) collective-permute-start(bf16[128,512]{0,1:T(8,128)(2,1)S(1)} %get-tuple-element.8), channel_id=1, source_target_pairs={{12,0},{16,4},{20,8},{24,12},{28,16},{32,20},{36,24},{40,28},{44,3... | collective-permute-start | bytes 393224 | tf_op jit(solution)/shard_map/ppermute | solution.py:15
  110.4 9.9 %collective-permute-start.10 = (bf16[128,512]{0,1:T(8,128)(2,1)S(1)}, bf16[128,512]{0,1:T(8,128)(2,1)S(1)}, u32[]{:S(2)}, u32[]{:S(2)}) collective-permute-start(bf16[128,512]{0,1:T(8,128)(2,1)S(1)} %get-tuple-element.9), channel_id=1, source_target_pairs={{8,0},{12,4},{16,8},{20,12},{24,16},{28,20},{32,24},{36,28},{40,32... | collective-permute-start | bytes 393224 | tf_op jit(solution)/shard_map/ppermute | solution.py:15
  111.7 11.6 %collective-permute-start.9 = (bf16[128,512]{0,1:T(8,128)(2,1)S(1)}, bf16[128,512]{0,1:T(8,128)(2,1)S(1)}, u32[]{:S(2)}, u32[]{:S(2)}) collective-permute-start(bf16[128,512]{0,1:T(8,128)(2,1)S(1)} %get-tuple-element.6), channel_id=1, source_target_pairs={{4,0},{8,4},{12,8},{16,12},{20,16},{24,20},{28,24},{32,28},{36,32}... | collective-permute-start | bytes 393224 | tf_op jit(solution)/shard_map/ppermute | solution.py:15
  123.4 7.7 %copy-start.16 = (bf16[128,512]{0,1:T(8,128)(2,1)}, bf16[128,512]{0,1:T(8,128)(2,1)S(1)}, u32[]{:S(2)}) copy-start(bf16[128,512]{0,1:T(8,128)(2,1)S(1)} %fusion.95) | copy-start | bytes 393220
  124.7 4.9 %collective-permute-start.13 = (f32[1024,256]{1,0:T(8,128)}, f32[1024,256]{1,0:T(8,128)}, u32[]{:S(2)}, u32[]{:S(2)}) collective-permute-start(f32[1024,256]{1,0:T(8,128)} %fusion.106), channel_id=1, source_target_pairs={{0,4},{4,0},{8,12},{12,8},{16,20},{20,16},{24,28},{28,24},{32,36},... | collective-permute-start | bytes 3145736 | tf_op jit(solution)/shard_map/ppermute | solution.py:20
  131.1 1.0 copy-start.3
  132.1 16.8 %collective-permute-start.14 = (bf16[512,256]{1,0:T(8,128)(2,1)S(1)}, bf16[512,256]{1,0:T(8,128)(2,1)}, u32[]{:S(2)}, u32[]{:S(2)}) collective-permute-start(bf16[512,256]{1,0:T(8,128)(2,1)S(1)} %slice.279), channel_id=1, source_target_pairs={{0,1},{1,0},{2,3},{3,2},{4,5},{5,4},{6,7},{7,6},{8,9},{9,8},{10,11... | collective-permute-start | bytes 786440 | tf_op jit(solution)/shard_map/ppermute | solution.py:20
  150.8 10.3 %collective-permute-start.15 = (bf16[256,256]{1,0:T(8,128)(2,1)}, bf16[256,256]{1,0:T(8,128)(2,1)S(1)}, u32[]{:S(2)}, u32[]{:S(2)}) collective-permute-start(bf16[256,256]{1,0:T(8,128)(2,1)} %select_convert_fusion), channel_id=1, source_target_pairs={{0,2},{1,3},{2,0},{3,1},{4,6},{5,7},{6,4},{7,5},{8,10},{9,11},{10,... | collective-permute-start | bytes 393224 | tf_op jit(solution)/shard_map/ppermute | solution.py:20
  161.1 0.7 copy-start.12
  161.8 36.1 %copy-start.5 = (bf16[640,512]{1,0:T(8,128)(2,1)S(1)}, bf16[640,512]{1,0:T(8,128)(2,1)}, u32[]{:S(2)}) copy-start(bf16[640,512]{1,0:T(8,128)(2,1)} %copy-done.4) | copy-start | bytes 1966084
  162.4 9.1 %collective-permute-start.16 = (f32[128,256]{1,0:T(8,128)}, f32[128,256]{1,0:T(8,128)}, u32[]{:S(2)}, u32[]{:S(2)}) collective-permute-start(f32[128,256]{1,0:T(8,128)} %slice_select_fusion), channel_id=1, source_target_pairs={{0,16},{4,20},{8,24},{12,28},{16,0},{20,4},{24,8},{28,12},{32,48},... | collective-permute-start | bytes 393224 | tf_op jit(solution)/shard_map/ppermute | solution.py:20
  172.6 9.9 %collective-permute-start.17 = (f32[64,256]{1,0:T(8,128)S(1)}, f32[64,256]{1,0:T(8,128)S(1)}, u32[]{:S(2)}, u32[]{:S(2)}) collective-permute-start(f32[64,256]{1,0:T(8,128)S(1)} %slice_select_fusion.1), channel_id=1, source_target_pairs={{0,64},{4,68},{8,72},{12,76},{16,80},{20,84},{24,88},{28,92},{32,9... | collective-permute-start | bytes 196616 | tf_op jit(solution)/shard_map/ppermute | solution.py:20
  183.1 9.2 %collective-permute-start.18 = (f32[64,256]{1,0:T(8,128)}, f32[64,256]{1,0:T(8,128)}, u32[]{:S(2)}, u32[]{:S(2)}) collective-permute-start(f32[64,256]{1,0:T(8,128)} %select_add_fusion.1), channel_id=1, source_target_pairs={{0,8},{4,12},{8,0},{12,4},{16,24},{20,28},{24,16},{28,20},{32,40},... | collective-permute-start | bytes 196616 | tf_op jit(solution)/shard_map/ppermute | solution.py:20
  187.3 27.7 %copy-start.9 = (bf16[4,128,640]{1,2,0:T(8,128)(2,1)S(1)}, bf16[4,128,640]{1,2,0:T(8,128)(2,1)}, u32[]{:S(2)}) copy-start(bf16[4,128,640]{1,2,0:T(8,128)(2,1)} %copy-done.8) | copy-start | bytes 1966084
  193.2 6.5 %collective-permute-start.19 = (f32[64,256]{1,0:T(8,128)S(1)}, f32[64,256]{1,0:T(8,128)S(1)}, u32[]{:S(2)}, u32[]{:S(2)}) collective-permute-start(f32[64,256]{1,0:T(8,128)S(1)} %add.124), channel_id=1, source_target_pairs={{0,32},{4,36},{8,40},{12,44},{16,48},{20,52},{24,56},{28,60},{32,0... | collective-permute-start | bytes 196616 | tf_op jit(solution)/shard_map/ppermute | solution.py:20
  199.3 19.8 %copy-start.7 = (bf16[4,128,640]{1,2,0:T(8,128)(2,1)S(1)}, bf16[4,128,640]{1,2,0:T(8,128)(2,1)}, u32[]{:S(2)}) copy-start(bf16[4,128,640]{1,2,0:T(8,128)(2,1)} %copy-done.6) | copy-start | bytes 1966084
  199.7 6.5 %collective-permute-start.20 = (f32[64,256]{1,0:T(8,128)S(1)}, f32[64,256]{1,0:T(8,128)S(1)}, u32[]{:S(2)}, u32[]{:S(2)}) collective-permute-start(f32[64,256]{1,0:T(8,128)S(1)} %add.125), channel_id=1, source_target_pairs={{0,128},{4,132},{8,136},{12,140},{16,144},{20,148},{24,152},{28,15... | collective-permute-start | bytes 196616 | tf_op jit(solution)/shard_map/ppermute | solution.py:20
  206.0 20.1 %copy-start.2 = (bf16[1024,512]{1,0:T(8,128)(2,1)S(1)}, bf16[1024,512]{1,0:T(8,128)(2,1)}, u32[]{:S(2)}) copy-start(bf16[1024,512]{1,0:T(8,128)(2,1)} %copy-done.1) | copy-start | bytes 3145732
  206.0 20.1 %copy-start.17 = (bf16[128,512]{0,1:T(8,128)(2,1)S(1)}, bf16[128,512]{0,1:T(8,128)(2,1)}, u32[]{:S(2)}) copy-start(bf16[128,512]{0,1:T(8,128)(2,1)} %copy-done.16) | copy-start | bytes 393220
  206.3 10.9 %collective-permute-start.21 = (f32[64,256]{1,0:T(8,128)S(1)}, f32[64,256]{1,0:T(8,128)S(1)}, u32[]{:S(2)}, u32[]{:S(2)}) collective-permute-start(f32[64,256]{1,0:T(8,128)S(1)} %add.126), channel_id=1, source_target_pairs={{0,256},{4,260},{8,264},{12,268},{16,272},{20,276},{24,280},{28,28... | collective-permute-start | bytes 196616 | tf_op jit(solution)/shard_map/ppermute | solution.py:20
  217.2 5.0 %collective-permute-start.22 = (f32[64,256]{1,0:T(8,128)S(1)}, f32[64,256]{1,0:T(8,128)S(1)}, u32[]{:S(2)}, u32[]{:S(2)}) collective-permute-start(f32[64,256]{1,0:T(8,128)S(1)} %add.127), channel_id=1, source_target_pairs={{0,64},{4,68},{8,72},{12,76},{16,80},{20,84},{24,88},{28,92},{32,9... | collective-permute-start | bytes 196616 | tf_op jit(solution)/shard_map/ppermute | solution.py:20
  222.2 6.2 %collective-permute-start.23 = (f32[128,256]{1,0:T(8,128)S(1)}, f32[128,256]{1,0:T(8,128)S(1)}, u32[]{:S(2)}, u32[]{:S(2)}) collective-permute-start(f32[128,256]{1,0:T(8,128)S(1)} %maximum_select_fusion.2), channel_id=1, source_target_pairs={{0,16},{4,20},{8,24},{12,28},{16,0},{20,4},{24,8},{28,12},{32,48},... | collective-permute-start | bytes 393224 | tf_op jit(solution)/shard_map/ppermute | solution.py:20
  228.4 13.5 %collective-permute-start.24 = (f32[256,256]{1,0:T(8,128)S(1)}, f32[256,256]{1,0:T(8,128)S(1)}, u32[]{:S(2)}, u32[]{:S(2)}) collective-permute-start(f32[256,256]{1,0:T(8,128)S(1)} %maximum_select_fusion.1), channel_id=1, source_target_pairs={{0,4},{4,0},{8,12},{12,8},{16,20},{20,16},{24,28},{28,24},{32,36},... | collective-permute-start | bytes 786440 | tf_op jit(solution)/shard_map/ppermute | solution.py:20

commit v10 on v9

--- a/solution.py
+++ b/solution.py
@@ -136,7 +136,7 @@
 def ring_gather(block):
     stream_count = lax.axis_size("stream")
     if stream_count != 4 or lax.axis_size("tm") % 4 or block.shape[1] % 256:
-        return lax.all_gather(block, "stream", axis=0, tiled=True)
+        return lax.all_gather(block, "stream", axis=0, tiled=True), 0
     rows, width = block.shape
     stream_index = lax.axis_index("stream")
     split = width // 2
@@ -144,9 +144,13 @@
         [ring_pull(block[:, :split], 2), ring_pull(block[:, split:], -2)], axis=1
     )
     stacked = jnp.concatenate([block, ring_pull(block, 1), two_away, ring_pull(block, -1)], axis=0)
-    doubled = jnp.concatenate([stacked, stacked], axis=0)
-    start = ((stream_count - stream_index) % stream_count) * rows
-    return lax.dynamic_slice_in_dim(doubled, start, stream_count * rows, 0)
+    return stacked, stream_index
+
+
+def rotate_cols(value, blocks, shift):
+    width = value.shape[1] // blocks
+    doubled = jnp.concatenate([value, value], axis=1)
+    return lax.dynamic_slice_in_dim(doubled, (shift % blocks) * width, value.shape[1], 1)
 
 
 def contract_last(left, right):
@@ -178,23 +182,30 @@
     if lax.axis_size("tm") % 2 == 0 and weights_local.shape[1] % 256 == 0:
         half_width = weights_local.shape[1] // 2
         core = lax.axis_index("tm") % 2
-        mine = ring_gather(lax.dynamic_slice_in_dim(weights_local, core * half_width, half_width, 1))
+        mine, rotation = ring_gather(
+            lax.dynamic_slice_in_dim(weights_local, core * half_width, half_width, 1)
+        )
         other = xor_swap(mine, "tm", 0)
         weights_full = jnp.concatenate(
             [jnp.where(core == 0, mine, other), jnp.where(core == 0, other, mine)], axis=1
         )
     else:
         weights_full = lax.all_gather(weights_local, "stream", axis=0, tiled=True)
+        rotation = 0
+    stream_count = lax.axis_size("stream")
+    rotated_rows = rotate_cols(record_rows, stream_count, rotation)
     query_full = weights_full[:, :query_width]
     keyval_full = weights_full[:, query_width : query_width + keyval_width]
     output_full = weights_full[:, query_width + keyval_width :]
-    queries = jnp.dot(record_rows, query_full, preferred_element_type=jnp.float32).astype(
+    queries = jnp.dot(rotated_rows, query_full, preferred_element_type=jnp.float32).astype(
         jnp.bfloat16
     )
-    keyvals = jnp.dot(record_rows, keyval_full, preferred_element_type=jnp.float32).astype(
+    keyvals = jnp.dot(rotated_rows, keyval_full, preferred_element_type=jnp.float32).astype(
         jnp.bfloat16
     )
-    attn_grad = contract_last(outer_grad, output_full).astype(jnp.bfloat16)
+    attn_grad = rotate_cols(
+        contract_last(outer_grad, output_full).astype(jnp.bfloat16), stream_count, -rotation
+    )
     earlier = [shifted(keyvals, "tm", offset) for offset in range(REACH, 0, -1)]
     window_keyvals = jnp.concatenate(earlier + [keyvals], axis=0)
     key_parts = []
@@ -278,7 +289,7 @@
     input_grad = contract_last(query_grad_all, query_full) + contract_last(
         keyval_grads, keyval_full
     )
-    input_grad = input_grad.astype(jnp.bfloat16)
+    input_grad = rotate_cols(input_grad.astype(jnp.bfloat16), stream_count, -rotation)
     weight_grad = grad_sum((record_rows, keyval_grads))
     return (input_grad[None], weight_grad)
 

time: 244 us -> 247 us (1.012)
  other arithmetic: 17.3 us -> 24.3 us
  starting transfers between devices: 116 us -> 110 us
    ppermute x13, starting transfers between devices: 72.9 us -> 63.9 us  [xor_swap(): lax.ppermute(value, axis, [(source, source ^ 1 << bit) for source in rang...]
    concatenate x0 -> x3, other arithmetic: none -> 8.26 us  [the longest x1 5.83 us: ring_gather(): jnp.concatenate([block, ring_pull(block, 1), two_away, ring_pull(block, -...]
    unnamed x3 -> x0, other arithmetic: 4.09 us -> none
    ppermute x8, starting transfers between devices: 22.7 us -> 26.8 us  [shifted(): lax.ppermute(value, axis, [(source, source + steps) for source in range(l...]
    ppermute x4, waiting for transfers between devices: 18.7 us -> 21.2 us  [ring_pull(): return lax.ppermute(value, ('tm', 'stream'), pairs)]
    unnamed x65 -> x69, local copies, waits for them, and re-layouts: 8.63 us -> 10.4 us
  transfers between devices with their start and end apart: 25 -> 25, of which waited for: 18 -> 17; matrix products, arithmetic and copies ran while one was open for 5% -> 7% of each run, Pallas kernels for 0% -> 0%
where the time goes in v10:
time: 247 us; the launch traced here: 246 us
  starting transfers between devices  110 us (45%)
  waiting for transfers between devices  67 us (27%)
  matrix products  26.5 us (11%)
  other arithmetic  24.3 us (10%)
  local copies, waits for them, and re-layouts  15.2 us (6%)
    ppermute x13, starting transfers between devices, xor_swap(): lax.ppermute(value, axis, [(source, source ^ 1 << bit) for source in rang...  63.9 us
    ppermute x13, waiting for transfers between devices, xor_swap(): lax.ppermute(value, axis, [(source, source ^ 1 << bit) for source in rang...  35.4 us
    ppermute x8, starting transfers between devices, shifted(): lax.ppermute(value, axis, [(source, source + steps) for source in range(l...  26.8 us
    ppermute x4, waiting for transfers between devices, ring_pull(): return lax.ppermute(value, ('tm', 'stream'), pairs)  21.2 us
    ppermute x4, starting transfers between devices, ring_pull(): return lax.ppermute(value, ('tm', 'stream'), pairs)  19.6 us
    sub x4, matrix products, per_device(): terms = jnp.where(allowed, jnp.exp(masked - row_max), 0.0)  11.5 us
    unnamed x69, local copies, waits for them, and re-layouts  10.4 us
    ppermute x8, waiting for transfers between devices, shifted(): lax.ppermute(value, axis, [(source, source + steps) for source in range(l...  10.4 us
  transfers between devices with their start and end apart: 25, of which 17 were waited for; matrix products, arithmetic and copies ran while one was open for 7% of the time, Pallas kernels for 0%

profile of v10, /device:TPU:1, one launch (start us, length us, event | category | flops | bytes accessed | tf_op | source)
XLA Modules:
  0.0 245.6 jit_solution(17695847444989835455)
XLA Ops:
  0.7 1.5 fusion.86
  2.2 4.8 %collective-permute-start.3 = (bf16[256,1280]{1,0:T(8,128)(2,1)S(1)}, bf16[256,1280]{1,0:T(8,128)(2,1)S(1)}, u32[]{:S(2)}, u32[]{:S(2)}) collective-permute-start(bf16[256,1280]{1,0:T(8,128)(2,1)S(1)} %fusion.86), channel_id=1, source_target_pairs={{11,0},{0,1},{1,2},{2,3},{15,4},{4,5},{5,6},{6,7},{3,8},{8,9},{9,1... | collective-permute-start | bytes 1966088 | tf_op jit(solution)/shard_map/ppermute | solution.py:133
  7.0 8.6 %collective-permute-start = (bf16[256,1280]{1,0:T(8,128)(2,1)S(1)}, bf16[256,1280]{1,0:T(8,128)(2,1)S(1)}, u32[]{:S(2)}, u32[]{:S(2)}) collective-permute-start(bf16[256,1280]{1,0:T(8,128)(2,1)S(1)} %fusion.86), channel_id=1, source_target_pairs={{1,0},{2,1},{3,2},{8,3},{5,4},{6,5},{7,6},{12,7},{9,8},{10,9},{11,... | collective-permute-start | bytes 1966088 | tf_op jit(solution)/shard_map/ppermute | solution.py:133
  15.7 3.4 %collective-permute-start.1 = (bf16[256,640]{1,0:T(8,128)(2,1)S(1)}, bf16[256,640]{1,0:T(8,128)(2,1)S(1)}, u32[]{:S(2)}, u32[]{:S(2)}) collective-permute-start(bf16[256,640]{1,0:T(8,128)(2,1)S(1)} %get-tuple-element.8), channel_id=1, source_target_pairs={{2,0},{3,1},{8,2},{9,3},{6,4},{7,5},{12,6},{13,7},{10,8},{11,9},{0... | collective-permute-start | bytes 983048 | tf_op jit(solution)/shard_map/ppermute | solution.py:133
  19.0 2.8 %collective-permute-start.2 = (bf16[256,640]{1,0:T(8,128)(2,1)S(1)}, bf16[256,640]{1,0:T(8,128)(2,1)S(1)}, u32[]{:S(2)}, u32[]{:S(2)}) collective-permute-start(bf16[256,640]{1,0:T(8,128)(2,1)S(1)} %get-tuple-element.9), channel_id=1, source_target_pairs={{10,0},{11,1},{0,2},{1,3},{14,4},{15,5},{4,6},{5,7},{2,8},{3,9},{8... | collective-permute-start | bytes 983048 | tf_op jit(solution)/shard_map/ppermute | solution.py:133
  21.9 21.2 %collective-permute-done.1 = bf16[256,640]{1,0:T(8,128)(2,1)S(1)} collective-permute-done((bf16[256,640]{1,0:T(8,128)(2,1)S(1)}, bf16[256,640]{1,0:T(8,128)(2,1)S(1)}, u32[]{:S(2)}, u32[]{:S(2)}) %collective-permute-start.1) | collective-permute-done | bytes 327712 | tf_op jit(solution)/shard_map/ppermute | solution.py:133
  43.1 5.8 %pad_maximum_fusion = bf16[1024,1280]{1,0:T(8,128)(2,1)S(1)} fusion(bf16[256,1280]{1,0:T(8,128)(2,1)S(1)} %collective-permute-done.3, bf16[256,640]{1,0:T(8,128)(2,1)S(1)} %collective-permute-done.2, bf16[256,640]{1,0:T(8,128)(2,1)S(1)} %collective-permute-done.1, bf16[256,1280]{1,0:T(8,128)(2,1)S(1)} %collective-permute-done, bf16[256,1280]{1,0:T(8,128)(2,1)S(1)} %fusion.86), kind=kLoop, calls=%fused_computation.4 | loop fusion | flops 13107200 | bytes 5242880 | tf_op jit(solution)/shard_map/concatenate | solution.py:146
  49.0 3.4 %collective-permute-start.4 = (bf16[1024,1280]{1,0:T(8,128)(2,1)S(1)}, bf16[1024,1280]{1,0:T(8,128)(2,1)}, u32[]{:S(2)}, u32[]{:S(2)}) collective-permute-start(bf16[1024,1280]{1,0:T(8,128)(2,1)S(1)} %pad_maximum_fusion), channel_id=1, source_target_pairs={{0,4},{4,0},{8,12},{12,8},{16,20},{20,16},{24,28},{28,24},{32,36},... | collective-permute-start | bytes 7864328 | tf_op jit(solution)/shard_map/ppermute | solution.py:20
  53.1 1.8 copy.120
  54.9 0.9 fusion.90
  55.9 1.2 collective-permute-done.4
  57.1 5.5 %broadcast_select_fusion.1 = (bf16[1024,1280]{1,0:T(8,128)(2,1)S(1)}, bf16[1024,1280]{1,0:T(8,128)(2,1)S(1)}) fusion(bf16[1024,1280]{1,0:T(8,128)(2,1)} %collective-permute-done.4, pred[]{:T(512)S(6)} %eq.27, bf16[256,1280]{1,0:T(8,128)(2,1)} %copy-done.12, bf16[256,640]{1,0:T(8,128)(2,1)} %copy-done.19, bf16[256,640]{1,0:T(8,128)(2,1)} %copy-done.18, ...), kind=kLoop, calls=%fused_computation.6 | loop fusion | flops 15728640 | bytes 10485761 | tf_op jit(solution)/shard_map/jit(_where)/select_n | solution.py:190
  63.5 1.0 convolution_convert_fusion
  64.5 6.4 %collective-permute-start.8 = (bf16[128,512]{1,0:T(8,128)(2,1)}, bf16[128,512]{1,0:T(8,128)(2,1)}, u32[]{:S(2)}, u32[]{:S(2)}) collective-permute-start(bf16[128,512]{1,0:T(8,128)(2,1)} %convolution_convert_fusion), channel_id=1, source_target_pairs={{0,4},{4,8},{8,12},{12,16},{16,20},{20,24},{24,28},{28,32},{32,36}... | collective-permute-start | bytes 393224 | tf_op jit(solution)/shard_map/ppermute | solution.py:15
  70.9 4.6 %collective-permute-start.7 = (bf16[128,512]{1,0:T(8,128)(2,1)}, bf16[128,512]{1,0:T(8,128)(2,1)}, u32[]{:S(2)}, u32[]{:S(2)}) collective-permute-start(bf16[128,512]{1,0:T(8,128)(2,1)} %convolution_convert_fusion), channel_id=1, source_target_pairs={{0,8},{4,12},{8,16},{12,20},{16,24},{20,28},{24,32},{28,36},{32,40... | collective-permute-start | bytes 393224 | tf_op jit(solution)/shard_map/ppermute | solution.py:15
  75.5 1.9 collective-permute-start.6
  77.5 3.1 %collective-permute-start.5 = (bf16[128,512]{1,0:T(8,128)(2,1)}, bf16[128,512]{1,0:T(8,128)(2,1)}, u32[]{:S(2)}, u32[]{:S(2)}) collective-permute-start(bf16[128,512]{1,0:T(8,128)(2,1)} %convolution_convert_fusion), channel_id=1, source_target_pairs={{0,16},{4,20},{8,24},{12,28},{16,32},{20,36},{24,40},{28,44},{32,4... | collective-permute-start | bytes 393224 | tf_op jit(solution)/shard_map/ppermute | solution.py:15
  81.8 0.9 fusion.93
  86.4 0.9 constant_dynamic-update-slice_fusion.4
  87.3 0.9 constant_dynamic-update-slice_fusion.3
  88.2 0.9 constant_dynamic-update-slice_fusion.2
  89.2 0.9 constant_dynamic-update-slice_fusion.1
  90.1 0.9 constant_dynamic-update-slice_fusion
  91.0 2.9 %fusion.135 = (f32[4,128]{1,0:T(4,128)S(1)}, f32[4,128,640]{1,2,0:T(8,128)}) fusion(bf16[128,4,64]{0,2,1:T(8,128)(2,1)} %bitcast.290, pred[128,640]{0,1:T(8,128)(4,1)} %fusion.90, bf16[640,512]{1,0:T(8,128)(2,1)S(1)} %constant_dynamic-update-slice_fusion), kind=kOutput, calls=%fused_computation.202 | convolution fusion | flops 43582080 | bytes 1705984 | tf_op jit(solution)/shard_map/sub | solution.py:245
  94.0 2.7 %fusion.137 = (f32[4,128]{1,0:T(4,128)S(1)}, f32[4,128,640]{1,2,0:T(8,128)}) fusion(bf16[128,4,64]{0,2,1:T(8,128)(2,1)} %bitcast.292, pred[128,640]{0,1:T(8,128)(4,1)} %fusion.90, bf16[640,512]{1,0:T(8,128)(2,1)S(1)} %constant_dynamic-update-slice_fusion), kind=kOutput, calls=%fused_computation.204 | convolution fusion | flops 43582080 | bytes 1705984 | tf_op jit(solution)/shard_map/sub | solution.py:245
  96.6 2.7 %fusion.136 = (f32[4,128]{1,0:T(4,128)S(1)}, f32[4,128,640]{1,2,0:T(8,128)}) fusion(bf16[128,4,64]{0,2,1:T(8,128)(2,1)} %bitcast.294, pred[128,640]{0,1:T(8,128)(4,1)} %fusion.90, bf16[640,512]{1,0:T(8,128)(2,1)S(1)} %constant_dynamic-update-slice_fusion), kind=kOutput, calls=%fused_computation.203 | convolution fusion | flops 43582080 | bytes 1705984 | tf_op jit(solution)/shard_map/sub | solution.py:245
  99.3 3.2 %fusion.138 = (f32[4,128]{1,0:T(4,128)}, f32[4,128,640]{1,2,0:T(8,128)}) fusion(bf16[128,4,64]{0,2,1:T(8,128)(2,1)} %bitcast.296, pred[128,640]{0,1:T(8,128)(4,1)} %fusion.90, bf16[640,512]{1,0:T(8,128)(2,1)S(1)} %constant_dynamic-update-slice_fusion), kind=kOutput, calls=%fused_computation.205 | convolution fusion | flops 43582080 | bytes 1705984 | tf_op jit(solution)/shard_map/sub | solution.py:245
  103.3 1.4 divide_convert_fusion.3
  113.2 6.8 %collective-permute-start.9 = (bf16[128,512]{0,1:T(8,128)(2,1)S(1)}, bf16[128,512]{0,1:T(8,128)(2,1)S(1)}, u32[]{:S(2)}, u32[]{:S(2)}) collective-permute-start(bf16[128,512]{0,1:T(8,128)(2,1)S(1)} %get-tuple-element.4), channel_id=1, source_target_pairs={{4,0},{8,4},{12,8},{16,12},{20,16},{24,20},{28,24},{32,28},{36,32}... | collective-permute-start | bytes 393224 | tf_op jit(solution)/shard_map/ppermute | solution.py:15
  120.1 1.3 collective-permute-start.12
  121.4 1.3 collective-permute-start.11
  122.7 1.3 collective-permute-start.10
  124.3 2.8 %collective-permute-done.12 = bf16[128,512]{0,1:T(8,128)(2,1)S(1)} collective-permute-done((bf16[128,512]{0,1:T(8,128)(2,1)S(1)}, bf16[128,512]{0,1:T(8,128)(2,1)S(1)}, u32[]{:S(2)}, u32[]{:S(2)}) %collective-permute-start.12) | collective-permute-done | bytes 131104 | tf_op jit(solution)/shard_map/ppermute | solution.py:15
  127.2 1.3 collective-permute-done.11
  128.4 6.0 %collective-permute-done.10 = bf16[128,512]{0,1:T(8,128)(2,1)S(1)} collective-permute-done((bf16[128,512]{0,1:T(8,128)(2,1)S(1)}, bf16[128,512]{0,1:T(8,128)(2,1)S(1)}, u32[]{:S(2)}, u32[]{:S(2)}) %collective-permute-start.10) | collective-permute-done | bytes 131104 | tf_op jit(solution)/shard_map/ppermute | solution.py:15
  134.5 1.3 fusion.107
  135.7 2.1 collective-permute-start.13
  137.9 2.7 %collective-permute-done.13 = f32[1024,256]{1,0:T(8,128)} collective-permute-done((f32[1024,256]{1,0:T(8,128)}, f32[1024,256]{1,0:T(8,128)}, u32[]{:S(2)}, u32[]{:S(2)}) %collective-permute-start.13) | collective-permute-done | bytes 1048608 | tf_op jit(solution)/shard_map/ppermute | solution.py:20
  140.6 1.5 convolution_add_fusion
  142.2 1.0 copy-done.3
  143.2 4.9 %collective-permute-start.14 = (bf16[512,256]{1,0:T(8,128)(2,1)S(1)}, bf16[512,256]{1,0:T(8,128)(2,1)}, u32[]{:S(2)}, u32[]{:S(2)}) collective-permute-start(bf16[512,256]{1,0:T(8,128)(2,1)S(1)} %slice.267), channel_id=1, source_target_pairs={{0,1},{1,0},{2,3},{3,2},{4,5},{5,4},{6,7},{7,6},{8,9},{9,8},{10,11... | collective-permute-start | bytes 786440 | tf_op jit(solution)/shard_map/ppermute | solution.py:20
  148.0 6.5 %collective-permute-done.14 = bf16[512,256]{1,0:T(8,128)(2,1)} collective-permute-done((bf16[512,256]{1,0:T(8,128)(2,1)S(1)}, bf16[512,256]{1,0:T(8,128)(2,1)}, u32[]{:S(2)}, u32[]{:S(2)}) %collective-permute-start.14) | collective-permute-done | bytes 262176 | tf_op jit(solution)/shard_map/ppermute | solution.py:20
  154.5 1.2 slice_add_fusion
  156.4 7.1 %collective-permute-start.15 = (bf16[256,256]{1,0:T(8,128)(2,1)}, bf16[256,256]{1,0:T(8,128)(2,1)S(1)}, u32[]{:S(2)}, u32[]{:S(2)}) collective-permute-start(bf16[256,256]{1,0:T(8,128)(2,1)} %select_convert_fusion), channel_id=1, source_target_pairs={{0,2},{1,3},{2,0},{3,1},{4,6},{5,7},{6,4},{7,5},{8,10},{9,11},{10,... | collective-permute-start | bytes 393224 | tf_op jit(solution)/shard_map/ppermute | solution.py:20
  163.5 6.9 %collective-permute-done.15 = bf16[256,256]{1,0:T(8,128)(2,1)S(1)} collective-permute-done((bf16[256,256]{1,0:T(8,128)(2,1)}, bf16[256,256]{1,0:T(8,128)(2,1)S(1)}, u32[]{:S(2)}, u32[]{:S(2)}) %collective-permute-start.15) | collective-permute-done | bytes 131104 | tf_op jit(solution)/shard_map/ppermute | solution.py:20
  171.8 3.0 %collective-permute-start.16 = (f32[128,256]{1,0:T(8,128)}, f32[128,256]{1,0:T(8,128)}, u32[]{:S(2)}, u32[]{:S(2)}) collective-permute-start(f32[128,256]{1,0:T(8,128)} %slice_select_fusion), channel_id=1, source_target_pairs={{0,16},{4,20},{8,24},{12,28},{16,0},{20,4},{24,8},{28,12},{32,48},... | collective-permute-start | bytes 393224 | tf_op jit(solution)/shard_map/ppermute | solution.py:20
  174.8 3.7 %collective-permute-done.16 = f32[128,256]{1,0:T(8,128)} collective-permute-done((f32[128,256]{1,0:T(8,128)}, f32[128,256]{1,0:T(8,128)}, u32[]{:S(2)}, u32[]{:S(2)}) %collective-permute-start.16) | collective-permute-done | bytes 131104 | tf_op jit(solution)/shard_map/ppermute | solution.py:20
  178.6 1.1 select_add_fusion
  179.6 4.9 %collective-permute-start.17 = (f32[64,256]{1,0:T(8,128)S(1)}, f32[64,256]{1,0:T(8,128)S(1)}, u32[]{:S(2)}, u32[]{:S(2)}) collective-permute-start(f32[64,256]{1,0:T(8,128)S(1)} %slice_select_fusion.1), channel_id=1, source_target_pairs={{0,64},{4,68},{8,72},{12,76},{16,80},{20,84},{24,88},{28,92},{32,9... | collective-permute-start | bytes 196616 | tf_op jit(solution)/shard_map/ppermute | solution.py:20
  184.5 1.6 collective-permute-done.17
  186.8 5.3 %collective-permute-start.18 = (f32[64,256]{1,0:T(8,128)}, f32[64,256]{1,0:T(8,128)}, u32[]{:S(2)}, u32[]{:S(2)}) collective-permute-start(f32[64,256]{1,0:T(8,128)} %select_add_fusion.1), channel_id=1, source_target_pairs={{0,8},{4,12},{8,0},{12,4},{16,24},{20,28},{24,16},{28,20},{32,40},... | collective-permute-start | bytes 196616 | tf_op jit(solution)/shard_map/ppermute | solution.py:20
  192.2 4.6 %collective-permute-done.18 = f32[64,256]{1,0:T(8,128)} collective-permute-done((f32[64,256]{1,0:T(8,128)}, f32[64,256]{1,0:T(8,128)}, u32[]{:S(2)}, u32[]{:S(2)}) %collective-permute-start.18) | collective-permute-done | bytes 65568 | tf_op jit(solution)/shard_map/ppermute | solution.py:20
  197.6 3.7 %collective-permute-start.19 = (f32[64,256]{1,0:T(8,128)S(1)}, f32[64,256]{1,0:T(8,128)S(1)}, u32[]{:S(2)}, u32[]{:S(2)}) collective-permute-start(f32[64,256]{1,0:T(8,128)S(1)} %add.134), channel_id=1, source_target_pairs={{0,32},{4,36},{8,40},{12,44},{16,48},{20,52},{24,56},{28,60},{32,0... | collective-permute-start | bytes 196616 | tf_op jit(solution)/shard_map/ppermute | solution.py:20
  201.4 1.3 convolution_convert_fusion.7
  202.7 1.4 collective-permute-done.19
  204.2 5.1 %collective-permute-start.20 = (f32[64,256]{1,0:T(8,128)S(1)}, f32[64,256]{1,0:T(8,128)S(1)}, u32[]{:S(2)}, u32[]{:S(2)}) collective-permute-start(f32[64,256]{1,0:T(8,128)S(1)} %add.135), channel_id=1, source_target_pairs={{0,128},{4,132},{8,136},{12,140},{16,144},{20,148},{24,152},{28,15... | collective-permute-start | bytes 196616 | tf_op jit(solution)/shard_map/ppermute | solution.py:20
  209.2 1.3 convolution_convert_fusion.3
  210.9 9.0 %collective-permute-start.21 = (f32[64,256]{1,0:T(8,128)S(1)}, f32[64,256]{1,0:T(8,128)S(1)}, u32[]{:S(2)}, u32[]{:S(2)}) collective-permute-start(f32[64,256]{1,0:T(8,128)S(1)} %add.136), channel_id=1, source_target_pairs={{0,256},{4,260},{8,264},{12,268},{16,272},{20,276},{24,280},{28,28... | collective-permute-start | bytes 196616 | tf_op jit(solution)/shard_map/ppermute | solution.py:20
  220.2 1.3 collective-permute-done.21
  221.5 1.9 collective-permute-start.22
  223.8 3.3 %collective-permute-done.22 = f32[64,256]{1,0:T(8,128)S(1)} collective-permute-done((f32[64,256]{1,0:T(8,128)S(1)}, f32[64,256]{1,0:T(8,128)S(1)}, u32[]{:S(2)}, u32[]{:S(2)}) %collective-permute-start.22) | collective-permute-done | bytes 65568 | tf_op jit(solution)/shard_map/ppermute | solution.py:20
  227.1 3.2 %collective-permute-start.23 = (f32[128,256]{1,0:T(8,128)S(1)}, f32[128,256]{1,0:T(8,128)S(1)}, u32[]{:S(2)}, u32[]{:S(2)}) collective-permute-start(f32[128,256]{1,0:T(8,128)S(1)} %maximum_select_fusion.2), channel_id=1, source_target_pairs={{0,16},{4,20},{8,24},{12,28},{16,0},{20,4},{24,8},{28,12},{32,48},... | collective-permute-start | bytes 393224 | tf_op jit(solution)/shard_map/ppermute | solution.py:20
  230.8 2.0 collective-permute-done.23
  232.8 10.3 %collective-permute-start.24 = (f32[256,256]{1,0:T(8,128)S(1)}, f32[256,256]{1,0:T(8,128)S(1)}, u32[]{:S(2)}, u32[]{:S(2)}) collective-permute-start(f32[256,256]{1,0:T(8,128)S(1)} %maximum_select_fusion.1), channel_id=1, source_target_pairs={{0,4},{4,0},{8,12},{12,8},{16,20},{20,16},{24,28},{28,24},{32,36},... | collective-permute-start | bytes 786440 | tf_op jit(solution)/shard_map/ppermute | solution.py:20
  (129 shorter events, 23.0 us)
Async XLA Ops:
  0.6 80.4 %copy-start = (bf16[1,128,1024]{2,1,0:T(8,128)(2,1)S(1)}, bf16[1,128,1024]{2,1,0:T(8,128)(2,1)}, u32[]{:S(2)}) copy-start(bf16[1,128,1024]{2,1,0:T(8,128)(2,1)} %param.7) | copy-start | bytes 786436
  2.2 40.9 %collective-permute-start.3 = (bf16[256,1280]{1,0:T(8,128)(2,1)S(1)}, bf16[256,1280]{1,0:T(8,128)(2,1)S(1)}, u32[]{:S(2)}, u32[]{:S(2)}) collective-permute-start(bf16[256,1280]{1,0:T(8,128)(2,1)S(1)} %fusion.86), channel_id=1, source_target_pairs={{11,0},{0,1},{1,2},{2,3},{15,4},{4,5},{5,6},{6,7},{3,8},{8,9},{9,1... | collective-permute-start | bytes 1966088 | tf_op jit(solution)/shard_map/ppermute | solution.py:133
  7.0 36.1 %collective-permute-start = (bf16[256,1280]{1,0:T(8,128)(2,1)S(1)}, bf16[256,1280]{1,0:T(8,128)(2,1)S(1)}, u32[]{:S(2)}, u32[]{:S(2)}) collective-permute-start(bf16[256,1280]{1,0:T(8,128)(2,1)S(1)} %fusion.86), channel_id=1, source_target_pairs={{1,0},{2,1},{3,2},{8,3},{5,4},{6,5},{7,6},{12,7},{9,8},{10,9},{11,... | collective-permute-start | bytes 1966088 | tf_op jit(solution)/shard_map/ppermute | solution.py:133
  15.7 27.4 %collective-permute-start.1 = (bf16[256,640]{1,0:T(8,128)(2,1)S(1)}, bf16[256,640]{1,0:T(8,128)(2,1)S(1)}, u32[]{:S(2)}, u32[]{:S(2)}) collective-permute-start(bf16[256,640]{1,0:T(8,128)(2,1)S(1)} %get-tuple-element.8), channel_id=1, source_target_pairs={{2,0},{3,1},{8,2},{9,3},{6,4},{7,5},{12,6},{13,7},{10,8},{11,9},{0... | collective-permute-start | bytes 983048 | tf_op jit(solution)/shard_map/ppermute | solution.py:133
  19.0 24.1 %collective-permute-start.2 = (bf16[256,640]{1,0:T(8,128)(2,1)S(1)}, bf16[256,640]{1,0:T(8,128)(2,1)S(1)}, u32[]{:S(2)}, u32[]{:S(2)}) collective-permute-start(bf16[256,640]{1,0:T(8,128)(2,1)S(1)} %get-tuple-element.9), channel_id=1, source_target_pairs={{10,0},{11,1},{0,2},{1,3},{14,4},{15,5},{4,6},{5,7},{2,8},{3,9},{8... | collective-permute-start | bytes 983048 | tf_op jit(solution)/shard_map/ppermute | solution.py:133
  43.1 5.9 %copy-start.18 = (bf16[256,640]{1,0:T(8,128)(2,1)}, bf16[256,640]{1,0:T(8,128)(2,1)S(1)}, u32[]{:S(2)}) copy-start(bf16[256,640]{1,0:T(8,128)(2,1)S(1)} %collective-permute-done.1) | copy-start | bytes 983044
  43.1 5.9 %copy-start.19 = (bf16[256,640]{1,0:T(8,128)(2,1)}, bf16[256,640]{1,0:T(8,128)(2,1)S(1)}, u32[]{:S(2)}) copy-start(bf16[256,640]{1,0:T(8,128)(2,1)S(1)} %collective-permute-done.2) | copy-start | bytes 983044
  43.1 5.9 %copy-start.12 = (bf16[256,1280]{1,0:T(8,128)(2,1)}, bf16[256,1280]{1,0:T(8,128)(2,1)S(1)}, u32[]{:S(2)}) copy-start(bf16[256,1280]{1,0:T(8,128)(2,1)S(1)} %collective-permute-done.3) | copy-start | bytes 1966084
  43.1 5.9 %copy-start.13 = (bf16[256,1280]{1,0:T(8,128)(2,1)}, bf16[256,1280]{1,0:T(8,128)(2,1)S(1)}, u32[]{:S(2)}) copy-start(bf16[256,1280]{1,0:T(8,128)(2,1)S(1)} %collective-permute-done) | copy-start | bytes 1966084
  49.0 8.1 %collective-permute-start.4 = (bf16[1024,1280]{1,0:T(8,128)(2,1)S(1)}, bf16[1024,1280]{1,0:T(8,128)(2,1)}, u32[]{:S(2)}, u32[]{:S(2)}) collective-permute-start(bf16[1024,1280]{1,0:T(8,128)(2,1)S(1)} %pad_maximum_fusion), channel_id=1, source_target_pairs={{0,4},{4,0},{8,12},{12,8},{16,20},{20,16},{24,28},{28,24},{32,36},... | collective-permute-start | bytes 7864328 | tf_op jit(solution)/shard_map/ppermute | solution.py:20
  62.6 1.0 copy-start.31
  62.7 18.4 %copy-start.1 = (bf16[1024,512]{1,0:T(8,128)(2,1)}, bf16[1024,512]{1,0:T(8,128)(2,1)S(1)}, u32[]{:S(2)}) copy-start(bf16[1024,512]{1,0:T(8,128)(2,1)S(1)} %pad_maximum_fusion.1) | copy-start | bytes 3145732
  64.5 24.7 %collective-permute-start.8 = (bf16[128,512]{1,0:T(8,128)(2,1)}, bf16[128,512]{1,0:T(8,128)(2,1)}, u32[]{:S(2)}, u32[]{:S(2)}) collective-permute-start(bf16[128,512]{1,0:T(8,128)(2,1)} %convolution_convert_fusion), channel_id=1, source_target_pairs={{0,4},{4,8},{8,12},{12,16},{16,20},{20,24},{24,28},{28,32},{32,36}... | collective-permute-start | bytes 393224 | tf_op jit(solution)/shard_map/ppermute | solution.py:15
  70.9 17.3 %collective-permute-start.7 = (bf16[128,512]{1,0:T(8,128)(2,1)}, bf16[128,512]{1,0:T(8,128)(2,1)}, u32[]{:S(2)}, u32[]{:S(2)}) collective-permute-start(bf16[128,512]{1,0:T(8,128)(2,1)} %convolution_convert_fusion), channel_id=1, source_target_pairs={{0,8},{4,12},{8,16},{12,20},{16,24},{20,28},{24,32},{28,36},{32,40... | collective-permute-start | bytes 393224 | tf_op jit(solution)/shard_map/ppermute | solution.py:15
  75.5 11.8 %collective-permute-start.6 = (bf16[128,512]{1,0:T(8,128)(2,1)}, bf16[128,512]{1,0:T(8,128)(2,1)}, u32[]{:S(2)}, u32[]{:S(2)}) collective-permute-start(bf16[128,512]{1,0:T(8,128)(2,1)} %convolution_convert_fusion), channel_id=1, source_target_pairs={{0,12},{4,16},{8,20},{12,24},{16,28},{20,32},{24,36},{28,40},{32,4... | collective-permute-start | bytes 393224 | tf_op jit(solution)/shard_map/ppermute | solution.py:15
  77.5 8.9 %collective-permute-start.5 = (bf16[128,512]{1,0:T(8,128)(2,1)}, bf16[128,512]{1,0:T(8,128)(2,1)}, u32[]{:S(2)}, u32[]{:S(2)}) collective-permute-start(bf16[128,512]{1,0:T(8,128)(2,1)} %convolution_convert_fusion), channel_id=1, source_target_pairs={{0,16},{4,20},{8,24},{12,28},{16,32},{20,36},{24,40},{28,44},{32,4... | collective-permute-start | bytes 393224 | tf_op jit(solution)/shard_map/ppermute | solution.py:15
  91.0 19.2 %copy-start.4 = (bf16[640,512]{1,0:T(8,128)(2,1)}, bf16[640,512]{1,0:T(8,128)(2,1)S(1)}, u32[]{:S(2)}) copy-start(bf16[640,512]{1,0:T(8,128)(2,1)S(1)} %constant_dynamic-update-slice_fusion) | copy-start | bytes 1966084
  102.6 2.2 copy-start.26
  104.7 0.8 copy-start.30
  105.0 1.4 copy-start.17
  105.5 0.8 copy-start.11
  105.5 1.0 copy-start.24
  106.5 1.3 copy-start.16
  107.2 3.9 %copy-start.10 = (bf16[4,128,640]{1,2,0:T(8,128)(2,1)}, bf16[4,128,640]{1,2,0:T(8,128)(2,1)S(1)}, u32[]{:S(2)}) copy-start(bf16[4,128,640]{1,2,0:T(8,128)(2,1)S(1)} %fusion.44) | copy-start | bytes 1966084
  107.2 1.0 copy-start.25
  107.9 1.3 copy-start.15
  108.9 1.8 copy-start.8
  108.9 0.9 copy-start.23
  109.4 1.3 copy-start.29
  110.2 0.8 copy-start.28
  110.2 1.1 copy-start.27
  110.7 1.0 copy-start.6
  113.0 10.9 %copy-start.22 = (bf16[1,128,1024]{1,2,0:T(8,128)(2,1)S(1)}, bf16[1,128,1024]{1,2,0:T(8,128)(2,1)}, u32[]{:S(2)}) copy-start(bf16[1,128,1024]{1,2,0:T(8,128)(2,1)} %copy.120) | copy-start | bytes 786436
  113.2 11.1 %collective-permute-start.9 = (bf16[128,512]{0,1:T(8,128)(2,1)S(1)}, bf16[128,512]{0,1:T(8,128)(2,1)S(1)}, u32[]{:S(2)}, u32[]{:S(2)}) collective-permute-start(bf16[128,512]{0,1:T(8,128)(2,1)S(1)} %get-tuple-element.4), channel_id=1, source_target_pairs={{4,0},{8,4},{12,8},{16,12},{20,16},{24,20},{28,24},{32,28},{36,32}... | collective-permute-start | bytes 393224 | tf_op jit(solution)/shard_map/ppermute | solution.py:15
  120.1 7.1 %collective-permute-start.12 = (bf16[128,512]{0,1:T(8,128)(2,1)S(1)}, bf16[128,512]{0,1:T(8,128)(2,1)S(1)}, u32[]{:S(2)}, u32[]{:S(2)}) collective-permute-start(bf16[128,512]{0,1:T(8,128)(2,1)S(1)} %get-tuple-element.5), channel_id=1, source_target_pairs={{16,0},{20,4},{24,8},{28,12},{32,16},{36,20},{40,24},{44,28},{48,3... | collective-permute-start | bytes 393224 | tf_op jit(solution)/shard_map/ppermute | solution.py:15
  121.4 7.1 %collective-permute-start.11 = (bf16[128,512]{0,1:T(8,128)(2,1)S(1)}, bf16[128,512]{0,1:T(8,128)(2,1)S(1)}, u32[]{:S(2)}, u32[]{:S(2)}) collective-permute-start(bf16[128,512]{0,1:T(8,128)(2,1)S(1)} %get-tuple-element.6), channel_id=1, source_target_pairs={{12,0},{16,4},{20,8},{24,12},{28,16},{32,20},{36,24},{40,28},{44,3... | collective-permute-start | bytes 393224 | tf_op jit(solution)/shard_map/ppermute | solution.py:15
  122.7 11.7 %collective-permute-start.10 = (bf16[128,512]{0,1:T(8,128)(2,1)S(1)}, bf16[128,512]{0,1:T(8,128)(2,1)S(1)}, u32[]{:S(2)}, u32[]{:S(2)}) collective-permute-start(bf16[128,512]{0,1:T(8,128)(2,1)S(1)} %get-tuple-element.7), channel_id=1, source_target_pairs={{8,0},{12,4},{16,8},{20,12},{24,16},{28,20},{32,24},{36,28},{40,32... | collective-permute-start | bytes 393224 | tf_op jit(solution)/shard_map/ppermute | solution.py:15
  134.5 7.7 %copy-start.20 = (bf16[128,512]{0,1:T(8,128)(2,1)}, bf16[128,512]{0,1:T(8,128)(2,1)S(1)}, u32[]{:S(2)}) copy-start(bf16[128,512]{0,1:T(8,128)(2,1)S(1)} %fusion.98) | copy-start | bytes 393220
  135.7 4.9 %collective-permute-start.13 = (f32[1024,256]{1,0:T(8,128)}, f32[1024,256]{1,0:T(8,128)}, u32[]{:S(2)}, u32[]{:S(2)}) collective-permute-start(f32[1024,256]{1,0:T(8,128)} %fusion.107), channel_id=1, source_target_pairs={{0,4},{4,0},{8,12},{12,8},{16,20},{20,16},{24,28},{28,24},{32,36},... | collective-permute-start | bytes 3145736 | tf_op jit(solution)/shard_map/ppermute | solution.py:20
  142.2 1.0 copy-start.3
  143.2 11.3 %collective-permute-start.14 = (bf16[512,256]{1,0:T(8,128)(2,1)S(1)}, bf16[512,256]{1,0:T(8,128)(2,1)}, u32[]{:S(2)}, u32[]{:S(2)}) collective-permute-start(bf16[512,256]{1,0:T(8,128)(2,1)S(1)} %slice.267), channel_id=1, source_target_pairs={{0,1},{1,0},{2,3},{3,2},{4,5},{5,4},{6,7},{7,6},{8,9},{9,8},{10,11... | collective-permute-start | bytes 786440 | tf_op jit(solution)/shard_map/ppermute | solution.py:20
  156.4 14.0 %collective-permute-start.15 = (bf16[256,256]{1,0:T(8,128)(2,1)}, bf16[256,256]{1,0:T(8,128)(2,1)S(1)}, u32[]{:S(2)}, u32[]{:S(2)}) collective-permute-start(bf16[256,256]{1,0:T(8,128)(2,1)} %select_convert_fusion), channel_id=1, source_target_pairs={{0,2},{1,3},{2,0},{3,1},{4,6},{5,7},{6,4},{7,5},{8,10},{9,11},{10,... | collective-permute-start | bytes 393224 | tf_op jit(solution)/shard_map/ppermute | solution.py:20
  170.4 0.7 copy-start.14
  171.1 30.3 %copy-start.5 = (bf16[640,512]{1,0:T(8,128)(2,1)S(1)}, bf16[640,512]{1,0:T(8,128)(2,1)}, u32[]{:S(2)}) copy-start(bf16[640,512]{1,0:T(8,128)(2,1)} %copy-done.4) | copy-start | bytes 1966084
  171.8 6.8 %collective-permute-start.16 = (f32[128,256]{1,0:T(8,128)}, f32[128,256]{1,0:T(8,128)}, u32[]{:S(2)}, u32[]{:S(2)}) collective-permute-start(f32[128,256]{1,0:T(8,128)} %slice_select_fusion), channel_id=1, source_target_pairs={{0,16},{4,20},{8,24},{12,28},{16,0},{20,4},{24,8},{28,12},{32,48},... | collective-permute-start | bytes 393224 | tf_op jit(solution)/shard_map/ppermute | solution.py:20
  179.6 6.5 %collective-permute-start.17 = (f32[64,256]{1,0:T(8,128)S(1)}, f32[64,256]{1,0:T(8,128)S(1)}, u32[]{:S(2)}, u32[]{:S(2)}) collective-permute-start(f32[64,256]{1,0:T(8,128)S(1)} %slice_select_fusion.1), channel_id=1, source_target_pairs={{0,64},{4,68},{8,72},{12,76},{16,80},{20,84},{24,88},{28,92},{32,9... | collective-permute-start | bytes 196616 | tf_op jit(solution)/shard_map/ppermute | solution.py:20
  186.8 9.9 %collective-permute-start.18 = (f32[64,256]{1,0:T(8,128)}, f32[64,256]{1,0:T(8,128)}, u32[]{:S(2)}, u32[]{:S(2)}) collective-permute-start(f32[64,256]{1,0:T(8,128)} %select_add_fusion.1), channel_id=1, source_target_pairs={{0,8},{4,12},{8,0},{12,4},{16,24},{20,28},{24,16},{28,20},{32,40},... | collective-permute-start | bytes 196616 | tf_op jit(solution)/shard_map/ppermute | solution.py:20
  192.2 27.7 %copy-start.9 = (bf16[4,128,640]{1,2,0:T(8,128)(2,1)S(1)}, bf16[4,128,640]{1,2,0:T(8,128)(2,1)}, u32[]{:S(2)}) copy-start(bf16[4,128,640]{1,2,0:T(8,128)(2,1)} %copy-done.8) | copy-start | bytes 1966084
  197.6 6.5 %collective-permute-start.19 = (f32[64,256]{1,0:T(8,128)S(1)}, f32[64,256]{1,0:T(8,128)S(1)}, u32[]{:S(2)}, u32[]{:S(2)}) collective-permute-start(f32[64,256]{1,0:T(8,128)S(1)} %add.134), channel_id=1, source_target_pairs={{0,32},{4,36},{8,40},{12,44},{16,48},{20,52},{24,56},{28,60},{32,0... | collective-permute-start | bytes 196616 | tf_op jit(solution)/shard_map/ppermute | solution.py:20
  202.7 20.7 %copy-start.7 = (bf16[4,128,640]{1,2,0:T(8,128)(2,1)S(1)}, bf16[4,128,640]{1,2,0:T(8,128)(2,1)}, u32[]{:S(2)}) copy-start(bf16[4,128,640]{1,2,0:T(8,128)(2,1)} %copy-done.6) | copy-start | bytes 1966084
  204.2 6.7 %collective-permute-start.20 = (f32[64,256]{1,0:T(8,128)S(1)}, f32[64,256]{1,0:T(8,128)S(1)}, u32[]{:S(2)}, u32[]{:S(2)}) collective-permute-start(f32[64,256]{1,0:T(8,128)S(1)} %add.135), channel_id=1, source_target_pairs={{0,128},{4,132},{8,136},{12,140},{16,144},{20,148},{24,152},{28,15... | collective-permute-start | bytes 196616 | tf_op jit(solution)/shard_map/ppermute | solution.py:20
  210.6 19.7 %copy-start.2 = (bf16[1024,512]{1,0:T(8,128)(2,1)S(1)}, bf16[1024,512]{1,0:T(8,128)(2,1)}, u32[]{:S(2)}) copy-start(bf16[1024,512]{1,0:T(8,128)(2,1)} %copy-done.1) | copy-start | bytes 3145732
  210.6 19.7 %copy-start.21 = (bf16[128,512]{0,1:T(8,128)(2,1)S(1)}, bf16[128,512]{0,1:T(8,128)(2,1)}, u32[]{:S(2)}) copy-start(bf16[128,512]{0,1:T(8,128)(2,1)} %copy-done.20) | copy-start | bytes 393220
  210.9 10.6 %collective-permute-start.21 = (f32[64,256]{1,0:T(8,128)S(1)}, f32[64,256]{1,0:T(8,128)S(1)}, u32[]{:S(2)}, u32[]{:S(2)}) collective-permute-start(f32[64,256]{1,0:T(8,128)S(1)} %add.136), channel_id=1, source_target_pairs={{0,256},{4,260},{8,264},{12,268},{16,272},{20,276},{24,280},{28,28... | collective-permute-start | bytes 196616 | tf_op jit(solution)/shard_map/ppermute | solution.py:20
  221.5 5.6 %collective-permute-start.22 = (f32[64,256]{1,0:T(8,128)S(1)}, f32[64,256]{1,0:T(8,128)S(1)}, u32[]{:S(2)}, u32[]{:S(2)}) collective-permute-start(f32[64,256]{1,0:T(8,128)S(1)} %add.137), channel_id=1, source_target_pairs={{0,64},{4,68},{8,72},{12,76},{16,80},{20,84},{24,88},{28,92},{32,9... | collective-permute-start | bytes 196616 | tf_op jit(solution)/shard_map/ppermute | solution.py:20
  227.1 5.7 %collective-permute-start.23 = (f32[128,256]{1,0:T(8,128)S(1)}, f32[128,256]{1,0:T(8,128)S(1)}, u32[]{:S(2)}, u32[]{:S(2)}) collective-permute-start(f32[128,256]{1,0:T(8,128)S(1)} %maximum_select_fusion.2), channel_id=1, source_target_pairs={{0,16},{4,20},{8,24},{12,28},{16,0},{20,4},{24,8},{28,12},{32,48},... | collective-permute-start | bytes 393224 | tf_op jit(solution)/shard_map/ppermute | solution.py:20
  232.8 12.0 %collective-permute-start.24 = (f32[256,256]{1,0:T(8,128)S(1)}, f32[256,256]{1,0:T(8,128)S(1)}, u32[]{:S(2)}, u32[]{:S(2)}) collective-permute-start(f32[256,256]{1,0:T(8,128)S(1)} %maximum_select_fusion.1), channel_id=1, source_target_pairs={{0,4},{4,0},{8,12},{12,8},{16,20},{20,16},{24,28},{28,24},{32,36},... | collective-permute-start | bytes 786440 | tf_op jit(solution)/shard_map/ppermute | solution.py:20

commit v11 on v9

--- a/solution.py
+++ b/solution.py
@@ -143,10 +143,15 @@
     two_away = jnp.concatenate(
         [ring_pull(block[:, :split], 2), ring_pull(block[:, split:], -2)], axis=1
     )
-    stacked = jnp.concatenate([block, ring_pull(block, 1), two_away, ring_pull(block, -1)], axis=0)
-    doubled = jnp.concatenate([stacked, stacked], axis=0)
-    start = ((stream_count - stream_index) % stream_count) * rows
-    return lax.dynamic_slice_in_dim(doubled, start, stream_count * rows, 0)
+    arrived = [block, ring_pull(block, 1), two_away, ring_pull(block, -1)]
+    placed = []
+    for position in range(stream_count):
+        offset = (position - stream_index) % stream_count
+        chosen = arrived[3]
+        for slot in (2, 1, 0):
+            chosen = jnp.where(offset == slot, arrived[slot], chosen)
+        placed.append(chosen)
+    return jnp.concatenate(placed, axis=0)
 
 
 def contract_last(left, right):

time: 244 us -> 236 us (0.967)
  local copies, waits for them, and re-layouts: 13.1 us -> 8.82 us
    ppermute x13, starting transfers between devices: 72.9 us -> 68.6 us  [xor_swap(): lax.ppermute(value, axis, [(source, source ^ 1 << bit) for source in rang...]
    unnamed x3 -> x0, other arithmetic: 4.09 us -> none
    ppermute x8, starting transfers between devices: 22.7 us -> 26.1 us  [shifted(): lax.ppermute(value, axis, [(source, source + steps) for source in range(l...]
    concatenate x0 -> x2, other arithmetic: none -> 3.19 us  [the longest x1 1.69 us: ring_gather(): return jnp.concatenate(placed, axis=0)]
    ppermute x13, waiting for transfers between devices: 36.2 us -> 33.2 us  [xor_swap(): lax.ppermute(value, axis, [(source, source ^ 1 << bit) for source in rang...]
    ppermute x4, waiting for transfers between devices: 18.7 us -> 21.1 us  [ring_pull(): return lax.ppermute(value, ('tm', 'stream'), pairs)]
    unnamed x65 -> x72, local copies, waits for them, and re-layouts: 8.63 us -> 7.18 us
  transfers between devices with their start and end apart: 25 -> 25, of which waited for: 18 -> 17; matrix products, arithmetic and copies ran while one was open for 5% -> 4% of each run, Pallas kernels for 0% -> 0%
where the time goes in v11:
time: 236 us; the launch traced here: 235 us
  starting transfers between devices  114 us (48%)
  waiting for transfers between devices  65.2 us (28%)
  matrix products  26.8 us (11%)
  other arithmetic  17.3 us (7%)
  local copies, waits for them, and re-layouts  8.82 us (4%)
  between operations  2.39 us (1%)
    ppermute x13, starting transfers between devices, xor_swap(): lax.ppermute(value, axis, [(source, source ^ 1 << bit) for source in rang...  68.6 us
    ppermute x13, waiting for transfers between devices, xor_swap(): lax.ppermute(value, axis, [(source, source ^ 1 << bit) for source in rang...  33.2 us
    ppermute x8, starting transfers between devices, shifted(): lax.ppermute(value, axis, [(source, source + steps) for source in range(l...  26.1 us
    ppermute x4, waiting for transfers between devices, ring_pull(): return lax.ppermute(value, ('tm', 'stream'), pairs)  21.1 us
    ppermute x4, starting transfers between devices, ring_pull(): return lax.ppermute(value, ('tm', 'stream'), pairs)  19.6 us
    sub x4, matrix products, per_device(): terms = jnp.where(allowed, jnp.exp(masked - row_max), 0.0)  11.6 us
    ppermute x8, waiting for transfers between devices, shifted(): lax.ppermute(value, axis, [(source, source + steps) for source in range(l...  10.9 us
    unnamed x72, local copies, waits for them, and re-layouts  7.18 us
  transfers between devices with their start and end apart: 25, of which 17 were waited for; matrix products, arithmetic and copies ran while one was open for 4% of the time, Pallas kernels for 0%

profile of v11, /device:TPU:1, one launch (start us, length us, event | category | flops | bytes accessed | tf_op | source)
XLA Modules:
  0.0 234.9 jit_solution(6770945327549746727)
XLA Ops:
  0.7 1.5 fusion.85
  2.2 4.8 %collective-permute-start.3 = (bf16[256,1280]{1,0:T(8,128)(2,1)S(1)}, bf16[256,1280]{1,0:T(8,128)(2,1)S(1)}, u32[]{:S(2)}, u32[]{:S(2)}) collective-permute-start(bf16[256,1280]{1,0:T(8,128)(2,1)S(1)} %fusion.85), channel_id=1, source_target_pairs={{11,0},{0,1},{1,2},{2,3},{15,4},{4,5},{5,6},{6,7},{3,8},{8,9},{9,1... | collective-permute-start | bytes 1966088 | tf_op jit(solution)/shard_map/ppermute | solution.py:133
  7.0 8.6 %collective-permute-start = (bf16[256,1280]{1,0:T(8,128)(2,1)S(1)}, bf16[256,1280]{1,0:T(8,128)(2,1)}, u32[]{:S(2)}, u32[]{:S(2)}) collective-permute-start(bf16[256,1280]{1,0:T(8,128)(2,1)S(1)} %fusion.85), channel_id=1, source_target_pairs={{1,0},{2,1},{3,2},{8,3},{5,4},{6,5},{7,6},{12,7},{9,8},{10,9},{11,... | collective-permute-start | bytes 1966088 | tf_op jit(solution)/shard_map/ppermute | solution.py:133
  15.7 3.4 %collective-permute-start.1 = (bf16[256,640]{1,0:T(8,128)(2,1)S(1)}, bf16[256,640]{1,0:T(8,128)(2,1)S(1)}, u32[]{:S(2)}, u32[]{:S(2)}) collective-permute-start(bf16[256,640]{1,0:T(8,128)(2,1)S(1)} %get-tuple-element.13), channel_id=1, source_target_pairs={{2,0},{3,1},{8,2},{9,3},{6,4},{7,5},{12,6},{13,7},{10,8},{11,9},{0... | collective-permute-start | bytes 983048 | tf_op jit(solution)/shard_map/ppermute | solution.py:133
  19.0 2.8 %collective-permute-start.2 = (bf16[256,640]{1,0:T(8,128)(2,1)S(1)}, bf16[256,640]{1,0:T(8,128)(2,1)S(1)}, u32[]{:S(2)}, u32[]{:S(2)}) collective-permute-start(bf16[256,640]{1,0:T(8,128)(2,1)S(1)} %get-tuple-element.12), channel_id=1, source_target_pairs={{10,0},{11,1},{0,2},{1,3},{14,4},{15,5},{4,6},{5,7},{2,8},{3,9},{8... | collective-permute-start | bytes 983048 | tf_op jit(solution)/shard_map/ppermute | solution.py:133
  22.0 21.1 %collective-permute-done.1 = bf16[256,640]{1,0:T(8,128)(2,1)S(1)} collective-permute-done((bf16[256,640]{1,0:T(8,128)(2,1)S(1)}, bf16[256,640]{1,0:T(8,128)(2,1)S(1)}, u32[]{:S(2)}, u32[]{:S(2)}) %collective-permute-start.1) | collective-permute-done | bytes 327712 | tf_op jit(solution)/shard_map/ppermute | solution.py:133
  43.2 0.9 copy-done.24
  44.1 1.6 select_select_fusion.3
  45.7 1.7 pad_maximum_fusion
  47.8 3.4 %collective-permute-start.4 = (bf16[1024,1280]{1,0:T(8,128)(2,1)}, bf16[1024,1280]{1,0:T(8,128)(2,1)}, u32[]{:S(2)}, u32[]{:S(2)}) collective-permute-start(bf16[1024,1280]{1,0:T(8,128)(2,1)} %pad_maximum_fusion), channel_id=1, source_target_pairs={{0,4},{4,0},{8,12},{12,8},{16,20},{20,16},{24,28},{28,24},{32,36},... | collective-permute-start | bytes 7864328 | tf_op jit(solution)/shard_map/ppermute | solution.py:20
  51.9 0.8 copy.104
  52.7 1.0 fusion.89
  53.7 2.3 collective-permute-done.4
  56.0 2.8 %broadcast_select_fusion.1 = (bf16[1024,1280]{1,0:T(8,128)(2,1)S(1)}, bf16[1024,1280]{1,0:T(8,128)(2,1)S(1)}) fusion(bf16[1024,1280]{1,0:T(8,128)(2,1)} %collective-permute-done.4, pred[]{:T(512)S(6)} %eq.64, bf16[256,1280]{1,0:T(8,128)(2,1)} %copy-done.5, bf16[256,1280]{1,0:T(8,128)(2,1)} %copy-done.3, bf16[256,1280]{1,0:T(8,128)(2,1)} %copy-done.4, ...), kind=kLoop, calls=%fused_computation.6 | loop fusion | flops 13107200 | bytes 10485761 | tf_op jit(solution)/shard_map/jit(_where)/select_n | solution.py:189
  58.9 0.9 copy-done.23
  60.1 6.4 %collective-permute-start.8 = (bf16[128,512]{1,0:T(8,128)(2,1)S(1)}, bf16[128,512]{1,0:T(8,128)(2,1)S(1)}, u32[]{:S(2)}, u32[]{:S(2)}) collective-permute-start(bf16[128,512]{1,0:T(8,128)(2,1)S(1)} %fusion.75), channel_id=1, source_target_pairs={{0,4},{4,8},{8,12},{12,16},{16,20},{20,24},{24,28},{28,32},{32,36}... | collective-permute-start | bytes 393224 | tf_op jit(solution)/shard_map/ppermute | solution.py:15
  66.5 4.0 %collective-permute-start.7 = (bf16[128,512]{1,0:T(8,128)(2,1)S(1)}, bf16[128,512]{1,0:T(8,128)(2,1)S(1)}, u32[]{:S(2)}, u32[]{:S(2)}) collective-permute-start(bf16[128,512]{1,0:T(8,128)(2,1)S(1)} %fusion.75), channel_id=1, source_target_pairs={{0,8},{4,12},{8,16},{12,20},{16,24},{20,28},{24,32},{28,36},{32,40... | collective-permute-start | bytes 393224 | tf_op jit(solution)/shard_map/ppermute | solution.py:15
  70.5 1.5 collective-permute-start.6
  72.0 3.5 %collective-permute-start.5 = (bf16[128,512]{1,0:T(8,128)(2,1)S(1)}, bf16[128,512]{1,0:T(8,128)(2,1)S(1)}, u32[]{:S(2)}, u32[]{:S(2)}) collective-permute-start(bf16[128,512]{1,0:T(8,128)(2,1)S(1)} %fusion.75), channel_id=1, source_target_pairs={{0,16},{4,20},{8,24},{12,28},{16,32},{20,36},{24,40},{28,44},{32,4... | collective-permute-start | bytes 393224 | tf_op jit(solution)/shard_map/ppermute | solution.py:15
  75.5 0.8 fusion.64
  78.6 2.9 %fusion.130 = (f32[4,128]{1,0:T(4,128)S(1)}, f32[4,128,640]{1,2,0:T(8,128)}) fusion(bf16[128,4,64]{0,2,1:T(8,128)(2,1)} %bitcast.298, pred[128,640]{0,1:T(8,128)(4,1)} %fusion.89, bf16[640,512]{1,0:T(8,128)(2,1)S(1)} %constant_dynamic-update-slice_fusion.2), kind=kOutput, calls=%fused_computation.199 | convolution fusion | flops 43582080 | bytes 1705984 | tf_op jit(solution)/shard_map/sub | solution.py:239
  81.5 2.6 %fusion.132 = (f32[4,128]{1,0:T(4,128)S(1)}, f32[4,128,640]{1,2,0:T(8,128)}) fusion(bf16[128,4,64]{0,2,1:T(8,128)(2,1)} %bitcast.300, pred[128,640]{0,1:T(8,128)(4,1)} %fusion.89, bf16[640,512]{1,0:T(8,128)(2,1)S(1)} %constant_dynamic-update-slice_fusion.2), kind=kOutput, calls=%fused_computation.201 | convolution fusion | flops 43582080 | bytes 1705984 | tf_op jit(solution)/shard_map/sub | solution.py:239
  84.2 2.7 %fusion.131 = (f32[4,128]{1,0:T(4,128)S(1)}, f32[4,128,640]{1,2,0:T(8,128)}) fusion(bf16[128,4,64]{0,2,1:T(8,128)(2,1)} %bitcast.302, pred[128,640]{0,1:T(8,128)(4,1)} %fusion.89, bf16[640,512]{1,0:T(8,128)(2,1)S(1)} %constant_dynamic-update-slice_fusion.2), kind=kOutput, calls=%fused_computation.200 | convolution fusion | flops 43582080 | bytes 1705984 | tf_op jit(solution)/shard_map/sub | solution.py:239
  86.9 3.3 %fusion.133 = (f32[4,128]{1,0:T(4,128)}, f32[4,128,640]{1,2,0:T(8,128)}) fusion(bf16[128,4,64]{0,2,1:T(8,128)(2,1)} %bitcast.304, pred[128,640]{0,1:T(8,128)(4,1)} %fusion.89, bf16[640,512]{1,0:T(8,128)(2,1)S(1)} %constant_dynamic-update-slice_fusion.2), kind=kOutput, calls=%fused_computation.202 | convolution fusion | flops 43582080 | bytes 1705984 | tf_op jit(solution)/shard_map/sub | solution.py:239
  90.1 0.7 broadcast_select_fusion.4
  90.9 1.4 divide_convert_fusion.3
  100.8 6.8 %collective-permute-start.9 = (bf16[128,512]{0,1:T(8,128)(2,1)S(1)}, bf16[128,512]{0,1:T(8,128)(2,1)S(1)}, u32[]{:S(2)}, u32[]{:S(2)}) collective-permute-start(bf16[128,512]{0,1:T(8,128)(2,1)S(1)} %get-tuple-element.8), channel_id=1, source_target_pairs={{4,0},{8,4},{12,8},{16,12},{20,16},{24,20},{28,24},{32,28},{36,32}... | collective-permute-start | bytes 393224 | tf_op jit(solution)/shard_map/ppermute | solution.py:15
  107.6 1.3 collective-permute-start.12
  108.9 1.3 collective-permute-start.11
  110.2 1.3 collective-permute-start.10
  111.9 1.7 collective-permute-done.12
  113.7 3.9 %collective-permute-done.11 = bf16[128,512]{0,1:T(8,128)(2,1)S(1)} collective-permute-done((bf16[128,512]{0,1:T(8,128)(2,1)S(1)}, bf16[128,512]{0,1:T(8,128)(2,1)S(1)}, u32[]{:S(2)}, u32[]{:S(2)}) %collective-permute-start.11) | collective-permute-done | bytes 131104 | tf_op jit(solution)/shard_map/ppermute | solution.py:15
  117.5 4.9 %collective-permute-done.10 = bf16[128,512]{0,1:T(8,128)(2,1)S(1)} collective-permute-done((bf16[128,512]{0,1:T(8,128)(2,1)S(1)}, bf16[128,512]{0,1:T(8,128)(2,1)S(1)}, u32[]{:S(2)}, u32[]{:S(2)}) %collective-permute-start.10) | collective-permute-done | bytes 131104 | tf_op jit(solution)/shard_map/ppermute | solution.py:15
  122.5 1.3 fusion.104
  123.8 2.3 collective-permute-start.13
  126.1 2.6 %collective-permute-done.13 = f32[1024,256]{1,0:T(8,128)} collective-permute-done((f32[1024,256]{1,0:T(8,128)}, f32[1024,256]{1,0:T(8,128)}, u32[]{:S(2)}, u32[]{:S(2)}) %collective-permute-start.13) | collective-permute-done | bytes 1048608 | tf_op jit(solution)/shard_map/ppermute | solution.py:20
  128.7 1.5 convolution_add_fusion
  130.3 1.0 copy-done.6
  131.3 4.8 %collective-permute-start.14 = (bf16[512,256]{1,0:T(8,128)(2,1)S(1)}, bf16[512,256]{1,0:T(8,128)(2,1)}, u32[]{:S(2)}, u32[]{:S(2)}) collective-permute-start(bf16[512,256]{1,0:T(8,128)(2,1)S(1)} %slice.279), channel_id=1, source_target_pairs={{0,1},{1,0},{2,3},{3,2},{4,5},{5,4},{6,7},{7,6},{8,9},{9,8},{10,11... | collective-permute-start | bytes 786440 | tf_op jit(solution)/shard_map/ppermute | solution.py:20
  136.1 6.6 %collective-permute-done.14 = bf16[512,256]{1,0:T(8,128)(2,1)} collective-permute-done((bf16[512,256]{1,0:T(8,128)(2,1)S(1)}, bf16[512,256]{1,0:T(8,128)(2,1)}, u32[]{:S(2)}, u32[]{:S(2)}) %collective-permute-start.14) | collective-permute-done | bytes 262176 | tf_op jit(solution)/shard_map/ppermute | solution.py:20
  142.7 1.2 slice_add_fusion
  144.5 6.6 %collective-permute-start.15 = (bf16[256,256]{1,0:T(8,128)(2,1)}, bf16[256,256]{1,0:T(8,128)(2,1)S(1)}, u32[]{:S(2)}, u32[]{:S(2)}) collective-permute-start(bf16[256,256]{1,0:T(8,128)(2,1)} %select_convert_fusion), channel_id=1, source_target_pairs={{0,2},{1,3},{2,0},{3,1},{4,6},{5,7},{6,4},{7,5},{8,10},{9,11},{10,... | collective-permute-start | bytes 393224 | tf_op jit(solution)/shard_map/ppermute | solution.py:20
  151.1 6.9 %collective-permute-done.15 = bf16[256,256]{1,0:T(8,128)(2,1)S(1)} collective-permute-done((bf16[256,256]{1,0:T(8,128)(2,1)}, bf16[256,256]{1,0:T(8,128)(2,1)S(1)}, u32[]{:S(2)}, u32[]{:S(2)}) %collective-permute-start.15) | collective-permute-done | bytes 131104 | tf_op jit(solution)/shard_map/ppermute | solution.py:20
  159.5 5.2 %collective-permute-start.16 = (f32[128,256]{1,0:T(8,128)}, f32[128,256]{1,0:T(8,128)}, u32[]{:S(2)}, u32[]{:S(2)}) collective-permute-start(f32[128,256]{1,0:T(8,128)} %slice_select_fusion), channel_id=1, source_target_pairs={{0,16},{4,20},{8,24},{12,28},{16,0},{20,4},{24,8},{28,12},{32,48},... | collective-permute-start | bytes 393224 | tf_op jit(solution)/shard_map/ppermute | solution.py:20
  164.7 3.7 %collective-permute-done.16 = f32[128,256]{1,0:T(8,128)} collective-permute-done((f32[128,256]{1,0:T(8,128)}, f32[128,256]{1,0:T(8,128)}, u32[]{:S(2)}, u32[]{:S(2)}) %collective-permute-start.16) | collective-permute-done | bytes 131104 | tf_op jit(solution)/shard_map/ppermute | solution.py:20
  168.5 1.1 select_add_fusion
  169.6 5.1 %collective-permute-start.17 = (f32[64,256]{1,0:T(8,128)S(1)}, f32[64,256]{1,0:T(8,128)S(1)}, u32[]{:S(2)}, u32[]{:S(2)}) collective-permute-start(f32[64,256]{1,0:T(8,128)S(1)} %slice_select_fusion.1), channel_id=1, source_target_pairs={{0,64},{4,68},{8,72},{12,76},{16,80},{20,84},{24,88},{28,92},{32,9... | collective-permute-start | bytes 196616 | tf_op jit(solution)/shard_map/ppermute | solution.py:20
  174.7 1.6 collective-permute-done.17
  177.0 6.2 %collective-permute-start.18 = (f32[64,256]{1,0:T(8,128)}, f32[64,256]{1,0:T(8,128)}, u32[]{:S(2)}, u32[]{:S(2)}) collective-permute-start(f32[64,256]{1,0:T(8,128)} %select_add_fusion.1), channel_id=1, source_target_pairs={{0,8},{4,12},{8,0},{12,4},{16,24},{20,28},{24,16},{28,20},{32,40},... | collective-permute-start | bytes 196616 | tf_op jit(solution)/shard_map/ppermute | solution.py:20
  183.2 3.1 %collective-permute-done.18 = f32[64,256]{1,0:T(8,128)} collective-permute-done((f32[64,256]{1,0:T(8,128)}, f32[64,256]{1,0:T(8,128)}, u32[]{:S(2)}, u32[]{:S(2)}) %collective-permute-start.18) | collective-permute-done | bytes 65568 | tf_op jit(solution)/shard_map/ppermute | solution.py:20
  186.3 0.9 add.132
  187.2 5.5 %collective-permute-start.19 = (f32[64,256]{1,0:T(8,128)S(1)}, f32[64,256]{1,0:T(8,128)S(1)}, u32[]{:S(2)}, u32[]{:S(2)}) collective-permute-start(f32[64,256]{1,0:T(8,128)S(1)} %add.132), channel_id=1, source_target_pairs={{0,32},{4,36},{8,40},{12,44},{16,48},{20,52},{24,56},{28,60},{32,0... | collective-permute-start | bytes 196616 | tf_op jit(solution)/shard_map/ppermute | solution.py:20
  192.7 1.3 convolution_convert_fusion.7
  194.3 5.3 %collective-permute-start.20 = (f32[64,256]{1,0:T(8,128)S(1)}, f32[64,256]{1,0:T(8,128)S(1)}, u32[]{:S(2)}, u32[]{:S(2)}) collective-permute-start(f32[64,256]{1,0:T(8,128)S(1)} %add.133), channel_id=1, source_target_pairs={{0,128},{4,132},{8,136},{12,140},{16,144},{20,148},{24,152},{28,15... | collective-permute-start | bytes 196616 | tf_op jit(solution)/shard_map/ppermute | solution.py:20
  199.6 1.3 convolution_convert_fusion.3
  201.3 7.5 %collective-permute-start.21 = (f32[64,256]{1,0:T(8,128)S(1)}, f32[64,256]{1,0:T(8,128)S(1)}, u32[]{:S(2)}, u32[]{:S(2)}) collective-permute-start(f32[64,256]{1,0:T(8,128)S(1)} %add.134), channel_id=1, source_target_pairs={{0,256},{4,260},{8,264},{12,268},{16,272},{20,276},{24,280},{28,28... | collective-permute-start | bytes 196616 | tf_op jit(solution)/shard_map/ppermute | solution.py:20
  209.2 1.3 collective-permute-done.21
  210.5 3.7 %collective-permute-start.22 = (f32[64,256]{1,0:T(8,128)S(1)}, f32[64,256]{1,0:T(8,128)S(1)}, u32[]{:S(2)}, u32[]{:S(2)}) collective-permute-start(f32[64,256]{1,0:T(8,128)S(1)} %add.135), channel_id=1, source_target_pairs={{0,64},{4,68},{8,72},{12,76},{16,80},{20,84},{24,88},{28,92},{32,9... | collective-permute-start | bytes 196616 | tf_op jit(solution)/shard_map/ppermute | solution.py:20
  214.6 2.3 collective-permute-done.22
  216.9 3.7 %collective-permute-start.23 = (f32[128,256]{1,0:T(8,128)S(1)}, f32[128,256]{1,0:T(8,128)S(1)}, u32[]{:S(2)}, u32[]{:S(2)}) collective-permute-start(f32[128,256]{1,0:T(8,128)S(1)} %maximum_select_fusion.2), channel_id=1, source_target_pairs={{0,16},{4,20},{8,24},{12,28},{16,0},{20,4},{24,8},{28,12},{32,48},... | collective-permute-start | bytes 393224 | tf_op jit(solution)/shard_map/ppermute | solution.py:20
  221.1 2.1 collective-permute-done.23
  223.2 9.3 %collective-permute-start.24 = (f32[256,256]{1,0:T(8,128)S(1)}, f32[256,256]{1,0:T(8,128)S(1)}, u32[]{:S(2)}, u32[]{:S(2)}) collective-permute-start(f32[256,256]{1,0:T(8,128)S(1)} %maximum_select_fusion.1), channel_id=1, source_target_pairs={{0,4},{4,0},{8,12},{12,8},{16,20},{20,16},{24,28},{28,24},{32,36},... | collective-permute-start | bytes 786440 | tf_op jit(solution)/shard_map/ppermute | solution.py:20
  232.5 1.5 fusion.58
  234.0 0.8 maximum_select_fusion
  (128 shorter events, 16.4 us)
Async XLA Ops:
  0.6 75.7 %copy-start = (bf16[1,128,1024]{2,1,0:T(8,128)(2,1)S(1)}, bf16[1,128,1024]{2,1,0:T(8,128)(2,1)}, u32[]{:S(2)}) copy-start(bf16[1,128,1024]{2,1,0:T(8,128)(2,1)} %param.7) | copy-start | bytes 786436
  2.2 41.0 %collective-permute-start.3 = (bf16[256,1280]{1,0:T(8,128)(2,1)S(1)}, bf16[256,1280]{1,0:T(8,128)(2,1)S(1)}, u32[]{:S(2)}, u32[]{:S(2)}) collective-permute-start(bf16[256,1280]{1,0:T(8,128)(2,1)S(1)} %fusion.85), channel_id=1, source_target_pairs={{11,0},{0,1},{1,2},{2,3},{15,4},{4,5},{5,6},{6,7},{3,8},{8,9},{9,1... | collective-permute-start | bytes 1966088 | tf_op jit(solution)/shard_map/ppermute | solution.py:133
  7.0 37.0 %collective-permute-start = (bf16[256,1280]{1,0:T(8,128)(2,1)S(1)}, bf16[256,1280]{1,0:T(8,128)(2,1)}, u32[]{:S(2)}, u32[]{:S(2)}) collective-permute-start(bf16[256,1280]{1,0:T(8,128)(2,1)S(1)} %fusion.85), channel_id=1, source_target_pairs={{1,0},{2,1},{3,2},{8,3},{5,4},{6,5},{7,6},{12,7},{9,8},{10,9},{11,... | collective-permute-start | bytes 1966088 | tf_op jit(solution)/shard_map/ppermute | solution.py:133
  15.7 27.4 %collective-permute-start.1 = (bf16[256,640]{1,0:T(8,128)(2,1)S(1)}, bf16[256,640]{1,0:T(8,128)(2,1)S(1)}, u32[]{:S(2)}, u32[]{:S(2)}) collective-permute-start(bf16[256,640]{1,0:T(8,128)(2,1)S(1)} %get-tuple-element.13), channel_id=1, source_target_pairs={{2,0},{3,1},{8,2},{9,3},{6,4},{7,5},{12,6},{13,7},{10,8},{11,9},{0... | collective-permute-start | bytes 983048 | tf_op jit(solution)/shard_map/ppermute | solution.py:133
  19.0 24.1 %collective-permute-start.2 = (bf16[256,640]{1,0:T(8,128)(2,1)S(1)}, bf16[256,640]{1,0:T(8,128)(2,1)S(1)}, u32[]{:S(2)}, u32[]{:S(2)}) collective-permute-start(bf16[256,640]{1,0:T(8,128)(2,1)S(1)} %get-tuple-element.12), channel_id=1, source_target_pairs={{10,0},{11,1},{0,2},{1,3},{14,4},{15,5},{4,6},{5,7},{2,8},{3,9},{8... | collective-permute-start | bytes 983048 | tf_op jit(solution)/shard_map/ppermute | solution.py:133
  43.2 0.9 copy-start.24
  45.6 1.7 copy-start.3
  45.7 1.9 copy-start.4
  45.7 2.1 copy-start.5
  45.7 6.2 %copy-start.22 = (bf16[1,128,1024]{2,1,0:T(8,128)(2,1)S(1)}, bf16[1,128,1024]{2,1,0:T(8,128)(2,1)}, u32[]{:S(2)}) copy-start(bf16[1,128,1024]{2,1,0:T(8,128)(2,1)} %param.6) | copy-start | bytes 786436
  47.8 8.3 %collective-permute-start.4 = (bf16[1024,1280]{1,0:T(8,128)(2,1)}, bf16[1024,1280]{1,0:T(8,128)(2,1)}, u32[]{:S(2)}, u32[]{:S(2)}) collective-permute-start(bf16[1024,1280]{1,0:T(8,128)(2,1)} %pad_maximum_fusion), channel_id=1, source_target_pairs={{0,4},{4,0},{8,12},{12,8},{16,20},{20,16},{24,28},{28,24},{32,36},... | collective-permute-start | bytes 7864328 | tf_op jit(solution)/shard_map/ppermute | solution.py:20
  58.8 1.0 copy-start.23
  59.8 16.5 %copy-start.1 = (bf16[1024,512]{1,0:T(8,128)(2,1)}, bf16[1024,512]{1,0:T(8,128)(2,1)S(1)}, u32[]{:S(2)}) copy-start(bf16[1024,512]{1,0:T(8,128)(2,1)S(1)} %pad_maximum_fusion.1) | copy-start | bytes 3145732
  60.1 18.4 %collective-permute-start.8 = (bf16[128,512]{1,0:T(8,128)(2,1)S(1)}, bf16[128,512]{1,0:T(8,128)(2,1)S(1)}, u32[]{:S(2)}, u32[]{:S(2)}) collective-permute-start(bf16[128,512]{1,0:T(8,128)(2,1)S(1)} %fusion.75), channel_id=1, source_target_pairs={{0,4},{4,8},{8,12},{12,16},{16,20},{20,24},{24,28},{28,32},{32,36}... | collective-permute-start | bytes 393224 | tf_op jit(solution)/shard_map/ppermute | solution.py:15
  66.5 12.0 %collective-permute-start.7 = (bf16[128,512]{1,0:T(8,128)(2,1)S(1)}, bf16[128,512]{1,0:T(8,128)(2,1)S(1)}, u32[]{:S(2)}, u32[]{:S(2)}) collective-permute-start(bf16[128,512]{1,0:T(8,128)(2,1)S(1)} %fusion.75), channel_id=1, source_target_pairs={{0,8},{4,12},{8,16},{12,20},{16,24},{20,28},{24,32},{28,36},{32,40... | collective-permute-start | bytes 393224 | tf_op jit(solution)/shard_map/ppermute | solution.py:15
  70.5 8.0 %collective-permute-start.6 = (bf16[128,512]{1,0:T(8,128)(2,1)S(1)}, bf16[128,512]{1,0:T(8,128)(2,1)S(1)}, u32[]{:S(2)}, u32[]{:S(2)}) collective-permute-start(bf16[128,512]{1,0:T(8,128)(2,1)S(1)} %fusion.75), channel_id=1, source_target_pairs={{0,12},{4,16},{8,20},{12,24},{16,28},{20,32},{24,36},{28,40},{32,4... | collective-permute-start | bytes 393224 | tf_op jit(solution)/shard_map/ppermute | solution.py:15
  72.0 6.5 %collective-permute-start.5 = (bf16[128,512]{1,0:T(8,128)(2,1)S(1)}, bf16[128,512]{1,0:T(8,128)(2,1)S(1)}, u32[]{:S(2)}, u32[]{:S(2)}) collective-permute-start(bf16[128,512]{1,0:T(8,128)(2,1)S(1)} %fusion.75), channel_id=1, source_target_pairs={{0,16},{4,20},{8,24},{12,28},{16,32},{20,36},{24,40},{28,44},{32,4... | collective-permute-start | bytes 393224 | tf_op jit(solution)/shard_map/ppermute | solution.py:15
  78.6 19.3 %copy-start.7 = (bf16[640,512]{1,0:T(8,128)(2,1)}, bf16[640,512]{1,0:T(8,128)(2,1)S(1)}, u32[]{:S(2)}) copy-start(bf16[640,512]{1,0:T(8,128)(2,1)S(1)} %constant_dynamic-update-slice_fusion.2) | copy-start | bytes 1966084
  90.1 2.2 copy-start.28
  92.3 0.8 copy-start.32
  92.6 1.4 copy-start.18
  93.1 0.8 copy-start.14
  93.1 1.0 copy-start.26
  94.1 1.3 copy-start.17
  94.7 3.9 %copy-start.13 = (bf16[4,128,640]{1,2,0:T(8,128)(2,1)}, bf16[4,128,640]{1,2,0:T(8,128)(2,1)S(1)}, u32[]{:S(2)}) copy-start(bf16[4,128,640]{1,2,0:T(8,128)(2,1)S(1)} %fusion.44) | copy-start | bytes 1966084
  94.7 1.0 copy-start.27
  95.5 1.3 copy-start.16
  96.5 1.8 copy-start.11
  96.5 0.9 copy-start.25
  97.0 1.3 copy-start.31
  97.8 0.8 copy-start.30
  97.8 1.1 copy-start.29
  98.3 1.0 copy-start.9
  100.6 10.9 %copy-start.21 = (bf16[1,128,1024]{1,2,0:T(8,128)(2,1)S(1)}, bf16[1,128,1024]{1,2,0:T(8,128)(2,1)}, u32[]{:S(2)}) copy-start(bf16[1,128,1024]{1,2,0:T(8,128)(2,1)} %copy.104) | copy-start | bytes 786436
  100.8 11.1 %collective-permute-start.9 = (bf16[128,512]{0,1:T(8,128)(2,1)S(1)}, bf16[128,512]{0,1:T(8,128)(2,1)S(1)}, u32[]{:S(2)}, u32[]{:S(2)}) collective-permute-start(bf16[128,512]{0,1:T(8,128)(2,1)S(1)} %get-tuple-element.8), channel_id=1, source_target_pairs={{4,0},{8,4},{12,8},{16,12},{20,16},{24,20},{28,24},{32,28},{36,32}... | collective-permute-start | bytes 393224 | tf_op jit(solution)/shard_map/ppermute | solution.py:15
  107.6 6.0 %collective-permute-start.12 = (bf16[128,512]{0,1:T(8,128)(2,1)S(1)}, bf16[128,512]{0,1:T(8,128)(2,1)S(1)}, u32[]{:S(2)}, u32[]{:S(2)}) collective-permute-start(bf16[128,512]{0,1:T(8,128)(2,1)S(1)} %get-tuple-element.9), channel_id=1, source_target_pairs={{16,0},{20,4},{24,8},{28,12},{32,16},{36,20},{40,24},{44,28},{48,3... | collective-permute-start | bytes 393224 | tf_op jit(solution)/shard_map/ppermute | solution.py:15
  108.9 8.6 %collective-permute-start.11 = (bf16[128,512]{0,1:T(8,128)(2,1)S(1)}, bf16[128,512]{0,1:T(8,128)(2,1)S(1)}, u32[]{:S(2)}, u32[]{:S(2)}) collective-permute-start(bf16[128,512]{0,1:T(8,128)(2,1)S(1)} %get-tuple-element.10), channel_id=1, source_target_pairs={{12,0},{16,4},{20,8},{24,12},{28,16},{32,20},{36,24},{40,28},{44,3... | collective-permute-start | bytes 393224 | tf_op jit(solution)/shard_map/ppermute | solution.py:15
  110.2 12.2 %collective-permute-start.10 = (bf16[128,512]{0,1:T(8,128)(2,1)S(1)}, bf16[128,512]{0,1:T(8,128)(2,1)S(1)}, u32[]{:S(2)}, u32[]{:S(2)}) collective-permute-start(bf16[128,512]{0,1:T(8,128)(2,1)S(1)} %get-tuple-element.11), channel_id=1, source_target_pairs={{8,0},{12,4},{16,8},{20,12},{24,16},{28,20},{32,24},{36,28},{40,32... | collective-permute-start | bytes 393224 | tf_op jit(solution)/shard_map/ppermute | solution.py:15
  122.5 7.7 %copy-start.19 = (bf16[128,512]{0,1:T(8,128)(2,1)}, bf16[128,512]{0,1:T(8,128)(2,1)S(1)}, u32[]{:S(2)}) copy-start(bf16[128,512]{0,1:T(8,128)(2,1)S(1)} %fusion.93) | copy-start | bytes 393220
  123.8 4.9 %collective-permute-start.13 = (f32[1024,256]{1,0:T(8,128)}, f32[1024,256]{1,0:T(8,128)}, u32[]{:S(2)}, u32[]{:S(2)}) collective-permute-start(f32[1024,256]{1,0:T(8,128)} %fusion.104), channel_id=1, source_target_pairs={{0,4},{4,0},{8,12},{12,8},{16,20},{20,16},{24,28},{28,24},{32,36},... | collective-permute-start | bytes 3145736 | tf_op jit(solution)/shard_map/ppermute | solution.py:20
  130.2 1.0 copy-start.6
  131.3 11.4 %collective-permute-start.14 = (bf16[512,256]{1,0:T(8,128)(2,1)S(1)}, bf16[512,256]{1,0:T(8,128)(2,1)}, u32[]{:S(2)}, u32[]{:S(2)}) collective-permute-start(bf16[512,256]{1,0:T(8,128)(2,1)S(1)} %slice.279), channel_id=1, source_target_pairs={{0,1},{1,0},{2,3},{3,2},{4,5},{5,4},{6,7},{7,6},{8,9},{9,8},{10,11... | collective-permute-start | bytes 786440 | tf_op jit(solution)/shard_map/ppermute | solution.py:20
  144.5 13.5 %collective-permute-start.15 = (bf16[256,256]{1,0:T(8,128)(2,1)}, bf16[256,256]{1,0:T(8,128)(2,1)S(1)}, u32[]{:S(2)}, u32[]{:S(2)}) collective-permute-start(bf16[256,256]{1,0:T(8,128)(2,1)} %select_convert_fusion), channel_id=1, source_target_pairs={{0,2},{1,3},{2,0},{3,1},{4,6},{5,7},{6,4},{7,5},{8,10},{9,11},{10,... | collective-permute-start | bytes 393224 | tf_op jit(solution)/shard_map/ppermute | solution.py:20
  158.1 0.7 copy-start.15
  158.8 33.9 %copy-start.8 = (bf16[640,512]{1,0:T(8,128)(2,1)S(1)}, bf16[640,512]{1,0:T(8,128)(2,1)}, u32[]{:S(2)}) copy-start(bf16[640,512]{1,0:T(8,128)(2,1)} %copy-done.7) | copy-start | bytes 1966084
  159.5 9.0 %collective-permute-start.16 = (f32[128,256]{1,0:T(8,128)}, f32[128,256]{1,0:T(8,128)}, u32[]{:S(2)}, u32[]{:S(2)}) collective-permute-start(f32[128,256]{1,0:T(8,128)} %slice_select_fusion), channel_id=1, source_target_pairs={{0,16},{4,20},{8,24},{12,28},{16,0},{20,4},{24,8},{28,12},{32,48},... | collective-permute-start | bytes 393224 | tf_op jit(solution)/shard_map/ppermute | solution.py:20
  169.6 6.8 %collective-permute-start.17 = (f32[64,256]{1,0:T(8,128)S(1)}, f32[64,256]{1,0:T(8,128)S(1)}, u32[]{:S(2)}, u32[]{:S(2)}) collective-permute-start(f32[64,256]{1,0:T(8,128)S(1)} %slice_select_fusion.1), channel_id=1, source_target_pairs={{0,64},{4,68},{8,72},{12,76},{16,80},{20,84},{24,88},{28,92},{32,9... | collective-permute-start | bytes 196616 | tf_op jit(solution)/shard_map/ppermute | solution.py:20
  177.0 9.3 %collective-permute-start.18 = (f32[64,256]{1,0:T(8,128)}, f32[64,256]{1,0:T(8,128)}, u32[]{:S(2)}, u32[]{:S(2)}) collective-permute-start(f32[64,256]{1,0:T(8,128)} %select_add_fusion.1), channel_id=1, source_target_pairs={{0,8},{4,12},{8,0},{12,4},{16,24},{20,28},{24,16},{28,20},{32,40},... | collective-permute-start | bytes 196616 | tf_op jit(solution)/shard_map/ppermute | solution.py:20
  183.2 25.6 %copy-start.12 = (bf16[4,128,640]{1,2,0:T(8,128)(2,1)S(1)}, bf16[4,128,640]{1,2,0:T(8,128)(2,1)}, u32[]{:S(2)}) copy-start(bf16[4,128,640]{1,2,0:T(8,128)(2,1)} %copy-done.11) | copy-start | bytes 1966084
  187.2 7.1 %collective-permute-start.19 = (f32[64,256]{1,0:T(8,128)S(1)}, f32[64,256]{1,0:T(8,128)S(1)}, u32[]{:S(2)}, u32[]{:S(2)}) collective-permute-start(f32[64,256]{1,0:T(8,128)S(1)} %add.132), channel_id=1, source_target_pairs={{0,32},{4,36},{8,40},{12,44},{16,48},{20,52},{24,56},{28,60},{32,0... | collective-permute-start | bytes 196616 | tf_op jit(solution)/shard_map/ppermute | solution.py:20
  194.0 20.2 %copy-start.10 = (bf16[4,128,640]{1,2,0:T(8,128)(2,1)S(1)}, bf16[4,128,640]{1,2,0:T(8,128)(2,1)}, u32[]{:S(2)}) copy-start(bf16[4,128,640]{1,2,0:T(8,128)(2,1)} %copy-done.9) | copy-start | bytes 1966084
  194.3 6.9 %collective-permute-start.20 = (f32[64,256]{1,0:T(8,128)S(1)}, f32[64,256]{1,0:T(8,128)S(1)}, u32[]{:S(2)}, u32[]{:S(2)}) collective-permute-start(f32[64,256]{1,0:T(8,128)S(1)} %add.133), channel_id=1, source_target_pairs={{0,128},{4,132},{8,136},{12,140},{16,144},{20,148},{24,152},{28,15... | collective-permute-start | bytes 196616 | tf_op jit(solution)/shard_map/ppermute | solution.py:20
  201.0 19.6 %copy-start.2 = (bf16[1024,512]{1,0:T(8,128)(2,1)S(1)}, bf16[1024,512]{1,0:T(8,128)(2,1)}, u32[]{:S(2)}) copy-start(bf16[1024,512]{1,0:T(8,128)(2,1)} %copy-done.1) | copy-start | bytes 3145732
  201.0 19.6 %copy-start.20 = (bf16[128,512]{0,1:T(8,128)(2,1)S(1)}, bf16[128,512]{0,1:T(8,128)(2,1)}, u32[]{:S(2)}) copy-start(bf16[128,512]{0,1:T(8,128)(2,1)} %copy-done.19) | copy-start | bytes 393220
  201.3 9.2 %collective-permute-start.21 = (f32[64,256]{1,0:T(8,128)S(1)}, f32[64,256]{1,0:T(8,128)S(1)}, u32[]{:S(2)}, u32[]{:S(2)}) collective-permute-start(f32[64,256]{1,0:T(8,128)S(1)} %add.134), channel_id=1, source_target_pairs={{0,256},{4,260},{8,264},{12,268},{16,272},{20,276},{24,280},{28,28... | collective-permute-start | bytes 196616 | tf_op jit(solution)/shard_map/ppermute | solution.py:20
  210.5 6.4 %collective-permute-start.22 = (f32[64,256]{1,0:T(8,128)S(1)}, f32[64,256]{1,0:T(8,128)S(1)}, u32[]{:S(2)}, u32[]{:S(2)}) collective-permute-start(f32[64,256]{1,0:T(8,128)S(1)} %add.135), channel_id=1, source_target_pairs={{0,64},{4,68},{8,72},{12,76},{16,80},{20,84},{24,88},{28,92},{32,9... | collective-permute-start | bytes 196616 | tf_op jit(solution)/shard_map/ppermute | solution.py:20
  216.9 6.3 %collective-permute-start.23 = (f32[128,256]{1,0:T(8,128)S(1)}, f32[128,256]{1,0:T(8,128)S(1)}, u32[]{:S(2)}, u32[]{:S(2)}) collective-permute-start(f32[128,256]{1,0:T(8,128)S(1)} %maximum_select_fusion.2), channel_id=1, source_target_pairs={{0,16},{4,20},{8,24},{12,28},{16,0},{20,4},{24,8},{28,12},{32,48},... | collective-permute-start | bytes 393224 | tf_op jit(solution)/shard_map/ppermute | solution.py:20
  223.2 10.8 %collective-permute-start.24 = (f32[256,256]{1,0:T(8,128)S(1)}, f32[256,256]{1,0:T(8,128)S(1)}, u32[]{:S(2)}, u32[]{:S(2)}) collective-permute-start(f32[256,256]{1,0:T(8,128)S(1)} %maximum_select_fusion.1), channel_id=1, source_target_pairs={{0,4},{4,0},{8,12},{12,8},{16,20},{20,16},{24,28},{28,24},{32,36},... | collective-permute-start | bytes 786440 | tf_op jit(solution)/shard_map/ppermute | solution.py:20

commit v12 on v11

--- a/solution.py
+++ b/solution.py
@@ -200,8 +200,14 @@
         jnp.bfloat16
     )
     attn_grad = contract_last(outer_grad, output_full).astype(jnp.bfloat16)
-    earlier = [shifted(keyvals, "tm", offset) for offset in range(REACH, 0, -1)]
-    window_keyvals = jnp.concatenate(earlier + [keyvals], axis=0)
+    if REACH == 4:
+        back_one = shifted(keyvals, "tm", 1)
+        back_pair = shifted(jnp.concatenate([back_one, keyvals], axis=0), "tm", 2)
+        back_four = shifted(keyvals, "tm", 4)
+        window_keyvals = jnp.concatenate([back_four, back_pair, back_one, keyvals], axis=0)
+    else:
+        earlier = [shifted(keyvals, "tm", offset) for offset in range(REACH, 0, -1)]
+        window_keyvals = jnp.concatenate(earlier + [keyvals], axis=0)
     key_parts = []
     value_parts = []
     query_grads = []
@@ -274,11 +280,19 @@
     def shard_slot(offset):
         return partial_value[(REACH - offset) * shard_tokens : (REACH - offset + 1) * shard_tokens]
 
-    summed = shard_slot(0)
-    for offset in range(1, REACH + 1):
-        summed = summed + shifted(shard_slot(offset).astype(jnp.bfloat16), "tm", -offset).astype(
-            jnp.float32
-        )
+    if REACH == 4:
+        pair_rows = jnp.concatenate([shard_slot(3), shard_slot(2)], axis=0)
+        from_pair = shifted(pair_rows.astype(jnp.bfloat16), "tm", -2).astype(jnp.float32)
+        from_four = shifted(shard_slot(4).astype(jnp.bfloat16), "tm", -4).astype(jnp.float32)
+        slot_one = shard_slot(1) + from_pair[:shard_tokens]
+        summed = shard_slot(0) + from_pair[shard_tokens:] + from_four
+        summed = summed + shifted(slot_one, "tm", -1)
+    else:
+        summed = shard_slot(0)
+        for offset in range(1, REACH + 1):
+            summed = summed + shifted(
+                shard_slot(offset).astype(jnp.bfloat16), "tm", -offset
+            ).astype(jnp.float32)
     keyval_grads = summed.astype(jnp.bfloat16)
     input_grad = contract_last(query_grad_all, query_full) + contract_last(
         keyval_grads, keyval_full

time: 236 us -> 258 us (1.093)
  waiting for transfers between devices: 65.2 us -> 83.8 us
  other arithmetic: 17.3 us -> 21.4 us
  starting transfers between devices: 114 us -> 110 us
  local copies, waits for them, and re-layouts: 8.82 us -> 12 us
    ppermute x8 -> x6, waiting for transfers between devices: 10.9 us -> 23.4 us  [shifted(): lax.ppermute(value, axis, [(source, source + steps) for source in range(l...]
    ppermute x13, waiting for transfers between devices: 33.2 us -> 39.2 us  [xor_swap(): lax.ppermute(value, axis, [(source, source ^ 1 << bit) for source in rang...]
    ppermute x8 -> x6, starting transfers between devices: 26.1 us -> 21.7 us  [shifted(): lax.ppermute(value, axis, [(source, source + steps) for source in range(l...]
  transfers between devices with their start and end apart: 25 -> 23, of which waited for: 17 -> 17; matrix products, arithmetic and copies ran while one was open for 4% -> 5% of each run, Pallas kernels for 0% -> 0%
where the time goes in v12:
time: 258 us; the launch traced here: 256 us
  starting transfers between devices  110 us (43%)
  waiting for transfers between devices  83.8 us (32%)
  matrix products  26.7 us (10%)
  other arithmetic  21.4 us (8%)
  local copies, waits for them, and re-layouts  12 us (5%)
    ppermute x13, starting transfers between devices, xor_swap(): lax.ppermute(value, axis, [(source, source ^ 1 << bit) for source in rang...  68.8 us
    ppermute x13, waiting for transfers between devices, xor_swap(): lax.ppermute(value, axis, [(source, source ^ 1 << bit) for source in rang...  39.2 us
    ppermute x6, waiting for transfers between devices, shifted(): lax.ppermute(value, axis, [(source, source + steps) for source in range(l...  23.4 us
    ppermute x6, starting transfers between devices, shifted(): lax.ppermute(value, axis, [(source, source + steps) for source in range(l...  21.7 us
    ppermute x4, waiting for transfers between devices, ring_pull(): return lax.ppermute(value, ('tm', 'stream'), pairs)  21.1 us
    ppermute x4, starting transfers between devices, ring_pull(): return lax.ppermute(value, ('tm', 'stream'), pairs)  19.6 us
    sub x4, matrix products, per_device(): terms = jnp.where(allowed, jnp.exp(masked - row_max), 0.0)  11.3 us
    unnamed x72, local copies, waits for them, and re-layouts  8.86 us
  transfers between devices with their start and end apart: 23, of which 17 were waited for; matrix products, arithmetic and copies ran while one was open for 5% of the time, Pallas kernels for 0%

profile of v12, /device:TPU:1, one launch (start us, length us, event | category | flops | bytes accessed | tf_op | source)
XLA Modules:
  0.0 256.5 jit_solution(5105919503322589820)
XLA Ops:
  0.7 1.5 fusion.85
  2.2 4.8 %collective-permute-start.3 = (bf16[256,1280]{1,0:T(8,128)(2,1)S(1)}, bf16[256,1280]{1,0:T(8,128)(2,1)S(1)}, u32[]{:S(2)}, u32[]{:S(2)}) collective-permute-start(bf16[256,1280]{1,0:T(8,128)(2,1)S(1)} %fusion.85), channel_id=1, source_target_pairs={{11,0},{0,1},{1,2},{2,3},{15,4},{4,5},{5,6},{6,7},{3,8},{8,9},{9,1... | collective-permute-start | bytes 1966088 | tf_op jit(solution)/shard_map/ppermute | solution.py:133
  7.0 8.6 %collective-permute-start = (bf16[256,1280]{1,0:T(8,128)(2,1)S(1)}, bf16[256,1280]{1,0:T(8,128)(2,1)}, u32[]{:S(2)}, u32[]{:S(2)}) collective-permute-start(bf16[256,1280]{1,0:T(8,128)(2,1)S(1)} %fusion.85), channel_id=1, source_target_pairs={{1,0},{2,1},{3,2},{8,3},{5,4},{6,5},{7,6},{12,7},{9,8},{10,9},{11,... | collective-permute-start | bytes 1966088 | tf_op jit(solution)/shard_map/ppermute | solution.py:133
  15.7 3.4 %collective-permute-start.1 = (bf16[256,640]{1,0:T(8,128)(2,1)S(1)}, bf16[256,640]{1,0:T(8,128)(2,1)S(1)}, u32[]{:S(2)}, u32[]{:S(2)}) collective-permute-start(bf16[256,640]{1,0:T(8,128)(2,1)S(1)} %get-tuple-element.9), channel_id=1, source_target_pairs={{2,0},{3,1},{8,2},{9,3},{6,4},{7,5},{12,6},{13,7},{10,8},{11,9},{0... | collective-permute-start | bytes 983048 | tf_op jit(solution)/shard_map/ppermute | solution.py:133
  19.0 2.8 %collective-permute-start.2 = (bf16[256,640]{1,0:T(8,128)(2,1)S(1)}, bf16[256,640]{1,0:T(8,128)(2,1)S(1)}, u32[]{:S(2)}, u32[]{:S(2)}) collective-permute-start(bf16[256,640]{1,0:T(8,128)(2,1)S(1)} %get-tuple-element.8), channel_id=1, source_target_pairs={{10,0},{11,1},{0,2},{1,3},{14,4},{15,5},{4,6},{5,7},{2,8},{3,9},{8... | collective-permute-start | bytes 983048 | tf_op jit(solution)/shard_map/ppermute | solution.py:133
  22.0 21.1 %collective-permute-done.1 = bf16[256,640]{1,0:T(8,128)(2,1)S(1)} collective-permute-done((bf16[256,640]{1,0:T(8,128)(2,1)S(1)}, bf16[256,640]{1,0:T(8,128)(2,1)S(1)}, u32[]{:S(2)}, u32[]{:S(2)}) %collective-permute-start.1) | collective-permute-done | bytes 327712 | tf_op jit(solution)/shard_map/ppermute | solution.py:133
  43.2 0.9 copy-done.26
  44.1 1.6 select_select_fusion.3
  45.7 1.8 pad_maximum_fusion
  47.8 3.4 %collective-permute-start.4 = (bf16[1024,1280]{1,0:T(8,128)(2,1)}, bf16[1024,1280]{1,0:T(8,128)(2,1)}, u32[]{:S(2)}, u32[]{:S(2)}) collective-permute-start(bf16[1024,1280]{1,0:T(8,128)(2,1)} %pad_maximum_fusion), channel_id=1, source_target_pairs={{0,4},{4,0},{8,12},{12,8},{16,20},{20,16},{24,28},{28,24},{32,36},... | collective-permute-start | bytes 7864328 | tf_op jit(solution)/shard_map/ppermute | solution.py:20
  51.9 1.0 fusion.89
  52.8 3.2 %collective-permute-done.4 = bf16[1024,1280]{1,0:T(8,128)(2,1)} collective-permute-done((bf16[1024,1280]{1,0:T(8,128)(2,1)}, bf16[1024,1280]{1,0:T(8,128)(2,1)}, u32[]{:S(2)}, u32[]{:S(2)}) %collective-permute-start.4) | collective-permute-done | bytes 2621472 | tf_op jit(solution)/shard_map/ppermute | solution.py:20
  56.0 2.8 %broadcast_select_fusion.1 = (bf16[1024,1280]{1,0:T(8,128)(2,1)S(1)}, bf16[1024,1280]{1,0:T(8,128)(2,1)S(1)}) fusion(bf16[1024,1280]{1,0:T(8,128)(2,1)} %collective-permute-done.4, pred[]{:T(512)S(6)} %eq.64, bf16[256,1280]{1,0:T(8,128)(2,1)} %copy-done.5, bf16[256,1280]{1,0:T(8,128)(2,1)} %copy-done.3, bf16[256,1280]{1,0:T(8,128)(2,1)} %copy-done.4, ...), kind=kLoop, calls=%fused_computation.6 | loop fusion | flops 13107200 | bytes 10485761 | tf_op jit(solution)/shard_map/jit(_where)/select_n | solution.py:189
  58.9 0.9 copy-done.25
  60.1 6.4 %collective-permute-start.6 = (bf16[128,512]{1,0:T(8,128)(2,1)S(1)}, bf16[128,512]{1,0:T(8,128)(2,1)S(1)}, u32[]{:S(2)}, u32[]{:S(2)}) collective-permute-start(bf16[128,512]{1,0:T(8,128)(2,1)S(1)} %fusion.75), channel_id=1, source_target_pairs={{0,4},{4,8},{8,12},{12,16},{16,20},{20,24},{24,28},{28,32},{32,36}... | collective-permute-start | bytes 393224 | tf_op jit(solution)/shard_map/ppermute | solution.py:15
  66.5 3.1 %collective-permute-start.5 = (bf16[128,512]{1,0:T(8,128)(2,1)S(1)}, bf16[128,512]{1,0:T(8,128)(2,1)S(1)}, u32[]{:S(2)}, u32[]{:S(2)}) collective-permute-start(bf16[128,512]{1,0:T(8,128)(2,1)S(1)} %fusion.75), channel_id=1, source_target_pairs={{0,16},{4,20},{8,24},{12,28},{16,32},{20,36},{24,40},{28,44},{32,4... | collective-permute-start | bytes 393224 | tf_op jit(solution)/shard_map/ppermute | solution.py:15
  71.2 4.0 %collective-permute-start.7 = (bf16[256,512]{1,0:T(8,128)(2,1)S(1)}, bf16[256,512]{1,0:T(8,128)(2,1)S(1)}, u32[]{:S(2)}, u32[]{:S(2)}) collective-permute-start(bf16[256,512]{1,0:T(8,128)(2,1)S(1)} %pad_maximum_fusion.3), channel_id=1, source_target_pairs={{0,8},{4,12},{8,16},{12,20},{16,24},{20,28},{24,32},{28,36},{32,40... | collective-permute-start | bytes 786440 | tf_op jit(solution)/shard_map/ppermute | solution.py:15
  76.6 2.3 collective-permute-done.7
  78.9 2.7 %fusion.128 = (f32[4,128]{1,0:T(4,128)S(1)}, f32[4,128,640]{1,2,0:T(8,128)}) fusion(bf16[128,4,64]{0,2,1:T(8,128)(2,1)} %bitcast.298, pred[128,640]{0,1:T(8,128)(4,1)} %fusion.89, bf16[640,512]{1,0:T(8,128)(2,1)S(1)} %pad_maximum_fusion.2), kind=kOutput, calls=%fused_computation.195 | convolution fusion | flops 43582080 | bytes 1705984 | tf_op jit(solution)/shard_map/sub | solution.py:245
  81.6 2.6 %fusion.130 = (f32[4,128]{1,0:T(4,128)S(1)}, f32[4,128,640]{1,2,0:T(8,128)}) fusion(bf16[128,4,64]{0,2,1:T(8,128)(2,1)} %bitcast.300, pred[128,640]{0,1:T(8,128)(4,1)} %fusion.89, bf16[640,512]{1,0:T(8,128)(2,1)S(1)} %pad_maximum_fusion.2), kind=kOutput, calls=%fused_computation.197 | convolution fusion | flops 43582080 | bytes 1705984 | tf_op jit(solution)/shard_map/sub | solution.py:245
  84.3 2.7 %fusion.129 = (f32[4,128]{1,0:T(4,128)S(1)}, f32[4,128,640]{1,2,0:T(8,128)}) fusion(bf16[128,4,64]{0,2,1:T(8,128)(2,1)} %bitcast.302, pred[128,640]{0,1:T(8,128)(4,1)} %fusion.89, bf16[640,512]{1,0:T(8,128)(2,1)S(1)} %pad_maximum_fusion.2), kind=kOutput, calls=%fused_computation.196 | convolution fusion | flops 43582080 | bytes 1705984 | tf_op jit(solution)/shard_map/sub | solution.py:245
  87.0 3.3 %fusion.131 = (f32[4,128]{1,0:T(4,128)}, f32[4,128,640]{1,2,0:T(8,128)}) fusion(bf16[128,4,64]{0,2,1:T(8,128)(2,1)} %bitcast.304, pred[128,640]{0,1:T(8,128)(4,1)} %fusion.89, bf16[640,512]{1,0:T(8,128)(2,1)S(1)} %pad_maximum_fusion.2), kind=kOutput, calls=%fused_computation.198 | convolution fusion | flops 43582080 | bytes 1705984 | tf_op jit(solution)/shard_map/sub | solution.py:245
  91.0 1.4 divide_convert_fusion.3
  100.9 1.3 collective-permute-start.8
  102.2 10.5 %collective-permute-done.8 = bf16[256,512]{0,1:T(8,128)(2,1)S(1)} collective-permute-done((bf16[256,512]{0,1:T(8,128)(2,1)S(1)}, bf16[256,512]{0,1:T(8,128)(2,1)S(1)}, u32[]{:S(2)}, u32[]{:S(2)}) %collective-permute-start.8) | collective-permute-done | bytes 262176 | tf_op jit(solution)/shard_map/ppermute | solution.py:15
  113.6 5.6 %collective-permute-start.10 = (f32[128,512]{0,1:T(8,128)}, f32[128,512]{0,1:T(8,128)}, u32[]{:S(2)}, u32[]{:S(2)}) collective-permute-start(f32[128,512]{0,1:T(8,128)} %slice_add_fusion.1), channel_id=1, source_target_pairs={{4,0},{8,4},{12,8},{16,12},{20,16},{24,20},{28,24},{32,28},{36,32}... | collective-permute-start | bytes 786440 | tf_op jit(solution)/shard_map/ppermute | solution.py:15
  119.2 1.8 copy.104
  121.0 0.9 slice.172
  121.9 1.3 collective-permute-start.9
  123.2 1.0 broadcast_select_fusion.3
  124.3 10.2 %collective-permute-done.9 = bf16[128,512]{0,1:T(8,128)(2,1)S(1)} collective-permute-done((bf16[128,512]{0,1:T(8,128)(2,1)S(1)}, bf16[128,512]{0,1:T(8,128)(2,1)S(1)}, u32[]{:S(2)}, u32[]{:S(2)}) %collective-permute-start.9) | collective-permute-done | bytes 131104 | tf_op jit(solution)/shard_map/ppermute | solution.py:15
  134.8 1.2 fusion.92
  136.0 1.3 fusion.103
  137.3 2.1 collective-permute-start.11
  139.4 2.7 %collective-permute-done.11 = f32[1024,256]{1,0:T(8,128)} collective-permute-done((f32[1024,256]{1,0:T(8,128)}, f32[1024,256]{1,0:T(8,128)}, u32[]{:S(2)}, u32[]{:S(2)}) %collective-permute-start.11) | collective-permute-done | bytes 1048608 | tf_op jit(solution)/shard_map/ppermute | solution.py:20
  142.2 1.7 convolution_add_fusion
  143.9 1.0 copy-done.7
  145.6 7.9 %collective-permute-start.12 = (bf16[512,256]{1,0:T(8,128)(2,1)}, bf16[512,256]{1,0:T(8,128)(2,1)}, u32[]{:S(2)}, u32[]{:S(2)}) collective-permute-start(bf16[512,256]{1,0:T(8,128)(2,1)} %slice.281), channel_id=1, source_target_pairs={{0,1},{1,0},{2,3},{3,2},{4,5},{5,4},{6,7},{7,6},{8,9},{9,8},{10,11... | collective-permute-start | bytes 786440 | tf_op jit(solution)/shard_map/ppermute | solution.py:20
  153.5 6.7 %collective-permute-done.12 = bf16[512,256]{1,0:T(8,128)(2,1)} collective-permute-done((bf16[512,256]{1,0:T(8,128)(2,1)}, bf16[512,256]{1,0:T(8,128)(2,1)}, u32[]{:S(2)}, u32[]{:S(2)}) %collective-permute-start.12) | collective-permute-done | bytes 262176 | tf_op jit(solution)/shard_map/ppermute | solution.py:20
  160.2 1.2 slice_add_fusion
  162.8 5.4 %collective-permute-start.13 = (bf16[256,256]{1,0:T(8,128)(2,1)}, bf16[256,256]{1,0:T(8,128)(2,1)}, u32[]{:S(2)}, u32[]{:S(2)}) collective-permute-start(bf16[256,256]{1,0:T(8,128)(2,1)} %select_convert_fusion), channel_id=1, source_target_pairs={{0,2},{1,3},{2,0},{3,1},{4,6},{5,7},{6,4},{7,5},{8,10},{9,11},{10,... | collective-permute-start | bytes 393224 | tf_op jit(solution)/shard_map/ppermute | solution.py:20
  168.2 7.0 %collective-permute-done.13 = bf16[256,256]{1,0:T(8,128)(2,1)} collective-permute-done((bf16[256,256]{1,0:T(8,128)(2,1)}, bf16[256,256]{1,0:T(8,128)(2,1)}, u32[]{:S(2)}, u32[]{:S(2)}) %collective-permute-start.13) | collective-permute-done | bytes 131104 | tf_op jit(solution)/shard_map/ppermute | solution.py:20
  175.2 1.1 convert_add_fusion
  177.7 3.4 %collective-permute-start.14 = (f32[128,256]{1,0:T(8,128)}, f32[128,256]{1,0:T(8,128)}, u32[]{:S(2)}, u32[]{:S(2)}) collective-permute-start(f32[128,256]{1,0:T(8,128)} %slice_select_fusion), channel_id=1, source_target_pairs={{0,16},{4,20},{8,24},{12,28},{16,0},{20,4},{24,8},{28,12},{32,48},... | collective-permute-start | bytes 393224 | tf_op jit(solution)/shard_map/ppermute | solution.py:20
  181.1 3.4 %collective-permute-done.14 = f32[128,256]{1,0:T(8,128)} collective-permute-done((f32[128,256]{1,0:T(8,128)}, f32[128,256]{1,0:T(8,128)}, u32[]{:S(2)}, u32[]{:S(2)}) %collective-permute-start.14) | collective-permute-done | bytes 131104 | tf_op jit(solution)/shard_map/ppermute | solution.py:20
  184.5 1.1 select_add_fusion
  185.5 9.4 %collective-permute-start.15 = (f32[64,256]{1,0:T(8,128)S(1)}, f32[64,256]{1,0:T(8,128)S(1)}, u32[]{:S(2)}, u32[]{:S(2)}) collective-permute-start(f32[64,256]{1,0:T(8,128)S(1)} %slice_select_fusion.1), channel_id=1, source_target_pairs={{0,64},{4,68},{8,72},{12,76},{16,80},{20,84},{24,88},{28,92},{32,9... | collective-permute-start | bytes 196616 | tf_op jit(solution)/shard_map/ppermute | solution.py:20
  195.0 1.6 collective-permute-done.15
  197.3 3.2 %collective-permute-start.16 = (f32[64,256]{1,0:T(8,128)}, f32[64,256]{1,0:T(8,128)}, u32[]{:S(2)}, u32[]{:S(2)}) collective-permute-start(f32[64,256]{1,0:T(8,128)} %select_add_fusion.1), channel_id=1, source_target_pairs={{0,8},{4,12},{8,0},{12,4},{16,24},{20,28},{24,16},{28,20},{32,40},... | collective-permute-start | bytes 196616 | tf_op jit(solution)/shard_map/ppermute | solution.py:20
  200.5 6.0 %collective-permute-done.16 = f32[64,256]{1,0:T(8,128)} collective-permute-done((f32[64,256]{1,0:T(8,128)}, f32[64,256]{1,0:T(8,128)}, u32[]{:S(2)}, u32[]{:S(2)}) %collective-permute-start.16) | collective-permute-done | bytes 65568 | tf_op jit(solution)/shard_map/ppermute | solution.py:20
  206.6 0.9 add.132
  207.5 4.1 %collective-permute-start.17 = (f32[64,256]{1,0:T(8,128)S(1)}, f32[64,256]{1,0:T(8,128)S(1)}, u32[]{:S(2)}, u32[]{:S(2)}) collective-permute-start(f32[64,256]{1,0:T(8,128)S(1)} %add.132), channel_id=1, source_target_pairs={{0,32},{4,36},{8,40},{12,44},{16,48},{20,52},{24,56},{28,60},{32,0... | collective-permute-start | bytes 196616 | tf_op jit(solution)/shard_map/ppermute | solution.py:20
  211.6 1.3 convolution_convert_fusion.7
  212.9 1.0 collective-permute-done.17
  214.0 7.4 %collective-permute-start.18 = (f32[64,256]{1,0:T(8,128)S(1)}, f32[64,256]{1,0:T(8,128)S(1)}, u32[]{:S(2)}, u32[]{:S(2)}) collective-permute-start(f32[64,256]{1,0:T(8,128)S(1)} %add.133), channel_id=1, source_target_pairs={{0,128},{4,132},{8,136},{12,140},{16,144},{20,148},{24,152},{28,15... | collective-permute-start | bytes 196616 | tf_op jit(solution)/shard_map/ppermute | solution.py:20
  221.4 1.3 convolution_convert_fusion.3
  223.0 7.8 %collective-permute-start.19 = (f32[64,256]{1,0:T(8,128)S(1)}, f32[64,256]{1,0:T(8,128)S(1)}, u32[]{:S(2)}, u32[]{:S(2)}) collective-permute-start(f32[64,256]{1,0:T(8,128)S(1)} %add.134), channel_id=1, source_target_pairs={{0,256},{4,260},{8,264},{12,268},{16,272},{20,276},{24,280},{28,28... | collective-permute-start | bytes 196616 | tf_op jit(solution)/shard_map/ppermute | solution.py:20
  231.2 1.4 collective-permute-done.19
  232.6 3.6 %collective-permute-start.20 = (f32[64,256]{1,0:T(8,128)S(1)}, f32[64,256]{1,0:T(8,128)S(1)}, u32[]{:S(2)}, u32[]{:S(2)}) collective-permute-start(f32[64,256]{1,0:T(8,128)S(1)} %add.135), channel_id=1, source_target_pairs={{0,64},{4,68},{8,72},{12,76},{16,80},{20,84},{24,88},{28,92},{32,9... | collective-permute-start | bytes 196616 | tf_op jit(solution)/shard_map/ppermute | solution.py:20
  236.5 2.4 collective-permute-done.20
  239.0 2.0 collective-permute-start.21
  241.4 3.4 %collective-permute-done.21 = f32[128,256]{1,0:T(8,128)S(1)} collective-permute-done((f32[128,256]{1,0:T(8,128)S(1)}, f32[128,256]{1,0:T(8,128)S(1)}, u32[]{:S(2)}, u32[]{:S(2)}) %collective-permute-start.21) | collective-permute-done | bytes 131104 | tf_op jit(solution)/shard_map/ppermute | solution.py:20
  244.9 9.2 %collective-permute-start.22 = (f32[256,256]{1,0:T(8,128)S(1)}, f32[256,256]{1,0:T(8,128)S(1)}, u32[]{:S(2)}, u32[]{:S(2)}) collective-permute-start(f32[256,256]{1,0:T(8,128)S(1)} %maximum_select_fusion.1), channel_id=1, source_target_pairs={{0,4},{4,0},{8,12},{12,8},{16,20},{20,16},{24,28},{28,24},{32,36},... | collective-permute-start | bytes 786440 | tf_op jit(solution)/shard_map/ppermute | solution.py:20
  254.1 1.5 fusion.58
  (128 shorter events, 20.5 us)
Async XLA Ops:
  0.6 69.8 %copy-start = (bf16[1,128,1024]{2,1,0:T(8,128)(2,1)S(1)}, bf16[1,128,1024]{2,1,0:T(8,128)(2,1)}, u32[]{:S(2)}) copy-start(bf16[1,128,1024]{2,1,0:T(8,128)(2,1)} %param.7) | copy-start | bytes 786436
  2.2 41.0 %collective-permute-start.3 = (bf16[256,1280]{1,0:T(8,128)(2,1)S(1)}, bf16[256,1280]{1,0:T(8,128)(2,1)S(1)}, u32[]{:S(2)}, u32[]{:S(2)}) collective-permute-start(bf16[256,1280]{1,0:T(8,128)(2,1)S(1)} %fusion.85), channel_id=1, source_target_pairs={{11,0},{0,1},{1,2},{2,3},{15,4},{4,5},{5,6},{6,7},{3,8},{8,9},{9,1... | collective-permute-start | bytes 1966088 | tf_op jit(solution)/shard_map/ppermute | solution.py:133
  7.0 37.1 %collective-permute-start = (bf16[256,1280]{1,0:T(8,128)(2,1)S(1)}, bf16[256,1280]{1,0:T(8,128)(2,1)}, u32[]{:S(2)}, u32[]{:S(2)}) collective-permute-start(bf16[256,1280]{1,0:T(8,128)(2,1)S(1)} %fusion.85), channel_id=1, source_target_pairs={{1,0},{2,1},{3,2},{8,3},{5,4},{6,5},{7,6},{12,7},{9,8},{10,9},{11,... | collective-permute-start | bytes 1966088 | tf_op jit(solution)/shard_map/ppermute | solution.py:133
  15.7 27.4 %collective-permute-start.1 = (bf16[256,640]{1,0:T(8,128)(2,1)S(1)}, bf16[256,640]{1,0:T(8,128)(2,1)S(1)}, u32[]{:S(2)}, u32[]{:S(2)}) collective-permute-start(bf16[256,640]{1,0:T(8,128)(2,1)S(1)} %get-tuple-element.9), channel_id=1, source_target_pairs={{2,0},{3,1},{8,2},{9,3},{6,4},{7,5},{12,6},{13,7},{10,8},{11,9},{0... | collective-permute-start | bytes 983048 | tf_op jit(solution)/shard_map/ppermute | solution.py:133
  19.0 24.1 %collective-permute-start.2 = (bf16[256,640]{1,0:T(8,128)(2,1)S(1)}, bf16[256,640]{1,0:T(8,128)(2,1)S(1)}, u32[]{:S(2)}, u32[]{:S(2)}) collective-permute-start(bf16[256,640]{1,0:T(8,128)(2,1)S(1)} %get-tuple-element.8), channel_id=1, source_target_pairs={{10,0},{11,1},{0,2},{1,3},{14,4},{15,5},{4,6},{5,7},{2,8},{3,9},{8... | collective-permute-start | bytes 983048 | tf_op jit(solution)/shard_map/ppermute | solution.py:133
  43.2 0.9 copy-start.26
  45.7 1.8 copy-start.3
  45.7 1.9 copy-start.4
  45.7 2.1 copy-start.5
  47.8 8.3 %collective-permute-start.4 = (bf16[1024,1280]{1,0:T(8,128)(2,1)}, bf16[1024,1280]{1,0:T(8,128)(2,1)}, u32[]{:S(2)}, u32[]{:S(2)}) collective-permute-start(bf16[1024,1280]{1,0:T(8,128)(2,1)} %pad_maximum_fusion), channel_id=1, source_target_pairs={{0,4},{4,0},{8,12},{12,8},{16,20},{20,16},{24,28},{28,24},{32,36},... | collective-permute-start | bytes 7864328 | tf_op jit(solution)/shard_map/ppermute | solution.py:20
  58.8 1.0 copy-start.25
  59.8 10.6 %copy-start.1 = (bf16[1024,512]{1,0:T(8,128)(2,1)}, bf16[1024,512]{1,0:T(8,128)(2,1)S(1)}, u32[]{:S(2)}) copy-start(bf16[1024,512]{1,0:T(8,128)(2,1)S(1)} %pad_maximum_fusion.1) | copy-start | bytes 3145732
  60.1 11.1 %collective-permute-start.6 = (bf16[128,512]{1,0:T(8,128)(2,1)S(1)}, bf16[128,512]{1,0:T(8,128)(2,1)S(1)}, u32[]{:S(2)}, u32[]{:S(2)}) collective-permute-start(bf16[128,512]{1,0:T(8,128)(2,1)S(1)} %fusion.75), channel_id=1, source_target_pairs={{0,4},{4,8},{8,12},{12,16},{16,20},{20,24},{24,28},{28,32},{32,36}... | collective-permute-start | bytes 393224 | tf_op jit(solution)/shard_map/ppermute | solution.py:15
  66.5 10.1 %collective-permute-start.5 = (bf16[128,512]{1,0:T(8,128)(2,1)S(1)}, bf16[128,512]{1,0:T(8,128)(2,1)S(1)}, u32[]{:S(2)}, u32[]{:S(2)}) collective-permute-start(bf16[128,512]{1,0:T(8,128)(2,1)S(1)} %fusion.75), channel_id=1, source_target_pairs={{0,16},{4,20},{8,24},{12,28},{16,32},{20,36},{24,40},{28,44},{32,4... | collective-permute-start | bytes 393224 | tf_op jit(solution)/shard_map/ppermute | solution.py:15
  71.2 7.7 %collective-permute-start.7 = (bf16[256,512]{1,0:T(8,128)(2,1)S(1)}, bf16[256,512]{1,0:T(8,128)(2,1)S(1)}, u32[]{:S(2)}, u32[]{:S(2)}) collective-permute-start(bf16[256,512]{1,0:T(8,128)(2,1)S(1)} %pad_maximum_fusion.3), channel_id=1, source_target_pairs={{0,8},{4,12},{8,16},{12,20},{16,24},{20,28},{24,32},{28,36},{32,40... | collective-permute-start | bytes 786440 | tf_op jit(solution)/shard_map/ppermute | solution.py:15
  90.3 2.1 copy-start.30
  92.4 0.8 copy-start.34
  92.7 1.4 copy-start.20
  93.2 0.8 copy-start.14
  93.3 1.0 copy-start.28
  94.2 1.3 copy-start.19
  94.9 3.9 %copy-start.13 = (bf16[4,128,640]{1,2,0:T(8,128)(2,1)}, bf16[4,128,640]{1,2,0:T(8,128)(2,1)S(1)}, u32[]{:S(2)}) copy-start(bf16[4,128,640]{1,2,0:T(8,128)(2,1)S(1)} %fusion.44) | copy-start | bytes 1966084
  94.9 1.0 copy-start.29
  95.6 1.3 copy-start.18
  96.6 1.8 copy-start.11
  96.6 1.0 copy-start.27
  97.1 1.3 copy-start.33
  98.0 0.8 copy-start.32
  98.0 1.2 copy-start.31
  98.4 1.0 copy-start.9
  100.8 11.9 %copy-start.8 = (f32[640,512]{0,1:T(8,128)}, f32[640,512]{0,1:T(8,128)S(1)}, u32[]{:S(2)}) copy-start(f32[640,512]{0,1:T(8,128)S(1)} %fusion.67) | copy-start | bytes 3932164
  100.8 12.7 %copy-start.17 = (bf16[640,512]{0,1:T(8,128)(2,1)}, bf16[640,512]{0,1:T(8,128)(2,1)S(1)}, u32[]{:S(2)}) copy-start(bf16[640,512]{0,1:T(8,128)(2,1)S(1)} %convert.11) | copy-start | bytes 1966084
  100.9 11.8 %collective-permute-start.8 = (bf16[256,512]{0,1:T(8,128)(2,1)S(1)}, bf16[256,512]{0,1:T(8,128)(2,1)S(1)}, u32[]{:S(2)}, u32[]{:S(2)}) collective-permute-start(bf16[256,512]{0,1:T(8,128)(2,1)S(1)} %concatenate.64), channel_id=1, source_target_pairs={{8,0},{12,4},{16,8},{20,12},{24,16},{28,20},{32,24},{36,28},{40,32... | collective-permute-start | bytes 786440 | tf_op jit(solution)/shard_map/ppermute | solution.py:15
  112.7 0.9 copy-start.16
  113.6 21.2 %collective-permute-start.10 = (f32[128,512]{0,1:T(8,128)}, f32[128,512]{0,1:T(8,128)}, u32[]{:S(2)}, u32[]{:S(2)}) collective-permute-start(f32[128,512]{0,1:T(8,128)} %slice_add_fusion.1), channel_id=1, source_target_pairs={{4,0},{8,4},{12,8},{16,12},{20,16},{24,20},{28,24},{32,28},{36,32}... | collective-permute-start | bytes 786440 | tf_op jit(solution)/shard_map/ppermute | solution.py:15
  121.9 12.5 %collective-permute-start.9 = (bf16[128,512]{0,1:T(8,128)(2,1)S(1)}, bf16[128,512]{0,1:T(8,128)(2,1)S(1)}, u32[]{:S(2)}, u32[]{:S(2)}) collective-permute-start(bf16[128,512]{0,1:T(8,128)(2,1)S(1)} %slice.172), channel_id=1, source_target_pairs={{16,0},{20,4},{24,8},{28,12},{32,16},{36,20},{40,24},{44,28},{48,3... | collective-permute-start | bytes 393224 | tf_op jit(solution)/shard_map/ppermute | solution.py:15
  124.2 11.8 %copy-start.21 = (bf16[128,2,1,256]{0,3,2,1:T(8,128)(2,1)}, bf16[128,2,1,256]{0,3,2,1:T(8,128)(2,1)S(1)}, u32[]{:S(2)}) copy-start(bf16[128,2,1,256]{0,3,2,1:T(8,128)(2,1)S(1)} %get-tuple-element.10) | copy-start | bytes 393220
  124.2 13.0 %copy-start.22 = (bf16[128,2,1,256]{0,3,2,1:T(8,128)(2,1)}, bf16[128,2,1,256]{0,3,2,1:T(8,128)(2,1)S(1)}, u32[]{:S(2)}) copy-start(bf16[128,2,1,256]{0,3,2,1:T(8,128)(2,1)S(1)} %get-tuple-element.11) | copy-start | bytes 393220
  136.0 1.3 copy-start.23
  137.3 4.9 %collective-permute-start.11 = (f32[1024,256]{1,0:T(8,128)}, f32[1024,256]{1,0:T(8,128)}, u32[]{:S(2)}, u32[]{:S(2)}) collective-permute-start(f32[1024,256]{1,0:T(8,128)} %fusion.103), channel_id=1, source_target_pairs={{0,4},{4,0},{8,12},{12,8},{16,20},{20,16},{24,28},{28,24},{32,36},... | collective-permute-start | bytes 3145736 | tf_op jit(solution)/shard_map/ppermute | solution.py:20
  143.9 1.0 copy-start.7
  145.6 14.6 %collective-permute-start.12 = (bf16[512,256]{1,0:T(8,128)(2,1)}, bf16[512,256]{1,0:T(8,128)(2,1)}, u32[]{:S(2)}, u32[]{:S(2)}) collective-permute-start(bf16[512,256]{1,0:T(8,128)(2,1)} %slice.281), channel_id=1, source_target_pairs={{0,1},{1,0},{2,3},{3,2},{4,5},{5,4},{6,7},{7,6},{8,9},{9,8},{10,11... | collective-permute-start | bytes 786440 | tf_op jit(solution)/shard_map/ppermute | solution.py:20
  161.3 0.8 copy-start.6
  162.8 12.4 %collective-permute-start.13 = (bf16[256,256]{1,0:T(8,128)(2,1)}, bf16[256,256]{1,0:T(8,128)(2,1)}, u32[]{:S(2)}, u32[]{:S(2)}) collective-permute-start(bf16[256,256]{1,0:T(8,128)(2,1)} %select_convert_fusion), channel_id=1, source_target_pairs={{0,2},{1,3},{2,0},{3,1},{4,6},{5,7},{6,4},{7,5},{8,10},{9,11},{10,... | collective-permute-start | bytes 393224 | tf_op jit(solution)/shard_map/ppermute | solution.py:20
  176.3 0.7 copy-start.15
  177.7 6.8 %collective-permute-start.14 = (f32[128,256]{1,0:T(8,128)}, f32[128,256]{1,0:T(8,128)}, u32[]{:S(2)}, u32[]{:S(2)}) collective-permute-start(f32[128,256]{1,0:T(8,128)} %slice_select_fusion), channel_id=1, source_target_pairs={{0,16},{4,20},{8,24},{12,28},{16,0},{20,4},{24,8},{28,12},{32,48},... | collective-permute-start | bytes 393224 | tf_op jit(solution)/shard_map/ppermute | solution.py:20
  185.5 11.1 %collective-permute-start.15 = (f32[64,256]{1,0:T(8,128)S(1)}, f32[64,256]{1,0:T(8,128)S(1)}, u32[]{:S(2)}, u32[]{:S(2)}) collective-permute-start(f32[64,256]{1,0:T(8,128)S(1)} %slice_select_fusion.1), channel_id=1, source_target_pairs={{0,64},{4,68},{8,72},{12,76},{16,80},{20,84},{24,88},{28,92},{32,9... | collective-permute-start | bytes 196616 | tf_op jit(solution)/shard_map/ppermute | solution.py:20
  197.3 9.3 %collective-permute-start.16 = (f32[64,256]{1,0:T(8,128)}, f32[64,256]{1,0:T(8,128)}, u32[]{:S(2)}, u32[]{:S(2)}) collective-permute-start(f32[64,256]{1,0:T(8,128)} %select_add_fusion.1), channel_id=1, source_target_pairs={{0,8},{4,12},{8,0},{12,4},{16,24},{20,28},{24,16},{28,20},{32,40},... | collective-permute-start | bytes 196616 | tf_op jit(solution)/shard_map/ppermute | solution.py:20
  200.5 30.3 %copy-start.12 = (bf16[4,128,640]{1,2,0:T(8,128)(2,1)S(1)}, bf16[4,128,640]{1,2,0:T(8,128)(2,1)}, u32[]{:S(2)}) copy-start(bf16[4,128,640]{1,2,0:T(8,128)(2,1)} %copy-done.11) | copy-start | bytes 1966084
  207.5 6.5 %collective-permute-start.17 = (f32[64,256]{1,0:T(8,128)S(1)}, f32[64,256]{1,0:T(8,128)S(1)}, u32[]{:S(2)}, u32[]{:S(2)}) collective-permute-start(f32[64,256]{1,0:T(8,128)S(1)} %add.132), channel_id=1, source_target_pairs={{0,32},{4,36},{8,40},{12,44},{16,48},{20,52},{24,56},{28,60},{32,0... | collective-permute-start | bytes 196616 | tf_op jit(solution)/shard_map/ppermute | solution.py:20
  212.9 23.3 %copy-start.10 = (bf16[4,128,640]{1,2,0:T(8,128)(2,1)S(1)}, bf16[4,128,640]{1,2,0:T(8,128)(2,1)}, u32[]{:S(2)}) copy-start(bf16[4,128,640]{1,2,0:T(8,128)(2,1)} %copy-done.9) | copy-start | bytes 1966084
  214.0 9.0 %collective-permute-start.18 = (f32[64,256]{1,0:T(8,128)S(1)}, f32[64,256]{1,0:T(8,128)S(1)}, u32[]{:S(2)}, u32[]{:S(2)}) collective-permute-start(f32[64,256]{1,0:T(8,128)S(1)} %add.133), channel_id=1, source_target_pairs={{0,128},{4,132},{8,136},{12,140},{16,144},{20,148},{24,152},{28,15... | collective-permute-start | bytes 196616 | tf_op jit(solution)/shard_map/ppermute | solution.py:20
  222.7 18.2 %copy-start.2 = (bf16[1024,512]{1,0:T(8,128)(2,1)S(1)}, bf16[1024,512]{1,0:T(8,128)(2,1)}, u32[]{:S(2)}) copy-start(bf16[1024,512]{1,0:T(8,128)(2,1)} %copy-done.1) | copy-start | bytes 3145732
  222.7 18.2 %copy-start.24 = (bf16[128,512]{0,1:T(8,128)(2,1)S(1)}, bf16[128,512]{0,1:T(8,128)(2,1)}, u32[]{:S(2)}) copy-start(bf16[128,512]{0,1:T(8,128)(2,1)} %copy-done.23) | copy-start | bytes 393220
  223.0 9.5 %collective-permute-start.19 = (f32[64,256]{1,0:T(8,128)S(1)}, f32[64,256]{1,0:T(8,128)S(1)}, u32[]{:S(2)}, u32[]{:S(2)}) collective-permute-start(f32[64,256]{1,0:T(8,128)S(1)} %add.134), channel_id=1, source_target_pairs={{0,256},{4,260},{8,264},{12,268},{16,272},{20,276},{24,280},{28,28... | collective-permute-start | bytes 196616 | tf_op jit(solution)/shard_map/ppermute | solution.py:20
  232.6 6.4 %collective-permute-start.20 = (f32[64,256]{1,0:T(8,128)S(1)}, f32[64,256]{1,0:T(8,128)S(1)}, u32[]{:S(2)}, u32[]{:S(2)}) collective-permute-start(f32[64,256]{1,0:T(8,128)S(1)} %add.135), channel_id=1, source_target_pairs={{0,64},{4,68},{8,72},{12,76},{16,80},{20,84},{24,88},{28,92},{32,9... | collective-permute-start | bytes 196616 | tf_op jit(solution)/shard_map/ppermute | solution.py:20
  239.0 5.9 %collective-permute-start.21 = (f32[128,256]{1,0:T(8,128)S(1)}, f32[128,256]{1,0:T(8,128)S(1)}, u32[]{:S(2)}, u32[]{:S(2)}) collective-permute-start(f32[128,256]{1,0:T(8,128)S(1)} %maximum_select_fusion.2), channel_id=1, source_target_pairs={{0,16},{4,20},{8,24},{12,28},{16,0},{20,4},{24,8},{28,12},{32,48},... | collective-permute-start | bytes 393224 | tf_op jit(solution)/shard_map/ppermute | solution.py:20
  244.9 10.7 %collective-permute-start.22 = (f32[256,256]{1,0:T(8,128)S(1)}, f32[256,256]{1,0:T(8,128)S(1)}, u32[]{:S(2)}, u32[]{:S(2)}) collective-permute-start(f32[256,256]{1,0:T(8,128)S(1)} %maximum_select_fusion.1), channel_id=1, source_target_pairs={{0,4},{4,0},{8,12},{12,8},{16,20},{20,16},{24,28},{28,24},{32,36},... | collective-permute-start | bytes 786440 | tf_op jit(solution)/shard_map/ppermute | solution.py:20

commit v13 on v11

--- a/solution.py
+++ b/solution.py
@@ -92,8 +92,8 @@
     mine_cols = lax.dynamic_slice_in_dim(grads, core * half_cols, half_cols, 1)
     other_cols = lax.dynamic_slice_in_dim(grads, (1 - core) * half_cols, half_cols, 1)
     current = contract_first(ordered, mine_cols) + xor_swap(
-        contract_first(ordered, other_cols), "tm", 0
-    )
+        contract_first(ordered, other_cols).astype(jnp.bfloat16), "tm", 0
+    ).astype(jnp.float32)
     half_rows = features // 2
     current = current[:half_rows] + xor_swap(
         current[half_rows:].astype(jnp.bfloat16), "stream", 0

time: 236 us -> 235 us (level)
  no operation moved by 1% of the time
where the time goes in v13:
time: 235 us; the launch traced here: 234 us
  starting transfers between devices  114 us (49%)
  waiting for transfers between devices  65.1 us (28%)
  matrix products  26.5 us (11%)
  other arithmetic  17.3 us (7%)
  local copies, waits for them, and re-layouts  8.82 us (4%)
  between operations  2.4 us (1%)
    ppermute x13, starting transfers between devices, xor_swap(): lax.ppermute(value, axis, [(source, source ^ 1 << bit) for source in rang...  68 us
    ppermute x13, waiting for transfers between devices, xor_swap(): lax.ppermute(value, axis, [(source, source ^ 1 << bit) for source in rang...  33.1 us
    ppermute x8, starting transfers between devices, shifted(): lax.ppermute(value, axis, [(source, source + steps) for source in range(l...  26.1 us
    ppermute x4, waiting for transfers between devices, ring_pull(): return lax.ppermute(value, ('tm', 'stream'), pairs)  21.1 us
    ppermute x4, starting transfers between devices, ring_pull(): return lax.ppermute(value, ('tm', 'stream'), pairs)  19.6 us
    sub x4, matrix products, per_device(): terms = jnp.where(allowed, jnp.exp(masked - row_max), 0.0)  11.6 us
    ppermute x8, waiting for transfers between devices, shifted(): lax.ppermute(value, axis, [(source, source + steps) for source in range(l...  10.9 us
    unnamed x72, local copies, waits for them, and re-layouts  7.17 us
  transfers between devices with their start and end apart: 25, of which 17 were waited for; matrix products, arithmetic and copies ran while one was open for 4% of the time, Pallas kernels for 0%

profile of v13, /device:TPU:1, one launch (start us, length us, event | category | flops | bytes accessed | tf_op | source)
XLA Modules:
  0.0 233.8 jit_solution(4738715345856510980)
XLA Ops:
  0.7 1.5 fusion.85
  2.2 4.8 %collective-permute-start.3 = (bf16[256,1280]{1,0:T(8,128)(2,1)S(1)}, bf16[256,1280]{1,0:T(8,128)(2,1)S(1)}, u32[]{:S(2)}, u32[]{:S(2)}) collective-permute-start(bf16[256,1280]{1,0:T(8,128)(2,1)S(1)} %fusion.85), channel_id=1, source_target_pairs={{11,0},{0,1},{1,2},{2,3},{15,4},{4,5},{5,6},{6,7},{3,8},{8,9},{9,1... | collective-permute-start | bytes 1966088 | tf_op jit(solution)/shard_map/ppermute | solution.py:133
  7.0 8.6 %collective-permute-start = (bf16[256,1280]{1,0:T(8,128)(2,1)S(1)}, bf16[256,1280]{1,0:T(8,128)(2,1)}, u32[]{:S(2)}, u32[]{:S(2)}) collective-permute-start(bf16[256,1280]{1,0:T(8,128)(2,1)S(1)} %fusion.85), channel_id=1, source_target_pairs={{1,0},{2,1},{3,2},{8,3},{5,4},{6,5},{7,6},{12,7},{9,8},{10,9},{11,... | collective-permute-start | bytes 1966088 | tf_op jit(solution)/shard_map/ppermute | solution.py:133
  15.7 3.4 %collective-permute-start.1 = (bf16[256,640]{1,0:T(8,128)(2,1)S(1)}, bf16[256,640]{1,0:T(8,128)(2,1)S(1)}, u32[]{:S(2)}, u32[]{:S(2)}) collective-permute-start(bf16[256,640]{1,0:T(8,128)(2,1)S(1)} %get-tuple-element.13), channel_id=1, source_target_pairs={{2,0},{3,1},{8,2},{9,3},{6,4},{7,5},{12,6},{13,7},{10,8},{11,9},{0... | collective-permute-start | bytes 983048 | tf_op jit(solution)/shard_map/ppermute | solution.py:133
  19.0 2.8 %collective-permute-start.2 = (bf16[256,640]{1,0:T(8,128)(2,1)S(1)}, bf16[256,640]{1,0:T(8,128)(2,1)S(1)}, u32[]{:S(2)}, u32[]{:S(2)}) collective-permute-start(bf16[256,640]{1,0:T(8,128)(2,1)S(1)} %get-tuple-element.12), channel_id=1, source_target_pairs={{10,0},{11,1},{0,2},{1,3},{14,4},{15,5},{4,6},{5,7},{2,8},{3,9},{8... | collective-permute-start | bytes 983048 | tf_op jit(solution)/shard_map/ppermute | solution.py:133
  22.0 21.1 %collective-permute-done.1 = bf16[256,640]{1,0:T(8,128)(2,1)S(1)} collective-permute-done((bf16[256,640]{1,0:T(8,128)(2,1)S(1)}, bf16[256,640]{1,0:T(8,128)(2,1)S(1)}, u32[]{:S(2)}, u32[]{:S(2)}) %collective-permute-start.1) | collective-permute-done | bytes 327712 | tf_op jit(solution)/shard_map/ppermute | solution.py:133
  43.2 0.9 copy-done.24
  44.1 1.6 select_select_fusion.3
  45.7 1.7 pad_maximum_fusion
  47.8 3.4 %collective-permute-start.4 = (bf16[1024,1280]{1,0:T(8,128)(2,1)}, bf16[1024,1280]{1,0:T(8,128)(2,1)}, u32[]{:S(2)}, u32[]{:S(2)}) collective-permute-start(bf16[1024,1280]{1,0:T(8,128)(2,1)} %pad_maximum_fusion), channel_id=1, source_target_pairs={{0,4},{4,0},{8,12},{12,8},{16,20},{20,16},{24,28},{28,24},{32,36},... | collective-permute-start | bytes 7864328 | tf_op jit(solution)/shard_map/ppermute | solution.py:20
  51.9 0.8 copy.104
  52.7 1.0 fusion.89
  53.7 2.3 %collective-permute-done.4 = bf16[1024,1280]{1,0:T(8,128)(2,1)} collective-permute-done((bf16[1024,1280]{1,0:T(8,128)(2,1)}, bf16[1024,1280]{1,0:T(8,128)(2,1)}, u32[]{:S(2)}, u32[]{:S(2)}) %collective-permute-start.4) | collective-permute-done | bytes 2621472 | tf_op jit(solution)/shard_map/ppermute | solution.py:20
  56.0 2.8 %broadcast_select_fusion.1 = (bf16[1024,1280]{1,0:T(8,128)(2,1)S(1)}, bf16[1024,1280]{1,0:T(8,128)(2,1)S(1)}) fusion(bf16[1024,1280]{1,0:T(8,128)(2,1)} %collective-permute-done.4, pred[]{:T(512)S(6)} %eq.64, bf16[256,1280]{1,0:T(8,128)(2,1)} %copy-done.5, bf16[256,1280]{1,0:T(8,128)(2,1)} %copy-done.3, bf16[256,1280]{1,0:T(8,128)(2,1)} %copy-done.4, ...), kind=kLoop, calls=%fused_computation.6 | loop fusion | flops 13107200 | bytes 10485761 | tf_op jit(solution)/shard_map/jit(_where)/select_n | solution.py:189
  58.9 0.9 copy-done.23
  60.1 6.4 %collective-permute-start.8 = (bf16[128,512]{1,0:T(8,128)(2,1)S(1)}, bf16[128,512]{1,0:T(8,128)(2,1)S(1)}, u32[]{:S(2)}, u32[]{:S(2)}) collective-permute-start(bf16[128,512]{1,0:T(8,128)(2,1)S(1)} %fusion.75), channel_id=1, source_target_pairs={{0,4},{4,8},{8,12},{12,16},{16,20},{20,24},{24,28},{28,32},{32,36}... | collective-permute-start | bytes 393224 | tf_op jit(solution)/shard_map/ppermute | solution.py:15
  66.5 4.0 %collective-permute-start.7 = (bf16[128,512]{1,0:T(8,128)(2,1)S(1)}, bf16[128,512]{1,0:T(8,128)(2,1)S(1)}, u32[]{:S(2)}, u32[]{:S(2)}) collective-permute-start(bf16[128,512]{1,0:T(8,128)(2,1)S(1)} %fusion.75), channel_id=1, source_target_pairs={{0,8},{4,12},{8,16},{12,20},{16,24},{20,28},{24,32},{28,36},{32,40... | collective-permute-start | bytes 393224 | tf_op jit(solution)/shard_map/ppermute | solution.py:15
  70.5 1.5 collective-permute-start.6
  72.0 3.5 %collective-permute-start.5 = (bf16[128,512]{1,0:T(8,128)(2,1)S(1)}, bf16[128,512]{1,0:T(8,128)(2,1)S(1)}, u32[]{:S(2)}, u32[]{:S(2)}) collective-permute-start(bf16[128,512]{1,0:T(8,128)(2,1)S(1)} %fusion.75), channel_id=1, source_target_pairs={{0,16},{4,20},{8,24},{12,28},{16,32},{20,36},{24,40},{28,44},{32,4... | collective-permute-start | bytes 393224 | tf_op jit(solution)/shard_map/ppermute | solution.py:15
  75.5 0.8 fusion.64
  78.6 2.9 %fusion.129 = (f32[4,128]{1,0:T(4,128)S(1)}, f32[4,128,640]{1,2,0:T(8,128)}) fusion(bf16[128,4,64]{0,2,1:T(8,128)(2,1)} %bitcast.298, pred[128,640]{0,1:T(8,128)(4,1)} %fusion.89, bf16[640,512]{1,0:T(8,128)(2,1)S(1)} %constant_dynamic-update-slice_fusion.2), kind=kOutput, calls=%fused_computation.199 | convolution fusion | flops 43582080 | bytes 1705984 | tf_op jit(solution)/shard_map/sub | solution.py:239
  81.5 2.6 %fusion.131 = (f32[4,128]{1,0:T(4,128)S(1)}, f32[4,128,640]{1,2,0:T(8,128)}) fusion(bf16[128,4,64]{0,2,1:T(8,128)(2,1)} %bitcast.300, pred[128,640]{0,1:T(8,128)(4,1)} %fusion.89, bf16[640,512]{1,0:T(8,128)(2,1)S(1)} %constant_dynamic-update-slice_fusion.2), kind=kOutput, calls=%fused_computation.201 | convolution fusion | flops 43582080 | bytes 1705984 | tf_op jit(solution)/shard_map/sub | solution.py:239
  84.2 2.7 %fusion.130 = (f32[4,128]{1,0:T(4,128)S(1)}, f32[4,128,640]{1,2,0:T(8,128)}) fusion(bf16[128,4,64]{0,2,1:T(8,128)(2,1)} %bitcast.302, pred[128,640]{0,1:T(8,128)(4,1)} %fusion.89, bf16[640,512]{1,0:T(8,128)(2,1)S(1)} %constant_dynamic-update-slice_fusion.2), kind=kOutput, calls=%fused_computation.200 | convolution fusion | flops 43582080 | bytes 1705984 | tf_op jit(solution)/shard_map/sub | solution.py:239
  86.9 3.3 %fusion.132 = (f32[4,128]{1,0:T(4,128)}, f32[4,128,640]{1,2,0:T(8,128)}) fusion(bf16[128,4,64]{0,2,1:T(8,128)(2,1)} %bitcast.304, pred[128,640]{0,1:T(8,128)(4,1)} %fusion.89, bf16[640,512]{1,0:T(8,128)(2,1)S(1)} %constant_dynamic-update-slice_fusion.2), kind=kOutput, calls=%fused_computation.202 | convolution fusion | flops 43582080 | bytes 1705984 | tf_op jit(solution)/shard_map/sub | solution.py:239
  90.1 0.7 broadcast_select_fusion.4
  90.9 1.4 divide_convert_fusion.3
  100.8 6.8 %collective-permute-start.9 = (bf16[128,512]{0,1:T(8,128)(2,1)S(1)}, bf16[128,512]{0,1:T(8,128)(2,1)S(1)}, u32[]{:S(2)}, u32[]{:S(2)}) collective-permute-start(bf16[128,512]{0,1:T(8,128)(2,1)S(1)} %get-tuple-element.8), channel_id=1, source_target_pairs={{4,0},{8,4},{12,8},{16,12},{20,16},{24,20},{28,24},{32,28},{36,32}... | collective-permute-start | bytes 393224 | tf_op jit(solution)/shard_map/ppermute | solution.py:15
  107.6 1.3 collective-permute-start.12
  108.9 1.3 collective-permute-start.11
  110.2 1.3 collective-permute-start.10
  111.9 1.7 collective-permute-done.12
  113.7 3.9 %collective-permute-done.11 = bf16[128,512]{0,1:T(8,128)(2,1)S(1)} collective-permute-done((bf16[128,512]{0,1:T(8,128)(2,1)S(1)}, bf16[128,512]{0,1:T(8,128)(2,1)S(1)}, u32[]{:S(2)}, u32[]{:S(2)}) %collective-permute-start.11) | collective-permute-done | bytes 131104 | tf_op jit(solution)/shard_map/ppermute | solution.py:15
  117.6 4.9 %collective-permute-done.10 = bf16[128,512]{0,1:T(8,128)(2,1)S(1)} collective-permute-done((bf16[128,512]{0,1:T(8,128)(2,1)S(1)}, bf16[128,512]{0,1:T(8,128)(2,1)S(1)}, u32[]{:S(2)}, u32[]{:S(2)}) %collective-permute-start.10) | collective-permute-done | bytes 131104 | tf_op jit(solution)/shard_map/ppermute | solution.py:15
  122.5 1.1 convolution_convert_fusion
  123.7 2.3 collective-permute-start.13
  125.9 1.9 collective-permute-done.13
  127.8 1.3 convolution_add_fusion
  129.2 1.0 copy-done.6
  130.2 5.0 %collective-permute-start.14 = (bf16[512,256]{1,0:T(8,128)(2,1)S(1)}, bf16[512,256]{1,0:T(8,128)(2,1)}, u32[]{:S(2)}, u32[]{:S(2)}) collective-permute-start(bf16[512,256]{1,0:T(8,128)(2,1)S(1)} %slice.279), channel_id=1, source_target_pairs={{0,1},{1,0},{2,3},{3,2},{4,5},{5,4},{6,7},{7,6},{8,9},{9,8},{10,11... | collective-permute-start | bytes 786440 | tf_op jit(solution)/shard_map/ppermute | solution.py:20
  135.1 6.5 %collective-permute-done.14 = bf16[512,256]{1,0:T(8,128)(2,1)} collective-permute-done((bf16[512,256]{1,0:T(8,128)(2,1)S(1)}, bf16[512,256]{1,0:T(8,128)(2,1)}, u32[]{:S(2)}, u32[]{:S(2)}) %collective-permute-start.14) | collective-permute-done | bytes 262176 | tf_op jit(solution)/shard_map/ppermute | solution.py:20
  141.6 1.2 slice_add_fusion
  143.4 6.6 %collective-permute-start.15 = (bf16[256,256]{1,0:T(8,128)(2,1)}, bf16[256,256]{1,0:T(8,128)(2,1)S(1)}, u32[]{:S(2)}, u32[]{:S(2)}) collective-permute-start(bf16[256,256]{1,0:T(8,128)(2,1)} %select_convert_fusion), channel_id=1, source_target_pairs={{0,2},{1,3},{2,0},{3,1},{4,6},{5,7},{6,4},{7,5},{8,10},{9,11},{10,... | collective-permute-start | bytes 393224 | tf_op jit(solution)/shard_map/ppermute | solution.py:20
  150.0 6.9 %collective-permute-done.15 = bf16[256,256]{1,0:T(8,128)(2,1)S(1)} collective-permute-done((bf16[256,256]{1,0:T(8,128)(2,1)}, bf16[256,256]{1,0:T(8,128)(2,1)S(1)}, u32[]{:S(2)}, u32[]{:S(2)}) %collective-permute-start.15) | collective-permute-done | bytes 131104 | tf_op jit(solution)/shard_map/ppermute | solution.py:20
  158.4 5.3 %collective-permute-start.16 = (f32[128,256]{1,0:T(8,128)}, f32[128,256]{1,0:T(8,128)}, u32[]{:S(2)}, u32[]{:S(2)}) collective-permute-start(f32[128,256]{1,0:T(8,128)} %slice_select_fusion), channel_id=1, source_target_pairs={{0,16},{4,20},{8,24},{12,28},{16,0},{20,4},{24,8},{28,12},{32,48},... | collective-permute-start | bytes 393224 | tf_op jit(solution)/shard_map/ppermute | solution.py:20
  163.6 3.7 %collective-permute-done.16 = f32[128,256]{1,0:T(8,128)} collective-permute-done((f32[128,256]{1,0:T(8,128)}, f32[128,256]{1,0:T(8,128)}, u32[]{:S(2)}, u32[]{:S(2)}) %collective-permute-start.16) | collective-permute-done | bytes 131104 | tf_op jit(solution)/shard_map/ppermute | solution.py:20
  167.4 1.1 select_add_fusion
  168.4 5.1 %collective-permute-start.17 = (f32[64,256]{1,0:T(8,128)S(1)}, f32[64,256]{1,0:T(8,128)S(1)}, u32[]{:S(2)}, u32[]{:S(2)}) collective-permute-start(f32[64,256]{1,0:T(8,128)S(1)} %slice_select_fusion.1), channel_id=1, source_target_pairs={{0,64},{4,68},{8,72},{12,76},{16,80},{20,84},{24,88},{28,92},{32,9... | collective-permute-start | bytes 196616 | tf_op jit(solution)/shard_map/ppermute | solution.py:20
  173.6 1.6 collective-permute-done.17
  175.9 6.2 %collective-permute-start.18 = (f32[64,256]{1,0:T(8,128)}, f32[64,256]{1,0:T(8,128)}, u32[]{:S(2)}, u32[]{:S(2)}) collective-permute-start(f32[64,256]{1,0:T(8,128)} %select_add_fusion.1), channel_id=1, source_target_pairs={{0,8},{4,12},{8,0},{12,4},{16,24},{20,28},{24,16},{28,20},{32,40},... | collective-permute-start | bytes 196616 | tf_op jit(solution)/shard_map/ppermute | solution.py:20
  182.1 3.1 %collective-permute-done.18 = f32[64,256]{1,0:T(8,128)} collective-permute-done((f32[64,256]{1,0:T(8,128)}, f32[64,256]{1,0:T(8,128)}, u32[]{:S(2)}, u32[]{:S(2)}) %collective-permute-start.18) | collective-permute-done | bytes 65568 | tf_op jit(solution)/shard_map/ppermute | solution.py:20
  185.2 0.9 add.132
  186.1 5.4 %collective-permute-start.19 = (f32[64,256]{1,0:T(8,128)S(1)}, f32[64,256]{1,0:T(8,128)S(1)}, u32[]{:S(2)}, u32[]{:S(2)}) collective-permute-start(f32[64,256]{1,0:T(8,128)S(1)} %add.132), channel_id=1, source_target_pairs={{0,32},{4,36},{8,40},{12,44},{16,48},{20,52},{24,56},{28,60},{32,0... | collective-permute-start | bytes 196616 | tf_op jit(solution)/shard_map/ppermute | solution.py:20
  191.6 1.3 convolution_convert_fusion.8
  193.2 5.3 %collective-permute-start.20 = (f32[64,256]{1,0:T(8,128)S(1)}, f32[64,256]{1,0:T(8,128)S(1)}, u32[]{:S(2)}, u32[]{:S(2)}) collective-permute-start(f32[64,256]{1,0:T(8,128)S(1)} %add.133), channel_id=1, source_target_pairs={{0,128},{4,132},{8,136},{12,140},{16,144},{20,148},{24,152},{28,15... | collective-permute-start | bytes 196616 | tf_op jit(solution)/shard_map/ppermute | solution.py:20
  198.5 1.3 convolution_convert_fusion.4
  200.1 8.2 %collective-permute-start.21 = (f32[64,256]{1,0:T(8,128)S(1)}, f32[64,256]{1,0:T(8,128)S(1)}, u32[]{:S(2)}, u32[]{:S(2)}) collective-permute-start(f32[64,256]{1,0:T(8,128)S(1)} %add.134), channel_id=1, source_target_pairs={{0,256},{4,260},{8,264},{12,268},{16,272},{20,276},{24,280},{28,28... | collective-permute-start | bytes 196616 | tf_op jit(solution)/shard_map/ppermute | solution.py:20
  208.7 1.3 collective-permute-done.21
  210.1 2.4 %collective-permute-start.22 = (f32[64,256]{1,0:T(8,128)S(1)}, f32[64,256]{1,0:T(8,128)S(1)}, u32[]{:S(2)}, u32[]{:S(2)}) collective-permute-start(f32[64,256]{1,0:T(8,128)S(1)} %add.135), channel_id=1, source_target_pairs={{0,64},{4,68},{8,72},{12,76},{16,80},{20,84},{24,88},{28,92},{32,9... | collective-permute-start | bytes 196616 | tf_op jit(solution)/shard_map/ppermute | solution.py:20
  212.9 3.0 %collective-permute-done.22 = f32[64,256]{1,0:T(8,128)S(1)} collective-permute-done((f32[64,256]{1,0:T(8,128)S(1)}, f32[64,256]{1,0:T(8,128)S(1)}, u32[]{:S(2)}, u32[]{:S(2)}) %collective-permute-start.22) | collective-permute-done | bytes 65568 | tf_op jit(solution)/shard_map/ppermute | solution.py:20
  215.9 3.6 %collective-permute-start.23 = (f32[128,256]{1,0:T(8,128)S(1)}, f32[128,256]{1,0:T(8,128)S(1)}, u32[]{:S(2)}, u32[]{:S(2)}) collective-permute-start(f32[128,256]{1,0:T(8,128)S(1)} %maximum_select_fusion.2), channel_id=1, source_target_pairs={{0,16},{4,20},{8,24},{12,28},{16,0},{20,4},{24,8},{28,12},{32,48},... | collective-permute-start | bytes 393224 | tf_op jit(solution)/shard_map/ppermute | solution.py:20
  220.0 2.1 collective-permute-done.23
  222.1 9.3 %collective-permute-start.24 = (f32[256,256]{1,0:T(8,128)S(1)}, f32[256,256]{1,0:T(8,128)S(1)}, u32[]{:S(2)}, u32[]{:S(2)}) collective-permute-start(f32[256,256]{1,0:T(8,128)S(1)} %maximum_select_fusion.1), channel_id=1, source_target_pairs={{0,4},{4,0},{8,12},{12,8},{16,20},{20,16},{24,28},{28,24},{32,36},... | collective-permute-start | bytes 786440 | tf_op jit(solution)/shard_map/ppermute | solution.py:20
  231.4 1.5 fusion.58
  232.9 0.8 maximum_select_fusion
  (128 shorter events, 16.4 us)
Async XLA Ops:
  0.6 75.7 %copy-start = (bf16[1,128,1024]{2,1,0:T(8,128)(2,1)S(1)}, bf16[1,128,1024]{2,1,0:T(8,128)(2,1)}, u32[]{:S(2)}) copy-start(bf16[1,128,1024]{2,1,0:T(8,128)(2,1)} %param.7) | copy-start | bytes 786436
  2.2 41.0 %collective-permute-start.3 = (bf16[256,1280]{1,0:T(8,128)(2,1)S(1)}, bf16[256,1280]{1,0:T(8,128)(2,1)S(1)}, u32[]{:S(2)}, u32[]{:S(2)}) collective-permute-start(bf16[256,1280]{1,0:T(8,128)(2,1)S(1)} %fusion.85), channel_id=1, source_target_pairs={{11,0},{0,1},{1,2},{2,3},{15,4},{4,5},{5,6},{6,7},{3,8},{8,9},{9,1... | collective-permute-start | bytes 1966088 | tf_op jit(solution)/shard_map/ppermute | solution.py:133
  7.0 37.0 %collective-permute-start = (bf16[256,1280]{1,0:T(8,128)(2,1)S(1)}, bf16[256,1280]{1,0:T(8,128)(2,1)}, u32[]{:S(2)}, u32[]{:S(2)}) collective-permute-start(bf16[256,1280]{1,0:T(8,128)(2,1)S(1)} %fusion.85), channel_id=1, source_target_pairs={{1,0},{2,1},{3,2},{8,3},{5,4},{6,5},{7,6},{12,7},{9,8},{10,9},{11,... | collective-permute-start | bytes 1966088 | tf_op jit(solution)/shard_map/ppermute | solution.py:133
  15.7 27.4 %collective-permute-start.1 = (bf16[256,640]{1,0:T(8,128)(2,1)S(1)}, bf16[256,640]{1,0:T(8,128)(2,1)S(1)}, u32[]{:S(2)}, u32[]{:S(2)}) collective-permute-start(bf16[256,640]{1,0:T(8,128)(2,1)S(1)} %get-tuple-element.13), channel_id=1, source_target_pairs={{2,0},{3,1},{8,2},{9,3},{6,4},{7,5},{12,6},{13,7},{10,8},{11,9},{0... | collective-permute-start | bytes 983048 | tf_op jit(solution)/shard_map/ppermute | solution.py:133
  19.0 24.1 %collective-permute-start.2 = (bf16[256,640]{1,0:T(8,128)(2,1)S(1)}, bf16[256,640]{1,0:T(8,128)(2,1)S(1)}, u32[]{:S(2)}, u32[]{:S(2)}) collective-permute-start(bf16[256,640]{1,0:T(8,128)(2,1)S(1)} %get-tuple-element.12), channel_id=1, source_target_pairs={{10,0},{11,1},{0,2},{1,3},{14,4},{15,5},{4,6},{5,7},{2,8},{3,9},{8... | collective-permute-start | bytes 983048 | tf_op jit(solution)/shard_map/ppermute | solution.py:133
  43.2 0.9 copy-start.24
  45.6 1.7 copy-start.3
  45.7 1.9 copy-start.4
  45.7 2.1 copy-start.5
  45.7 6.2 %copy-start.22 = (bf16[1,128,1024]{2,1,0:T(8,128)(2,1)S(1)}, bf16[1,128,1024]{2,1,0:T(8,128)(2,1)}, u32[]{:S(2)}) copy-start(bf16[1,128,1024]{2,1,0:T(8,128)(2,1)} %param.6) | copy-start | bytes 786436
  47.8 8.3 %collective-permute-start.4 = (bf16[1024,1280]{1,0:T(8,128)(2,1)}, bf16[1024,1280]{1,0:T(8,128)(2,1)}, u32[]{:S(2)}, u32[]{:S(2)}) collective-permute-start(bf16[1024,1280]{1,0:T(8,128)(2,1)} %pad_maximum_fusion), channel_id=1, source_target_pairs={{0,4},{4,0},{8,12},{12,8},{16,20},{20,16},{24,28},{28,24},{32,36},... | collective-permute-start | bytes 7864328 | tf_op jit(solution)/shard_map/ppermute | solution.py:20
  58.8 1.0 copy-start.23
  59.8 16.5 %copy-start.1 = (bf16[1024,512]{1,0:T(8,128)(2,1)}, bf16[1024,512]{1,0:T(8,128)(2,1)S(1)}, u32[]{:S(2)}) copy-start(bf16[1024,512]{1,0:T(8,128)(2,1)S(1)} %pad_maximum_fusion.1) | copy-start | bytes 3145732
  60.1 18.4 %collective-permute-start.8 = (bf16[128,512]{1,0:T(8,128)(2,1)S(1)}, bf16[128,512]{1,0:T(8,128)(2,1)S(1)}, u32[]{:S(2)}, u32[]{:S(2)}) collective-permute-start(bf16[128,512]{1,0:T(8,128)(2,1)S(1)} %fusion.75), channel_id=1, source_target_pairs={{0,4},{4,8},{8,12},{12,16},{16,20},{20,24},{24,28},{28,32},{32,36}... | collective-permute-start | bytes 393224 | tf_op jit(solution)/shard_map/ppermute | solution.py:15
  66.5 12.0 %collective-permute-start.7 = (bf16[128,512]{1,0:T(8,128)(2,1)S(1)}, bf16[128,512]{1,0:T(8,128)(2,1)S(1)}, u32[]{:S(2)}, u32[]{:S(2)}) collective-permute-start(bf16[128,512]{1,0:T(8,128)(2,1)S(1)} %fusion.75), channel_id=1, source_target_pairs={{0,8},{4,12},{8,16},{12,20},{16,24},{20,28},{24,32},{28,36},{32,40... | collective-permute-start | bytes 393224 | tf_op jit(solution)/shard_map/ppermute | solution.py:15
  70.5 8.0 %collective-permute-start.6 = (bf16[128,512]{1,0:T(8,128)(2,1)S(1)}, bf16[128,512]{1,0:T(8,128)(2,1)S(1)}, u32[]{:S(2)}, u32[]{:S(2)}) collective-permute-start(bf16[128,512]{1,0:T(8,128)(2,1)S(1)} %fusion.75), channel_id=1, source_target_pairs={{0,12},{4,16},{8,20},{12,24},{16,28},{20,32},{24,36},{28,40},{32,4... | collective-permute-start | bytes 393224 | tf_op jit(solution)/shard_map/ppermute | solution.py:15
  72.0 6.5 %collective-permute-start.5 = (bf16[128,512]{1,0:T(8,128)(2,1)S(1)}, bf16[128,512]{1,0:T(8,128)(2,1)S(1)}, u32[]{:S(2)}, u32[]{:S(2)}) collective-permute-start(bf16[128,512]{1,0:T(8,128)(2,1)S(1)} %fusion.75), channel_id=1, source_target_pairs={{0,16},{4,20},{8,24},{12,28},{16,32},{20,36},{24,40},{28,44},{32,4... | collective-permute-start | bytes 393224 | tf_op jit(solution)/shard_map/ppermute | solution.py:15
  78.6 19.2 %copy-start.7 = (bf16[640,512]{1,0:T(8,128)(2,1)}, bf16[640,512]{1,0:T(8,128)(2,1)S(1)}, u32[]{:S(2)}) copy-start(bf16[640,512]{1,0:T(8,128)(2,1)S(1)} %constant_dynamic-update-slice_fusion.2) | copy-start | bytes 1966084
  90.1 2.2 copy-start.28
  92.3 0.8 copy-start.32
  92.6 1.4 copy-start.18
  93.1 0.8 copy-start.14
  93.1 1.0 copy-start.26
  94.1 1.3 copy-start.17
  94.7 3.9 %copy-start.13 = (bf16[4,128,640]{1,2,0:T(8,128)(2,1)}, bf16[4,128,640]{1,2,0:T(8,128)(2,1)S(1)}, u32[]{:S(2)}) copy-start(bf16[4,128,640]{1,2,0:T(8,128)(2,1)S(1)} %fusion.44) | copy-start | bytes 1966084
  94.7 1.0 copy-start.27
  95.5 1.3 copy-start.16
  96.5 1.8 copy-start.11
  96.5 0.9 copy-start.25
  96.9 1.3 copy-start.31
  97.8 0.8 copy-start.30
  97.8 1.1 copy-start.29
  98.3 1.0 copy-start.9
  100.6 10.9 %copy-start.21 = (bf16[1,128,1024]{1,2,0:T(8,128)(2,1)S(1)}, bf16[1,128,1024]{1,2,0:T(8,128)(2,1)}, u32[]{:S(2)}) copy-start(bf16[1,128,1024]{1,2,0:T(8,128)(2,1)} %copy.104) | copy-start | bytes 786436
  100.8 11.1 %collective-permute-start.9 = (bf16[128,512]{0,1:T(8,128)(2,1)S(1)}, bf16[128,512]{0,1:T(8,128)(2,1)S(1)}, u32[]{:S(2)}, u32[]{:S(2)}) collective-permute-start(bf16[128,512]{0,1:T(8,128)(2,1)S(1)} %get-tuple-element.8), channel_id=1, source_target_pairs={{4,0},{8,4},{12,8},{16,12},{20,16},{24,20},{28,24},{32,28},{36,32}... | collective-permute-start | bytes 393224 | tf_op jit(solution)/shard_map/ppermute | solution.py:15
  107.6 6.0 %collective-permute-start.12 = (bf16[128,512]{0,1:T(8,128)(2,1)S(1)}, bf16[128,512]{0,1:T(8,128)(2,1)S(1)}, u32[]{:S(2)}, u32[]{:S(2)}) collective-permute-start(bf16[128,512]{0,1:T(8,128)(2,1)S(1)} %get-tuple-element.9), channel_id=1, source_target_pairs={{16,0},{20,4},{24,8},{28,12},{32,16},{36,20},{40,24},{44,28},{48,3... | collective-permute-start | bytes 393224 | tf_op jit(solution)/shard_map/ppermute | solution.py:15
  108.9 8.6 %collective-permute-start.11 = (bf16[128,512]{0,1:T(8,128)(2,1)S(1)}, bf16[128,512]{0,1:T(8,128)(2,1)S(1)}, u32[]{:S(2)}, u32[]{:S(2)}) collective-permute-start(bf16[128,512]{0,1:T(8,128)(2,1)S(1)} %get-tuple-element.10), channel_id=1, source_target_pairs={{12,0},{16,4},{20,8},{24,12},{28,16},{32,20},{36,24},{40,28},{44,3... | collective-permute-start | bytes 393224 | tf_op jit(solution)/shard_map/ppermute | solution.py:15
  110.2 12.2 %collective-permute-start.10 = (bf16[128,512]{0,1:T(8,128)(2,1)S(1)}, bf16[128,512]{0,1:T(8,128)(2,1)S(1)}, u32[]{:S(2)}, u32[]{:S(2)}) collective-permute-start(bf16[128,512]{0,1:T(8,128)(2,1)S(1)} %get-tuple-element.11), channel_id=1, source_target_pairs={{8,0},{12,4},{16,8},{20,12},{24,16},{28,20},{32,24},{36,28},{40,32... | collective-permute-start | bytes 393224 | tf_op jit(solution)/shard_map/ppermute | solution.py:15
  122.5 6.6 %copy-start.19 = (bf16[128,512]{0,1:T(8,128)(2,1)}, bf16[128,512]{0,1:T(8,128)(2,1)S(1)}, u32[]{:S(2)}) copy-start(bf16[128,512]{0,1:T(8,128)(2,1)S(1)} %fusion.93) | copy-start | bytes 393220
  123.7 4.1 %collective-permute-start.13 = (bf16[1024,256]{1,0:T(8,128)(2,1)}, bf16[1024,256]{1,0:T(8,128)(2,1)}, u32[]{:S(2)}, u32[]{:S(2)}) collective-permute-start(bf16[1024,256]{1,0:T(8,128)(2,1)} %convolution_convert_fusion), channel_id=1, source_target_pairs={{0,4},{4,0},{8,12},{12,8},{16,20},{20,16},{24,28},{28,24},{32,36},... | collective-permute-start | bytes 1572872 | tf_op jit(solution)/shard_map/ppermute | solution.py:20
  129.1 1.0 copy-start.6
  130.2 11.4 %collective-permute-start.14 = (bf16[512,256]{1,0:T(8,128)(2,1)S(1)}, bf16[512,256]{1,0:T(8,128)(2,1)}, u32[]{:S(2)}, u32[]{:S(2)}) collective-permute-start(bf16[512,256]{1,0:T(8,128)(2,1)S(1)} %slice.279), channel_id=1, source_target_pairs={{0,1},{1,0},{2,3},{3,2},{4,5},{5,4},{6,7},{7,6},{8,9},{9,8},{10,11... | collective-permute-start | bytes 786440 | tf_op jit(solution)/shard_map/ppermute | solution.py:20
  143.4 13.5 %collective-permute-start.15 = (bf16[256,256]{1,0:T(8,128)(2,1)}, bf16[256,256]{1,0:T(8,128)(2,1)S(1)}, u32[]{:S(2)}, u32[]{:S(2)}) collective-permute-start(bf16[256,256]{1,0:T(8,128)(2,1)} %select_convert_fusion), channel_id=1, source_target_pairs={{0,2},{1,3},{2,0},{3,1},{4,6},{5,7},{6,4},{7,5},{8,10},{9,11},{10,... | collective-permute-start | bytes 393224 | tf_op jit(solution)/shard_map/ppermute | solution.py:20
  157.0 0.7 copy-start.15
  157.7 33.9 %copy-start.8 = (bf16[640,512]{1,0:T(8,128)(2,1)S(1)}, bf16[640,512]{1,0:T(8,128)(2,1)}, u32[]{:S(2)}) copy-start(bf16[640,512]{1,0:T(8,128)(2,1)} %copy-done.7) | copy-start | bytes 1966084
  158.4 9.0 %collective-permute-start.16 = (f32[128,256]{1,0:T(8,128)}, f32[128,256]{1,0:T(8,128)}, u32[]{:S(2)}, u32[]{:S(2)}) collective-permute-start(f32[128,256]{1,0:T(8,128)} %slice_select_fusion), channel_id=1, source_target_pairs={{0,16},{4,20},{8,24},{12,28},{16,0},{20,4},{24,8},{28,12},{32,48},... | collective-permute-start | bytes 393224 | tf_op jit(solution)/shard_map/ppermute | solution.py:20
  168.4 6.8 %collective-permute-start.17 = (f32[64,256]{1,0:T(8,128)S(1)}, f32[64,256]{1,0:T(8,128)S(1)}, u32[]{:S(2)}, u32[]{:S(2)}) collective-permute-start(f32[64,256]{1,0:T(8,128)S(1)} %slice_select_fusion.1), channel_id=1, source_target_pairs={{0,64},{4,68},{8,72},{12,76},{16,80},{20,84},{24,88},{28,92},{32,9... | collective-permute-start | bytes 196616 | tf_op jit(solution)/shard_map/ppermute | solution.py:20
  175.9 9.3 %collective-permute-start.18 = (f32[64,256]{1,0:T(8,128)}, f32[64,256]{1,0:T(8,128)}, u32[]{:S(2)}, u32[]{:S(2)}) collective-permute-start(f32[64,256]{1,0:T(8,128)} %select_add_fusion.1), channel_id=1, source_target_pairs={{0,8},{4,12},{8,0},{12,4},{16,24},{20,28},{24,16},{28,20},{32,40},... | collective-permute-start | bytes 196616 | tf_op jit(solution)/shard_map/ppermute | solution.py:20
  182.1 26.3 %copy-start.12 = (bf16[4,128,640]{1,2,0:T(8,128)(2,1)S(1)}, bf16[4,128,640]{1,2,0:T(8,128)(2,1)}, u32[]{:S(2)}) copy-start(bf16[4,128,640]{1,2,0:T(8,128)(2,1)} %copy-done.11) | copy-start | bytes 1966084
  186.1 7.1 %collective-permute-start.19 = (f32[64,256]{1,0:T(8,128)S(1)}, f32[64,256]{1,0:T(8,128)S(1)}, u32[]{:S(2)}, u32[]{:S(2)}) collective-permute-start(f32[64,256]{1,0:T(8,128)S(1)} %add.132), channel_id=1, source_target_pairs={{0,32},{4,36},{8,40},{12,44},{16,48},{20,52},{24,56},{28,60},{32,0... | collective-permute-start | bytes 196616 | tf_op jit(solution)/shard_map/ppermute | solution.py:20
  192.9 19.6 %copy-start.10 = (bf16[4,128,640]{1,2,0:T(8,128)(2,1)S(1)}, bf16[4,128,640]{1,2,0:T(8,128)(2,1)}, u32[]{:S(2)}) copy-start(bf16[4,128,640]{1,2,0:T(8,128)(2,1)} %copy-done.9) | copy-start | bytes 1966084
  193.2 6.9 %collective-permute-start.20 = (f32[64,256]{1,0:T(8,128)S(1)}, f32[64,256]{1,0:T(8,128)S(1)}, u32[]{:S(2)}, u32[]{:S(2)}) collective-permute-start(f32[64,256]{1,0:T(8,128)S(1)} %add.133), channel_id=1, source_target_pairs={{0,128},{4,132},{8,136},{12,140},{16,144},{20,148},{24,152},{28,15... | collective-permute-start | bytes 196616 | tf_op jit(solution)/shard_map/ppermute | solution.py:20
  199.8 19.7 %copy-start.2 = (bf16[1024,512]{1,0:T(8,128)(2,1)S(1)}, bf16[1024,512]{1,0:T(8,128)(2,1)}, u32[]{:S(2)}) copy-start(bf16[1024,512]{1,0:T(8,128)(2,1)} %copy-done.1) | copy-start | bytes 3145732
  199.8 19.7 %copy-start.20 = (bf16[128,512]{0,1:T(8,128)(2,1)S(1)}, bf16[128,512]{0,1:T(8,128)(2,1)}, u32[]{:S(2)}) copy-start(bf16[128,512]{0,1:T(8,128)(2,1)} %copy-done.19) | copy-start | bytes 393220
  200.1 9.9 %collective-permute-start.21 = (f32[64,256]{1,0:T(8,128)S(1)}, f32[64,256]{1,0:T(8,128)S(1)}, u32[]{:S(2)}, u32[]{:S(2)}) collective-permute-start(f32[64,256]{1,0:T(8,128)S(1)} %add.134), channel_id=1, source_target_pairs={{0,256},{4,260},{8,264},{12,268},{16,272},{20,276},{24,280},{28,28... | collective-permute-start | bytes 196616 | tf_op jit(solution)/shard_map/ppermute | solution.py:20
  210.1 5.8 %collective-permute-start.22 = (f32[64,256]{1,0:T(8,128)S(1)}, f32[64,256]{1,0:T(8,128)S(1)}, u32[]{:S(2)}, u32[]{:S(2)}) collective-permute-start(f32[64,256]{1,0:T(8,128)S(1)} %add.135), channel_id=1, source_target_pairs={{0,64},{4,68},{8,72},{12,76},{16,80},{20,84},{24,88},{28,92},{32,9... | collective-permute-start | bytes 196616 | tf_op jit(solution)/shard_map/ppermute | solution.py:20
  215.9 6.2 %collective-permute-start.23 = (f32[128,256]{1,0:T(8,128)S(1)}, f32[128,256]{1,0:T(8,128)S(1)}, u32[]{:S(2)}, u32[]{:S(2)}) collective-permute-start(f32[128,256]{1,0:T(8,128)S(1)} %maximum_select_fusion.2), channel_id=1, source_target_pairs={{0,16},{4,20},{8,24},{12,28},{16,0},{20,4},{24,8},{28,12},{32,48},... | collective-permute-start | bytes 393224 | tf_op jit(solution)/shard_map/ppermute | solution.py:20
  222.1 10.8 %collective-permute-start.24 = (f32[256,256]{1,0:T(8,128)S(1)}, f32[256,256]{1,0:T(8,128)S(1)}, u32[]{:S(2)}, u32[]{:S(2)}) collective-permute-start(f32[256,256]{1,0:T(8,128)S(1)} %maximum_select_fusion.1), channel_id=1, source_target_pairs={{0,4},{4,0},{8,12},{12,8},{16,20},{20,16},{24,28},{28,24},{32,36},... | collective-permute-start | bytes 786440 | tf_op jit(solution)/shard_map/ppermute | solution.py:20

commit v14 on v13

--- a/solution.py
+++ b/solution.py
@@ -202,74 +202,57 @@
     attn_grad = contract_last(outer_grad, output_full).astype(jnp.bfloat16)
     earlier = [shifted(keyvals, "tm", offset) for offset in range(REACH, 0, -1)]
     window_keyvals = jnp.concatenate(earlier + [keyvals], axis=0)
-    key_parts = []
-    value_parts = []
-    query_grads = []
-    for head_group in range(KV_HEADS):
-        query_cols = slice(
-            head_group * group_size * HEAD_DIM, (head_group + 1) * group_size * HEAD_DIM
-        )
-        key_cols = slice(head_group * HEAD_DIM, (head_group + 1) * HEAD_DIM)
-        value_cols = slice(
-            key_width + head_group * HEAD_DIM, key_width + (head_group + 1) * HEAD_DIM
-        )
-        group_key = None
-        group_value = None
-        query_tile = queries[0:tile_rows, query_cols].reshape(tile_rows, group_size, HEAD_DIM)
-        key_tile = window_keyvals[0:key_span, key_cols]
-        value_tile = window_keyvals[0:key_span, value_cols]
-        query_pos = anchor + 0 + jnp.arange(tile_rows, dtype=jnp.int32)
-        key_pos = anchor - REACH * shard_tokens + 0 + jnp.arange(key_span, dtype=jnp.int32)
-        live_rows = query_pos < valid_count
-        allowed = (key_pos[None, :] <= query_pos[:, None]) & (
-            query_pos[:, None] - key_pos[None, :] < REACH * shard_tokens
-        )
-        allowed = (
-            allowed
-            & (key_pos[None, :] >= 0)
-            & (key_pos[None, :] < valid_count)
-            & live_rows[:, None]
-        )
-        scores = (
-            jnp.einsum("qjd,kd->jqk", query_tile, key_tile, preferred_element_type=jnp.float32)
-            * score_scale
-        )
-        masked = jnp.where(allowed, scores, -1e30)
-        row_max = jnp.max(masked, axis=-1, keepdims=True)
-        terms = jnp.where(allowed, jnp.exp(masked - row_max), 0.0)
-        denom = jnp.sum(terms, axis=-1, keepdims=True)
-        denom = jnp.where(live_rows[:, None], denom, 1.0)
-        attn_probs = (terms / denom).astype(jnp.bfloat16)
-        attn_tile = jnp.einsum(
-            "jqk,kd->qjd", attn_probs, value_tile, preferred_element_type=jnp.float32
-        ).astype(jnp.bfloat16)
-        grad_tile = attn_grad[0:tile_rows, query_cols].reshape(tile_rows, group_size, HEAD_DIM)
-        row_delta = jnp.sum(
-            grad_tile.astype(jnp.float32) * attn_tile.astype(jnp.float32), axis=-1
-        ).T[:, :, None]
-        prob_grad = jnp.einsum(
-            "qjd,kd->jqk", grad_tile, value_tile, preferred_element_type=jnp.float32
-        )
-        score_grad = (
-            attn_probs.astype(jnp.float32) * (prob_grad - row_delta) * score_scale
-        ).astype(jnp.bfloat16)
-        query_grad = jnp.einsum(
-            "jqk,kd->qjd", score_grad, key_tile, preferred_element_type=jnp.float32
-        ).astype(jnp.bfloat16)
-        key_grad = jnp.einsum(
-            "jqk,qjd->kd", score_grad, query_tile, preferred_element_type=jnp.float32
-        )
-        value_grad = jnp.einsum(
-            "jqk,qjd->kd", attn_probs, grad_tile, preferred_element_type=jnp.float32
-        )
-        group_key = key_grad
-        group_value = value_grad
-        tile_list = query_grad.reshape(tile_rows, group_size * HEAD_DIM)
-        key_parts.append(group_key)
-        value_parts.append(group_value)
-        query_grads.append(tile_list)
-    query_grad_all = jnp.concatenate(query_grads, axis=1)
-    partial_value = jnp.concatenate(key_parts + value_parts, axis=1)
+    query_block = queries[0:tile_rows].reshape(tile_rows, KV_HEADS, group_size, HEAD_DIM)
+    key_block = window_keyvals[0:key_span, :key_width].reshape(key_span, KV_HEADS, HEAD_DIM)
+    value_block = window_keyvals[0:key_span, key_width:].reshape(key_span, KV_HEADS, HEAD_DIM)
+    query_pos = anchor + jnp.arange(tile_rows, dtype=jnp.int32)
+    key_pos = anchor - REACH * shard_tokens + jnp.arange(key_span, dtype=jnp.int32)
+    live_rows = query_pos < valid_count
+    allowed = (key_pos[None, :] <= query_pos[:, None]) & (
+        query_pos[:, None] - key_pos[None, :] < REACH * shard_tokens
+    )
+    allowed = (
+        allowed
+        & (key_pos[None, :] >= 0)
+        & (key_pos[None, :] < valid_count)
+        & live_rows[:, None]
+    )
+    scores = (
+        jnp.einsum("qgjd,kgd->gjqk", query_block, key_block, preferred_element_type=jnp.float32)
+        * score_scale
+    )
+    masked = jnp.where(allowed, scores, -1e30)
+    row_max = jnp.max(masked, axis=-1, keepdims=True)
+    terms = jnp.where(allowed, jnp.exp(masked - row_max), 0.0)
+    denom = jnp.sum(terms, axis=-1, keepdims=True)
+    denom = jnp.where(live_rows[:, None], denom, 1.0)
+    attn_probs = (terms / denom).astype(jnp.bfloat16)
+    attn_block = jnp.einsum(
+        "gjqk,kgd->qgjd", attn_probs, value_block, preferred_element_type=jnp.float32
+    ).astype(jnp.bfloat16)
+    grad_block = attn_grad[0:tile_rows].reshape(tile_rows, KV_HEADS, group_size, HEAD_DIM)
+    row_delta = jnp.transpose(
+        jnp.sum(grad_block.astype(jnp.float32) * attn_block.astype(jnp.float32), axis=-1),
+        (1, 2, 0),
+    )[..., None]
+    prob_grad = jnp.einsum(
+        "qgjd,kgd->gjqk", grad_block, value_block, preferred_element_type=jnp.float32
+    )
+    score_grad = (
+        attn_probs.astype(jnp.float32) * (prob_grad - row_delta) * score_scale
+    ).astype(jnp.bfloat16)
+    query_grad_all = (
+        jnp.einsum("gjqk,kgd->qgjd", score_grad, key_block, preferred_element_type=jnp.float32)
+        .astype(jnp.bfloat16)
+        .reshape(tile_rows, KV_HEADS * group_size * HEAD_DIM)
+    )
+    key_grad = jnp.einsum(
+        "gjqk,qgjd->kgd", score_grad, query_block, preferred_element_type=jnp.float32
+    ).reshape(key_span, key_width)
+    value_grad = jnp.einsum(
+        "gjqk,qgjd->kgd", attn_probs, grad_block, preferred_element_type=jnp.float32
+    ).reshape(key_span, key_width)
+    partial_value = jnp.concatenate([key_grad, value_grad], axis=1)
 
     def shard_slot(offset):
         return partial_value[(REACH - offset) * shard_tokens : (REACH - offset + 1) * shard_tokens]

time: 235 us -> 221 us (0.940)
  matrix products: 26.5 us -> 15.8 us
  local copies, waits for them, and re-layouts: 8.82 us -> 4.2 us
    sub x4 -> x1, matrix products: 11.6 us -> 4.41 us  [per_device(): terms = jnp.where(allowed, jnp.exp(masked - row_max), 0.0)]
    unnamed x72 -> x34, local copies, waits for them, and re-layouts: 7.17 us -> 3.51 us
    dot_general x20 -> x5, matrix products: 8.67 us -> 5.12 us  [the longest x1 1.55 us: per_device(): jnp.einsum('gjqk,kgd->qgjd', score_grad, key_block, preferred_element_typ...]
  transfers between devices with their start and end apart: 25 -> 25, of which waited for: 17 -> 18; matrix products, arithmetic and copies ran while one was open for 4% -> 3% of each run, Pallas kernels for 0% -> 0%
where the time goes in v14:
time: 221 us; the launch traced here: 220 us
  starting transfers between devices  115 us (52%)
  waiting for transfers between devices  67.2 us (30%)
  other arithmetic  16.2 us (7%)
  matrix products  15.8 us (7%)
  local copies, waits for them, and re-layouts  4.2 us (2%)
    ppermute x13, starting transfers between devices, xor_swap(): lax.ppermute(value, axis, [(source, source ^ 1 << bit) for source in rang...  69.3 us
    ppermute x13, waiting for transfers between devices, xor_swap(): lax.ppermute(value, axis, [(source, source ^ 1 << bit) for source in rang...  34.5 us
    ppermute x8, starting transfers between devices, shifted(): lax.ppermute(value, axis, [(source, source + steps) for source in range(l...  25.8 us
    ppermute x4, waiting for transfers between devices, ring_pull(): return lax.ppermute(value, ('tm', 'stream'), pairs)  21.1 us
    ppermute x4, starting transfers between devices, ring_pull(): return lax.ppermute(value, ('tm', 'stream'), pairs)  19.6 us
    ppermute x8, waiting for transfers between devices, shifted(): lax.ppermute(value, axis, [(source, source + steps) for source in range(l...  11.6 us
  transfers between devices with their start and end apart: 25, of which 18 were waited for; matrix products, arithmetic and copies ran while one was open for 3% of the time, Pallas kernels for 0%

profile of v14, /device:TPU:1, one launch (start us, length us, event | category | flops | bytes accessed | tf_op | source)
XLA Modules:
  0.0 220.2 jit_solution(6667316772147691410)
XLA Ops:
  0.7 1.5 fusion.34
  2.2 4.8 %collective-permute-start.3 = (bf16[256,1280]{1,0:T(8,128)(2,1)S(1)}, bf16[256,1280]{1,0:T(8,128)(2,1)S(1)}, u32[]{:S(2)}, u32[]{:S(2)}) collective-permute-start(bf16[256,1280]{1,0:T(8,128)(2,1)S(1)} %fusion.34), channel_id=1, source_target_pairs={{11,0},{0,1},{1,2},{2,3},{15,4},{4,5},{5,6},{6,7},{3,8},{8,9},{9,1... | collective-permute-start | bytes 1966088 | tf_op jit(solution)/shard_map/ppermute | solution.py:133
  7.0 8.6 %collective-permute-start = (bf16[256,1280]{1,0:T(8,128)(2,1)S(1)}, bf16[256,1280]{1,0:T(8,128)(2,1)}, u32[]{:S(2)}, u32[]{:S(2)}) collective-permute-start(bf16[256,1280]{1,0:T(8,128)(2,1)S(1)} %fusion.34), channel_id=1, source_target_pairs={{1,0},{2,1},{3,2},{8,3},{5,4},{6,5},{7,6},{12,7},{9,8},{10,9},{11,... | collective-permute-start | bytes 1966088 | tf_op jit(solution)/shard_map/ppermute | solution.py:133
  15.7 3.4 %collective-permute-start.1 = (bf16[256,640]{1,0:T(8,128)(2,1)S(1)}, bf16[256,640]{1,0:T(8,128)(2,1)S(1)}, u32[]{:S(2)}, u32[]{:S(2)}) collective-permute-start(bf16[256,640]{1,0:T(8,128)(2,1)S(1)} %get-tuple-element.15), channel_id=1, source_target_pairs={{2,0},{3,1},{8,2},{9,3},{6,4},{7,5},{12,6},{13,7},{10,8},{11,9},{0... | collective-permute-start | bytes 983048 | tf_op jit(solution)/shard_map/ppermute | solution.py:133
  19.0 2.8 %collective-permute-start.2 = (bf16[256,640]{1,0:T(8,128)(2,1)S(1)}, bf16[256,640]{1,0:T(8,128)(2,1)S(1)}, u32[]{:S(2)}, u32[]{:S(2)}) collective-permute-start(bf16[256,640]{1,0:T(8,128)(2,1)S(1)} %get-tuple-element.14), channel_id=1, source_target_pairs={{10,0},{11,1},{0,2},{1,3},{14,4},{15,5},{4,6},{5,7},{2,8},{3,9},{8... | collective-permute-start | bytes 983048 | tf_op jit(solution)/shard_map/ppermute | solution.py:133
  22.0 21.1 %collective-permute-done.1 = bf16[256,640]{1,0:T(8,128)(2,1)S(1)} collective-permute-done((bf16[256,640]{1,0:T(8,128)(2,1)S(1)}, bf16[256,640]{1,0:T(8,128)(2,1)S(1)}, u32[]{:S(2)}, u32[]{:S(2)}) %collective-permute-start.1) | collective-permute-done | bytes 327712 | tf_op jit(solution)/shard_map/ppermute | solution.py:133
  43.2 0.8 copy-done.10
  44.0 1.6 select_select_fusion.3
  45.6 1.7 pad_maximum_fusion
  47.3 3.4 %collective-permute-start.4 = (bf16[1024,1280]{1,0:T(8,128)(2,1)}, bf16[1024,1280]{1,0:T(8,128)(2,1)}, u32[]{:S(2)}, u32[]{:S(2)}) collective-permute-start(bf16[1024,1280]{1,0:T(8,128)(2,1)} %pad_maximum_fusion), channel_id=1, source_target_pairs={{0,4},{4,0},{8,12},{12,8},{16,20},{20,16},{24,28},{28,24},{32,36},... | collective-permute-start | bytes 7864328 | tf_op jit(solution)/shard_map/ppermute | solution.py:20
  51.4 0.8 copy.28
  52.3 1.0 fusion.40
  53.2 2.3 %collective-permute-done.4 = bf16[1024,1280]{1,0:T(8,128)(2,1)} collective-permute-done((bf16[1024,1280]{1,0:T(8,128)(2,1)}, bf16[1024,1280]{1,0:T(8,128)(2,1)}, u32[]{:S(2)}, u32[]{:S(2)}) %collective-permute-start.4) | collective-permute-done | bytes 2621472 | tf_op jit(solution)/shard_map/ppermute | solution.py:20
  55.6 2.4 %broadcast_select_fusion = (bf16[1024,1280]{1,0:T(8,128)(2,1)S(1)}, bf16[1024,1280]{1,0:T(8,128)(2,1)S(1)}) fusion(bf16[1024,1280]{1,0:T(8,128)(2,1)} %collective-permute-done.4, pred[]{:T(512)S(6)} %eq.64, bf16[256,1280]{1,0:T(8,128)(2,1)S(1)} %get-tuple-element.7, bf16[256,1280]{1,0:T(8,128)(2,1)S(1)} %get-tuple-element.5, ...), kind=kLoop, calls=%fused_computation.13 | loop fusion | flops 13107200 | bytes 10485761 | tf_op jit(solution)/shard_map/jit(_where)/select_n | solution.py:189
  58.4 6.4 %collective-permute-start.8 = (bf16[128,512]{1,0:T(8,128)(2,1)S(1)}, bf16[128,512]{1,0:T(8,128)(2,1)S(1)}, u32[]{:S(2)}, u32[]{:S(2)}) collective-permute-start(bf16[128,512]{1,0:T(8,128)(2,1)S(1)} %fusion.32), channel_id=1, source_target_pairs={{0,4},{4,8},{8,12},{12,16},{16,20},{20,24},{24,28},{28,32},{32,36}... | collective-permute-start | bytes 393224 | tf_op jit(solution)/shard_map/ppermute | solution.py:15
  64.8 3.9 %collective-permute-start.7 = (bf16[128,512]{1,0:T(8,128)(2,1)S(1)}, bf16[128,512]{1,0:T(8,128)(2,1)S(1)}, u32[]{:S(2)}, u32[]{:S(2)}) collective-permute-start(bf16[128,512]{1,0:T(8,128)(2,1)S(1)} %fusion.32), channel_id=1, source_target_pairs={{0,8},{4,12},{8,16},{12,20},{16,24},{20,28},{24,32},{28,36},{32,40... | collective-permute-start | bytes 393224 | tf_op jit(solution)/shard_map/ppermute | solution.py:15
  68.7 1.5 collective-permute-start.6
  70.3 3.5 %collective-permute-start.5 = (bf16[128,512]{1,0:T(8,128)(2,1)S(1)}, bf16[128,512]{1,0:T(8,128)(2,1)S(1)}, u32[]{:S(2)}, u32[]{:S(2)}) collective-permute-start(bf16[128,512]{1,0:T(8,128)(2,1)S(1)} %fusion.32), channel_id=1, source_target_pairs={{0,16},{4,20},{8,24},{12,28},{16,32},{20,36},{24,40},{28,44},{32,4... | collective-permute-start | bytes 393224 | tf_op jit(solution)/shard_map/ppermute | solution.py:15
  73.8 0.8 fusion.18
  75.3 1.3 collective-permute-done.5
  77.2 4.4 %fusion.63 = (f32[4,4,128]{2,1,0:T(4,128)S(1)}, f32[4,4,128,640]{2,3,1,0:T(8,128)}) fusion(pred[128,640]{0,1:T(8,128)(4,1)S(1)} %copy-done.13, bf16[640,4,64,1]{0,2,3,1:T(8,128)(2,1)S(1)} %bitcast.94, bf16[128,4,4,64]{0,3,2,1:T(8,128)(2,1)S(1)} %bitcast.105), kind=kOutput, calls=%fused_computation.102 | convolution fusion | flops 174326400 | bytes 5922816 | tf_op jit(solution)/shard_map/sub | solution.py:226
  81.6 3.1 %divide_convert_fusion = bf16[4,4,128,640]{2,3,1,0:T(8,128)(2,1)S(1)} fusion(f32[4,4,128,640]{2,3,1,0:T(8,128)} %get-tuple-element.19, f32[4,4,128]{2,1,0:T(4,128)S(1)} %broadcast_select_fusion.4), kind=kLoop, calls=%fused_computation.6 | loop fusion | flops 2621440 | bytes 7872512 | tf_op jit(solution)/shard_map/convert_element_type | solution.py:229
  85.4 0.9 fusion.65
  86.3 1.2 fusion.3
  87.5 0.9 fusion.64
  88.6 6.5 %collective-permute-start.9 = (bf16[128,512]{0,1:T(8,128)(2,1)S(1)}, bf16[128,512]{0,1:T(8,128)(2,1)S(1)}, u32[]{:S(2)}, u32[]{:S(2)}) collective-permute-start(bf16[128,512]{0,1:T(8,128)(2,1)S(1)} %get-tuple-element.8), channel_id=1, source_target_pairs={{4,0},{8,4},{12,8},{16,12},{20,16},{24,20},{28,24},{32,28},{36,32}... | collective-permute-start | bytes 393224 | tf_op jit(solution)/shard_map/ppermute | solution.py:15
  95.1 1.3 collective-permute-start.12
  96.4 1.3 collective-permute-start.11
  97.7 1.3 collective-permute-start.10
  99.4 2.2 collective-permute-done.12
  101.5 3.9 %collective-permute-done.11 = bf16[128,512]{0,1:T(8,128)(2,1)S(1)} collective-permute-done((bf16[128,512]{0,1:T(8,128)(2,1)S(1)}, bf16[128,512]{0,1:T(8,128)(2,1)S(1)}, u32[]{:S(2)}, u32[]{:S(2)}) %collective-permute-start.11) | collective-permute-done | bytes 131104 | tf_op jit(solution)/shard_map/ppermute | solution.py:15
  105.4 3.9 %collective-permute-done.10 = bf16[128,512]{0,1:T(8,128)(2,1)S(1)} collective-permute-done((bf16[128,512]{0,1:T(8,128)(2,1)S(1)}, bf16[128,512]{0,1:T(8,128)(2,1)S(1)}, u32[]{:S(2)}, u32[]{:S(2)}) %collective-permute-start.10) | collective-permute-done | bytes 131104 | tf_op jit(solution)/shard_map/ppermute | solution.py:15
  109.4 1.1 convolution_convert_fusion
  110.6 2.2 %collective-permute-start.13 = (bf16[1024,256]{1,0:T(8,128)(2,1)}, bf16[1024,256]{1,0:T(8,128)(2,1)}, u32[]{:S(2)}, u32[]{:S(2)}) collective-permute-start(bf16[1024,256]{1,0:T(8,128)(2,1)} %convolution_convert_fusion), channel_id=1, source_target_pairs={{0,4},{4,0},{8,12},{12,8},{16,20},{20,16},{24,28},{28,24},{32,36},... | collective-permute-start | bytes 1572872 | tf_op jit(solution)/shard_map/ppermute | solution.py:20
  112.8 1.9 collective-permute-done.13
  114.7 1.3 convolution_add_fusion
  116.0 1.0 copy-done.5
  117.1 5.6 %collective-permute-start.14 = (bf16[512,256]{1,0:T(8,128)(2,1)S(1)}, bf16[512,256]{1,0:T(8,128)(2,1)}, u32[]{:S(2)}, u32[]{:S(2)}) collective-permute-start(bf16[512,256]{1,0:T(8,128)(2,1)S(1)} %slice.165), channel_id=1, source_target_pairs={{0,1},{1,0},{2,3},{3,2},{4,5},{5,4},{6,7},{7,6},{8,9},{9,8},{10,11... | collective-permute-start | bytes 786440 | tf_op jit(solution)/shard_map/ppermute | solution.py:20
  122.7 6.6 %collective-permute-done.14 = bf16[512,256]{1,0:T(8,128)(2,1)} collective-permute-done((bf16[512,256]{1,0:T(8,128)(2,1)S(1)}, bf16[512,256]{1,0:T(8,128)(2,1)}, u32[]{:S(2)}, u32[]{:S(2)}) %collective-permute-start.14) | collective-permute-done | bytes 262176 | tf_op jit(solution)/shard_map/ppermute | solution.py:20
  129.3 1.2 slice_add_fusion
  131.2 6.5 %collective-permute-start.15 = (bf16[256,256]{1,0:T(8,128)(2,1)}, bf16[256,256]{1,0:T(8,128)(2,1)}, u32[]{:S(2)}, u32[]{:S(2)}) collective-permute-start(bf16[256,256]{1,0:T(8,128)(2,1)} %select_convert_fusion), channel_id=1, source_target_pairs={{0,2},{1,3},{2,0},{3,1},{4,6},{5,7},{6,4},{7,5},{8,10},{9,11},{10,... | collective-permute-start | bytes 393224 | tf_op jit(solution)/shard_map/ppermute | solution.py:20
  137.7 7.0 %collective-permute-done.15 = bf16[256,256]{1,0:T(8,128)(2,1)} collective-permute-done((bf16[256,256]{1,0:T(8,128)(2,1)}, bf16[256,256]{1,0:T(8,128)(2,1)}, u32[]{:S(2)}, u32[]{:S(2)}) %collective-permute-start.15) | collective-permute-done | bytes 131104 | tf_op jit(solution)/shard_map/ppermute | solution.py:20
  144.7 0.9 convert_add_fusion
  146.4 5.9 %collective-permute-start.16 = (f32[128,256]{1,0:T(8,128)S(1)}, f32[128,256]{1,0:T(8,128)S(1)}, u32[]{:S(2)}, u32[]{:S(2)}) collective-permute-start(f32[128,256]{1,0:T(8,128)S(1)} %slice_select_fusion), channel_id=1, source_target_pairs={{0,16},{4,20},{8,24},{12,28},{16,0},{20,4},{24,8},{28,12},{32,48},... | collective-permute-start | bytes 393224 | tf_op jit(solution)/shard_map/ppermute | solution.py:20
  152.3 3.4 %collective-permute-done.16 = f32[128,256]{1,0:T(8,128)S(1)} collective-permute-done((f32[128,256]{1,0:T(8,128)S(1)}, f32[128,256]{1,0:T(8,128)S(1)}, u32[]{:S(2)}, u32[]{:S(2)}) %collective-permute-start.16) | collective-permute-done | bytes 131104 | tf_op jit(solution)/shard_map/ppermute | solution.py:20
  155.7 1.0 select_add_fusion
  156.7 4.7 %collective-permute-start.17 = (f32[64,256]{1,0:T(8,128)S(1)}, f32[64,256]{1,0:T(8,128)S(1)}, u32[]{:S(2)}, u32[]{:S(2)}) collective-permute-start(f32[64,256]{1,0:T(8,128)S(1)} %slice_select_fusion.1), channel_id=1, source_target_pairs={{0,64},{4,68},{8,72},{12,76},{16,80},{20,84},{24,88},{28,92},{32,9... | collective-permute-start | bytes 196616 | tf_op jit(solution)/shard_map/ppermute | solution.py:20
  161.5 1.6 collective-permute-done.17
  163.1 6.3 %collective-permute-start.18 = (f32[64,256]{1,0:T(8,128)S(1)}, f32[64,256]{1,0:T(8,128)S(1)}, u32[]{:S(2)}, u32[]{:S(2)}) collective-permute-start(f32[64,256]{1,0:T(8,128)S(1)} %select_add_fusion.1), channel_id=1, source_target_pairs={{0,8},{4,12},{8,0},{12,4},{16,24},{20,28},{24,16},{28,20},{32,40},... | collective-permute-start | bytes 196616 | tf_op jit(solution)/shard_map/ppermute | solution.py:20
  169.4 2.8 %collective-permute-done.18 = f32[64,256]{1,0:T(8,128)S(1)} collective-permute-done((f32[64,256]{1,0:T(8,128)S(1)}, f32[64,256]{1,0:T(8,128)S(1)}, u32[]{:S(2)}, u32[]{:S(2)}) %collective-permute-start.18) | collective-permute-done | bytes 65568 | tf_op jit(solution)/shard_map/ppermute | solution.py:20
  172.2 5.5 %collective-permute-start.19 = (f32[64,256]{1,0:T(8,128)S(1)}, f32[64,256]{1,0:T(8,128)S(1)}, u32[]{:S(2)}, u32[]{:S(2)}) collective-permute-start(f32[64,256]{1,0:T(8,128)S(1)} %add.120), channel_id=1, source_target_pairs={{0,32},{4,36},{8,40},{12,44},{16,48},{20,52},{24,56},{28,60},{32,0... | collective-permute-start | bytes 196616 | tf_op jit(solution)/shard_map/ppermute | solution.py:20
  177.6 1.6 collective-permute-done.19
  179.3 5.2 %collective-permute-start.20 = (f32[64,256]{1,0:T(8,128)S(1)}, f32[64,256]{1,0:T(8,128)S(1)}, u32[]{:S(2)}, u32[]{:S(2)}) collective-permute-start(f32[64,256]{1,0:T(8,128)S(1)} %add.121), channel_id=1, source_target_pairs={{0,128},{4,132},{8,136},{12,140},{16,144},{20,148},{24,152},{28,15... | collective-permute-start | bytes 196616 | tf_op jit(solution)/shard_map/ppermute | solution.py:20
  184.4 1.6 collective-permute-done.20
  186.1 8.4 %collective-permute-start.21 = (f32[64,256]{1,0:T(8,128)S(1)}, f32[64,256]{1,0:T(8,128)S(1)}, u32[]{:S(2)}, u32[]{:S(2)}) collective-permute-start(f32[64,256]{1,0:T(8,128)S(1)} %add.122), channel_id=1, source_target_pairs={{0,256},{4,260},{8,264},{12,268},{16,272},{20,276},{24,280},{28,28... | collective-permute-start | bytes 196616 | tf_op jit(solution)/shard_map/ppermute | solution.py:20
  194.5 1.6 collective-permute-done.21
  196.1 2.6 %collective-permute-start.22 = (f32[64,256]{1,0:T(8,128)S(1)}, f32[64,256]{1,0:T(8,128)S(1)}, u32[]{:S(2)}, u32[]{:S(2)}) collective-permute-start(f32[64,256]{1,0:T(8,128)S(1)} %add.123), channel_id=1, source_target_pairs={{0,64},{4,68},{8,72},{12,76},{16,80},{20,84},{24,88},{28,92},{32,9... | collective-permute-start | bytes 196616 | tf_op jit(solution)/shard_map/ppermute | solution.py:20
  198.8 1.6 convolution_convert_fusion.1
  200.3 1.8 collective-permute-done.22
  202.1 3.7 %collective-permute-start.23 = (f32[128,256]{1,0:T(8,128)S(1)}, f32[128,256]{1,0:T(8,128)S(1)}, u32[]{:S(2)}, u32[]{:S(2)}) collective-permute-start(f32[128,256]{1,0:T(8,128)S(1)} %maximum_select_fusion.2), channel_id=1, source_target_pairs={{0,16},{4,20},{8,24},{12,28},{16,0},{20,4},{24,8},{28,12},{32,48},... | collective-permute-start | bytes 393224 | tf_op jit(solution)/shard_map/ppermute | solution.py:20
  206.3 2.1 collective-permute-done.23
  208.5 9.3 %collective-permute-start.24 = (f32[256,256]{1,0:T(8,128)S(1)}, f32[256,256]{1,0:T(8,128)S(1)}, u32[]{:S(2)}, u32[]{:S(2)}) collective-permute-start(f32[256,256]{1,0:T(8,128)S(1)} %maximum_select_fusion.1), channel_id=1, source_target_pairs={{0,4},{4,0},{8,12},{12,8},{16,20},{20,16},{24,28},{28,24},{32,36},... | collective-permute-start | bytes 786440 | tf_op jit(solution)/shard_map/ppermute | solution.py:20
  217.8 1.5 fusion.29
  219.4 0.8 maximum_select_fusion
  (70 shorter events, 5.0 us)
Async XLA Ops:
  0.6 73.9 %copy-start = (bf16[1,128,1024]{2,1,0:T(8,128)(2,1)S(1)}, bf16[1,128,1024]{2,1,0:T(8,128)(2,1)}, u32[]{:S(2)}) copy-start(bf16[1,128,1024]{2,1,0:T(8,128)(2,1)} %param.7) | copy-start | bytes 786436
  2.2 41.0 %collective-permute-start.3 = (bf16[256,1280]{1,0:T(8,128)(2,1)S(1)}, bf16[256,1280]{1,0:T(8,128)(2,1)S(1)}, u32[]{:S(2)}, u32[]{:S(2)}) collective-permute-start(bf16[256,1280]{1,0:T(8,128)(2,1)S(1)} %fusion.34), channel_id=1, source_target_pairs={{11,0},{0,1},{1,2},{2,3},{15,4},{4,5},{5,6},{6,7},{3,8},{8,9},{9,1... | collective-permute-start | bytes 1966088 | tf_op jit(solution)/shard_map/ppermute | solution.py:133
  7.0 37.0 %collective-permute-start = (bf16[256,1280]{1,0:T(8,128)(2,1)S(1)}, bf16[256,1280]{1,0:T(8,128)(2,1)}, u32[]{:S(2)}, u32[]{:S(2)}) collective-permute-start(bf16[256,1280]{1,0:T(8,128)(2,1)S(1)} %fusion.34), channel_id=1, source_target_pairs={{1,0},{2,1},{3,2},{8,3},{5,4},{6,5},{7,6},{12,7},{9,8},{10,9},{11,... | collective-permute-start | bytes 1966088 | tf_op jit(solution)/shard_map/ppermute | solution.py:133
  15.7 27.4 %collective-permute-start.1 = (bf16[256,640]{1,0:T(8,128)(2,1)S(1)}, bf16[256,640]{1,0:T(8,128)(2,1)S(1)}, u32[]{:S(2)}, u32[]{:S(2)}) collective-permute-start(bf16[256,640]{1,0:T(8,128)(2,1)S(1)} %get-tuple-element.15), channel_id=1, source_target_pairs={{2,0},{3,1},{8,2},{9,3},{6,4},{7,5},{12,6},{13,7},{10,8},{11,9},{0... | collective-permute-start | bytes 983048 | tf_op jit(solution)/shard_map/ppermute | solution.py:133
  19.0 24.1 %collective-permute-start.2 = (bf16[256,640]{1,0:T(8,128)(2,1)S(1)}, bf16[256,640]{1,0:T(8,128)(2,1)S(1)}, u32[]{:S(2)}, u32[]{:S(2)}) collective-permute-start(bf16[256,640]{1,0:T(8,128)(2,1)S(1)} %get-tuple-element.14), channel_id=1, source_target_pairs={{10,0},{11,1},{0,2},{1,3},{14,4},{15,5},{4,6},{5,7},{2,8},{3,9},{8... | collective-permute-start | bytes 983048 | tf_op jit(solution)/shard_map/ppermute | solution.py:133
  43.2 0.9 copy-start.10
  45.6 5.7 %copy-start.9 = (bf16[1,128,1024]{2,1,0:T(8,128)(2,1)S(1)}, bf16[1,128,1024]{2,1,0:T(8,128)(2,1)}, u32[]{:S(2)}) copy-start(bf16[1,128,1024]{2,1,0:T(8,128)(2,1)} %param.6) | copy-start | bytes 786436
  47.3 8.3 %collective-permute-start.4 = (bf16[1024,1280]{1,0:T(8,128)(2,1)}, bf16[1024,1280]{1,0:T(8,128)(2,1)}, u32[]{:S(2)}, u32[]{:S(2)}) collective-permute-start(bf16[1024,1280]{1,0:T(8,128)(2,1)} %pad_maximum_fusion), channel_id=1, source_target_pairs={{0,4},{4,0},{8,12},{12,8},{16,20},{20,16},{24,28},{28,24},{32,36},... | collective-permute-start | bytes 7864328 | tf_op jit(solution)/shard_map/ppermute | solution.py:20
  57.9 15.9 %copy-start.1 = (bf16[1024,1280]{1,0:T(8,128)(2,1)}, bf16[1024,1280]{1,0:T(8,128)(2,1)S(1)}, u32[]{:S(2)}) copy-start(bf16[1024,1280]{1,0:T(8,128)(2,1)S(1)} %get-tuple-element.3) | copy-start | bytes 7864324
  58.0 17.3 %copy-start.3 = (bf16[1024,512]{1,0:T(8,128)(2,1)}, bf16[1024,512]{1,0:T(8,128)(2,1)S(1)}, u32[]{:S(2)}) copy-start(bf16[1024,512]{1,0:T(8,128)(2,1)S(1)} %pad_maximum_fusion.2) | copy-start | bytes 3145732
  58.4 18.3 %collective-permute-start.8 = (bf16[128,512]{1,0:T(8,128)(2,1)S(1)}, bf16[128,512]{1,0:T(8,128)(2,1)S(1)}, u32[]{:S(2)}, u32[]{:S(2)}) collective-permute-start(bf16[128,512]{1,0:T(8,128)(2,1)S(1)} %fusion.32), channel_id=1, source_target_pairs={{0,4},{4,8},{8,12},{12,16},{16,20},{20,24},{24,28},{28,32},{32,36}... | collective-permute-start | bytes 393224 | tf_op jit(solution)/shard_map/ppermute | solution.py:15
  64.8 11.9 %collective-permute-start.7 = (bf16[128,512]{1,0:T(8,128)(2,1)S(1)}, bf16[128,512]{1,0:T(8,128)(2,1)S(1)}, u32[]{:S(2)}, u32[]{:S(2)}) collective-permute-start(bf16[128,512]{1,0:T(8,128)(2,1)S(1)} %fusion.32), channel_id=1, source_target_pairs={{0,8},{4,12},{8,16},{12,20},{16,24},{20,28},{24,32},{28,36},{32,40... | collective-permute-start | bytes 393224 | tf_op jit(solution)/shard_map/ppermute | solution.py:15
  68.7 7.9 %collective-permute-start.6 = (bf16[128,512]{1,0:T(8,128)(2,1)S(1)}, bf16[128,512]{1,0:T(8,128)(2,1)S(1)}, u32[]{:S(2)}, u32[]{:S(2)}) collective-permute-start(bf16[128,512]{1,0:T(8,128)(2,1)S(1)} %fusion.32), channel_id=1, source_target_pairs={{0,12},{4,16},{8,20},{12,24},{16,28},{20,32},{24,36},{28,40},{32,4... | collective-permute-start | bytes 393224 | tf_op jit(solution)/shard_map/ppermute | solution.py:15
  70.3 6.3 %collective-permute-start.5 = (bf16[128,512]{1,0:T(8,128)(2,1)S(1)}, bf16[128,512]{1,0:T(8,128)(2,1)S(1)}, u32[]{:S(2)}, u32[]{:S(2)}) collective-permute-start(bf16[128,512]{1,0:T(8,128)(2,1)S(1)} %fusion.32), channel_id=1, source_target_pairs={{0,16},{4,20},{8,24},{12,28},{16,32},{20,36},{24,40},{28,44},{32,4... | collective-permute-start | bytes 393224 | tf_op jit(solution)/shard_map/ppermute | solution.py:15
  74.6 2.6 %copy-start.11 = (bf16[1024,128]{1,0:T(8,128)(2,1)}, bf16[1024,128]{1,0:T(8,128)(2,1)S(1)}, u32[]{:S(2)}) copy-start(bf16[1024,128]{1,0:T(8,128)(2,1)S(1)} %fusion.18) | copy-start | bytes 786436
  75.3 1.9 copy-start.13
  77.2 4.4 %copy-start.7 = (bf16[640,256]{0,1:T(8,128)(2,1)}, bf16[640,256]{0,1:T(8,128)(2,1)S(1)}, u32[]{:S(2)}) copy-start(bf16[640,256]{0,1:T(8,128)(2,1)S(1)} %copy.22) | copy-start | bytes 983044
  86.3 1.2 copy-start.12
  87.5 11.5 %copy-start.8 = (bf16[1,128,1024]{1,2,0:T(8,128)(2,1)S(1)}, bf16[1,128,1024]{1,2,0:T(8,128)(2,1)}, u32[]{:S(2)}) copy-start(bf16[1,128,1024]{1,2,0:T(8,128)(2,1)} %copy.28) | copy-start | bytes 786436
  88.6 10.8 %collective-permute-start.9 = (bf16[128,512]{0,1:T(8,128)(2,1)S(1)}, bf16[128,512]{0,1:T(8,128)(2,1)S(1)}, u32[]{:S(2)}, u32[]{:S(2)}) collective-permute-start(bf16[128,512]{0,1:T(8,128)(2,1)S(1)} %get-tuple-element.8), channel_id=1, source_target_pairs={{4,0},{8,4},{12,8},{16,12},{20,16},{24,20},{28,24},{32,28},{36,32}... | collective-permute-start | bytes 393224 | tf_op jit(solution)/shard_map/ppermute | solution.py:15
  95.1 6.4 %collective-permute-start.12 = (bf16[128,512]{0,1:T(8,128)(2,1)S(1)}, bf16[128,512]{0,1:T(8,128)(2,1)S(1)}, u32[]{:S(2)}, u32[]{:S(2)}) collective-permute-start(bf16[128,512]{0,1:T(8,128)(2,1)S(1)} %get-tuple-element.9), channel_id=1, source_target_pairs={{16,0},{20,4},{24,8},{28,12},{32,16},{36,20},{40,24},{44,28},{48,3... | collective-permute-start | bytes 393224 | tf_op jit(solution)/shard_map/ppermute | solution.py:15
  96.4 9.0 %collective-permute-start.11 = (bf16[128,512]{0,1:T(8,128)(2,1)S(1)}, bf16[128,512]{0,1:T(8,128)(2,1)S(1)}, u32[]{:S(2)}, u32[]{:S(2)}) collective-permute-start(bf16[128,512]{0,1:T(8,128)(2,1)S(1)} %get-tuple-element.10), channel_id=1, source_target_pairs={{12,0},{16,4},{20,8},{24,12},{28,16},{32,20},{36,24},{40,28},{44,3... | collective-permute-start | bytes 393224 | tf_op jit(solution)/shard_map/ppermute | solution.py:15
  97.7 11.6 %collective-permute-start.10 = (bf16[128,512]{0,1:T(8,128)(2,1)S(1)}, bf16[128,512]{0,1:T(8,128)(2,1)S(1)}, u32[]{:S(2)}, u32[]{:S(2)}) collective-permute-start(bf16[128,512]{0,1:T(8,128)(2,1)S(1)} %get-tuple-element.11), channel_id=1, source_target_pairs={{8,0},{12,4},{16,8},{20,12},{24,16},{28,20},{32,24},{36,28},{40,32... | collective-permute-start | bytes 393224 | tf_op jit(solution)/shard_map/ppermute | solution.py:15
  110.6 4.1 %collective-permute-start.13 = (bf16[1024,256]{1,0:T(8,128)(2,1)}, bf16[1024,256]{1,0:T(8,128)(2,1)}, u32[]{:S(2)}, u32[]{:S(2)}) collective-permute-start(bf16[1024,256]{1,0:T(8,128)(2,1)} %convolution_convert_fusion), channel_id=1, source_target_pairs={{0,4},{4,0},{8,12},{12,8},{16,20},{20,16},{24,28},{28,24},{32,36},... | collective-permute-start | bytes 1572872 | tf_op jit(solution)/shard_map/ppermute | solution.py:20
  116.0 1.0 copy-start.5
  117.1 12.3 %collective-permute-start.14 = (bf16[512,256]{1,0:T(8,128)(2,1)S(1)}, bf16[512,256]{1,0:T(8,128)(2,1)}, u32[]{:S(2)}, u32[]{:S(2)}) collective-permute-start(bf16[512,256]{1,0:T(8,128)(2,1)S(1)} %slice.165), channel_id=1, source_target_pairs={{0,1},{1,0},{2,3},{3,2},{4,5},{5,4},{6,7},{7,6},{8,9},{9,8},{10,11... | collective-permute-start | bytes 786440 | tf_op jit(solution)/shard_map/ppermute | solution.py:20
  131.2 13.5 %collective-permute-start.15 = (bf16[256,256]{1,0:T(8,128)(2,1)}, bf16[256,256]{1,0:T(8,128)(2,1)}, u32[]{:S(2)}, u32[]{:S(2)}) collective-permute-start(bf16[256,256]{1,0:T(8,128)(2,1)} %select_convert_fusion), channel_id=1, source_target_pairs={{0,2},{1,3},{2,0},{3,1},{4,6},{5,7},{6,4},{7,5},{8,10},{9,11},{10,... | collective-permute-start | bytes 393224 | tf_op jit(solution)/shard_map/ppermute | solution.py:20
  145.7 0.7 copy-start.6
  146.4 9.3 %collective-permute-start.16 = (f32[128,256]{1,0:T(8,128)S(1)}, f32[128,256]{1,0:T(8,128)S(1)}, u32[]{:S(2)}, u32[]{:S(2)}) collective-permute-start(f32[128,256]{1,0:T(8,128)S(1)} %slice_select_fusion), channel_id=1, source_target_pairs={{0,16},{4,20},{8,24},{12,28},{16,0},{20,4},{24,8},{28,12},{32,48},... | collective-permute-start | bytes 393224 | tf_op jit(solution)/shard_map/ppermute | solution.py:20
  156.7 6.4 %collective-permute-start.17 = (f32[64,256]{1,0:T(8,128)S(1)}, f32[64,256]{1,0:T(8,128)S(1)}, u32[]{:S(2)}, u32[]{:S(2)}) collective-permute-start(f32[64,256]{1,0:T(8,128)S(1)} %slice_select_fusion.1), channel_id=1, source_target_pairs={{0,64},{4,68},{8,72},{12,76},{16,80},{20,84},{24,88},{28,92},{32,9... | collective-permute-start | bytes 196616 | tf_op jit(solution)/shard_map/ppermute | solution.py:20
  163.1 9.0 %collective-permute-start.18 = (f32[64,256]{1,0:T(8,128)S(1)}, f32[64,256]{1,0:T(8,128)S(1)}, u32[]{:S(2)}, u32[]{:S(2)}) collective-permute-start(f32[64,256]{1,0:T(8,128)S(1)} %select_add_fusion.1), channel_id=1, source_target_pairs={{0,8},{4,12},{8,0},{12,4},{16,24},{20,28},{24,16},{28,20},{32,40},... | collective-permute-start | bytes 196616 | tf_op jit(solution)/shard_map/ppermute | solution.py:20
  172.2 7.1 %collective-permute-start.19 = (f32[64,256]{1,0:T(8,128)S(1)}, f32[64,256]{1,0:T(8,128)S(1)}, u32[]{:S(2)}, u32[]{:S(2)}) collective-permute-start(f32[64,256]{1,0:T(8,128)S(1)} %add.120), channel_id=1, source_target_pairs={{0,32},{4,36},{8,40},{12,44},{16,48},{20,52},{24,56},{28,60},{32,0... | collective-permute-start | bytes 196616 | tf_op jit(solution)/shard_map/ppermute | solution.py:20
  179.3 6.8 %collective-permute-start.20 = (f32[64,256]{1,0:T(8,128)S(1)}, f32[64,256]{1,0:T(8,128)S(1)}, u32[]{:S(2)}, u32[]{:S(2)}) collective-permute-start(f32[64,256]{1,0:T(8,128)S(1)} %add.121), channel_id=1, source_target_pairs={{0,128},{4,132},{8,136},{12,140},{16,144},{20,148},{24,152},{28,15... | collective-permute-start | bytes 196616 | tf_op jit(solution)/shard_map/ppermute | solution.py:20
  186.1 10.0 %collective-permute-start.21 = (f32[64,256]{1,0:T(8,128)S(1)}, f32[64,256]{1,0:T(8,128)S(1)}, u32[]{:S(2)}, u32[]{:S(2)}) collective-permute-start(f32[64,256]{1,0:T(8,128)S(1)} %add.122), channel_id=1, source_target_pairs={{0,256},{4,260},{8,264},{12,268},{16,272},{20,276},{24,280},{28,28... | collective-permute-start | bytes 196616 | tf_op jit(solution)/shard_map/ppermute | solution.py:20
  194.5 11.4 %copy-start.4 = (bf16[1024,512]{1,0:T(8,128)(2,1)S(1)}, bf16[1024,512]{1,0:T(8,128)(2,1)}, u32[]{:S(2)}) copy-start(bf16[1024,512]{1,0:T(8,128)(2,1)} %copy-done.3) | copy-start | bytes 3145732
  196.1 21.7 %copy-start.2 = (bf16[1024,1280]{1,0:T(8,128)(2,1)S(1)}, bf16[1024,1280]{1,0:T(8,128)(2,1)}, u32[]{:S(2)}) copy-start(bf16[1024,1280]{1,0:T(8,128)(2,1)} %copy-done.1) | copy-start | bytes 7864324
  196.1 6.0 %collective-permute-start.22 = (f32[64,256]{1,0:T(8,128)S(1)}, f32[64,256]{1,0:T(8,128)S(1)}, u32[]{:S(2)}, u32[]{:S(2)}) collective-permute-start(f32[64,256]{1,0:T(8,128)S(1)} %add.123), channel_id=1, source_target_pairs={{0,64},{4,68},{8,72},{12,76},{16,80},{20,84},{24,88},{28,92},{32,9... | collective-permute-start | bytes 196616 | tf_op jit(solution)/shard_map/ppermute | solution.py:20
  202.1 6.4 %collective-permute-start.23 = (f32[128,256]{1,0:T(8,128)S(1)}, f32[128,256]{1,0:T(8,128)S(1)}, u32[]{:S(2)}, u32[]{:S(2)}) collective-permute-start(f32[128,256]{1,0:T(8,128)S(1)} %maximum_select_fusion.2), channel_id=1, source_target_pairs={{0,16},{4,20},{8,24},{12,28},{16,0},{20,4},{24,8},{28,12},{32,48},... | collective-permute-start | bytes 393224 | tf_op jit(solution)/shard_map/ppermute | solution.py:20
  208.5 10.9 %collective-permute-start.24 = (f32[256,256]{1,0:T(8,128)S(1)}, f32[256,256]{1,0:T(8,128)S(1)}, u32[]{:S(2)}, u32[]{:S(2)}) collective-permute-start(f32[256,256]{1,0:T(8,128)S(1)} %maximum_select_fusion.1), channel_id=1, source_target_pairs={{0,4},{4,0},{8,12},{12,8},{16,20},{20,16},{24,28},{28,24},{32,36},... | collective-permute-start | bytes 786440 | tf_op jit(solution)/shard_map/ppermute | solution.py:20

commit v15 on v14

--- a/solution.py
+++ b/solution.py
@@ -103,10 +103,11 @@
     near = [bit for bit in NEAR_BITS if bit < tm_bits]
     near = near[: max(0, current.shape[0].bit_length() - 1)]
     for bit in near:
-        current = halve_stage(current, "tm", bit, jnp.float32)
+        current = halve_stage(current, "tm", bit, jnp.bfloat16)
     for bit in range(1, tm_bits):
         if bit not in near:
-            current = current + xor_swap(current, "tm", bit)
+            rounded = current.astype(jnp.bfloat16)
+            current = rounded.astype(jnp.float32) + xor_swap(rounded, "tm", bit).astype(jnp.float32)
     for bit in reversed(near):
         current = double_stage(current, "tm", bit)
     other = xor_swap(current, "tm", 0)

time: 221 us -> 218 us (0.986)
  waiting for transfers between devices: 67.2 us -> 64.1 us
    ppermute x13, waiting for transfers between devices: 34.5 us -> 31.4 us  [xor_swap(): lax.ppermute(value, axis, [(source, source ^ 1 << bit) for source in rang...]
where the time goes in v15:
time: 218 us; the launch traced here: 217 us
  starting transfers between devices  114 us (52%)
  waiting for transfers between devices  64.1 us (29%)
  other arithmetic  16.2 us (7%)
  matrix products  15.8 us (7%)
  local copies, waits for them, and re-layouts  4.2 us (2%)
    ppermute x13, starting transfers between devices, xor_swap(): lax.ppermute(value, axis, [(source, source ^ 1 << bit) for source in rang...  68.9 us
    ppermute x13, waiting for transfers between devices, xor_swap(): lax.ppermute(value, axis, [(source, source ^ 1 << bit) for source in rang...  31.4 us
    ppermute x8, starting transfers between devices, shifted(): lax.ppermute(value, axis, [(source, source + steps) for source in range(l...  25.8 us
    ppermute x4, waiting for transfers between devices, ring_pull(): return lax.ppermute(value, ('tm', 'stream'), pairs)  21.1 us
    ppermute x4, starting transfers between devices, ring_pull(): return lax.ppermute(value, ('tm', 'stream'), pairs)  19.6 us
    ppermute x8, waiting for transfers between devices, shifted(): lax.ppermute(value, axis, [(source, source + steps) for source in range(l...  11.6 us
    sub x1, matrix products, per_device(): terms = jnp.where(allowed, jnp.exp(masked - row_max), 0.0)  4.41 us
  transfers between devices with their start and end apart: 25, of which 18 were waited for; matrix products, arithmetic and copies ran while one was open for 3% of the time, Pallas kernels for 0%

profile of v15, /device:TPU:1, one launch (start us, length us, event | category | flops | bytes accessed | tf_op | source)
XLA Modules:
  0.0 216.7 jit_solution(494196859366141201)
XLA Ops:
  0.7 1.5 fusion.34
  2.2 4.8 %collective-permute-start.3 = (bf16[256,1280]{1,0:T(8,128)(2,1)S(1)}, bf16[256,1280]{1,0:T(8,128)(2,1)S(1)}, u32[]{:S(2)}, u32[]{:S(2)}) collective-permute-start(bf16[256,1280]{1,0:T(8,128)(2,1)S(1)} %fusion.34), channel_id=1, source_target_pairs={{11,0},{0,1},{1,2},{2,3},{15,4},{4,5},{5,6},{6,7},{3,8},{8,9},{9,1... | collective-permute-start | bytes 1966088 | tf_op jit(solution)/shard_map/ppermute | solution.py:134
  7.0 8.6 %collective-permute-start = (bf16[256,1280]{1,0:T(8,128)(2,1)S(1)}, bf16[256,1280]{1,0:T(8,128)(2,1)}, u32[]{:S(2)}, u32[]{:S(2)}) collective-permute-start(bf16[256,1280]{1,0:T(8,128)(2,1)S(1)} %fusion.34), channel_id=1, source_target_pairs={{1,0},{2,1},{3,2},{8,3},{5,4},{6,5},{7,6},{12,7},{9,8},{10,9},{11,... | collective-permute-start | bytes 1966088 | tf_op jit(solution)/shard_map/ppermute | solution.py:134
  15.7 3.4 %collective-permute-start.1 = (bf16[256,640]{1,0:T(8,128)(2,1)S(1)}, bf16[256,640]{1,0:T(8,128)(2,1)S(1)}, u32[]{:S(2)}, u32[]{:S(2)}) collective-permute-start(bf16[256,640]{1,0:T(8,128)(2,1)S(1)} %get-tuple-element.15), channel_id=1, source_target_pairs={{2,0},{3,1},{8,2},{9,3},{6,4},{7,5},{12,6},{13,7},{10,8},{11,9},{0... | collective-permute-start | bytes 983048 | tf_op jit(solution)/shard_map/ppermute | solution.py:134
  19.0 2.8 %collective-permute-start.2 = (bf16[256,640]{1,0:T(8,128)(2,1)S(1)}, bf16[256,640]{1,0:T(8,128)(2,1)S(1)}, u32[]{:S(2)}, u32[]{:S(2)}) collective-permute-start(bf16[256,640]{1,0:T(8,128)(2,1)S(1)} %get-tuple-element.14), channel_id=1, source_target_pairs={{10,0},{11,1},{0,2},{1,3},{14,4},{15,5},{4,6},{5,7},{2,8},{3,9},{8... | collective-permute-start | bytes 983048 | tf_op jit(solution)/shard_map/ppermute | solution.py:134
  22.0 21.1 %collective-permute-done.1 = bf16[256,640]{1,0:T(8,128)(2,1)S(1)} collective-permute-done((bf16[256,640]{1,0:T(8,128)(2,1)S(1)}, bf16[256,640]{1,0:T(8,128)(2,1)S(1)}, u32[]{:S(2)}, u32[]{:S(2)}) %collective-permute-start.1) | collective-permute-done | bytes 327712 | tf_op jit(solution)/shard_map/ppermute | solution.py:134
  43.2 0.8 copy-done.10
  44.0 1.6 select_select_fusion.3
  45.6 1.7 pad_maximum_fusion
  47.3 3.4 %collective-permute-start.4 = (bf16[1024,1280]{1,0:T(8,128)(2,1)}, bf16[1024,1280]{1,0:T(8,128)(2,1)}, u32[]{:S(2)}, u32[]{:S(2)}) collective-permute-start(bf16[1024,1280]{1,0:T(8,128)(2,1)} %pad_maximum_fusion), channel_id=1, source_target_pairs={{0,4},{4,0},{8,12},{12,8},{16,20},{20,16},{24,28},{28,24},{32,36},... | collective-permute-start | bytes 7864328 | tf_op jit(solution)/shard_map/ppermute | solution.py:20
  51.4 0.8 copy.28
  52.3 1.0 fusion.40
  53.2 2.3 %collective-permute-done.4 = bf16[1024,1280]{1,0:T(8,128)(2,1)} collective-permute-done((bf16[1024,1280]{1,0:T(8,128)(2,1)}, bf16[1024,1280]{1,0:T(8,128)(2,1)}, u32[]{:S(2)}, u32[]{:S(2)}) %collective-permute-start.4) | collective-permute-done | bytes 2621472 | tf_op jit(solution)/shard_map/ppermute | solution.py:20
  55.6 2.4 %broadcast_select_fusion = (bf16[1024,1280]{1,0:T(8,128)(2,1)S(1)}, bf16[1024,1280]{1,0:T(8,128)(2,1)S(1)}) fusion(bf16[1024,1280]{1,0:T(8,128)(2,1)} %collective-permute-done.4, pred[]{:T(512)S(6)} %eq.64, bf16[256,1280]{1,0:T(8,128)(2,1)S(1)} %get-tuple-element.7, bf16[256,1280]{1,0:T(8,128)(2,1)S(1)} %get-tuple-element.5, ...), kind=kLoop, calls=%fused_computation.13 | loop fusion | flops 13107200 | bytes 10485761 | tf_op jit(solution)/shard_map/jit(_where)/select_n | solution.py:190
  58.4 6.4 %collective-permute-start.8 = (bf16[128,512]{1,0:T(8,128)(2,1)S(1)}, bf16[128,512]{1,0:T(8,128)(2,1)S(1)}, u32[]{:S(2)}, u32[]{:S(2)}) collective-permute-start(bf16[128,512]{1,0:T(8,128)(2,1)S(1)} %fusion.32), channel_id=1, source_target_pairs={{0,4},{4,8},{8,12},{12,16},{16,20},{20,24},{24,28},{28,32},{32,36}... | collective-permute-start | bytes 393224 | tf_op jit(solution)/shard_map/ppermute | solution.py:15
  64.8 3.9 %collective-permute-start.7 = (bf16[128,512]{1,0:T(8,128)(2,1)S(1)}, bf16[128,512]{1,0:T(8,128)(2,1)S(1)}, u32[]{:S(2)}, u32[]{:S(2)}) collective-permute-start(bf16[128,512]{1,0:T(8,128)(2,1)S(1)} %fusion.32), channel_id=1, source_target_pairs={{0,8},{4,12},{8,16},{12,20},{16,24},{20,28},{24,32},{28,36},{32,40... | collective-permute-start | bytes 393224 | tf_op jit(solution)/shard_map/ppermute | solution.py:15
  68.7 1.5 collective-permute-start.6
  70.3 3.5 %collective-permute-start.5 = (bf16[128,512]{1,0:T(8,128)(2,1)S(1)}, bf16[128,512]{1,0:T(8,128)(2,1)S(1)}, u32[]{:S(2)}, u32[]{:S(2)}) collective-permute-start(bf16[128,512]{1,0:T(8,128)(2,1)S(1)} %fusion.32), channel_id=1, source_target_pairs={{0,16},{4,20},{8,24},{12,28},{16,32},{20,36},{24,40},{28,44},{32,4... | collective-permute-start | bytes 393224 | tf_op jit(solution)/shard_map/ppermute | solution.py:15
  73.8 0.8 fusion.18
  75.3 1.3 collective-permute-done.5
  77.2 4.4 %fusion.63 = (f32[4,4,128]{2,1,0:T(4,128)S(1)}, f32[4,4,128,640]{2,3,1,0:T(8,128)}) fusion(pred[128,640]{0,1:T(8,128)(4,1)S(1)} %copy-done.13, bf16[640,4,64,1]{0,2,3,1:T(8,128)(2,1)S(1)} %bitcast.94, bf16[128,4,4,64]{0,3,2,1:T(8,128)(2,1)S(1)} %bitcast.105), kind=kOutput, calls=%fused_computation.106 | convolution fusion | flops 174326400 | bytes 5922816 | tf_op jit(solution)/shard_map/sub | solution.py:227
  81.6 3.1 %divide_convert_fusion = bf16[4,4,128,640]{2,3,1,0:T(8,128)(2,1)S(1)} fusion(f32[4,4,128,640]{2,3,1,0:T(8,128)} %get-tuple-element.19, f32[4,4,128]{2,1,0:T(4,128)S(1)} %broadcast_select_fusion.4), kind=kLoop, calls=%fused_computation.6 | loop fusion | flops 2621440 | bytes 7872512 | tf_op jit(solution)/shard_map/convert_element_type | solution.py:230
  85.4 0.9 fusion.65
  86.3 1.2 fusion.3
  87.5 0.9 fusion.64
  88.6 6.5 %collective-permute-start.9 = (bf16[128,512]{0,1:T(8,128)(2,1)S(1)}, bf16[128,512]{0,1:T(8,128)(2,1)S(1)}, u32[]{:S(2)}, u32[]{:S(2)}) collective-permute-start(bf16[128,512]{0,1:T(8,128)(2,1)S(1)} %get-tuple-element.8), channel_id=1, source_target_pairs={{4,0},{8,4},{12,8},{16,12},{20,16},{24,20},{28,24},{32,28},{36,32}... | collective-permute-start | bytes 393224 | tf_op jit(solution)/shard_map/ppermute | solution.py:15
  95.1 1.3 collective-permute-start.12
  96.4 1.3 collective-permute-start.11
  97.7 1.3 collective-permute-start.10
  99.4 2.2 collective-permute-done.12
  101.5 3.9 %collective-permute-done.11 = bf16[128,512]{0,1:T(8,128)(2,1)S(1)} collective-permute-done((bf16[128,512]{0,1:T(8,128)(2,1)S(1)}, bf16[128,512]{0,1:T(8,128)(2,1)S(1)}, u32[]{:S(2)}, u32[]{:S(2)}) %collective-permute-start.11) | collective-permute-done | bytes 131104 | tf_op jit(solution)/shard_map/ppermute | solution.py:15
  105.4 3.9 %collective-permute-done.10 = bf16[128,512]{0,1:T(8,128)(2,1)S(1)} collective-permute-done((bf16[128,512]{0,1:T(8,128)(2,1)S(1)}, bf16[128,512]{0,1:T(8,128)(2,1)S(1)}, u32[]{:S(2)}, u32[]{:S(2)}) %collective-permute-start.10) | collective-permute-done | bytes 131104 | tf_op jit(solution)/shard_map/ppermute | solution.py:15
  109.4 1.1 convolution_convert_fusion
  110.6 2.2 %collective-permute-start.13 = (bf16[1024,256]{1,0:T(8,128)(2,1)}, bf16[1024,256]{1,0:T(8,128)(2,1)}, u32[]{:S(2)}, u32[]{:S(2)}) collective-permute-start(bf16[1024,256]{1,0:T(8,128)(2,1)} %convolution_convert_fusion), channel_id=1, source_target_pairs={{0,4},{4,0},{8,12},{12,8},{16,20},{20,16},{24,28},{28,24},{32,36},... | collective-permute-start | bytes 1572872 | tf_op jit(solution)/shard_map/ppermute | solution.py:20
  112.8 1.9 collective-permute-done.13
  114.7 1.3 convolution_add_fusion
  116.0 1.0 copy-done.5
  117.1 5.6 %collective-permute-start.14 = (bf16[512,256]{1,0:T(8,128)(2,1)S(1)}, bf16[512,256]{1,0:T(8,128)(2,1)}, u32[]{:S(2)}, u32[]{:S(2)}) collective-permute-start(bf16[512,256]{1,0:T(8,128)(2,1)S(1)} %slice.165), channel_id=1, source_target_pairs={{0,1},{1,0},{2,3},{3,2},{4,5},{5,4},{6,7},{7,6},{8,9},{9,8},{10,11... | collective-permute-start | bytes 786440 | tf_op jit(solution)/shard_map/ppermute | solution.py:20
  122.7 6.6 %collective-permute-done.14 = bf16[512,256]{1,0:T(8,128)(2,1)} collective-permute-done((bf16[512,256]{1,0:T(8,128)(2,1)S(1)}, bf16[512,256]{1,0:T(8,128)(2,1)}, u32[]{:S(2)}, u32[]{:S(2)}) %collective-permute-start.14) | collective-permute-done | bytes 262176 | tf_op jit(solution)/shard_map/ppermute | solution.py:20
  129.3 1.2 slice_add_fusion
  131.2 6.5 %collective-permute-start.15 = (bf16[256,256]{1,0:T(8,128)(2,1)}, bf16[256,256]{1,0:T(8,128)(2,1)}, u32[]{:S(2)}, u32[]{:S(2)}) collective-permute-start(bf16[256,256]{1,0:T(8,128)(2,1)} %select_convert_fusion), channel_id=1, source_target_pairs={{0,2},{1,3},{2,0},{3,1},{4,6},{5,7},{6,4},{7,5},{8,10},{9,11},{10,... | collective-permute-start | bytes 393224 | tf_op jit(solution)/shard_map/ppermute | solution.py:20
  137.7 7.0 %collective-permute-done.15 = bf16[256,256]{1,0:T(8,128)(2,1)} collective-permute-done((bf16[256,256]{1,0:T(8,128)(2,1)}, bf16[256,256]{1,0:T(8,128)(2,1)}, u32[]{:S(2)}, u32[]{:S(2)}) %collective-permute-start.15) | collective-permute-done | bytes 131104 | tf_op jit(solution)/shard_map/ppermute | solution.py:20
  144.7 0.9 convert_add_fusion
  146.4 5.9 %collective-permute-start.16 = (bf16[128,256]{1,0:T(8,128)(2,1)S(1)}, bf16[128,256]{1,0:T(8,128)(2,1)S(1)}, u32[]{:S(2)}, u32[]{:S(2)}) collective-permute-start(bf16[128,256]{1,0:T(8,128)(2,1)S(1)} %select_convert_fusion.1), channel_id=1, source_target_pairs={{0,16},{4,20},{8,24},{12,28},{16,0},{20,4},{24,8},{28,12},{32,48},... | collective-permute-start | bytes 196616 | tf_op jit(solution)/shard_map/ppermute | solution.py:20
  152.3 2.0 collective-permute-done.16
  154.3 1.0 convert_add_fusion.1
  155.3 4.7 %collective-permute-start.17 = (bf16[64,256]{1,0:T(8,128)(2,1)S(1)}, bf16[64,256]{1,0:T(8,128)(2,1)S(1)}, u32[]{:S(2)}, u32[]{:S(2)}) collective-permute-start(bf16[64,256]{1,0:T(8,128)(2,1)S(1)} %select_convert_fusion.2), channel_id=1, source_target_pairs={{0,64},{4,68},{8,72},{12,76},{16,80},{20,84},{24,88},{28,92},{32,9... | collective-permute-start | bytes 98312 | tf_op jit(solution)/shard_map/ppermute | solution.py:20
  160.0 1.3 collective-permute-done.17
  161.3 6.0 %collective-permute-start.18 = (bf16[64,256]{1,0:T(8,128)(2,1)S(1)}, bf16[64,256]{1,0:T(8,128)(2,1)S(1)}, u32[]{:S(2)}, u32[]{:S(2)}) collective-permute-start(bf16[64,256]{1,0:T(8,128)(2,1)S(1)} %add_convert_fusion.3), channel_id=1, source_target_pairs={{0,8},{4,12},{8,0},{12,4},{16,24},{20,28},{24,16},{28,20},{32,40},... | collective-permute-start | bytes 98312 | tf_op jit(solution)/shard_map/ppermute | solution.py:20
  167.3 2.6 %collective-permute-done.18 = bf16[64,256]{1,0:T(8,128)(2,1)S(1)} collective-permute-done((bf16[64,256]{1,0:T(8,128)(2,1)S(1)}, bf16[64,256]{1,0:T(8,128)(2,1)S(1)}, u32[]{:S(2)}, u32[]{:S(2)}) %collective-permute-start.18) | collective-permute-done | bytes 32800 | tf_op jit(solution)/shard_map/ppermute | solution.py:20
  169.9 4.9 %collective-permute-start.19 = (bf16[64,256]{1,0:T(8,128)(2,1)S(1)}, bf16[64,256]{1,0:T(8,128)(2,1)S(1)}, u32[]{:S(2)}, u32[]{:S(2)}) collective-permute-start(bf16[64,256]{1,0:T(8,128)(2,1)S(1)} %add_convert_fusion.2), channel_id=1, source_target_pairs={{0,32},{4,36},{8,40},{12,44},{16,48},{20,52},{24,56},{28,60},{32,0... | collective-permute-start | bytes 98312 | tf_op jit(solution)/shard_map/ppermute | solution.py:20
  174.8 1.3 collective-permute-done.19
  176.1 5.8 %collective-permute-start.20 = (bf16[64,256]{1,0:T(8,128)(2,1)S(1)}, bf16[64,256]{1,0:T(8,128)(2,1)S(1)}, u32[]{:S(2)}, u32[]{:S(2)}) collective-permute-start(bf16[64,256]{1,0:T(8,128)(2,1)S(1)} %add_convert_fusion.1), channel_id=1, source_target_pairs={{0,128},{4,132},{8,136},{12,140},{16,144},{20,148},{24,152},{28,15... | collective-permute-start | bytes 98312 | tf_op jit(solution)/shard_map/ppermute | solution.py:20
  181.8 1.3 collective-permute-done.20
  183.1 7.4 %collective-permute-start.21 = (bf16[64,256]{1,0:T(8,128)(2,1)S(1)}, bf16[64,256]{1,0:T(8,128)(2,1)S(1)}, u32[]{:S(2)}, u32[]{:S(2)}) collective-permute-start(bf16[64,256]{1,0:T(8,128)(2,1)S(1)} %add_convert_fusion), channel_id=1, source_target_pairs={{0,256},{4,260},{8,264},{12,268},{16,272},{20,276},{24,280},{28,28... | collective-permute-start | bytes 98312 | tf_op jit(solution)/shard_map/ppermute | solution.py:20
  190.6 1.6 collective-permute-done.21
  192.2 3.0 %collective-permute-start.22 = (f32[64,256]{1,0:T(8,128)S(1)}, f32[64,256]{1,0:T(8,128)S(1)}, u32[]{:S(2)}, u32[]{:S(2)}) collective-permute-start(f32[64,256]{1,0:T(8,128)S(1)} %convert_add_fusion.2), channel_id=1, source_target_pairs={{0,64},{4,68},{8,72},{12,76},{16,80},{20,84},{24,88},{28,92},{32,9... | collective-permute-start | bytes 196616 | tf_op jit(solution)/shard_map/ppermute | solution.py:20
  195.2 1.6 convolution_convert_fusion.1
  196.7 1.0 collective-permute-done.22
  197.8 2.9 %collective-permute-start.23 = (f32[128,256]{1,0:T(8,128)S(1)}, f32[128,256]{1,0:T(8,128)S(1)}, u32[]{:S(2)}, u32[]{:S(2)}) collective-permute-start(f32[128,256]{1,0:T(8,128)S(1)} %maximum_select_fusion.2), channel_id=1, source_target_pairs={{0,16},{4,20},{8,24},{12,28},{16,0},{20,4},{24,8},{28,12},{32,48},... | collective-permute-start | bytes 393224 | tf_op jit(solution)/shard_map/ppermute | solution.py:20
  201.1 2.4 %collective-permute-done.23 = f32[128,256]{1,0:T(8,128)S(1)} collective-permute-done((f32[128,256]{1,0:T(8,128)S(1)}, f32[128,256]{1,0:T(8,128)S(1)}, u32[]{:S(2)}, u32[]{:S(2)}) %collective-permute-start.23) | collective-permute-done | bytes 131104 | tf_op jit(solution)/shard_map/ppermute | solution.py:20
  203.5 10.8 %collective-permute-start.24 = (f32[256,256]{1,0:T(8,128)S(1)}, f32[256,256]{1,0:T(8,128)S(1)}, u32[]{:S(2)}, u32[]{:S(2)}) collective-permute-start(f32[256,256]{1,0:T(8,128)S(1)} %maximum_select_fusion.1), channel_id=1, source_target_pairs={{0,4},{4,0},{8,12},{12,8},{16,20},{20,16},{24,28},{28,24},{32,36},... | collective-permute-start | bytes 786440 | tf_op jit(solution)/shard_map/ppermute | solution.py:20
  214.3 1.5 fusion.29
  215.9 0.8 maximum_select_fusion
  (70 shorter events, 5.0 us)
Async XLA Ops:
  0.6 73.9 %copy-start = (bf16[1,128,1024]{2,1,0:T(8,128)(2,1)S(1)}, bf16[1,128,1024]{2,1,0:T(8,128)(2,1)}, u32[]{:S(2)}) copy-start(bf16[1,128,1024]{2,1,0:T(8,128)(2,1)} %param.7) | copy-start | bytes 786436
  2.2 41.0 %collective-permute-start.3 = (bf16[256,1280]{1,0:T(8,128)(2,1)S(1)}, bf16[256,1280]{1,0:T(8,128)(2,1)S(1)}, u32[]{:S(2)}, u32[]{:S(2)}) collective-permute-start(bf16[256,1280]{1,0:T(8,128)(2,1)S(1)} %fusion.34), channel_id=1, source_target_pairs={{11,0},{0,1},{1,2},{2,3},{15,4},{4,5},{5,6},{6,7},{3,8},{8,9},{9,1... | collective-permute-start | bytes 1966088 | tf_op jit(solution)/shard_map/ppermute | solution.py:134
  7.0 37.0 %collective-permute-start = (bf16[256,1280]{1,0:T(8,128)(2,1)S(1)}, bf16[256,1280]{1,0:T(8,128)(2,1)}, u32[]{:S(2)}, u32[]{:S(2)}) collective-permute-start(bf16[256,1280]{1,0:T(8,128)(2,1)S(1)} %fusion.34), channel_id=1, source_target_pairs={{1,0},{2,1},{3,2},{8,3},{5,4},{6,5},{7,6},{12,7},{9,8},{10,9},{11,... | collective-permute-start | bytes 1966088 | tf_op jit(solution)/shard_map/ppermute | solution.py:134
  15.7 27.4 %collective-permute-start.1 = (bf16[256,640]{1,0:T(8,128)(2,1)S(1)}, bf16[256,640]{1,0:T(8,128)(2,1)S(1)}, u32[]{:S(2)}, u32[]{:S(2)}) collective-permute-start(bf16[256,640]{1,0:T(8,128)(2,1)S(1)} %get-tuple-element.15), channel_id=1, source_target_pairs={{2,0},{3,1},{8,2},{9,3},{6,4},{7,5},{12,6},{13,7},{10,8},{11,9},{0... | collective-permute-start | bytes 983048 | tf_op jit(solution)/shard_map/ppermute | solution.py:134
  19.0 24.1 %collective-permute-start.2 = (bf16[256,640]{1,0:T(8,128)(2,1)S(1)}, bf16[256,640]{1,0:T(8,128)(2,1)S(1)}, u32[]{:S(2)}, u32[]{:S(2)}) collective-permute-start(bf16[256,640]{1,0:T(8,128)(2,1)S(1)} %get-tuple-element.14), channel_id=1, source_target_pairs={{10,0},{11,1},{0,2},{1,3},{14,4},{15,5},{4,6},{5,7},{2,8},{3,9},{8... | collective-permute-start | bytes 983048 | tf_op jit(solution)/shard_map/ppermute | solution.py:134
  43.2 0.9 copy-start.10
  45.6 5.7 %copy-start.9 = (bf16[1,128,1024]{2,1,0:T(8,128)(2,1)S(1)}, bf16[1,128,1024]{2,1,0:T(8,128)(2,1)}, u32[]{:S(2)}) copy-start(bf16[1,128,1024]{2,1,0:T(8,128)(2,1)} %param.6) | copy-start | bytes 786436
  47.3 8.3 %collective-permute-start.4 = (bf16[1024,1280]{1,0:T(8,128)(2,1)}, bf16[1024,1280]{1,0:T(8,128)(2,1)}, u32[]{:S(2)}, u32[]{:S(2)}) collective-permute-start(bf16[1024,1280]{1,0:T(8,128)(2,1)} %pad_maximum_fusion), channel_id=1, source_target_pairs={{0,4},{4,0},{8,12},{12,8},{16,20},{20,16},{24,28},{28,24},{32,36},... | collective-permute-start | bytes 7864328 | tf_op jit(solution)/shard_map/ppermute | solution.py:20
  57.9 15.9 %copy-start.1 = (bf16[1024,1280]{1,0:T(8,128)(2,1)}, bf16[1024,1280]{1,0:T(8,128)(2,1)S(1)}, u32[]{:S(2)}) copy-start(bf16[1024,1280]{1,0:T(8,128)(2,1)S(1)} %get-tuple-element.3) | copy-start | bytes 7864324
  58.0 17.3 %copy-start.3 = (bf16[1024,512]{1,0:T(8,128)(2,1)}, bf16[1024,512]{1,0:T(8,128)(2,1)S(1)}, u32[]{:S(2)}) copy-start(bf16[1024,512]{1,0:T(8,128)(2,1)S(1)} %pad_maximum_fusion.2) | copy-start | bytes 3145732
  58.4 18.3 %collective-permute-start.8 = (bf16[128,512]{1,0:T(8,128)(2,1)S(1)}, bf16[128,512]{1,0:T(8,128)(2,1)S(1)}, u32[]{:S(2)}, u32[]{:S(2)}) collective-permute-start(bf16[128,512]{1,0:T(8,128)(2,1)S(1)} %fusion.32), channel_id=1, source_target_pairs={{0,4},{4,8},{8,12},{12,16},{16,20},{20,24},{24,28},{28,32},{32,36}... | collective-permute-start | bytes 393224 | tf_op jit(solution)/shard_map/ppermute | solution.py:15
  64.8 11.9 %collective-permute-start.7 = (bf16[128,512]{1,0:T(8,128)(2,1)S(1)}, bf16[128,512]{1,0:T(8,128)(2,1)S(1)}, u32[]{:S(2)}, u32[]{:S(2)}) collective-permute-start(bf16[128,512]{1,0:T(8,128)(2,1)S(1)} %fusion.32), channel_id=1, source_target_pairs={{0,8},{4,12},{8,16},{12,20},{16,24},{20,28},{24,32},{28,36},{32,40... | collective-permute-start | bytes 393224 | tf_op jit(solution)/shard_map/ppermute | solution.py:15
  68.7 7.9 %collective-permute-start.6 = (bf16[128,512]{1,0:T(8,128)(2,1)S(1)}, bf16[128,512]{1,0:T(8,128)(2,1)S(1)}, u32[]{:S(2)}, u32[]{:S(2)}) collective-permute-start(bf16[128,512]{1,0:T(8,128)(2,1)S(1)} %fusion.32), channel_id=1, source_target_pairs={{0,12},{4,16},{8,20},{12,24},{16,28},{20,32},{24,36},{28,40},{32,4... | collective-permute-start | bytes 393224 | tf_op jit(solution)/shard_map/ppermute | solution.py:15
  70.3 6.3 %collective-permute-start.5 = (bf16[128,512]{1,0:T(8,128)(2,1)S(1)}, bf16[128,512]{1,0:T(8,128)(2,1)S(1)}, u32[]{:S(2)}, u32[]{:S(2)}) collective-permute-start(bf16[128,512]{1,0:T(8,128)(2,1)S(1)} %fusion.32), channel_id=1, source_target_pairs={{0,16},{4,20},{8,24},{12,28},{16,32},{20,36},{24,40},{28,44},{32,4... | collective-permute-start | bytes 393224 | tf_op jit(solution)/shard_map/ppermute | solution.py:15
  74.6 2.6 %copy-start.11 = (bf16[1024,128]{1,0:T(8,128)(2,1)}, bf16[1024,128]{1,0:T(8,128)(2,1)S(1)}, u32[]{:S(2)}) copy-start(bf16[1024,128]{1,0:T(8,128)(2,1)S(1)} %fusion.18) | copy-start | bytes 786436
  75.3 1.9 copy-start.13
  77.2 4.4 %copy-start.7 = (bf16[640,256]{0,1:T(8,128)(2,1)}, bf16[640,256]{0,1:T(8,128)(2,1)S(1)}, u32[]{:S(2)}) copy-start(bf16[640,256]{0,1:T(8,128)(2,1)S(1)} %copy.22) | copy-start | bytes 983044
  86.3 1.2 copy-start.12
  87.5 11.5 %copy-start.8 = (bf16[1,128,1024]{1,2,0:T(8,128)(2,1)S(1)}, bf16[1,128,1024]{1,2,0:T(8,128)(2,1)}, u32[]{:S(2)}) copy-start(bf16[1,128,1024]{1,2,0:T(8,128)(2,1)} %copy.28) | copy-start | bytes 786436
  88.6 10.8 %collective-permute-start.9 = (bf16[128,512]{0,1:T(8,128)(2,1)S(1)}, bf16[128,512]{0,1:T(8,128)(2,1)S(1)}, u32[]{:S(2)}, u32[]{:S(2)}) collective-permute-start(bf16[128,512]{0,1:T(8,128)(2,1)S(1)} %get-tuple-element.8), channel_id=1, source_target_pairs={{4,0},{8,4},{12,8},{16,12},{20,16},{24,20},{28,24},{32,28},{36,32}... | collective-permute-start | bytes 393224 | tf_op jit(solution)/shard_map/ppermute | solution.py:15
  95.1 6.4 %collective-permute-start.12 = (bf16[128,512]{0,1:T(8,128)(2,1)S(1)}, bf16[128,512]{0,1:T(8,128)(2,1)S(1)}, u32[]{:S(2)}, u32[]{:S(2)}) collective-permute-start(bf16[128,512]{0,1:T(8,128)(2,1)S(1)} %get-tuple-element.9), channel_id=1, source_target_pairs={{16,0},{20,4},{24,8},{28,12},{32,16},{36,20},{40,24},{44,28},{48,3... | collective-permute-start | bytes 393224 | tf_op jit(solution)/shard_map/ppermute | solution.py:15
  96.4 9.0 %collective-permute-start.11 = (bf16[128,512]{0,1:T(8,128)(2,1)S(1)}, bf16[128,512]{0,1:T(8,128)(2,1)S(1)}, u32[]{:S(2)}, u32[]{:S(2)}) collective-permute-start(bf16[128,512]{0,1:T(8,128)(2,1)S(1)} %get-tuple-element.10), channel_id=1, source_target_pairs={{12,0},{16,4},{20,8},{24,12},{28,16},{32,20},{36,24},{40,28},{44,3... | collective-permute-start | bytes 393224 | tf_op jit(solution)/shard_map/ppermute | solution.py:15
  97.7 11.6 %collective-permute-start.10 = (bf16[128,512]{0,1:T(8,128)(2,1)S(1)}, bf16[128,512]{0,1:T(8,128)(2,1)S(1)}, u32[]{:S(2)}, u32[]{:S(2)}) collective-permute-start(bf16[128,512]{0,1:T(8,128)(2,1)S(1)} %get-tuple-element.11), channel_id=1, source_target_pairs={{8,0},{12,4},{16,8},{20,12},{24,16},{28,20},{32,24},{36,28},{40,32... | collective-permute-start | bytes 393224 | tf_op jit(solution)/shard_map/ppermute | solution.py:15
  110.6 4.1 %collective-permute-start.13 = (bf16[1024,256]{1,0:T(8,128)(2,1)}, bf16[1024,256]{1,0:T(8,128)(2,1)}, u32[]{:S(2)}, u32[]{:S(2)}) collective-permute-start(bf16[1024,256]{1,0:T(8,128)(2,1)} %convolution_convert_fusion), channel_id=1, source_target_pairs={{0,4},{4,0},{8,12},{12,8},{16,20},{20,16},{24,28},{28,24},{32,36},... | collective-permute-start | bytes 1572872 | tf_op jit(solution)/shard_map/ppermute | solution.py:20
  116.0 1.0 copy-start.5
  117.1 12.3 %collective-permute-start.14 = (bf16[512,256]{1,0:T(8,128)(2,1)S(1)}, bf16[512,256]{1,0:T(8,128)(2,1)}, u32[]{:S(2)}, u32[]{:S(2)}) collective-permute-start(bf16[512,256]{1,0:T(8,128)(2,1)S(1)} %slice.165), channel_id=1, source_target_pairs={{0,1},{1,0},{2,3},{3,2},{4,5},{5,4},{6,7},{7,6},{8,9},{9,8},{10,11... | collective-permute-start | bytes 786440 | tf_op jit(solution)/shard_map/ppermute | solution.py:20
  131.2 13.5 %collective-permute-start.15 = (bf16[256,256]{1,0:T(8,128)(2,1)}, bf16[256,256]{1,0:T(8,128)(2,1)}, u32[]{:S(2)}, u32[]{:S(2)}) collective-permute-start(bf16[256,256]{1,0:T(8,128)(2,1)} %select_convert_fusion), channel_id=1, source_target_pairs={{0,2},{1,3},{2,0},{3,1},{4,6},{5,7},{6,4},{7,5},{8,10},{9,11},{10,... | collective-permute-start | bytes 393224 | tf_op jit(solution)/shard_map/ppermute | solution.py:20
  145.7 0.7 copy-start.6
  146.4 7.9 %collective-permute-start.16 = (bf16[128,256]{1,0:T(8,128)(2,1)S(1)}, bf16[128,256]{1,0:T(8,128)(2,1)S(1)}, u32[]{:S(2)}, u32[]{:S(2)}) collective-permute-start(bf16[128,256]{1,0:T(8,128)(2,1)S(1)} %select_convert_fusion.1), channel_id=1, source_target_pairs={{0,16},{4,20},{8,24},{12,28},{16,0},{20,4},{24,8},{28,12},{32,48},... | collective-permute-start | bytes 196616 | tf_op jit(solution)/shard_map/ppermute | solution.py:20
  155.3 6.0 %collective-permute-start.17 = (bf16[64,256]{1,0:T(8,128)(2,1)S(1)}, bf16[64,256]{1,0:T(8,128)(2,1)S(1)}, u32[]{:S(2)}, u32[]{:S(2)}) collective-permute-start(bf16[64,256]{1,0:T(8,128)(2,1)S(1)} %select_convert_fusion.2), channel_id=1, source_target_pairs={{0,64},{4,68},{8,72},{12,76},{16,80},{20,84},{24,88},{28,92},{32,9... | collective-permute-start | bytes 98312 | tf_op jit(solution)/shard_map/ppermute | solution.py:20
  161.3 8.6 %collective-permute-start.18 = (bf16[64,256]{1,0:T(8,128)(2,1)S(1)}, bf16[64,256]{1,0:T(8,128)(2,1)S(1)}, u32[]{:S(2)}, u32[]{:S(2)}) collective-permute-start(bf16[64,256]{1,0:T(8,128)(2,1)S(1)} %add_convert_fusion.3), channel_id=1, source_target_pairs={{0,8},{4,12},{8,0},{12,4},{16,24},{20,28},{24,16},{28,20},{32,40},... | collective-permute-start | bytes 98312 | tf_op jit(solution)/shard_map/ppermute | solution.py:20
  169.9 6.2 %collective-permute-start.19 = (bf16[64,256]{1,0:T(8,128)(2,1)S(1)}, bf16[64,256]{1,0:T(8,128)(2,1)S(1)}, u32[]{:S(2)}, u32[]{:S(2)}) collective-permute-start(bf16[64,256]{1,0:T(8,128)(2,1)S(1)} %add_convert_fusion.2), channel_id=1, source_target_pairs={{0,32},{4,36},{8,40},{12,44},{16,48},{20,52},{24,56},{28,60},{32,0... | collective-permute-start | bytes 98312 | tf_op jit(solution)/shard_map/ppermute | solution.py:20
  176.1 7.1 %collective-permute-start.20 = (bf16[64,256]{1,0:T(8,128)(2,1)S(1)}, bf16[64,256]{1,0:T(8,128)(2,1)S(1)}, u32[]{:S(2)}, u32[]{:S(2)}) collective-permute-start(bf16[64,256]{1,0:T(8,128)(2,1)S(1)} %add_convert_fusion.1), channel_id=1, source_target_pairs={{0,128},{4,132},{8,136},{12,140},{16,144},{20,148},{24,152},{28,15... | collective-permute-start | bytes 98312 | tf_op jit(solution)/shard_map/ppermute | solution.py:20
  183.1 9.0 %collective-permute-start.21 = (bf16[64,256]{1,0:T(8,128)(2,1)S(1)}, bf16[64,256]{1,0:T(8,128)(2,1)S(1)}, u32[]{:S(2)}, u32[]{:S(2)}) collective-permute-start(bf16[64,256]{1,0:T(8,128)(2,1)S(1)} %add_convert_fusion), channel_id=1, source_target_pairs={{0,256},{4,260},{8,264},{12,268},{16,272},{20,276},{24,280},{28,28... | collective-permute-start | bytes 98312 | tf_op jit(solution)/shard_map/ppermute | solution.py:20
  190.6 10.1 %copy-start.4 = (bf16[1024,512]{1,0:T(8,128)(2,1)S(1)}, bf16[1024,512]{1,0:T(8,128)(2,1)}, u32[]{:S(2)}) copy-start(bf16[1024,512]{1,0:T(8,128)(2,1)} %copy-done.3) | copy-start | bytes 3145732
  192.2 22.1 %copy-start.2 = (bf16[1024,1280]{1,0:T(8,128)(2,1)S(1)}, bf16[1024,1280]{1,0:T(8,128)(2,1)}, u32[]{:S(2)}) copy-start(bf16[1024,1280]{1,0:T(8,128)(2,1)} %copy-done.1) | copy-start | bytes 7864324
  192.2 5.6 %collective-permute-start.22 = (f32[64,256]{1,0:T(8,128)S(1)}, f32[64,256]{1,0:T(8,128)S(1)}, u32[]{:S(2)}, u32[]{:S(2)}) collective-permute-start(f32[64,256]{1,0:T(8,128)S(1)} %convert_add_fusion.2), channel_id=1, source_target_pairs={{0,64},{4,68},{8,72},{12,76},{16,80},{20,84},{24,88},{28,92},{32,9... | collective-permute-start | bytes 196616 | tf_op jit(solution)/shard_map/ppermute | solution.py:20
  197.8 5.7 %collective-permute-start.23 = (f32[128,256]{1,0:T(8,128)S(1)}, f32[128,256]{1,0:T(8,128)S(1)}, u32[]{:S(2)}, u32[]{:S(2)}) collective-permute-start(f32[128,256]{1,0:T(8,128)S(1)} %maximum_select_fusion.2), channel_id=1, source_target_pairs={{0,16},{4,20},{8,24},{12,28},{16,0},{20,4},{24,8},{28,12},{32,48},... | collective-permute-start | bytes 393224 | tf_op jit(solution)/shard_map/ppermute | solution.py:20
  203.5 12.3 %collective-permute-start.24 = (f32[256,256]{1,0:T(8,128)S(1)}, f32[256,256]{1,0:T(8,128)S(1)}, u32[]{:S(2)}, u32[]{:S(2)}) collective-permute-start(f32[256,256]{1,0:T(8,128)S(1)} %maximum_select_fusion.1), channel_id=1, source_target_pairs={{0,4},{4,0},{8,12},{12,8},{16,20},{20,16},{24,28},{28,24},{32,36},... | collective-permute-start | bytes 786440 | tf_op jit(solution)/shard_map/ppermute | solution.py:20

commit v16 on v15

--- a/solution.py
+++ b/solution.py
@@ -227,7 +227,7 @@
     terms = jnp.where(allowed, jnp.exp(masked - row_max), 0.0)
     denom = jnp.sum(terms, axis=-1, keepdims=True)
     denom = jnp.where(live_rows[:, None], denom, 1.0)
-    attn_probs = (terms / denom).astype(jnp.bfloat16)
+    attn_probs = (terms * (1.0 / denom)).astype(jnp.bfloat16)
     attn_block = jnp.einsum(
         "gjqk,kgd->qgjd", attn_probs, value_block, preferred_element_type=jnp.float32
     ).astype(jnp.bfloat16)

time: 218 us -> 218 us (level)
  no operation moved by 1% of the time
where the time goes in v16:
time: 218 us; the launch traced here: 217 us
  starting transfers between devices  114 us (52%)
  waiting for transfers between devices  64.1 us (29%)
  other arithmetic  16.2 us (7%)
  matrix products  15.8 us (7%)
  local copies, waits for them, and re-layouts  4.2 us (2%)
    ppermute x13, starting transfers between devices, xor_swap(): lax.ppermute(value, axis, [(source, source ^ 1 << bit) for source in rang...  68.8 us
    ppermute x13, waiting for transfers between devices, xor_swap(): lax.ppermute(value, axis, [(source, source ^ 1 << bit) for source in rang...  31.4 us
    ppermute x8, starting transfers between devices, shifted(): lax.ppermute(value, axis, [(source, source + steps) for source in range(l...  25.8 us
    ppermute x4, waiting for transfers between devices, ring_pull(): return lax.ppermute(value, ('tm', 'stream'), pairs)  21.1 us
    ppermute x4, starting transfers between devices, ring_pull(): return lax.ppermute(value, ('tm', 'stream'), pairs)  19.6 us
    ppermute x8, waiting for transfers between devices, shifted(): lax.ppermute(value, axis, [(source, source + steps) for source in range(l...  11.6 us
    sub x1, matrix products, per_device(): terms = jnp.where(allowed, jnp.exp(masked - row_max), 0.0)  4.41 us
  transfers between devices with their start and end apart: 25, of which 18 were waited for; matrix products, arithmetic and copies ran while one was open for 3% of the time, Pallas kernels for 0%

profile of v16, /device:TPU:1, one launch (start us, length us, event | category | flops | bytes accessed | tf_op | source)
XLA Modules:
  0.0 216.7 jit_solution(17059722848851808645)
XLA Ops:
  0.7 1.5 fusion.34
  2.2 4.8 %collective-permute-start.3 = (bf16[256,1280]{1,0:T(8,128)(2,1)S(1)}, bf16[256,1280]{1,0:T(8,128)(2,1)S(1)}, u32[]{:S(2)}, u32[]{:S(2)}) collective-permute-start(bf16[256,1280]{1,0:T(8,128)(2,1)S(1)} %fusion.34), channel_id=1, source_target_pairs={{11,0},{0,1},{1,2},{2,3},{15,4},{4,5},{5,6},{6,7},{3,8},{8,9},{9,1... | collective-permute-start | bytes 1966088 | tf_op jit(solution)/shard_map/ppermute | solution.py:134
  7.0 8.6 %collective-permute-start = (bf16[256,1280]{1,0:T(8,128)(2,1)S(1)}, bf16[256,1280]{1,0:T(8,128)(2,1)}, u32[]{:S(2)}, u32[]{:S(2)}) collective-permute-start(bf16[256,1280]{1,0:T(8,128)(2,1)S(1)} %fusion.34), channel_id=1, source_target_pairs={{1,0},{2,1},{3,2},{8,3},{5,4},{6,5},{7,6},{12,7},{9,8},{10,9},{11,... | collective-permute-start | bytes 1966088 | tf_op jit(solution)/shard_map/ppermute | solution.py:134
  15.7 3.4 %collective-permute-start.1 = (bf16[256,640]{1,0:T(8,128)(2,1)S(1)}, bf16[256,640]{1,0:T(8,128)(2,1)S(1)}, u32[]{:S(2)}, u32[]{:S(2)}) collective-permute-start(bf16[256,640]{1,0:T(8,128)(2,1)S(1)} %get-tuple-element.15), channel_id=1, source_target_pairs={{2,0},{3,1},{8,2},{9,3},{6,4},{7,5},{12,6},{13,7},{10,8},{11,9},{0... | collective-permute-start | bytes 983048 | tf_op jit(solution)/shard_map/ppermute | solution.py:134
  19.0 2.8 %collective-permute-start.2 = (bf16[256,640]{1,0:T(8,128)(2,1)S(1)}, bf16[256,640]{1,0:T(8,128)(2,1)S(1)}, u32[]{:S(2)}, u32[]{:S(2)}) collective-permute-start(bf16[256,640]{1,0:T(8,128)(2,1)S(1)} %get-tuple-element.14), channel_id=1, source_target_pairs={{10,0},{11,1},{0,2},{1,3},{14,4},{15,5},{4,6},{5,7},{2,8},{3,9},{8... | collective-permute-start | bytes 983048 | tf_op jit(solution)/shard_map/ppermute | solution.py:134
  22.0 21.1 %collective-permute-done.1 = bf16[256,640]{1,0:T(8,128)(2,1)S(1)} collective-permute-done((bf16[256,640]{1,0:T(8,128)(2,1)S(1)}, bf16[256,640]{1,0:T(8,128)(2,1)S(1)}, u32[]{:S(2)}, u32[]{:S(2)}) %collective-permute-start.1) | collective-permute-done | bytes 327712 | tf_op jit(solution)/shard_map/ppermute | solution.py:134
  43.2 0.8 copy-done.10
  44.0 1.6 select_select_fusion.3
  45.6 1.7 pad_maximum_fusion
  47.3 3.4 %collective-permute-start.4 = (bf16[1024,1280]{1,0:T(8,128)(2,1)}, bf16[1024,1280]{1,0:T(8,128)(2,1)}, u32[]{:S(2)}, u32[]{:S(2)}) collective-permute-start(bf16[1024,1280]{1,0:T(8,128)(2,1)} %pad_maximum_fusion), channel_id=1, source_target_pairs={{0,4},{4,0},{8,12},{12,8},{16,20},{20,16},{24,28},{28,24},{32,36},... | collective-permute-start | bytes 7864328 | tf_op jit(solution)/shard_map/ppermute | solution.py:20
  51.4 0.8 copy.28
  52.3 1.0 fusion.40
  53.2 2.3 %collective-permute-done.4 = bf16[1024,1280]{1,0:T(8,128)(2,1)} collective-permute-done((bf16[1024,1280]{1,0:T(8,128)(2,1)}, bf16[1024,1280]{1,0:T(8,128)(2,1)}, u32[]{:S(2)}, u32[]{:S(2)}) %collective-permute-start.4) | collective-permute-done | bytes 2621472 | tf_op jit(solution)/shard_map/ppermute | solution.py:20
  55.6 2.4 %broadcast_select_fusion = (bf16[1024,1280]{1,0:T(8,128)(2,1)S(1)}, bf16[1024,1280]{1,0:T(8,128)(2,1)S(1)}) fusion(bf16[1024,1280]{1,0:T(8,128)(2,1)} %collective-permute-done.4, pred[]{:T(512)S(6)} %eq.64, bf16[256,1280]{1,0:T(8,128)(2,1)S(1)} %get-tuple-element.7, bf16[256,1280]{1,0:T(8,128)(2,1)S(1)} %get-tuple-element.5, ...), kind=kLoop, calls=%fused_computation.13 | loop fusion | flops 13107200 | bytes 10485761 | tf_op jit(solution)/shard_map/jit(_where)/select_n | solution.py:190
  58.4 6.4 %collective-permute-start.8 = (bf16[128,512]{1,0:T(8,128)(2,1)S(1)}, bf16[128,512]{1,0:T(8,128)(2,1)S(1)}, u32[]{:S(2)}, u32[]{:S(2)}) collective-permute-start(bf16[128,512]{1,0:T(8,128)(2,1)S(1)} %fusion.32), channel_id=1, source_target_pairs={{0,4},{4,8},{8,12},{12,16},{16,20},{20,24},{24,28},{28,32},{32,36}... | collective-permute-start | bytes 393224 | tf_op jit(solution)/shard_map/ppermute | solution.py:15
  64.8 3.9 %collective-permute-start.7 = (bf16[128,512]{1,0:T(8,128)(2,1)S(1)}, bf16[128,512]{1,0:T(8,128)(2,1)S(1)}, u32[]{:S(2)}, u32[]{:S(2)}) collective-permute-start(bf16[128,512]{1,0:T(8,128)(2,1)S(1)} %fusion.32), channel_id=1, source_target_pairs={{0,8},{4,12},{8,16},{12,20},{16,24},{20,28},{24,32},{28,36},{32,40... | collective-permute-start | bytes 393224 | tf_op jit(solution)/shard_map/ppermute | solution.py:15
  68.7 1.5 collective-permute-start.6
  70.3 3.5 %collective-permute-start.5 = (bf16[128,512]{1,0:T(8,128)(2,1)S(1)}, bf16[128,512]{1,0:T(8,128)(2,1)S(1)}, u32[]{:S(2)}, u32[]{:S(2)}) collective-permute-start(bf16[128,512]{1,0:T(8,128)(2,1)S(1)} %fusion.32), channel_id=1, source_target_pairs={{0,16},{4,20},{8,24},{12,28},{16,32},{20,36},{24,40},{28,44},{32,4... | collective-permute-start | bytes 393224 | tf_op jit(solution)/shard_map/ppermute | solution.py:15
  73.8 0.8 fusion.18
  75.3 1.3 collective-permute-done.5
  77.2 4.4 %fusion.63 = (f32[4,4,128]{2,1,0:T(4,128)S(1)}, f32[4,4,128,640]{2,3,1,0:T(8,128)}) fusion(pred[128,640]{0,1:T(8,128)(4,1)S(1)} %copy-done.13, bf16[640,4,64,1]{0,2,3,1:T(8,128)(2,1)S(1)} %bitcast.94, bf16[128,4,4,64]{0,3,2,1:T(8,128)(2,1)S(1)} %bitcast.105), kind=kOutput, calls=%fused_computation.106 | convolution fusion | flops 174326400 | bytes 5922816 | tf_op jit(solution)/shard_map/sub | solution.py:227
  81.6 3.1 %multiply_convert_fusion = bf16[4,4,128,640]{2,3,1,0:T(8,128)(2,1)S(1)} fusion(f32[4,4,128,640]{2,3,1,0:T(8,128)} %get-tuple-element.19, f32[4,4,128]{2,1,0:T(4,128)S(1)} %select_divide_fusion), kind=kLoop, calls=%fused_computation.6 | loop fusion | flops 2621440 | bytes 7872512 | tf_op jit(solution)/shard_map/convert_element_type | solution.py:230
  85.4 0.9 fusion.65
  86.3 1.2 fusion.3
  87.5 0.9 fusion.64
  88.6 6.5 %collective-permute-start.9 = (bf16[128,512]{0,1:T(8,128)(2,1)S(1)}, bf16[128,512]{0,1:T(8,128)(2,1)S(1)}, u32[]{:S(2)}, u32[]{:S(2)}) collective-permute-start(bf16[128,512]{0,1:T(8,128)(2,1)S(1)} %get-tuple-element.8), channel_id=1, source_target_pairs={{4,0},{8,4},{12,8},{16,12},{20,16},{24,20},{28,24},{32,28},{36,32}... | collective-permute-start | bytes 393224 | tf_op jit(solution)/shard_map/ppermute | solution.py:15
  95.1 1.3 collective-permute-start.12
  96.4 1.3 collective-permute-start.11
  97.7 1.3 collective-permute-start.10
  99.4 2.2 collective-permute-done.12
  101.5 3.9 %collective-permute-done.11 = bf16[128,512]{0,1:T(8,128)(2,1)S(1)} collective-permute-done((bf16[128,512]{0,1:T(8,128)(2,1)S(1)}, bf16[128,512]{0,1:T(8,128)(2,1)S(1)}, u32[]{:S(2)}, u32[]{:S(2)}) %collective-permute-start.11) | collective-permute-done | bytes 131104 | tf_op jit(solution)/shard_map/ppermute | solution.py:15
  105.4 3.9 %collective-permute-done.10 = bf16[128,512]{0,1:T(8,128)(2,1)S(1)} collective-permute-done((bf16[128,512]{0,1:T(8,128)(2,1)S(1)}, bf16[128,512]{0,1:T(8,128)(2,1)S(1)}, u32[]{:S(2)}, u32[]{:S(2)}) %collective-permute-start.10) | collective-permute-done | bytes 131104 | tf_op jit(solution)/shard_map/ppermute | solution.py:15
  109.4 1.1 convolution_convert_fusion
  110.6 2.2 %collective-permute-start.13 = (bf16[1024,256]{1,0:T(8,128)(2,1)}, bf16[1024,256]{1,0:T(8,128)(2,1)}, u32[]{:S(2)}, u32[]{:S(2)}) collective-permute-start(bf16[1024,256]{1,0:T(8,128)(2,1)} %convolution_convert_fusion), channel_id=1, source_target_pairs={{0,4},{4,0},{8,12},{12,8},{16,20},{20,16},{24,28},{28,24},{32,36},... | collective-permute-start | bytes 1572872 | tf_op jit(solution)/shard_map/ppermute | solution.py:20
  112.8 1.9 collective-permute-done.13
  114.7 1.3 convolution_add_fusion
  116.0 1.0 copy-done.5
  117.1 5.6 %collective-permute-start.14 = (bf16[512,256]{1,0:T(8,128)(2,1)S(1)}, bf16[512,256]{1,0:T(8,128)(2,1)}, u32[]{:S(2)}, u32[]{:S(2)}) collective-permute-start(bf16[512,256]{1,0:T(8,128)(2,1)S(1)} %slice.165), channel_id=1, source_target_pairs={{0,1},{1,0},{2,3},{3,2},{4,5},{5,4},{6,7},{7,6},{8,9},{9,8},{10,11... | collective-permute-start | bytes 786440 | tf_op jit(solution)/shard_map/ppermute | solution.py:20
  122.7 6.6 %collective-permute-done.14 = bf16[512,256]{1,0:T(8,128)(2,1)} collective-permute-done((bf16[512,256]{1,0:T(8,128)(2,1)S(1)}, bf16[512,256]{1,0:T(8,128)(2,1)}, u32[]{:S(2)}, u32[]{:S(2)}) %collective-permute-start.14) | collective-permute-done | bytes 262176 | tf_op jit(solution)/shard_map/ppermute | solution.py:20
  129.3 1.2 slice_add_fusion
  131.2 6.5 %collective-permute-start.15 = (bf16[256,256]{1,0:T(8,128)(2,1)}, bf16[256,256]{1,0:T(8,128)(2,1)}, u32[]{:S(2)}, u32[]{:S(2)}) collective-permute-start(bf16[256,256]{1,0:T(8,128)(2,1)} %select_convert_fusion), channel_id=1, source_target_pairs={{0,2},{1,3},{2,0},{3,1},{4,6},{5,7},{6,4},{7,5},{8,10},{9,11},{10,... | collective-permute-start | bytes 393224 | tf_op jit(solution)/shard_map/ppermute | solution.py:20
  137.7 7.0 %collective-permute-done.15 = bf16[256,256]{1,0:T(8,128)(2,1)} collective-permute-done((bf16[256,256]{1,0:T(8,128)(2,1)}, bf16[256,256]{1,0:T(8,128)(2,1)}, u32[]{:S(2)}, u32[]{:S(2)}) %collective-permute-start.15) | collective-permute-done | bytes 131104 | tf_op jit(solution)/shard_map/ppermute | solution.py:20
  144.7 0.9 convert_add_fusion
  146.4 5.9 %collective-permute-start.16 = (bf16[128,256]{1,0:T(8,128)(2,1)S(1)}, bf16[128,256]{1,0:T(8,128)(2,1)S(1)}, u32[]{:S(2)}, u32[]{:S(2)}) collective-permute-start(bf16[128,256]{1,0:T(8,128)(2,1)S(1)} %select_convert_fusion.1), channel_id=1, source_target_pairs={{0,16},{4,20},{8,24},{12,28},{16,0},{20,4},{24,8},{28,12},{32,48},... | collective-permute-start | bytes 196616 | tf_op jit(solution)/shard_map/ppermute | solution.py:20
  152.3 2.0 collective-permute-done.16
  154.3 1.0 convert_add_fusion.1
  155.3 4.7 %collective-permute-start.17 = (bf16[64,256]{1,0:T(8,128)(2,1)S(1)}, bf16[64,256]{1,0:T(8,128)(2,1)S(1)}, u32[]{:S(2)}, u32[]{:S(2)}) collective-permute-start(bf16[64,256]{1,0:T(8,128)(2,1)S(1)} %select_convert_fusion.2), channel_id=1, source_target_pairs={{0,64},{4,68},{8,72},{12,76},{16,80},{20,84},{24,88},{28,92},{32,9... | collective-permute-start | bytes 98312 | tf_op jit(solution)/shard_map/ppermute | solution.py:20
  160.0 1.3 collective-permute-done.17
  161.3 6.0 %collective-permute-start.18 = (bf16[64,256]{1,0:T(8,128)(2,1)S(1)}, bf16[64,256]{1,0:T(8,128)(2,1)S(1)}, u32[]{:S(2)}, u32[]{:S(2)}) collective-permute-start(bf16[64,256]{1,0:T(8,128)(2,1)S(1)} %add_convert_fusion.3), channel_id=1, source_target_pairs={{0,8},{4,12},{8,0},{12,4},{16,24},{20,28},{24,16},{28,20},{32,40},... | collective-permute-start | bytes 98312 | tf_op jit(solution)/shard_map/ppermute | solution.py:20
  167.3 2.6 %collective-permute-done.18 = bf16[64,256]{1,0:T(8,128)(2,1)S(1)} collective-permute-done((bf16[64,256]{1,0:T(8,128)(2,1)S(1)}, bf16[64,256]{1,0:T(8,128)(2,1)S(1)}, u32[]{:S(2)}, u32[]{:S(2)}) %collective-permute-start.18) | collective-permute-done | bytes 32800 | tf_op jit(solution)/shard_map/ppermute | solution.py:20
  169.9 4.8 %collective-permute-start.19 = (bf16[64,256]{1,0:T(8,128)(2,1)S(1)}, bf16[64,256]{1,0:T(8,128)(2,1)S(1)}, u32[]{:S(2)}, u32[]{:S(2)}) collective-permute-start(bf16[64,256]{1,0:T(8,128)(2,1)S(1)} %add_convert_fusion.2), channel_id=1, source_target_pairs={{0,32},{4,36},{8,40},{12,44},{16,48},{20,52},{24,56},{28,60},{32,0... | collective-permute-start | bytes 98312 | tf_op jit(solution)/shard_map/ppermute | solution.py:20
  174.8 1.3 collective-permute-done.19
  176.1 5.7 %collective-permute-start.20 = (bf16[64,256]{1,0:T(8,128)(2,1)S(1)}, bf16[64,256]{1,0:T(8,128)(2,1)S(1)}, u32[]{:S(2)}, u32[]{:S(2)}) collective-permute-start(bf16[64,256]{1,0:T(8,128)(2,1)S(1)} %add_convert_fusion.1), channel_id=1, source_target_pairs={{0,128},{4,132},{8,136},{12,140},{16,144},{20,148},{24,152},{28,15... | collective-permute-start | bytes 98312 | tf_op jit(solution)/shard_map/ppermute | solution.py:20
  181.8 1.3 collective-permute-done.20
  183.1 7.4 %collective-permute-start.21 = (bf16[64,256]{1,0:T(8,128)(2,1)S(1)}, bf16[64,256]{1,0:T(8,128)(2,1)S(1)}, u32[]{:S(2)}, u32[]{:S(2)}) collective-permute-start(bf16[64,256]{1,0:T(8,128)(2,1)S(1)} %add_convert_fusion), channel_id=1, source_target_pairs={{0,256},{4,260},{8,264},{12,268},{16,272},{20,276},{24,280},{28,28... | collective-permute-start | bytes 98312 | tf_op jit(solution)/shard_map/ppermute | solution.py:20
  190.5 1.6 collective-permute-done.21
  192.2 3.0 %collective-permute-start.22 = (f32[64,256]{1,0:T(8,128)S(1)}, f32[64,256]{1,0:T(8,128)S(1)}, u32[]{:S(2)}, u32[]{:S(2)}) collective-permute-start(f32[64,256]{1,0:T(8,128)S(1)} %convert_add_fusion.2), channel_id=1, source_target_pairs={{0,64},{4,68},{8,72},{12,76},{16,80},{20,84},{24,88},{28,92},{32,9... | collective-permute-start | bytes 196616 | tf_op jit(solution)/shard_map/ppermute | solution.py:20
  195.2 1.5 convolution_convert_fusion.1
  196.7 1.1 collective-permute-done.22
  197.8 2.9 %collective-permute-start.23 = (f32[128,256]{1,0:T(8,128)S(1)}, f32[128,256]{1,0:T(8,128)S(1)}, u32[]{:S(2)}, u32[]{:S(2)}) collective-permute-start(f32[128,256]{1,0:T(8,128)S(1)} %maximum_select_fusion.2), channel_id=1, source_target_pairs={{0,16},{4,20},{8,24},{12,28},{16,0},{20,4},{24,8},{28,12},{32,48},... | collective-permute-start | bytes 393224 | tf_op jit(solution)/shard_map/ppermute | solution.py:20
  201.1 2.4 %collective-permute-done.23 = f32[128,256]{1,0:T(8,128)S(1)} collective-permute-done((f32[128,256]{1,0:T(8,128)S(1)}, f32[128,256]{1,0:T(8,128)S(1)}, u32[]{:S(2)}, u32[]{:S(2)}) %collective-permute-start.23) | collective-permute-done | bytes 131104 | tf_op jit(solution)/shard_map/ppermute | solution.py:20
  203.5 10.8 %collective-permute-start.24 = (f32[256,256]{1,0:T(8,128)S(1)}, f32[256,256]{1,0:T(8,128)S(1)}, u32[]{:S(2)}, u32[]{:S(2)}) collective-permute-start(f32[256,256]{1,0:T(8,128)S(1)} %maximum_select_fusion.1), channel_id=1, source_target_pairs={{0,4},{4,0},{8,12},{12,8},{16,20},{20,16},{24,28},{28,24},{32,36},... | collective-permute-start | bytes 786440 | tf_op jit(solution)/shard_map/ppermute | solution.py:20
  214.3 1.5 fusion.29
  215.8 0.8 maximum_select_fusion
  (70 shorter events, 5.0 us)
Async XLA Ops:
  0.6 73.9 %copy-start = (bf16[1,128,1024]{2,1,0:T(8,128)(2,1)S(1)}, bf16[1,128,1024]{2,1,0:T(8,128)(2,1)}, u32[]{:S(2)}) copy-start(bf16[1,128,1024]{2,1,0:T(8,128)(2,1)} %param.7) | copy-start | bytes 786436
  2.2 41.0 %collective-permute-start.3 = (bf16[256,1280]{1,0:T(8,128)(2,1)S(1)}, bf16[256,1280]{1,0:T(8,128)(2,1)S(1)}, u32[]{:S(2)}, u32[]{:S(2)}) collective-permute-start(bf16[256,1280]{1,0:T(8,128)(2,1)S(1)} %fusion.34), channel_id=1, source_target_pairs={{11,0},{0,1},{1,2},{2,3},{15,4},{4,5},{5,6},{6,7},{3,8},{8,9},{9,1... | collective-permute-start | bytes 1966088 | tf_op jit(solution)/shard_map/ppermute | solution.py:134
  7.0 37.0 %collective-permute-start = (bf16[256,1280]{1,0:T(8,128)(2,1)S(1)}, bf16[256,1280]{1,0:T(8,128)(2,1)}, u32[]{:S(2)}, u32[]{:S(2)}) collective-permute-start(bf16[256,1280]{1,0:T(8,128)(2,1)S(1)} %fusion.34), channel_id=1, source_target_pairs={{1,0},{2,1},{3,2},{8,3},{5,4},{6,5},{7,6},{12,7},{9,8},{10,9},{11,... | collective-permute-start | bytes 1966088 | tf_op jit(solution)/shard_map/ppermute | solution.py:134
  15.7 27.4 %collective-permute-start.1 = (bf16[256,640]{1,0:T(8,128)(2,1)S(1)}, bf16[256,640]{1,0:T(8,128)(2,1)S(1)}, u32[]{:S(2)}, u32[]{:S(2)}) collective-permute-start(bf16[256,640]{1,0:T(8,128)(2,1)S(1)} %get-tuple-element.15), channel_id=1, source_target_pairs={{2,0},{3,1},{8,2},{9,3},{6,4},{7,5},{12,6},{13,7},{10,8},{11,9},{0... | collective-permute-start | bytes 983048 | tf_op jit(solution)/shard_map/ppermute | solution.py:134
  19.0 24.1 %collective-permute-start.2 = (bf16[256,640]{1,0:T(8,128)(2,1)S(1)}, bf16[256,640]{1,0:T(8,128)(2,1)S(1)}, u32[]{:S(2)}, u32[]{:S(2)}) collective-permute-start(bf16[256,640]{1,0:T(8,128)(2,1)S(1)} %get-tuple-element.14), channel_id=1, source_target_pairs={{10,0},{11,1},{0,2},{1,3},{14,4},{15,5},{4,6},{5,7},{2,8},{3,9},{8... | collective-permute-start | bytes 983048 | tf_op jit(solution)/shard_map/ppermute | solution.py:134
  43.2 0.9 copy-start.10
  45.6 5.7 %copy-start.9 = (bf16[1,128,1024]{2,1,0:T(8,128)(2,1)S(1)}, bf16[1,128,1024]{2,1,0:T(8,128)(2,1)}, u32[]{:S(2)}) copy-start(bf16[1,128,1024]{2,1,0:T(8,128)(2,1)} %param.6) | copy-start | bytes 786436
  47.3 8.3 %collective-permute-start.4 = (bf16[1024,1280]{1,0:T(8,128)(2,1)}, bf16[1024,1280]{1,0:T(8,128)(2,1)}, u32[]{:S(2)}, u32[]{:S(2)}) collective-permute-start(bf16[1024,1280]{1,0:T(8,128)(2,1)} %pad_maximum_fusion), channel_id=1, source_target_pairs={{0,4},{4,0},{8,12},{12,8},{16,20},{20,16},{24,28},{28,24},{32,36},... | collective-permute-start | bytes 7864328 | tf_op jit(solution)/shard_map/ppermute | solution.py:20
  57.9 15.9 %copy-start.1 = (bf16[1024,1280]{1,0:T(8,128)(2,1)}, bf16[1024,1280]{1,0:T(8,128)(2,1)S(1)}, u32[]{:S(2)}) copy-start(bf16[1024,1280]{1,0:T(8,128)(2,1)S(1)} %get-tuple-element.3) | copy-start | bytes 7864324
  58.0 17.3 %copy-start.3 = (bf16[1024,512]{1,0:T(8,128)(2,1)}, bf16[1024,512]{1,0:T(8,128)(2,1)S(1)}, u32[]{:S(2)}) copy-start(bf16[1024,512]{1,0:T(8,128)(2,1)S(1)} %pad_maximum_fusion.2) | copy-start | bytes 3145732
  58.4 18.3 %collective-permute-start.8 = (bf16[128,512]{1,0:T(8,128)(2,1)S(1)}, bf16[128,512]{1,0:T(8,128)(2,1)S(1)}, u32[]{:S(2)}, u32[]{:S(2)}) collective-permute-start(bf16[128,512]{1,0:T(8,128)(2,1)S(1)} %fusion.32), channel_id=1, source_target_pairs={{0,4},{4,8},{8,12},{12,16},{16,20},{20,24},{24,28},{28,32},{32,36}... | collective-permute-start | bytes 393224 | tf_op jit(solution)/shard_map/ppermute | solution.py:15
  64.8 11.9 %collective-permute-start.7 = (bf16[128,512]{1,0:T(8,128)(2,1)S(1)}, bf16[128,512]{1,0:T(8,128)(2,1)S(1)}, u32[]{:S(2)}, u32[]{:S(2)}) collective-permute-start(bf16[128,512]{1,0:T(8,128)(2,1)S(1)} %fusion.32), channel_id=1, source_target_pairs={{0,8},{4,12},{8,16},{12,20},{16,24},{20,28},{24,32},{28,36},{32,40... | collective-permute-start | bytes 393224 | tf_op jit(solution)/shard_map/ppermute | solution.py:15
  68.7 7.9 %collective-permute-start.6 = (bf16[128,512]{1,0:T(8,128)(2,1)S(1)}, bf16[128,512]{1,0:T(8,128)(2,1)S(1)}, u32[]{:S(2)}, u32[]{:S(2)}) collective-permute-start(bf16[128,512]{1,0:T(8,128)(2,1)S(1)} %fusion.32), channel_id=1, source_target_pairs={{0,12},{4,16},{8,20},{12,24},{16,28},{20,32},{24,36},{28,40},{32,4... | collective-permute-start | bytes 393224 | tf_op jit(solution)/shard_map/ppermute | solution.py:15
  70.3 6.3 %collective-permute-start.5 = (bf16[128,512]{1,0:T(8,128)(2,1)S(1)}, bf16[128,512]{1,0:T(8,128)(2,1)S(1)}, u32[]{:S(2)}, u32[]{:S(2)}) collective-permute-start(bf16[128,512]{1,0:T(8,128)(2,1)S(1)} %fusion.32), channel_id=1, source_target_pairs={{0,16},{4,20},{8,24},{12,28},{16,32},{20,36},{24,40},{28,44},{32,4... | collective-permute-start | bytes 393224 | tf_op jit(solution)/shard_map/ppermute | solution.py:15
  74.6 2.6 %copy-start.11 = (bf16[1024,128]{1,0:T(8,128)(2,1)}, bf16[1024,128]{1,0:T(8,128)(2,1)S(1)}, u32[]{:S(2)}) copy-start(bf16[1024,128]{1,0:T(8,128)(2,1)S(1)} %fusion.18) | copy-start | bytes 786436
  75.3 1.9 copy-start.13
  77.2 4.4 %copy-start.7 = (bf16[640,256]{0,1:T(8,128)(2,1)}, bf16[640,256]{0,1:T(8,128)(2,1)S(1)}, u32[]{:S(2)}) copy-start(bf16[640,256]{0,1:T(8,128)(2,1)S(1)} %copy.22) | copy-start | bytes 983044
  86.3 1.2 copy-start.12
  87.5 11.5 %copy-start.8 = (bf16[1,128,1024]{1,2,0:T(8,128)(2,1)S(1)}, bf16[1,128,1024]{1,2,0:T(8,128)(2,1)}, u32[]{:S(2)}) copy-start(bf16[1,128,1024]{1,2,0:T(8,128)(2,1)} %copy.28) | copy-start | bytes 786436
  88.6 10.8 %collective-permute-start.9 = (bf16[128,512]{0,1:T(8,128)(2,1)S(1)}, bf16[128,512]{0,1:T(8,128)(2,1)S(1)}, u32[]{:S(2)}, u32[]{:S(2)}) collective-permute-start(bf16[128,512]{0,1:T(8,128)(2,1)S(1)} %get-tuple-element.8), channel_id=1, source_target_pairs={{4,0},{8,4},{12,8},{16,12},{20,16},{24,20},{28,24},{32,28},{36,32}... | collective-permute-start | bytes 393224 | tf_op jit(solution)/shard_map/ppermute | solution.py:15
  95.1 6.4 %collective-permute-start.12 = (bf16[128,512]{0,1:T(8,128)(2,1)S(1)}, bf16[128,512]{0,1:T(8,128)(2,1)S(1)}, u32[]{:S(2)}, u32[]{:S(2)}) collective-permute-start(bf16[128,512]{0,1:T(8,128)(2,1)S(1)} %get-tuple-element.9), channel_id=1, source_target_pairs={{16,0},{20,4},{24,8},{28,12},{32,16},{36,20},{40,24},{44,28},{48,3... | collective-permute-start | bytes 393224 | tf_op jit(solution)/shard_map/ppermute | solution.py:15
  96.4 9.0 %collective-permute-start.11 = (bf16[128,512]{0,1:T(8,128)(2,1)S(1)}, bf16[128,512]{0,1:T(8,128)(2,1)S(1)}, u32[]{:S(2)}, u32[]{:S(2)}) collective-permute-start(bf16[128,512]{0,1:T(8,128)(2,1)S(1)} %get-tuple-element.10), channel_id=1, source_target_pairs={{12,0},{16,4},{20,8},{24,12},{28,16},{32,20},{36,24},{40,28},{44,3... | collective-permute-start | bytes 393224 | tf_op jit(solution)/shard_map/ppermute | solution.py:15
  97.7 11.6 %collective-permute-start.10 = (bf16[128,512]{0,1:T(8,128)(2,1)S(1)}, bf16[128,512]{0,1:T(8,128)(2,1)S(1)}, u32[]{:S(2)}, u32[]{:S(2)}) collective-permute-start(bf16[128,512]{0,1:T(8,128)(2,1)S(1)} %get-tuple-element.11), channel_id=1, source_target_pairs={{8,0},{12,4},{16,8},{20,12},{24,16},{28,20},{32,24},{36,28},{40,32... | collective-permute-start | bytes 393224 | tf_op jit(solution)/shard_map/ppermute | solution.py:15
  110.6 4.1 %collective-permute-start.13 = (bf16[1024,256]{1,0:T(8,128)(2,1)}, bf16[1024,256]{1,0:T(8,128)(2,1)}, u32[]{:S(2)}, u32[]{:S(2)}) collective-permute-start(bf16[1024,256]{1,0:T(8,128)(2,1)} %convolution_convert_fusion), channel_id=1, source_target_pairs={{0,4},{4,0},{8,12},{12,8},{16,20},{20,16},{24,28},{28,24},{32,36},... | collective-permute-start | bytes 1572872 | tf_op jit(solution)/shard_map/ppermute | solution.py:20
  116.0 1.0 copy-start.5
  117.1 12.2 %collective-permute-start.14 = (bf16[512,256]{1,0:T(8,128)(2,1)S(1)}, bf16[512,256]{1,0:T(8,128)(2,1)}, u32[]{:S(2)}, u32[]{:S(2)}) collective-permute-start(bf16[512,256]{1,0:T(8,128)(2,1)S(1)} %slice.165), channel_id=1, source_target_pairs={{0,1},{1,0},{2,3},{3,2},{4,5},{5,4},{6,7},{7,6},{8,9},{9,8},{10,11... | collective-permute-start | bytes 786440 | tf_op jit(solution)/shard_map/ppermute | solution.py:20
  131.2 13.6 %collective-permute-start.15 = (bf16[256,256]{1,0:T(8,128)(2,1)}, bf16[256,256]{1,0:T(8,128)(2,1)}, u32[]{:S(2)}, u32[]{:S(2)}) collective-permute-start(bf16[256,256]{1,0:T(8,128)(2,1)} %select_convert_fusion), channel_id=1, source_target_pairs={{0,2},{1,3},{2,0},{3,1},{4,6},{5,7},{6,4},{7,5},{8,10},{9,11},{10,... | collective-permute-start | bytes 393224 | tf_op jit(solution)/shard_map/ppermute | solution.py:20
  145.7 0.7 copy-start.6
  146.4 7.9 %collective-permute-start.16 = (bf16[128,256]{1,0:T(8,128)(2,1)S(1)}, bf16[128,256]{1,0:T(8,128)(2,1)S(1)}, u32[]{:S(2)}, u32[]{:S(2)}) collective-permute-start(bf16[128,256]{1,0:T(8,128)(2,1)S(1)} %select_convert_fusion.1), channel_id=1, source_target_pairs={{0,16},{4,20},{8,24},{12,28},{16,0},{20,4},{24,8},{28,12},{32,48},... | collective-permute-start | bytes 196616 | tf_op jit(solution)/shard_map/ppermute | solution.py:20
  155.3 6.0 %collective-permute-start.17 = (bf16[64,256]{1,0:T(8,128)(2,1)S(1)}, bf16[64,256]{1,0:T(8,128)(2,1)S(1)}, u32[]{:S(2)}, u32[]{:S(2)}) collective-permute-start(bf16[64,256]{1,0:T(8,128)(2,1)S(1)} %select_convert_fusion.2), channel_id=1, source_target_pairs={{0,64},{4,68},{8,72},{12,76},{16,80},{20,84},{24,88},{28,92},{32,9... | collective-permute-start | bytes 98312 | tf_op jit(solution)/shard_map/ppermute | solution.py:20
  161.3 8.6 %collective-permute-start.18 = (bf16[64,256]{1,0:T(8,128)(2,1)S(1)}, bf16[64,256]{1,0:T(8,128)(2,1)S(1)}, u32[]{:S(2)}, u32[]{:S(2)}) collective-permute-start(bf16[64,256]{1,0:T(8,128)(2,1)S(1)} %add_convert_fusion.3), channel_id=1, source_target_pairs={{0,8},{4,12},{8,0},{12,4},{16,24},{20,28},{24,16},{28,20},{32,40},... | collective-permute-start | bytes 98312 | tf_op jit(solution)/shard_map/ppermute | solution.py:20
  169.9 6.2 %collective-permute-start.19 = (bf16[64,256]{1,0:T(8,128)(2,1)S(1)}, bf16[64,256]{1,0:T(8,128)(2,1)S(1)}, u32[]{:S(2)}, u32[]{:S(2)}) collective-permute-start(bf16[64,256]{1,0:T(8,128)(2,1)S(1)} %add_convert_fusion.2), channel_id=1, source_target_pairs={{0,32},{4,36},{8,40},{12,44},{16,48},{20,52},{24,56},{28,60},{32,0... | collective-permute-start | bytes 98312 | tf_op jit(solution)/shard_map/ppermute | solution.py:20
  176.1 7.0 %collective-permute-start.20 = (bf16[64,256]{1,0:T(8,128)(2,1)S(1)}, bf16[64,256]{1,0:T(8,128)(2,1)S(1)}, u32[]{:S(2)}, u32[]{:S(2)}) collective-permute-start(bf16[64,256]{1,0:T(8,128)(2,1)S(1)} %add_convert_fusion.1), channel_id=1, source_target_pairs={{0,128},{4,132},{8,136},{12,140},{16,144},{20,148},{24,152},{28,15... | collective-permute-start | bytes 98312 | tf_op jit(solution)/shard_map/ppermute | solution.py:20
  183.1 9.1 %collective-permute-start.21 = (bf16[64,256]{1,0:T(8,128)(2,1)S(1)}, bf16[64,256]{1,0:T(8,128)(2,1)S(1)}, u32[]{:S(2)}, u32[]{:S(2)}) collective-permute-start(bf16[64,256]{1,0:T(8,128)(2,1)S(1)} %add_convert_fusion), channel_id=1, source_target_pairs={{0,256},{4,260},{8,264},{12,268},{16,272},{20,276},{24,280},{28,28... | collective-permute-start | bytes 98312 | tf_op jit(solution)/shard_map/ppermute | solution.py:20
  190.5 10.1 %copy-start.4 = (bf16[1024,512]{1,0:T(8,128)(2,1)S(1)}, bf16[1024,512]{1,0:T(8,128)(2,1)}, u32[]{:S(2)}) copy-start(bf16[1024,512]{1,0:T(8,128)(2,1)} %copy-done.3) | copy-start | bytes 3145732
  192.2 22.1 %copy-start.2 = (bf16[1024,1280]{1,0:T(8,128)(2,1)S(1)}, bf16[1024,1280]{1,0:T(8,128)(2,1)}, u32[]{:S(2)}) copy-start(bf16[1024,1280]{1,0:T(8,128)(2,1)} %copy-done.1) | copy-start | bytes 7864324
  192.2 5.6 %collective-permute-start.22 = (f32[64,256]{1,0:T(8,128)S(1)}, f32[64,256]{1,0:T(8,128)S(1)}, u32[]{:S(2)}, u32[]{:S(2)}) collective-permute-start(f32[64,256]{1,0:T(8,128)S(1)} %convert_add_fusion.2), channel_id=1, source_target_pairs={{0,64},{4,68},{8,72},{12,76},{16,80},{20,84},{24,88},{28,92},{32,9... | collective-permute-start | bytes 196616 | tf_op jit(solution)/shard_map/ppermute | solution.py:20
  197.8 5.7 %collective-permute-start.23 = (f32[128,256]{1,0:T(8,128)S(1)}, f32[128,256]{1,0:T(8,128)S(1)}, u32[]{:S(2)}, u32[]{:S(2)}) collective-permute-start(f32[128,256]{1,0:T(8,128)S(1)} %maximum_select_fusion.2), channel_id=1, source_target_pairs={{0,16},{4,20},{8,24},{12,28},{16,0},{20,4},{24,8},{28,12},{32,48},... | collective-permute-start | bytes 393224 | tf_op jit(solution)/shard_map/ppermute | solution.py:20
  203.5 12.3 %collective-permute-start.24 = (f32[256,256]{1,0:T(8,128)S(1)}, f32[256,256]{1,0:T(8,128)S(1)}, u32[]{:S(2)}, u32[]{:S(2)}) collective-permute-start(f32[256,256]{1,0:T(8,128)S(1)} %maximum_select_fusion.1), channel_id=1, source_target_pairs={{0,4},{4,0},{8,12},{12,8},{16,20},{20,16},{24,28},{28,24},{32,36},... | collective-permute-start | bytes 786440 | tf_op jit(solution)/shard_map/ppermute | solution.py:20

commit v17 on v16

--- a/solution.py
+++ b/solution.py
@@ -155,6 +155,31 @@
     return jnp.concatenate(placed, axis=0)
 
 
+def ring_gather_both(block, core):
+    stream_count = lax.axis_size("stream")
+    stream_index = lax.axis_index("stream")
+    split = block.shape[1] // 2
+    two_away = jnp.concatenate(
+        [ring_pull(block[:, :split], 2), ring_pull(block[:, split:], -2)], axis=1
+    )
+    arrived = [block, ring_pull(block, 1), two_away, ring_pull(block, -1)]
+    partner = [xor_swap(piece, "tm", 0) for piece in arrived]
+    halves = []
+    for first in (True, False):
+        pieces = [
+            jnp.where((core == 0) == first, own, theirs) for own, theirs in zip(arrived, partner)
+        ]
+        placed = []
+        for position in range(stream_count):
+            offset = (position - stream_index) % stream_count
+            chosen = pieces[3]
+            for slot in (2, 1, 0):
+                chosen = jnp.where(offset == slot, pieces[slot], chosen)
+            placed.append(chosen)
+        halves.append(jnp.concatenate(placed, axis=0))
+    return jnp.concatenate(halves, axis=1)
+
+
 def contract_last(left, right):
     return lax.dot_general(
         left, right, (((1,), (1,)), ((), ())), preferred_element_type=jnp.float32
@@ -184,11 +209,15 @@
     if lax.axis_size("tm") % 2 == 0 and weights_local.shape[1] % 256 == 0:
         half_width = weights_local.shape[1] // 2
         core = lax.axis_index("tm") % 2
-        mine = ring_gather(lax.dynamic_slice_in_dim(weights_local, core * half_width, half_width, 1))
-        other = xor_swap(mine, "tm", 0)
-        weights_full = jnp.concatenate(
-            [jnp.where(core == 0, mine, other), jnp.where(core == 0, other, mine)], axis=1
-        )
+        mine = lax.dynamic_slice_in_dim(weights_local, core * half_width, half_width, 1)
+        if lax.axis_size("stream") == 4 and half_width % 256 == 0:
+            weights_full = ring_gather_both(mine, core)
+        else:
+            mine = ring_gather(mine)
+            other = xor_swap(mine, "tm", 0)
+            weights_full = jnp.concatenate(
+                [jnp.where(core == 0, mine, other), jnp.where(core == 0, other, mine)], axis=1
+            )
     else:
         weights_full = lax.all_gather(weights_local, "stream", axis=0, tiled=True)
     query_full = weights_full[:, :query_width]

time: 218 us -> 215 us (0.986)
  other arithmetic: 16.2 us -> 11.1 us
    ppermute x4, waiting for transfers between devices: 21.1 us -> 14.4 us  [ring_pull(): return lax.ppermute(value, ('tm', 'stream'), pairs)]
    ppermute x13 -> x16, starting transfers between devices: 68.8 us -> 73.1 us  [xor_swap(): lax.ppermute(value, axis, [(source, source ^ 1 << bit) for source in rang...]
    select_n x2, other arithmetic: 3.95 us -> 1.09 us  [ring_gather_both(): chosen = jnp.where(offset == slot, pieces[slot], chosen)]
    ppermute x8, waiting for transfers between devices: 11.6 us -> 14.4 us  [shifted(): lax.ppermute(value, axis, [(source, source + steps) for source in range(l...]
    ppermute x8, starting transfers between devices: 25.8 us -> 23.6 us  [shifted(): lax.ppermute(value, axis, [(source, source + steps) for source in range(l...]
    ppermute x13 -> x16, waiting for transfers between devices: 31.4 us -> 33.5 us  [xor_swap(): lax.ppermute(value, axis, [(source, source ^ 1 << bit) for source in rang...]
  transfers between devices with their start and end apart: 25 -> 28, of which waited for: 18 -> 19; matrix products, arithmetic and copies ran while one was open for 3% -> 4% of each run, Pallas kernels for 0% -> 0%
where the time goes in v17:
time: 215 us; the launch traced here: 214 us
  starting transfers between devices  116 us (54%)
  waiting for transfers between devices  62.3 us (29%)
  matrix products  15.7 us (7%)
  other arithmetic  11.1 us (5%)
  local copies, waits for them, and re-layouts  6.05 us (3%)
  between operations  2.25 us (1%)
    ppermute x16, starting transfers between devices, xor_swap(): lax.ppermute(value, axis, [(source, source ^ 1 << bit) for source in rang...  73.1 us
    ppermute x16, waiting for transfers between devices, xor_swap(): lax.ppermute(value, axis, [(source, source ^ 1 << bit) for source in rang...  33.5 us
    ppermute x8, starting transfers between devices, shifted(): lax.ppermute(value, axis, [(source, source + steps) for source in range(l...  23.6 us
    ppermute x4, starting transfers between devices, ring_pull(): return lax.ppermute(value, ('tm', 'stream'), pairs)  19.6 us
    ppermute x8, waiting for transfers between devices, shifted(): lax.ppermute(value, axis, [(source, source + steps) for source in range(l...  14.4 us
    ppermute x4, waiting for transfers between devices, ring_pull(): return lax.ppermute(value, ('tm', 'stream'), pairs)  14.4 us
    sub x1, matrix products, per_device(): terms = jnp.where(allowed, jnp.exp(masked - row_max), 0.0)  4.38 us
  transfers between devices with their start and end apart: 28, of which 19 were waited for; matrix products, arithmetic and copies ran while one was open for 4% of the time, Pallas kernels for 0%

profile of v17, /device:TPU:1, one launch (start us, length us, event | category | flops | bytes accessed | tf_op | source)
XLA Modules:
  0.0 213.7 jit_solution(16784947568328563261)
XLA Ops:
  0.7 1.5 fusion.19
  2.2 11.5 %collective-permute-start.1 = (bf16[256,1280]{1,0:T(8,128)(2,1)S(1)}, bf16[256,1280]{1,0:T(8,128)(2,1)S(1)}, u32[]{:S(2)}, u32[]{:S(2)}) collective-permute-start(bf16[256,1280]{1,0:T(8,128)(2,1)S(1)} %fusion.19), channel_id=1, source_target_pairs={{1,0},{2,1},{3,2},{8,3},{5,4},{6,5},{7,6},{12,7},{9,8},{10,9},{11,... | collective-permute-start | bytes 1966088 | tf_op jit(solution)/shard_map/ppermute | solution.py:134
  13.7 1.9 collective-permute-start.6
  16.4 3.3 %collective-permute-start.3 = (bf16[256,640]{1,0:T(8,128)(2,1)}, bf16[256,640]{1,0:T(8,128)(2,1)}, u32[]{:S(2)}, u32[]{:S(2)}) collective-permute-start(bf16[256,640]{1,0:T(8,128)(2,1)} %get-tuple-element.30), channel_id=1, source_target_pairs={{2,0},{3,1},{8,2},{9,3},{6,4},{7,5},{12,6},{13,7},{10,8},{11,9},{0... | collective-permute-start | bytes 983048 | tf_op jit(solution)/shard_map/ppermute | solution.py:134
  19.8 2.8 %collective-permute-start.4 = (bf16[256,640]{1,0:T(8,128)(2,1)S(1)}, bf16[256,640]{1,0:T(8,128)(2,1)}, u32[]{:S(2)}, u32[]{:S(2)}) collective-permute-start(bf16[256,640]{1,0:T(8,128)(2,1)S(1)} %get-tuple-element.29), channel_id=1, source_target_pairs={{10,0},{11,1},{0,2},{1,3},{14,4},{15,5},{4,6},{5,7},{2,8},{3,9},{8... | collective-permute-start | bytes 983048 | tf_op jit(solution)/shard_map/ppermute | solution.py:134
  22.6 3.4 %collective-permute-start = (bf16[256,1280]{1,0:T(8,128)(2,1)S(1)}, bf16[256,1280]{1,0:T(8,128)(2,1)S(1)}, u32[]{:S(2)}, u32[]{:S(2)}) collective-permute-start(bf16[256,1280]{1,0:T(8,128)(2,1)S(1)} %fusion.19), channel_id=1, source_target_pairs={{0,4},{4,0},{8,12},{12,8},{16,20},{20,16},{24,28},{28,24},{32,36},... | collective-permute-start | bytes 1966088 | tf_op jit(solution)/shard_map/ppermute | solution.py:20
  26.7 0.9 copy.28
  27.6 13.7 %collective-permute-done.3 = bf16[256,640]{1,0:T(8,128)(2,1)} collective-permute-done((bf16[256,640]{1,0:T(8,128)(2,1)}, bf16[256,640]{1,0:T(8,128)(2,1)}, u32[]{:S(2)}, u32[]{:S(2)}) %collective-permute-start.3) | collective-permute-done | bytes 327712 | tf_op jit(solution)/shard_map/ppermute | solution.py:134
  41.3 1.0 constant_dynamic-update-slice_fusion.1
  43.0 1.0 constant_dynamic-update-slice_fusion
  44.0 3.7 %collective-permute-start.5 = (bf16[256,1280]{1,0:T(8,128)(2,1)S(1)}, bf16[256,1280]{1,0:T(8,128)(2,1)S(1)}, u32[]{:S(2)}, u32[]{:S(2)}) collective-permute-start(bf16[256,1280]{1,0:T(8,128)(2,1)S(1)} %constant_dynamic-update-slice_fusion), channel_id=1, source_target_pairs={{0,4},{4,0},{8,12},{12,8},{16,20},{20,16},{24,28},{28,24},{32,36},... | collective-permute-start | bytes 1966088 | tf_op jit(solution)/shard_map/ppermute | solution.py:20
  47.7 1.9 collective-permute-start.2
  49.7 2.4 %collective-permute-start.7 = (bf16[256,1280]{1,0:T(8,128)(2,1)S(1)}, bf16[256,1280]{1,0:T(8,128)(2,1)S(1)}, u32[]{:S(2)}, u32[]{:S(2)}) collective-permute-start(bf16[256,1280]{1,0:T(8,128)(2,1)S(1)} %collective-permute-done.6), channel_id=1, source_target_pairs={{0,4},{4,0},{8,12},{12,8},{16,20},{20,16},{24,28},{28,24},{32,36},... | collective-permute-start | bytes 1966088 | tf_op jit(solution)/shard_map/ppermute | solution.py:20
  52.5 1.3 collective-permute-done.7
  55.4 3.1 %collective-permute-start.8 = (bf16[128,512]{1,0:T(8,128)(2,1)S(1)}, bf16[128,512]{1,0:T(8,128)(2,1)S(1)}, u32[]{:S(2)}, u32[]{:S(2)}) collective-permute-start(bf16[128,512]{1,0:T(8,128)(2,1)S(1)} %fusion.16), channel_id=1, source_target_pairs={{0,16},{4,20},{8,24},{12,28},{16,32},{20,36},{24,40},{28,44},{32,4... | collective-permute-start | bytes 393224 | tf_op jit(solution)/shard_map/ppermute | solution.py:15
  58.5 3.7 %collective-permute-start.9 = (bf16[128,512]{1,0:T(8,128)(2,1)S(1)}, bf16[128,512]{1,0:T(8,128)(2,1)S(1)}, u32[]{:S(2)}, u32[]{:S(2)}) collective-permute-start(bf16[128,512]{1,0:T(8,128)(2,1)S(1)} %fusion.16), channel_id=1, source_target_pairs={{0,12},{4,16},{8,20},{12,24},{16,28},{20,32},{24,36},{28,40},{32,4... | collective-permute-start | bytes 393224 | tf_op jit(solution)/shard_map/ppermute | solution.py:15
  62.2 4.0 %collective-permute-start.10 = (bf16[128,512]{1,0:T(8,128)(2,1)S(1)}, bf16[128,512]{1,0:T(8,128)(2,1)S(1)}, u32[]{:S(2)}, u32[]{:S(2)}) collective-permute-start(bf16[128,512]{1,0:T(8,128)(2,1)S(1)} %fusion.16), channel_id=1, source_target_pairs={{0,8},{4,12},{8,16},{12,20},{16,24},{20,28},{24,32},{28,36},{32,40... | collective-permute-start | bytes 393224 | tf_op jit(solution)/shard_map/ppermute | solution.py:15
  66.2 7.0 %collective-permute-start.11 = (bf16[128,512]{1,0:T(8,128)(2,1)S(1)}, bf16[128,512]{1,0:T(8,128)(2,1)S(1)}, u32[]{:S(2)}, u32[]{:S(2)}) collective-permute-start(bf16[128,512]{1,0:T(8,128)(2,1)S(1)} %fusion.16), channel_id=1, source_target_pairs={{0,4},{4,8},{8,12},{12,16},{16,20},{20,24},{24,28},{28,32},{32,36}... | collective-permute-start | bytes 393224 | tf_op jit(solution)/shard_map/ppermute | solution.py:15
  74.8 1.3 collective-permute-done.11
  76.4 4.4 %fusion.51 = (f32[4,4,128]{2,1,0:T(4,128)S(1)}, f32[4,4,128,640]{2,3,1,0:T(8,128)}) fusion(pred[128,640]{0,1:T(8,128)(4,1)S(1)} %fusion.25, bf16[640,4,64,1]{0,2,3,1:T(8,128)(2,1)S(1)} %bitcast.94, bf16[128,4,4,64]{0,3,2,1:T(8,128)(2,1)S(1)} %bitcast.105), kind=kOutput, calls=%fused_computation.126 | convolution fusion | flops 174326400 | bytes 5922816 | tf_op jit(solution)/shard_map/sub | solution.py:256
  81.0 3.1 %multiply_convert_fusion = bf16[4,4,128,640]{2,3,1,0:T(8,128)(2,1)S(1)} fusion(f32[4,4,128,640]{2,3,1,0:T(8,128)} %get-tuple-element.34, f32[4,4,128]{2,1,0:T(4,128)S(1)} %select_divide_fusion), kind=kLoop, calls=%fused_computation.6 | loop fusion | flops 2621440 | bytes 7872512 | tf_op jit(solution)/shard_map/convert_element_type | solution.py:259
  84.1 0.9 fusion.53
  85.7 1.2 fusion.3
  86.9 0.9 fusion.52
  88.0 1.9 collective-permute-start.12
  89.9 1.3 collective-permute-start.13
  91.2 1.3 collective-permute-start.14
  92.5 1.3 collective-permute-start.15
  93.8 5.1 %collective-permute-done.12 = bf16[128,512]{0,1:T(8,128)(2,1)S(1)} collective-permute-done((bf16[128,512]{0,1:T(8,128)(2,1)S(1)}, bf16[128,512]{0,1:T(8,128)(2,1)S(1)}, u32[]{:S(2)}, u32[]{:S(2)}) %collective-permute-start.12) | collective-permute-done | bytes 131104 | tf_op jit(solution)/shard_map/ppermute | solution.py:15
  98.9 3.2 %collective-permute-done.13 = bf16[128,512]{0,1:T(8,128)(2,1)S(1)} collective-permute-done((bf16[128,512]{0,1:T(8,128)(2,1)S(1)}, bf16[128,512]{0,1:T(8,128)(2,1)S(1)}, u32[]{:S(2)}, u32[]{:S(2)}) %collective-permute-start.13) | collective-permute-done | bytes 131104 | tf_op jit(solution)/shard_map/ppermute | solution.py:15
  102.1 2.4 %collective-permute-done.14 = bf16[128,512]{0,1:T(8,128)(2,1)S(1)} collective-permute-done((bf16[128,512]{0,1:T(8,128)(2,1)S(1)}, bf16[128,512]{0,1:T(8,128)(2,1)S(1)}, u32[]{:S(2)}, u32[]{:S(2)}) %collective-permute-start.14) | collective-permute-done | bytes 131104 | tf_op jit(solution)/shard_map/ppermute | solution.py:15
  104.5 2.5 %collective-permute-done.15 = bf16[128,512]{0,1:T(8,128)(2,1)S(1)} collective-permute-done((bf16[128,512]{0,1:T(8,128)(2,1)S(1)}, bf16[128,512]{0,1:T(8,128)(2,1)S(1)}, u32[]{:S(2)}, u32[]{:S(2)}) %collective-permute-start.15) | collective-permute-done | bytes 131104 | tf_op jit(solution)/shard_map/ppermute | solution.py:15
  107.0 1.1 convolution_convert_fusion
  108.1 2.7 %collective-permute-start.16 = (bf16[1024,256]{1,0:T(8,128)(2,1)}, bf16[1024,256]{1,0:T(8,128)(2,1)}, u32[]{:S(2)}, u32[]{:S(2)}) collective-permute-start(bf16[1024,256]{1,0:T(8,128)(2,1)} %convolution_convert_fusion), channel_id=1, source_target_pairs={{0,4},{4,0},{8,12},{12,8},{16,20},{20,16},{24,28},{28,24},{32,36},... | collective-permute-start | bytes 1572872 | tf_op jit(solution)/shard_map/ppermute | solution.py:20
  110.8 1.8 collective-permute-done.16
  112.7 1.3 convolution_add_fusion
  114.0 1.0 copy-done.3
  115.1 9.4 %collective-permute-start.17 = (bf16[512,256]{1,0:T(8,128)(2,1)S(1)}, bf16[512,256]{1,0:T(8,128)(2,1)}, u32[]{:S(2)}, u32[]{:S(2)}) collective-permute-start(bf16[512,256]{1,0:T(8,128)(2,1)S(1)} %slice.147), channel_id=1, source_target_pairs={{0,1},{1,0},{2,3},{3,2},{4,5},{5,4},{6,7},{7,6},{8,9},{9,8},{10,11... | collective-permute-start | bytes 786440 | tf_op jit(solution)/shard_map/ppermute | solution.py:20
  124.5 6.5 %collective-permute-done.17 = bf16[512,256]{1,0:T(8,128)(2,1)} collective-permute-done((bf16[512,256]{1,0:T(8,128)(2,1)S(1)}, bf16[512,256]{1,0:T(8,128)(2,1)}, u32[]{:S(2)}, u32[]{:S(2)}) %collective-permute-start.17) | collective-permute-done | bytes 262176 | tf_op jit(solution)/shard_map/ppermute | solution.py:20
  130.9 1.2 slice_add_fusion
  132.8 1.9 collective-permute-start.18
  134.7 8.5 %collective-permute-done.18 = bf16[256,256]{1,0:T(8,128)(2,1)} collective-permute-done((bf16[256,256]{1,0:T(8,128)(2,1)}, bf16[256,256]{1,0:T(8,128)(2,1)}, u32[]{:S(2)}, u32[]{:S(2)}) %collective-permute-start.18) | collective-permute-done | bytes 131104 | tf_op jit(solution)/shard_map/ppermute | solution.py:20
  143.2 0.9 convert_add_fusion
  144.9 1.9 collective-permute-start.19
  146.8 3.1 %collective-permute-done.19 = bf16[128,256]{1,0:T(8,128)(2,1)S(1)} collective-permute-done((bf16[128,256]{1,0:T(8,128)(2,1)S(1)}, bf16[128,256]{1,0:T(8,128)(2,1)S(1)}, u32[]{:S(2)}, u32[]{:S(2)}) %collective-permute-start.19) | collective-permute-done | bytes 65568 | tf_op jit(solution)/shard_map/ppermute | solution.py:20
  149.9 1.0 convert_add_fusion.1
  150.9 4.3 %collective-permute-start.20 = (bf16[64,256]{1,0:T(8,128)(2,1)S(1)}, bf16[64,256]{1,0:T(8,128)(2,1)S(1)}, u32[]{:S(2)}, u32[]{:S(2)}) collective-permute-start(bf16[64,256]{1,0:T(8,128)(2,1)S(1)} %select_convert_fusion.2), channel_id=1, source_target_pairs={{0,64},{4,68},{8,72},{12,76},{16,80},{20,84},{24,88},{28,92},{32,9... | collective-permute-start | bytes 98312 | tf_op jit(solution)/shard_map/ppermute | solution.py:20
  155.2 1.3 collective-permute-done.20
  156.5 6.0 %collective-permute-start.21 = (bf16[64,256]{1,0:T(8,128)(2,1)S(1)}, bf16[64,256]{1,0:T(8,128)(2,1)S(1)}, u32[]{:S(2)}, u32[]{:S(2)}) collective-permute-start(bf16[64,256]{1,0:T(8,128)(2,1)S(1)} %add_convert_fusion.3), channel_id=1, source_target_pairs={{0,8},{4,12},{8,0},{12,4},{16,24},{20,28},{24,16},{28,20},{32,40},... | collective-permute-start | bytes 98312 | tf_op jit(solution)/shard_map/ppermute | solution.py:20
  162.6 2.5 %collective-permute-done.21 = bf16[64,256]{1,0:T(8,128)(2,1)S(1)} collective-permute-done((bf16[64,256]{1,0:T(8,128)(2,1)S(1)}, bf16[64,256]{1,0:T(8,128)(2,1)S(1)}, u32[]{:S(2)}, u32[]{:S(2)}) %collective-permute-start.21) | collective-permute-done | bytes 32800 | tf_op jit(solution)/shard_map/ppermute | solution.py:20
  165.1 4.3 %collective-permute-start.22 = (bf16[64,256]{1,0:T(8,128)(2,1)S(1)}, bf16[64,256]{1,0:T(8,128)(2,1)S(1)}, u32[]{:S(2)}, u32[]{:S(2)}) collective-permute-start(bf16[64,256]{1,0:T(8,128)(2,1)S(1)} %add_convert_fusion.2), channel_id=1, source_target_pairs={{0,32},{4,36},{8,40},{12,44},{16,48},{20,52},{24,56},{28,60},{32,0... | collective-permute-start | bytes 98312 | tf_op jit(solution)/shard_map/ppermute | solution.py:20
  169.4 1.8 collective-permute-done.22
  171.3 5.9 %collective-permute-start.23 = (bf16[64,256]{1,0:T(8,128)(2,1)S(1)}, bf16[64,256]{1,0:T(8,128)(2,1)S(1)}, u32[]{:S(2)}, u32[]{:S(2)}) collective-permute-start(bf16[64,256]{1,0:T(8,128)(2,1)S(1)} %add_convert_fusion.1), channel_id=1, source_target_pairs={{0,128},{4,132},{8,136},{12,140},{16,144},{20,148},{24,152},{28,15... | collective-permute-start | bytes 98312 | tf_op jit(solution)/shard_map/ppermute | solution.py:20
  177.1 1.3 collective-permute-done.23
  178.4 8.3 %collective-permute-start.24 = (bf16[64,256]{1,0:T(8,128)(2,1)S(1)}, bf16[64,256]{1,0:T(8,128)(2,1)S(1)}, u32[]{:S(2)}, u32[]{:S(2)}) collective-permute-start(bf16[64,256]{1,0:T(8,128)(2,1)S(1)} %add_convert_fusion), channel_id=1, source_target_pairs={{0,256},{4,260},{8,264},{12,268},{16,272},{20,276},{24,280},{28,28... | collective-permute-start | bytes 98312 | tf_op jit(solution)/shard_map/ppermute | solution.py:20
  186.8 1.3 collective-permute-done.24
  188.1 2.4 %collective-permute-start.25 = (f32[64,256]{1,0:T(8,128)S(1)}, f32[64,256]{1,0:T(8,128)S(1)}, u32[]{:S(2)}, u32[]{:S(2)}) collective-permute-start(f32[64,256]{1,0:T(8,128)S(1)} %convert_add_fusion.2), channel_id=1, source_target_pairs={{0,64},{4,68},{8,72},{12,76},{16,80},{20,84},{24,88},{28,92},{32,9... | collective-permute-start | bytes 196616 | tf_op jit(solution)/shard_map/ppermute | solution.py:20
  190.6 1.6 convolution_convert_fusion.2
  192.1 1.1 collective-permute-done.25
  193.3 2.2 %collective-permute-start.26 = (f32[128,256]{1,0:T(8,128)S(1)}, f32[128,256]{1,0:T(8,128)S(1)}, u32[]{:S(2)}, u32[]{:S(2)}) collective-permute-start(f32[128,256]{1,0:T(8,128)S(1)} %maximum_select_fusion.2), channel_id=1, source_target_pairs={{0,16},{4,20},{8,24},{12,28},{16,0},{20,4},{24,8},{28,12},{32,48},... | collective-permute-start | bytes 393224 | tf_op jit(solution)/shard_map/ppermute | solution.py:20
  196.0 3.0 %collective-permute-done.26 = f32[128,256]{1,0:T(8,128)S(1)} collective-permute-done((f32[128,256]{1,0:T(8,128)S(1)}, f32[128,256]{1,0:T(8,128)S(1)}, u32[]{:S(2)}, u32[]{:S(2)}) %collective-permute-start.26) | collective-permute-done | bytes 131104 | tf_op jit(solution)/shard_map/ppermute | solution.py:20
  199.0 12.2 %collective-permute-start.27 = (f32[256,256]{1,0:T(8,128)S(1)}, f32[256,256]{1,0:T(8,128)S(1)}, u32[]{:S(2)}, u32[]{:S(2)}) collective-permute-start(f32[256,256]{1,0:T(8,128)S(1)} %maximum_select_fusion.1), channel_id=1, source_target_pairs={{0,4},{4,0},{8,12},{12,8},{16,20},{20,16},{24,28},{28,24},{32,36},... | collective-permute-start | bytes 786440 | tf_op jit(solution)/shard_map/ppermute | solution.py:20
  211.3 1.5 fusion.15
  212.8 0.8 maximum_select_fusion
  (83 shorter events, 8.2 us)
Async XLA Ops:
  0.6 73.4 %copy-start = (bf16[1,128,1024]{2,1,0:T(8,128)(2,1)S(1)}, bf16[1,128,1024]{2,1,0:T(8,128)(2,1)}, u32[]{:S(2)}) copy-start(bf16[1,128,1024]{2,1,0:T(8,128)(2,1)} %param.7) | copy-start | bytes 786436
  0.6 26.1 %copy-start.15 = (bf16[1,128,1024]{2,1,0:T(8,128)(2,1)S(1)}, bf16[1,128,1024]{2,1,0:T(8,128)(2,1)}, u32[]{:S(2)}) copy-start(bf16[1,128,1024]{2,1,0:T(8,128)(2,1)} %param.6) | copy-start | bytes 786436
  2.2 45.5 %collective-permute-start.1 = (bf16[256,1280]{1,0:T(8,128)(2,1)S(1)}, bf16[256,1280]{1,0:T(8,128)(2,1)S(1)}, u32[]{:S(2)}, u32[]{:S(2)}) collective-permute-start(bf16[256,1280]{1,0:T(8,128)(2,1)S(1)} %fusion.19), channel_id=1, source_target_pairs={{1,0},{2,1},{3,2},{8,3},{5,4},{6,5},{7,6},{12,7},{9,8},{10,9},{11,... | collective-permute-start | bytes 1966088 | tf_op jit(solution)/shard_map/ppermute | solution.py:134
  13.7 35.9 %collective-permute-start.6 = (bf16[256,1280]{1,0:T(8,128)(2,1)S(1)}, bf16[256,1280]{1,0:T(8,128)(2,1)S(1)}, u32[]{:S(2)}, u32[]{:S(2)}) collective-permute-start(bf16[256,1280]{1,0:T(8,128)(2,1)S(1)} %fusion.19), channel_id=1, source_target_pairs={{11,0},{0,1},{1,2},{2,3},{15,4},{4,5},{5,6},{6,7},{3,8},{8,9},{9,1... | collective-permute-start | bytes 1966088 | tf_op jit(solution)/shard_map/ppermute | solution.py:134
  16.4 24.9 %collective-permute-start.3 = (bf16[256,640]{1,0:T(8,128)(2,1)}, bf16[256,640]{1,0:T(8,128)(2,1)}, u32[]{:S(2)}, u32[]{:S(2)}) collective-permute-start(bf16[256,640]{1,0:T(8,128)(2,1)} %get-tuple-element.30), channel_id=1, source_target_pairs={{2,0},{3,1},{8,2},{9,3},{6,4},{7,5},{12,6},{13,7},{10,8},{11,9},{0... | collective-permute-start | bytes 983048 | tf_op jit(solution)/shard_map/ppermute | solution.py:134
  19.8 23.2 %collective-permute-start.4 = (bf16[256,640]{1,0:T(8,128)(2,1)S(1)}, bf16[256,640]{1,0:T(8,128)(2,1)}, u32[]{:S(2)}, u32[]{:S(2)}) collective-permute-start(bf16[256,640]{1,0:T(8,128)(2,1)S(1)} %get-tuple-element.29), channel_id=1, source_target_pairs={{10,0},{11,1},{0,2},{1,3},{14,4},{15,5},{4,6},{5,7},{2,8},{3,9},{8... | collective-permute-start | bytes 983048 | tf_op jit(solution)/shard_map/ppermute | solution.py:134
  22.6 29.9 %collective-permute-start = (bf16[256,1280]{1,0:T(8,128)(2,1)S(1)}, bf16[256,1280]{1,0:T(8,128)(2,1)S(1)}, u32[]{:S(2)}, u32[]{:S(2)}) collective-permute-start(bf16[256,1280]{1,0:T(8,128)(2,1)S(1)} %fusion.19), channel_id=1, source_target_pairs={{0,4},{4,0},{8,12},{12,8},{16,20},{20,16},{24,28},{28,24},{32,36},... | collective-permute-start | bytes 1966088 | tf_op jit(solution)/shard_map/ppermute | solution.py:20
  44.0 8.5 %collective-permute-start.5 = (bf16[256,1280]{1,0:T(8,128)(2,1)S(1)}, bf16[256,1280]{1,0:T(8,128)(2,1)S(1)}, u32[]{:S(2)}, u32[]{:S(2)}) collective-permute-start(bf16[256,1280]{1,0:T(8,128)(2,1)S(1)} %constant_dynamic-update-slice_fusion), channel_id=1, source_target_pairs={{0,4},{4,0},{8,12},{12,8},{16,20},{20,16},{24,28},{28,24},{32,36},... | collective-permute-start | bytes 1966088 | tf_op jit(solution)/shard_map/ppermute | solution.py:20
  47.7 4.8 %collective-permute-start.2 = (bf16[256,1280]{1,0:T(8,128)(2,1)S(1)}, bf16[256,1280]{1,0:T(8,128)(2,1)S(1)}, u32[]{:S(2)}, u32[]{:S(2)}) collective-permute-start(bf16[256,1280]{1,0:T(8,128)(2,1)S(1)} %collective-permute-done.1), channel_id=1, source_target_pairs={{0,4},{4,0},{8,12},{12,8},{16,20},{20,16},{24,28},{28,24},{32,36},... | collective-permute-start | bytes 1966088 | tf_op jit(solution)/shard_map/ppermute | solution.py:20
  49.7 4.1 %collective-permute-start.7 = (bf16[256,1280]{1,0:T(8,128)(2,1)S(1)}, bf16[256,1280]{1,0:T(8,128)(2,1)S(1)}, u32[]{:S(2)}, u32[]{:S(2)}) collective-permute-start(bf16[256,1280]{1,0:T(8,128)(2,1)S(1)} %collective-permute-done.6), channel_id=1, source_target_pairs={{0,4},{4,0},{8,12},{12,8},{16,20},{20,16},{24,28},{28,24},{32,36},... | collective-permute-start | bytes 1966088 | tf_op jit(solution)/shard_map/ppermute | solution.py:20
  54.5 18.7 %copy-start.4 = (bf16[256,1280]{1,0:T(8,128)(2,1)}, bf16[256,1280]{1,0:T(8,128)(2,1)S(1)}, u32[]{:S(2)}) copy-start(bf16[256,1280]{1,0:T(8,128)(2,1)S(1)} %get-tuple-element.12) | copy-start | bytes 1966084
  54.9 18.3 %copy-start.6 = (bf16[256,1280]{1,0:T(8,128)(2,1)}, bf16[256,1280]{1,0:T(8,128)(2,1)S(1)}, u32[]{:S(2)}) copy-start(bf16[256,1280]{1,0:T(8,128)(2,1)S(1)} %get-tuple-element.35) | copy-start | bytes 1966084
  54.9 18.3 %copy-start.8 = (bf16[256,1280]{1,0:T(8,128)(2,1)}, bf16[256,1280]{1,0:T(8,128)(2,1)S(1)}, u32[]{:S(2)}) copy-start(bf16[256,1280]{1,0:T(8,128)(2,1)S(1)} %get-tuple-element.36) | copy-start | bytes 1966084
  54.9 18.3 %copy-start.10 = (bf16[256,1280]{1,0:T(8,128)(2,1)}, bf16[256,1280]{1,0:T(8,128)(2,1)S(1)}, u32[]{:S(2)}) copy-start(bf16[256,1280]{1,0:T(8,128)(2,1)S(1)} %get-tuple-element.37) | copy-start | bytes 1966084
  55.0 19.0 %copy-start.1 = (bf16[1024,512]{1,0:T(8,128)(2,1)}, bf16[1024,512]{1,0:T(8,128)(2,1)S(1)}, u32[]{:S(2)}) copy-start(bf16[1024,512]{1,0:T(8,128)(2,1)S(1)} %fusion.17) | copy-start | bytes 3145732
  55.4 19.4 %collective-permute-start.8 = (bf16[128,512]{1,0:T(8,128)(2,1)S(1)}, bf16[128,512]{1,0:T(8,128)(2,1)S(1)}, u32[]{:S(2)}, u32[]{:S(2)}) collective-permute-start(bf16[128,512]{1,0:T(8,128)(2,1)S(1)} %fusion.16), channel_id=1, source_target_pairs={{0,16},{4,20},{8,24},{12,28},{16,32},{20,36},{24,40},{28,44},{32,4... | collective-permute-start | bytes 393224 | tf_op jit(solution)/shard_map/ppermute | solution.py:15
  58.5 16.3 %collective-permute-start.9 = (bf16[128,512]{1,0:T(8,128)(2,1)S(1)}, bf16[128,512]{1,0:T(8,128)(2,1)S(1)}, u32[]{:S(2)}, u32[]{:S(2)}) collective-permute-start(bf16[128,512]{1,0:T(8,128)(2,1)S(1)} %fusion.16), channel_id=1, source_target_pairs={{0,12},{4,16},{8,20},{12,24},{16,28},{20,32},{24,36},{28,40},{32,4... | collective-permute-start | bytes 393224 | tf_op jit(solution)/shard_map/ppermute | solution.py:15
  62.2 12.6 %collective-permute-start.10 = (bf16[128,512]{1,0:T(8,128)(2,1)S(1)}, bf16[128,512]{1,0:T(8,128)(2,1)S(1)}, u32[]{:S(2)}, u32[]{:S(2)}) collective-permute-start(bf16[128,512]{1,0:T(8,128)(2,1)S(1)} %fusion.16), channel_id=1, source_target_pairs={{0,8},{4,12},{8,16},{12,20},{16,24},{20,28},{24,32},{28,36},{32,40... | collective-permute-start | bytes 393224 | tf_op jit(solution)/shard_map/ppermute | solution.py:15
  66.2 10.0 %collective-permute-start.11 = (bf16[128,512]{1,0:T(8,128)(2,1)S(1)}, bf16[128,512]{1,0:T(8,128)(2,1)S(1)}, u32[]{:S(2)}, u32[]{:S(2)}) collective-permute-start(bf16[128,512]{1,0:T(8,128)(2,1)S(1)} %fusion.16), channel_id=1, source_target_pairs={{0,4},{4,8},{8,12},{12,16},{16,20},{20,24},{24,28},{28,32},{32,36}... | collective-permute-start | bytes 393224 | tf_op jit(solution)/shard_map/ppermute | solution.py:15
  74.0 2.4 %copy-start.16 = (bf16[1024,128]{1,0:T(8,128)(2,1)}, bf16[1024,128]{1,0:T(8,128)(2,1)S(1)}, u32[]{:S(2)}) copy-start(bf16[1024,128]{1,0:T(8,128)(2,1)S(1)} %convolution_convert_fusion.1) | copy-start | bytes 786436
  76.4 4.4 %copy-start.13 = (bf16[640,256]{0,1:T(8,128)(2,1)}, bf16[640,256]{0,1:T(8,128)(2,1)S(1)}, u32[]{:S(2)}) copy-start(bf16[640,256]{0,1:T(8,128)(2,1)S(1)} %copy.22) | copy-start | bytes 983044
  85.7 1.2 copy-start.17
  86.9 6.9 %copy-start.14 = (bf16[1,128,1024]{1,2,0:T(8,128)(2,1)S(1)}, bf16[1,128,1024]{1,2,0:T(8,128)(2,1)}, u32[]{:S(2)}) copy-start(bf16[1,128,1024]{1,2,0:T(8,128)(2,1)} %copy.28) | copy-start | bytes 786436
  88.0 11.0 %collective-permute-start.12 = (bf16[128,512]{0,1:T(8,128)(2,1)S(1)}, bf16[128,512]{0,1:T(8,128)(2,1)S(1)}, u32[]{:S(2)}, u32[]{:S(2)}) collective-permute-start(bf16[128,512]{0,1:T(8,128)(2,1)S(1)} %get-tuple-element.23), channel_id=1, source_target_pairs={{4,0},{8,4},{12,8},{16,12},{20,16},{24,20},{28,24},{32,28},{36,32}... | collective-permute-start | bytes 393224 | tf_op jit(solution)/shard_map/ppermute | solution.py:15
  89.9 12.3 %collective-permute-start.13 = (bf16[128,512]{0,1:T(8,128)(2,1)S(1)}, bf16[128,512]{0,1:T(8,128)(2,1)S(1)}, u32[]{:S(2)}, u32[]{:S(2)}) collective-permute-start(bf16[128,512]{0,1:T(8,128)(2,1)S(1)} %get-tuple-element.26), channel_id=1, source_target_pairs={{8,0},{12,4},{16,8},{20,12},{24,16},{28,20},{32,24},{36,28},{40,32... | collective-permute-start | bytes 393224 | tf_op jit(solution)/shard_map/ppermute | solution.py:15
  91.2 13.3 %collective-permute-start.14 = (bf16[128,512]{0,1:T(8,128)(2,1)S(1)}, bf16[128,512]{0,1:T(8,128)(2,1)S(1)}, u32[]{:S(2)}, u32[]{:S(2)}) collective-permute-start(bf16[128,512]{0,1:T(8,128)(2,1)S(1)} %get-tuple-element.25), channel_id=1, source_target_pairs={{12,0},{16,4},{20,8},{24,12},{28,16},{32,20},{36,24},{40,28},{44,3... | collective-permute-start | bytes 393224 | tf_op jit(solution)/shard_map/ppermute | solution.py:15
  92.5 14.5 %collective-permute-start.15 = (bf16[128,512]{0,1:T(8,128)(2,1)S(1)}, bf16[128,512]{0,1:T(8,128)(2,1)S(1)}, u32[]{:S(2)}, u32[]{:S(2)}) collective-permute-start(bf16[128,512]{0,1:T(8,128)(2,1)S(1)} %get-tuple-element.24), channel_id=1, source_target_pairs={{16,0},{20,4},{24,8},{28,12},{32,16},{36,20},{40,24},{44,28},{48,3... | collective-permute-start | bytes 393224 | tf_op jit(solution)/shard_map/ppermute | solution.py:15
  108.1 4.6 %collective-permute-start.16 = (bf16[1024,256]{1,0:T(8,128)(2,1)}, bf16[1024,256]{1,0:T(8,128)(2,1)}, u32[]{:S(2)}, u32[]{:S(2)}) collective-permute-start(bf16[1024,256]{1,0:T(8,128)(2,1)} %convolution_convert_fusion), channel_id=1, source_target_pairs={{0,4},{4,0},{8,12},{12,8},{16,20},{20,16},{24,28},{28,24},{32,36},... | collective-permute-start | bytes 1572872 | tf_op jit(solution)/shard_map/ppermute | solution.py:20
  114.0 1.0 copy-start.3
  115.1 15.9 %collective-permute-start.17 = (bf16[512,256]{1,0:T(8,128)(2,1)S(1)}, bf16[512,256]{1,0:T(8,128)(2,1)}, u32[]{:S(2)}, u32[]{:S(2)}) collective-permute-start(bf16[512,256]{1,0:T(8,128)(2,1)S(1)} %slice.147), channel_id=1, source_target_pairs={{0,1},{1,0},{2,3},{3,2},{4,5},{5,4},{6,7},{7,6},{8,9},{9,8},{10,11... | collective-permute-start | bytes 786440 | tf_op jit(solution)/shard_map/ppermute | solution.py:20
  132.8 10.4 %collective-permute-start.18 = (bf16[256,256]{1,0:T(8,128)(2,1)}, bf16[256,256]{1,0:T(8,128)(2,1)}, u32[]{:S(2)}, u32[]{:S(2)}) collective-permute-start(bf16[256,256]{1,0:T(8,128)(2,1)} %select_convert_fusion), channel_id=1, source_target_pairs={{0,2},{1,3},{2,0},{3,1},{4,6},{5,7},{6,4},{7,5},{8,10},{9,11},{10,... | collective-permute-start | bytes 393224 | tf_op jit(solution)/shard_map/ppermute | solution.py:20
  144.1 0.7 copy-start.12
  144.9 5.0 %collective-permute-start.19 = (bf16[128,256]{1,0:T(8,128)(2,1)S(1)}, bf16[128,256]{1,0:T(8,128)(2,1)S(1)}, u32[]{:S(2)}, u32[]{:S(2)}) collective-permute-start(bf16[128,256]{1,0:T(8,128)(2,1)S(1)} %select_convert_fusion.1), channel_id=1, source_target_pairs={{0,16},{4,20},{8,24},{12,28},{16,0},{20,4},{24,8},{28,12},{32,48},... | collective-permute-start | bytes 196616 | tf_op jit(solution)/shard_map/ppermute | solution.py:20
  150.9 5.6 %collective-permute-start.20 = (bf16[64,256]{1,0:T(8,128)(2,1)S(1)}, bf16[64,256]{1,0:T(8,128)(2,1)S(1)}, u32[]{:S(2)}, u32[]{:S(2)}) collective-permute-start(bf16[64,256]{1,0:T(8,128)(2,1)S(1)} %select_convert_fusion.2), channel_id=1, source_target_pairs={{0,64},{4,68},{8,72},{12,76},{16,80},{20,84},{24,88},{28,92},{32,9... | collective-permute-start | bytes 98312 | tf_op jit(solution)/shard_map/ppermute | solution.py:20
  156.5 8.6 %collective-permute-start.21 = (bf16[64,256]{1,0:T(8,128)(2,1)S(1)}, bf16[64,256]{1,0:T(8,128)(2,1)S(1)}, u32[]{:S(2)}, u32[]{:S(2)}) collective-permute-start(bf16[64,256]{1,0:T(8,128)(2,1)S(1)} %add_convert_fusion.3), channel_id=1, source_target_pairs={{0,8},{4,12},{8,0},{12,4},{16,24},{20,28},{24,16},{28,20},{32,40},... | collective-permute-start | bytes 98312 | tf_op jit(solution)/shard_map/ppermute | solution.py:20
  165.1 6.2 %collective-permute-start.22 = (bf16[64,256]{1,0:T(8,128)(2,1)S(1)}, bf16[64,256]{1,0:T(8,128)(2,1)S(1)}, u32[]{:S(2)}, u32[]{:S(2)}) collective-permute-start(bf16[64,256]{1,0:T(8,128)(2,1)S(1)} %add_convert_fusion.2), channel_id=1, source_target_pairs={{0,32},{4,36},{8,40},{12,44},{16,48},{20,52},{24,56},{28,60},{32,0... | collective-permute-start | bytes 98312 | tf_op jit(solution)/shard_map/ppermute | solution.py:20
  171.3 7.2 %collective-permute-start.23 = (bf16[64,256]{1,0:T(8,128)(2,1)S(1)}, bf16[64,256]{1,0:T(8,128)(2,1)S(1)}, u32[]{:S(2)}, u32[]{:S(2)}) collective-permute-start(bf16[64,256]{1,0:T(8,128)(2,1)S(1)} %add_convert_fusion.1), channel_id=1, source_target_pairs={{0,128},{4,132},{8,136},{12,140},{16,144},{20,148},{24,152},{28,15... | collective-permute-start | bytes 98312 | tf_op jit(solution)/shard_map/ppermute | solution.py:20
  178.4 9.6 %collective-permute-start.24 = (bf16[64,256]{1,0:T(8,128)(2,1)S(1)}, bf16[64,256]{1,0:T(8,128)(2,1)S(1)}, u32[]{:S(2)}, u32[]{:S(2)}) collective-permute-start(bf16[64,256]{1,0:T(8,128)(2,1)S(1)} %add_convert_fusion), channel_id=1, source_target_pairs={{0,256},{4,260},{8,264},{12,268},{16,272},{20,276},{24,280},{28,28... | collective-permute-start | bytes 98312 | tf_op jit(solution)/shard_map/ppermute | solution.py:20
  186.8 8.7 %copy-start.2 = (bf16[1024,512]{1,0:T(8,128)(2,1)S(1)}, bf16[1024,512]{1,0:T(8,128)(2,1)}, u32[]{:S(2)}) copy-start(bf16[1024,512]{1,0:T(8,128)(2,1)} %copy-done.1) | copy-start | bytes 3145732
  188.1 23.2 %copy-start.5 = (bf16[256,1280]{1,0:T(8,128)(2,1)S(1)}, bf16[256,1280]{1,0:T(8,128)(2,1)}, u32[]{:S(2)}) copy-start(bf16[256,1280]{1,0:T(8,128)(2,1)} %copy-done.4) | copy-start | bytes 1966084
  188.1 23.2 %copy-start.7 = (bf16[256,1280]{1,0:T(8,128)(2,1)S(1)}, bf16[256,1280]{1,0:T(8,128)(2,1)}, u32[]{:S(2)}) copy-start(bf16[256,1280]{1,0:T(8,128)(2,1)} %copy-done.6) | copy-start | bytes 1966084
  188.1 23.2 %copy-start.9 = (bf16[256,1280]{1,0:T(8,128)(2,1)S(1)}, bf16[256,1280]{1,0:T(8,128)(2,1)}, u32[]{:S(2)}) copy-start(bf16[256,1280]{1,0:T(8,128)(2,1)} %copy-done.8) | copy-start | bytes 1966084
  188.1 23.2 %copy-start.11 = (bf16[256,1280]{1,0:T(8,128)(2,1)S(1)}, bf16[256,1280]{1,0:T(8,128)(2,1)}, u32[]{:S(2)}) copy-start(bf16[256,1280]{1,0:T(8,128)(2,1)} %copy-done.10) | copy-start | bytes 1966084
  188.1 5.1 %collective-permute-start.25 = (f32[64,256]{1,0:T(8,128)S(1)}, f32[64,256]{1,0:T(8,128)S(1)}, u32[]{:S(2)}, u32[]{:S(2)}) collective-permute-start(f32[64,256]{1,0:T(8,128)S(1)} %convert_add_fusion.2), channel_id=1, source_target_pairs={{0,64},{4,68},{8,72},{12,76},{16,80},{20,84},{24,88},{28,92},{32,9... | collective-permute-start | bytes 196616 | tf_op jit(solution)/shard_map/ppermute | solution.py:20
  193.3 5.7 %collective-permute-start.26 = (f32[128,256]{1,0:T(8,128)S(1)}, f32[128,256]{1,0:T(8,128)S(1)}, u32[]{:S(2)}, u32[]{:S(2)}) collective-permute-start(f32[128,256]{1,0:T(8,128)S(1)} %maximum_select_fusion.2), channel_id=1, source_target_pairs={{0,16},{4,20},{8,24},{12,28},{16,0},{20,4},{24,8},{28,12},{32,48},... | collective-permute-start | bytes 393224 | tf_op jit(solution)/shard_map/ppermute | solution.py:20
  199.0 13.8 %collective-permute-start.27 = (f32[256,256]{1,0:T(8,128)S(1)}, f32[256,256]{1,0:T(8,128)S(1)}, u32[]{:S(2)}, u32[]{:S(2)}) collective-permute-start(f32[256,256]{1,0:T(8,128)S(1)} %maximum_select_fusion.1), channel_id=1, source_target_pairs={{0,4},{4,0},{8,12},{12,8},{16,20},{20,16},{24,28},{28,24},{32,36},... | collective-permute-start | bytes 786440 | tf_op jit(solution)/shard_map/ppermute | solution.py:20
